TPU v7x, 256 devices: a whole 4x4x8 slice. The times are simulated.
256 devices in a mesh: dp: 8 (over x, core), ctx: 32 (over y, z).
Axes of the slice: x: 4, y: 4, z: 8, core: 2. Of those that a mesh axis runs over, the one named last changes fastest.
Arguments:
- tokens: bfloat16 [8, 8192, 1024], P('dp', 'ctx'), may hold values from -6 to 6
- log_decay: float32 [8, 8, 8192], P('dp', None, 'ctx'), may hold values from -2.2 to 0
- lengths: int32 [8, 2], P('dp'), may hold values from 1 to 5120, 8192 in all within a row
- label_ids: int32 [8, 8192], P('dp', 'ctx'), may hold values from 0 to 511
- w_query: bfloat16 [1024, 1024], replicated, may hold values from -0.1875 to 0.1875
- w_key: bfloat16 [1024, 1024], replicated, may hold values from -0.1875 to 0.1875
- w_value: bfloat16 [1024, 1024], replicated, may hold values from -0.1875 to 0.1875
- norm_gain: float32 [1024], replicated, may hold values from 0.1 to 1.9
- label_query: bfloat16 [512, 1024], replicated, may hold values from -24 to 24
- label_weight: bfloat16 [512, 1024], replicated, may hold values from -0.75 to 0.75
Outputs:
- retention_out: bfloat16 [8, 8192, 1024], P('dp', 'ctx')
- logits: float32 [8, 2, 512], P('dp')
- recording_loss: float32 [8, 2], P('dp')
- mean_loss: float32 [], replicated
Inputs may be any that keep to these rules, and one draw needn't show every extreme that they name: Row g lists the lengths of the 2 recordings packed in order into the 8192 tokens of group g; they sum to 8192.
All inputs are finite; a program needn't handle non-finite values.
Results may differ from a plain program's by a relative error of at most 0.0058.
The roundings to bfloat16 on the way count: a program that leaves them out, or rounds other values in their place, can miss the bound.
Values sent between devices are 32-bit elements; how exact they have to be, the bound alone decides.
No kernel may reach another device: no remote copies, remote signals or barrier semaphores. Data moves between devices by JAX's collectives and lax.ppermute only.
A program may use at most 128 MiB of HBM per device.

v0:
```python
import jax
import jax.numpy as jnp
from jax import lax
from jax.sharding import PartitionSpec as P

NEG_FILL = -1e30


def passed_along(x, axis, by):
    count = lax.axis_size(axis)
    pairs = [(i, i + by) for i in range(count) if 0 <= i + by < count]
    return lax.ppermute(x, axis, pairs)


def record_ids(length_row, positions):
    starts = jnp.cumsum(length_row) - length_row
    return jnp.sum((starts[:, None] <= positions[None, :]).astype(jnp.int32), axis=0) - 1


def local(
    tokens,
    log_decay,
    lengths,
    label_ids,
    w_query,
    w_key,
    w_value,
    norm_gain,
    label_query,
    label_weight,
):
    tok_rows = tokens.shape[1]
    model_width = tokens.shape[2]
    head_count = log_decay.shape[1]
    head_dim = model_width // head_count
    qk_scale = head_dim ** (-0.5)
    record_count = lengths.shape[1]
    label_count = label_query.shape[0]
    shard_start = lax.axis_index("ctx") * tok_rows
    local_pos = jnp.arange(tok_rows, dtype=jnp.int32)
    record = record_ids(lengths[0], shard_start + local_pos)
    before_rec = record_ids(lengths[0], jnp.reshape(shard_start - 1, (1,)))[0]
    features = tokens[0]
    queries = jnp.dot(features, w_query, preferred_element_type=jnp.float32).astype(jnp.bfloat16)
    key_rows = jnp.dot(features, w_key, preferred_element_type=jnp.float32).astype(jnp.bfloat16)
    value_rows = jnp.dot(features, w_value, preferred_element_type=jnp.float32).astype(jnp.bfloat16)
    decay_cum = jnp.cumsum(log_decay[0], axis=1)
    pair_mask = (local_pos[:, None] >= local_pos[None, :]) & (record[:, None] == record[None, :])
    linked = record == before_rec
    tail_rec = record == record[tok_rows - 1]

    def local_head(head_idx):
        q_head = lax.dynamic_slice_in_dim(queries, head_idx * head_dim, head_dim, 1)
        k_head = lax.dynamic_slice_in_dim(key_rows, head_idx * head_dim, head_dim, 1)
        v_head = lax.dynamic_slice_in_dim(value_rows, head_idx * head_dim, head_dim, 1)
        cum_head = lax.dynamic_index_in_dim(decay_cum, head_idx, 0, keepdims=False)
        scores = (
            jnp.einsum("td,sd->ts", q_head, k_head, preferred_element_type=jnp.float32) * qk_scale
        )
        decay_pair = jnp.exp(jnp.minimum(cum_head[:, None] - cum_head[None, :], 0.0))
        weights = jnp.where(pair_mask, scores * decay_pair, 0.0).astype(jnp.bfloat16)
        intra_sum = jnp.dot(weights, v_head, preferred_element_type=jnp.float32)
        k_decayed = (
            k_head.astype(jnp.float32)
            * jnp.where(tail_rec, jnp.exp(cum_head[tok_rows - 1] - cum_head), 0.0)[:, None]
        ).astype(jnp.bfloat16)
        local_state = jnp.dot(k_decayed.T, v_head, preferred_element_type=jnp.float32)
        carry_factor = jnp.where(linked[tok_rows - 1], jnp.exp(cum_head[tok_rows - 1]), 0.0)
        return (intra_sum, local_state, carry_factor)

    intra_all, local_state, carry_factor = lax.map(
        local_head, jnp.arange(head_count, dtype=jnp.int32)
    )

    def relay(turn_index, pair_state):
        outgoing, incoming = pair_state
        received = passed_along(outgoing, "ctx", 1)
        return (carry_factor[:, None, None] * received + local_state, received)

    outgoing, incoming = lax.fori_loop(
        0, lax.axis_size("ctx") - 1, relay, (local_state, jnp.zeros_like(local_state))
    )

    def finish_head(inputs):
        head_idx, intra_head, state_head = inputs
        q_head = lax.dynamic_slice_in_dim(queries, head_idx * head_dim, head_dim, 1)
        cum_head = lax.dynamic_index_in_dim(decay_cum, head_idx, 0, keepdims=False)
        q_decayed = q_head.astype(jnp.float32) * jnp.where(linked, jnp.exp(cum_head), 0.0)[:, None]
        total_out = (
            intra_head + jnp.dot(q_decayed, state_head, precision=lax.Precision.HIGH) * qk_scale
        )
        centred = total_out - jnp.mean(total_out, axis=1, keepdims=True)
        variance = jnp.mean(centred * centred, axis=1, keepdims=True)
        gain_head = lax.dynamic_slice_in_dim(norm_gain, head_idx * head_dim, head_dim, 0)
        return centred * lax.rsqrt(variance + 1e-05) * gain_head[None, :]

    normed = lax.map(finish_head, (jnp.arange(head_count, dtype=jnp.int32), intra_all, incoming))
    out_rows = jnp.transpose(normed, (1, 0, 2)).reshape(tok_rows, model_width).astype(jnp.bfloat16)
    member = record[None, :] == jnp.arange(record_count, dtype=jnp.int32)[:, None]
    member_float = member.astype(jnp.float32)

    def pool_head(head_idx):
        k_head = lax.dynamic_slice_in_dim(features, head_idx * head_dim, head_dim, 1)
        q_label = lax.dynamic_slice_in_dim(label_query, head_idx * head_dim, head_dim, 1)
        y_head = lax.dynamic_slice_in_dim(out_rows, head_idx * head_dim, head_dim, 1)
        w_head = lax.dynamic_slice_in_dim(label_weight, head_idx * head_dim, head_dim, 1)
        scores = (
            jnp.einsum("ld,td->lt", q_label, k_head, preferred_element_type=jnp.float32) * qk_scale
        )
        maxima = jnp.max(jnp.where(member[:, None, :], scores[None, :, :], NEG_FILL), axis=2)
        maxima_tok = jnp.sum(jnp.where(member[:, None, :], maxima[:, :, None], 0.0), axis=0)
        pool_weight = jnp.exp(scores - maxima_tok)
        label_value = jnp.einsum("ld,td->lt", w_head, y_head, preferred_element_type=jnp.float32)
        mass_part = jnp.einsum(
            "lt,rt->rl", pool_weight, member_float, precision=lax.Precision.HIGHEST
        )
        weighted = jnp.einsum(
            "lt,rt->rl", pool_weight * label_value, member_float, precision=lax.Precision.HIGHEST
        )
        return (maxima, mass_part, weighted)

    maxima, mass_part, weighted = lax.map(pool_head, jnp.arange(head_count, dtype=jnp.int32))
    label_hot = (label_ids[0][:, None] == jnp.arange(label_count, dtype=jnp.int32)[None, :]).astype(
        jnp.bfloat16
    )
    counts = jnp.dot(member.astype(jnp.bfloat16), label_hot, preferred_element_type=jnp.float32)
    top_score = lax.pmax(maxima, "ctx")
    rescale = jnp.exp(maxima - top_score)
    mass_all, weighted_all, counts_all = lax.psum(
        (mass_part * rescale, weighted * rescale, counts), "ctx"
    )
    logits = jnp.sum(weighted_all / mass_all, axis=0)
    target = (counts_all + 0.5) / (lengths[0].astype(jnp.float32)[:, None] + 1.0)
    rec_loss = jnp.mean(jax.nn.softplus(logits) - target * logits, axis=1)
    mean_loss = lax.psum(jnp.sum(rec_loss), "dp") / (lax.axis_size("dp") * record_count)
    return (out_rows[None], logits[None], rec_loss[None], mean_loss)


def solution(mesh):
    return jax.shard_map(
        local,
        mesh=mesh,
        in_specs=(
            P("dp", "ctx", None),
            P("dp", None, "ctx"),
            P("dp", None),
            P("dp", "ctx"),
            P(),
            P(),
            P(),
            P(),
            P(),
            P(),
        ),
        out_specs=(P("dp", "ctx", None), P("dp", None, None), P("dp", None), P()),
        check_vma=False,
    )
```

profile of v0, /device:TPU:1, one launch (start us, length us, event | category | flops | bytes accessed | tf_op | source)
XLA Modules:
  0.0 1003.7 jit_solution(2532073772796337082)
XLA Ops:
  19.6 74.5 %while.55 = (s32[]{:T(128)}, f32[8,256,128]{2,1,0:T(8,128)}, f32[8,128,128]{2,1,0:T(8,128)S(1)}, f32[8]{0:T(128)S(1)}, s32[8]{0:T(128)S(1)}, /*index=5*/bf16[256...) while((s32[]{:T(128)}, f32[8,256,128]{2,1,0:T(8,128)}, ...), condition=%wide.region_6.7_spmd.clone, body=%wide.region_5.6_spmd.clone.sunk | while | flops 42631688 | bytes 537676 | solution.py:71
  95.7 466.1 %while.53 = (s32[]{:T(128)}, f32[8,128,128]{2,1,0:T(8,128)}, f32[8,128,128]{2,1,0:T(8,128)}, f32[8]{0:T(128)S(1)}, f32[8,128,128]{2,1,0:T(8,128)S(1)}, /*index=5*/s32[]{:T(128)}) while((s32[]{:T(128)}, f32[8,128,128]{2,1,0:T(8,128)}, f32[8,128,128]{2,1,0:T(8,128)}, f32[8]{0:T(128)S(1)}, f32[8,128,128]{2,1,0:T(8,128)S(1)}, ...), condition=%wide.region_8.9_spmd, body=%wide.region_7.8_spmd.sunk | while | flops 262146 | bytes 5767337 | solution.py:80
  100.1 10.9 %collective-permute-done = f32[8,128,128]{2,1,0:T(8,128)S(1)} collective-permute-done((f32[8,128,128]{2,1,0:T(8,128)}, f32[8,128,128]{2,1,0:T(8,128)S(1)}, u32[]{:S(2)}, u32[]{:S(2)}) %collective-permute-start) | collective-permute-done | bytes 524320 | tf_op jit(solution)/shard_map/while/body/eval_jaxpr/ppermute | solution.py:12
  116.0 9.9 collective-permute-done
  130.9 9.0 collective-permute-done
  144.9 8.1 collective-permute-done
  159.1 7.2 collective-permute-done
  172.5 6.4 collective-permute-done
  185.1 6.4 collective-permute-done
  197.7 6.4 collective-permute-done
  210.3 6.8 collective-permute-done
  223.4 7.9 collective-permute-done
  237.8 8.9 collective-permute-done
  253.5 10.0 collective-permute-done
  270.2 11.0 %collective-permute-done = f32[8,128,128]{2,1,0:T(8,128)S(1)} collective-permute-done((f32[8,128,128]{2,1,0:T(8,128)}, f32[8,128,128]{2,1,0:T(8,128)S(1)}, u32[]{:S(2)}, u32[]{:S(2)}) %collective-permute-start) | collective-permute-done | bytes 524320 | tf_op jit(solution)/shard_map/while/body/eval_jaxpr/ppermute | solution.py:12
  288.1 11.8 %collective-permute-done = f32[8,128,128]{2,1,0:T(8,128)S(1)} collective-permute-done((f32[8,128,128]{2,1,0:T(8,128)}, f32[8,128,128]{2,1,0:T(8,128)S(1)}, u32[]{:S(2)}, u32[]{:S(2)}) %collective-permute-start) | collective-permute-done | bytes 524320 | tf_op jit(solution)/shard_map/while/body/eval_jaxpr/ppermute | solution.py:12
  306.2 10.7 %collective-permute-done = f32[8,128,128]{2,1,0:T(8,128)S(1)} collective-permute-done((f32[8,128,128]{2,1,0:T(8,128)}, f32[8,128,128]{2,1,0:T(8,128)S(1)}, u32[]{:S(2)}, u32[]{:S(2)}) %collective-permute-start) | collective-permute-done | bytes 524320 | tf_op jit(solution)/shard_map/while/body/eval_jaxpr/ppermute | solution.py:12
  322.5 9.4 collective-permute-done
  337.8 8.4 collective-permute-done
  352.5 7.5 collective-permute-done
  366.2 6.6 collective-permute-done
  379.0 6.4 collective-permute-done
  386.3 6.2 collective-permute-start
  392.5 6.4 collective-permute-done
  405.3 6.4 collective-permute-done
  412.7 6.8 collective-permute-start
  419.5 6.4 collective-permute-done
  426.9 6.1 collective-permute-start
  433.0 6.5 collective-permute-done
  440.5 6.1 collective-permute-start
  446.7 7.3 collective-permute-done
  454.9 6.1 collective-permute-start
  461.1 8.1 collective-permute-done
  470.1 6.1 collective-permute-start
  476.3 8.9 collective-permute-done
  486.1 6.1 collective-permute-start
  492.2 9.6 collective-permute-done
  502.8 7.3 collective-permute-start
  510.2 10.7 %collective-permute-done = f32[8,128,128]{2,1,0:T(8,128)S(1)} collective-permute-done((f32[8,128,128]{2,1,0:T(8,128)}, f32[8,128,128]{2,1,0:T(8,128)S(1)}, u32[]{:S(2)}, u32[]{:S(2)}) %collective-permute-start) | collective-permute-done | bytes 524320 | tf_op jit(solution)/shard_map/while/body/eval_jaxpr/ppermute | solution.py:12
  521.9 7.6 collective-permute-start
  529.5 11.9 %collective-permute-done = f32[8,128,128]{2,1,0:T(8,128)S(1)} collective-permute-done((f32[8,128,128]{2,1,0:T(8,128)}, f32[8,128,128]{2,1,0:T(8,128)S(1)}, u32[]{:S(2)}, u32[]{:S(2)}) %collective-permute-start) | collective-permute-done | bytes 524320 | tf_op jit(solution)/shard_map/while/body/eval_jaxpr/ppermute | solution.py:12
  542.3 7.6 collective-permute-start
  549.9 10.9 %collective-permute-done = f32[8,128,128]{2,1,0:T(8,128)S(1)} collective-permute-done((f32[8,128,128]{2,1,0:T(8,128)}, f32[8,128,128]{2,1,0:T(8,128)S(1)}, u32[]{:S(2)}, u32[]{:S(2)}) %collective-permute-start) | collective-permute-done | bytes 524320 | tf_op jit(solution)/shard_map/while/body/eval_jaxpr/ppermute | solution.py:12
  561.8 55.7 %while.54 = (s32[]{:T(128)}, bf16[8,256,128]{1,2,0:T(8,128)(2,1)}, f32[8,256,128]{2,1,0:T(8,128)}, s32[8]{0:T(128)S(1)}, bf16[256,1024]{1,0:T(8,128)(2,1)}, /*in...) while((s32[]{:T(128)}, bf16[8,256,128]{1,2,0:T(8,128)(2,1)}, ...), condition=%wide.region_12.13_spmd, body=%wide.region_9.12_spmd.sunk | while | flops 25526792 | bytes 1328113 | solution.py:97
  617.6 41.3 %while.56 = (s32[]{:T(128)}, f32[8,2,512]{2,1,0:T(2,128)S(1)}, f32[8,2,512]{2,1,0:T(2,128)S(1)}, f32[8,2,512]{2,1,0:T(2,128)S(1)}, s32[8]{0:T(128)S(1)}, /*index...) while((s32[]{:T(128)}, f32[8,2,512]{2,1,0:T(2,128)S(1)}, ...), condition=%wide.region_16.17_spmd.clone.clone, body=%wide.region_13.16_spmd.clone.clone.sunk | while | flops 74843648 | bytes 5143243 | solution.py:122
  658.9 125.8 %pmax.7 = f32[8,2,512]{2,1,0:T(2,128)S(1)} all-reduce(f32[8,2,512]{2,1,0:T(2,128)S(1)} %get-tuple-element.206), channel_id=1, replica_groups=mesh['dp'=8,'ctx'=32] {'ctx'}, use_global_device_ids=true, to_apply=%region_17.18 | all-reduce | flops 8192 | bytes 65536 | tf_op jit(solution)/shard_map/pmax | solution.py:127
  788.3 186.9 %all-reduce.3.cloned.1.call-done = (f32[8,2,512]{2,1,0:T(2,128)}, f32[8,2,512]{2,1,0:T(2,128)}, f32[2,512]{1,0:T(2,128)}) async-done(((f32[8,2,512]{2,1,0:T(2,128)}, f32[8,2,512]{2,1,0:T(2,128)}, f32[2,512]{1,0:T(2,128)}), (f32[8,2,512]{2,1,0:T(2,128)}, f32[8,2,512]{2,1,0:T(2,128)}, f32[2,512]{1,0:T(2,128)})) %all-reduce.3.cloned.1.call-update) | async-done | bytes 69648 | tf_op jit(solution)/shard_map/psum | solution.py:129
  977.9 17.2 %psum.31 = f32[]{:T(128)} all-reduce(f32[]{:T(128)} %get-tuple-element.395), channel_id=1, replica_groups=mesh['dp'=8,'ctx'=32] {'dp'}, use_global_device_ids=true, to_apply=%region_24.25 | all-reduce | flops 1 | bytes 8 | tf_op jit(solution)/shard_map/psum | solution.py:135
  (389 shorter events, 271.3 us)
Async XLA Ops:
  7.2 5.9 copy-start
  7.2 8.6 copy-start.2
  7.2 967.9 %all-reduce.3.cloned.1.call-start = ((), (), s32[]{:S(2)}) async-start(), calls=%async_computation | async-start | bytes 139264 | tf_op jit(solution)/shard_map/psum | solution.py:129
  13.0 2.8 copy-start.5
  15.8 1.6 copy-start.6
  95.7 15.3 %collective-permute-start = (f32[8,128,128]{2,1,0:T(8,128)}, f32[8,128,128]{2,1,0:T(8,128)S(1)}, u32[]{:S(2)}, u32[]{:S(2)}) collective-permute-start(f32[8,128,128]{2,1,0:T(8,128)} %get-tuple-element.685), channel_id=1, source_target_pairs={{0,1},{1,2},{2,3},{3,4},{4,5},{5,6},{6,7},{7,8},{8,9},{9,10},{10,1... | collective-permute-start | bytes 1572872 | tf_op jit(solution)/shard_map/while/body/eval_jaxpr/ppermute | solution.py:12
  111.0 1.0 copy-start.1
  111.9 14.0 %collective-permute-start = (f32[8,128,128]{2,1,0:T(8,128)}, f32[8,128,128]{2,1,0:T(8,128)S(1)}, u32[]{:S(2)}, u32[]{:S(2)}) collective-permute-start(f32[8,128,128]{2,1,0:T(8,128)} %get-tuple-element.685), channel_id=1, source_target_pairs={{0,1},{1,2},{2,3},{3,4},{4,5},{5,6},{6,7},{7,8},{8,9},{9,10},{10,1... | collective-permute-start | bytes 1572872 | tf_op jit(solution)/shard_map/while/body/eval_jaxpr/ppermute | solution.py:12
  126.9 13.0 %collective-permute-start = (f32[8,128,128]{2,1,0:T(8,128)}, f32[8,128,128]{2,1,0:T(8,128)S(1)}, u32[]{:S(2)}, u32[]{:S(2)}) collective-permute-start(f32[8,128,128]{2,1,0:T(8,128)} %get-tuple-element.685), channel_id=1, source_target_pairs={{0,1},{1,2},{2,3},{3,4},{4,5},{5,6},{6,7},{7,8},{8,9},{9,10},{10,1... | collective-permute-start | bytes 1572872 | tf_op jit(solution)/shard_map/while/body/eval_jaxpr/ppermute | solution.py:12
  140.9 12.1 %collective-permute-start = (f32[8,128,128]{2,1,0:T(8,128)}, f32[8,128,128]{2,1,0:T(8,128)S(1)}, u32[]{:S(2)}, u32[]{:S(2)}) collective-permute-start(f32[8,128,128]{2,1,0:T(8,128)} %get-tuple-element.685), channel_id=1, source_target_pairs={{0,1},{1,2},{2,3},{3,4},{4,5},{5,6},{6,7},{7,8},{8,9},{9,10},{10,1... | collective-permute-start | bytes 1572872 | tf_op jit(solution)/shard_map/while/body/eval_jaxpr/ppermute | solution.py:12
  153.0 1.0 copy-start.1
  154.0 12.2 %collective-permute-start = (f32[8,128,128]{2,1,0:T(8,128)}, f32[8,128,128]{2,1,0:T(8,128)S(1)}, u32[]{:S(2)}, u32[]{:S(2)}) collective-permute-start(f32[8,128,128]{2,1,0:T(8,128)} %get-tuple-element.685), channel_id=1, source_target_pairs={{0,1},{1,2},{2,3},{3,4},{4,5},{5,6},{6,7},{7,8},{8,9},{9,10},{10,1... | collective-permute-start | bytes 1572872 | tf_op jit(solution)/shard_map/while/body/eval_jaxpr/ppermute | solution.py:12
  166.3 1.0 copy-start.1
  167.3 11.6 %collective-permute-start = (f32[8,128,128]{2,1,0:T(8,128)}, f32[8,128,128]{2,1,0:T(8,128)S(1)}, u32[]{:S(2)}, u32[]{:S(2)}) collective-permute-start(f32[8,128,128]{2,1,0:T(8,128)} %get-tuple-element.685), channel_id=1, source_target_pairs={{0,1},{1,2},{2,3},{3,4},{4,5},{5,6},{6,7},{7,8},{8,9},{9,10},{10,1... | collective-permute-start | bytes 1572872 | tf_op jit(solution)/shard_map/while/body/eval_jaxpr/ppermute | solution.py:12
  179.9 11.6 %collective-permute-start = (f32[8,128,128]{2,1,0:T(8,128)}, f32[8,128,128]{2,1,0:T(8,128)S(1)}, u32[]{:S(2)}, u32[]{:S(2)}) collective-permute-start(f32[8,128,128]{2,1,0:T(8,128)} %get-tuple-element.685), channel_id=1, source_target_pairs={{0,1},{1,2},{2,3},{3,4},{4,5},{5,6},{6,7},{7,8},{8,9},{9,10},{10,1... | collective-permute-start | bytes 1572872 | tf_op jit(solution)/shard_map/while/body/eval_jaxpr/ppermute | solution.py:12
  191.5 1.0 copy-start.1
  192.5 11.6 %collective-permute-start = (f32[8,128,128]{2,1,0:T(8,128)}, f32[8,128,128]{2,1,0:T(8,128)S(1)}, u32[]{:S(2)}, u32[]{:S(2)}) collective-permute-start(f32[8,128,128]{2,1,0:T(8,128)} %get-tuple-element.685), channel_id=1, source_target_pairs={{0,1},{1,2},{2,3},{3,4},{4,5},{5,6},{6,7},{7,8},{8,9},{9,10},{10,1... | collective-permute-start | bytes 1572872 | tf_op jit(solution)/shard_map/while/body/eval_jaxpr/ppermute | solution.py:12
  205.1 12.0 %collective-permute-start = (f32[8,128,128]{2,1,0:T(8,128)}, f32[8,128,128]{2,1,0:T(8,128)S(1)}, u32[]{:S(2)}, u32[]{:S(2)}) collective-permute-start(f32[8,128,128]{2,1,0:T(8,128)} %get-tuple-element.685), channel_id=1, source_target_pairs={{0,1},{1,2},{2,3},{3,4},{4,5},{5,6},{6,7},{7,8},{8,9},{9,10},{10,1... | collective-permute-start | bytes 1572872 | tf_op jit(solution)/shard_map/while/body/eval_jaxpr/ppermute | solution.py:12
  218.1 13.1 %collective-permute-start = (f32[8,128,128]{2,1,0:T(8,128)}, f32[8,128,128]{2,1,0:T(8,128)S(1)}, u32[]{:S(2)}, u32[]{:S(2)}) collective-permute-start(f32[8,128,128]{2,1,0:T(8,128)} %get-tuple-element.685), channel_id=1, source_target_pairs={{0,1},{1,2},{2,3},{3,4},{4,5},{5,6},{6,7},{7,8},{8,9},{9,10},{10,1... | collective-permute-start | bytes 1572872 | tf_op jit(solution)/shard_map/while/body/eval_jaxpr/ppermute | solution.py:12
  232.2 14.4 %collective-permute-start = (f32[8,128,128]{2,1,0:T(8,128)}, f32[8,128,128]{2,1,0:T(8,128)S(1)}, u32[]{:S(2)}, u32[]{:S(2)}) collective-permute-start(f32[8,128,128]{2,1,0:T(8,128)} %get-tuple-element.685), channel_id=1, source_target_pairs={{0,1},{1,2},{2,3},{3,4},{4,5},{5,6},{6,7},{7,8},{8,9},{9,10},{10,1... | collective-permute-start | bytes 1572872 | tf_op jit(solution)/shard_map/while/body/eval_jaxpr/ppermute | solution.py:12
  247.6 15.8 %collective-permute-start = (f32[8,128,128]{2,1,0:T(8,128)}, f32[8,128,128]{2,1,0:T(8,128)S(1)}, u32[]{:S(2)}, u32[]{:S(2)}) collective-permute-start(f32[8,128,128]{2,1,0:T(8,128)} %get-tuple-element.685), channel_id=1, source_target_pairs={{0,1},{1,2},{2,3},{3,4},{4,5},{5,6},{6,7},{7,8},{8,9},{9,10},{10,1... | collective-permute-start | bytes 1572872 | tf_op jit(solution)/shard_map/while/body/eval_jaxpr/ppermute | solution.py:12
  264.4 16.9 %collective-permute-start = (f32[8,128,128]{2,1,0:T(8,128)}, f32[8,128,128]{2,1,0:T(8,128)S(1)}, u32[]{:S(2)}, u32[]{:S(2)}) collective-permute-start(f32[8,128,128]{2,1,0:T(8,128)} %get-tuple-element.685), channel_id=1, source_target_pairs={{0,1},{1,2},{2,3},{3,4},{4,5},{5,6},{6,7},{7,8},{8,9},{9,10},{10,1... | collective-permute-start | bytes 1572872 | tf_op jit(solution)/shard_map/while/body/eval_jaxpr/ppermute | solution.py:12
  282.3 17.6 %collective-permute-start = (f32[8,128,128]{2,1,0:T(8,128)}, f32[8,128,128]{2,1,0:T(8,128)S(1)}, u32[]{:S(2)}, u32[]{:S(2)}) collective-permute-start(f32[8,128,128]{2,1,0:T(8,128)} %get-tuple-element.685), channel_id=1, source_target_pairs={{0,1},{1,2},{2,3},{3,4},{4,5},{5,6},{6,7},{7,8},{8,9},{9,10},{10,1... | collective-permute-start | bytes 1572872 | tf_op jit(solution)/shard_map/while/body/eval_jaxpr/ppermute | solution.py:12
  299.9 1.0 copy-start.1
  300.9 16.0 %collective-permute-start = (f32[8,128,128]{2,1,0:T(8,128)}, f32[8,128,128]{2,1,0:T(8,128)S(1)}, u32[]{:S(2)}, u32[]{:S(2)}) collective-permute-start(f32[8,128,128]{2,1,0:T(8,128)} %get-tuple-element.685), channel_id=1, source_target_pairs={{0,1},{1,2},{2,3},{3,4},{4,5},{5,6},{6,7},{7,8},{8,9},{9,10},{10,1... | collective-permute-start | bytes 1572872 | tf_op jit(solution)/shard_map/while/body/eval_jaxpr/ppermute | solution.py:12
  317.9 14.0 %collective-permute-start = (f32[8,128,128]{2,1,0:T(8,128)}, f32[8,128,128]{2,1,0:T(8,128)S(1)}, u32[]{:S(2)}, u32[]{:S(2)}) collective-permute-start(f32[8,128,128]{2,1,0:T(8,128)} %get-tuple-element.685), channel_id=1, source_target_pairs={{0,1},{1,2},{2,3},{3,4},{4,5},{5,6},{6,7},{7,8},{8,9},{9,10},{10,1... | collective-permute-start | bytes 1572872 | tf_op jit(solution)/shard_map/while/body/eval_jaxpr/ppermute | solution.py:12
  332.9 13.4 %collective-permute-start = (f32[8,128,128]{2,1,0:T(8,128)}, f32[8,128,128]{2,1,0:T(8,128)S(1)}, u32[]{:S(2)}, u32[]{:S(2)}) collective-permute-start(f32[8,128,128]{2,1,0:T(8,128)} %get-tuple-element.685), channel_id=1, source_target_pairs={{0,1},{1,2},{2,3},{3,4},{4,5},{5,6},{6,7},{7,8},{8,9},{9,10},{10,1... | collective-permute-start | bytes 1572872 | tf_op jit(solution)/shard_map/while/body/eval_jaxpr/ppermute | solution.py:12
  346.2 1.0 copy-start.1
  347.2 12.7 %collective-permute-start = (f32[8,128,128]{2,1,0:T(8,128)}, f32[8,128,128]{2,1,0:T(8,128)S(1)}, u32[]{:S(2)}, u32[]{:S(2)}) collective-permute-start(f32[8,128,128]{2,1,0:T(8,128)} %get-tuple-element.685), channel_id=1, source_target_pairs={{0,1},{1,2},{2,3},{3,4},{4,5},{5,6},{6,7},{7,8},{8,9},{9,10},{10,1... | collective-permute-start | bytes 1572872 | tf_op jit(solution)/shard_map/while/body/eval_jaxpr/ppermute | solution.py:12
  360.0 1.0 copy-start.1
  360.9 11.8 %collective-permute-start = (f32[8,128,128]{2,1,0:T(8,128)}, f32[8,128,128]{2,1,0:T(8,128)S(1)}, u32[]{:S(2)}, u32[]{:S(2)}) collective-permute-start(f32[8,128,128]{2,1,0:T(8,128)} %get-tuple-element.685), channel_id=1, source_target_pairs={{0,1},{1,2},{2,3},{3,4},{4,5},{5,6},{6,7},{7,8},{8,9},{9,10},{10,1... | collective-permute-start | bytes 1572872 | tf_op jit(solution)/shard_map/while/body/eval_jaxpr/ppermute | solution.py:12
  372.7 1.0 copy-start.1
  373.7 11.6 %collective-permute-start = (f32[8,128,128]{2,1,0:T(8,128)}, f32[8,128,128]{2,1,0:T(8,128)S(1)}, u32[]{:S(2)}, u32[]{:S(2)}) collective-permute-start(f32[8,128,128]{2,1,0:T(8,128)} %get-tuple-element.685), channel_id=1, source_target_pairs={{0,1},{1,2},{2,3},{3,4},{4,5},{5,6},{6,7},{7,8},{8,9},{9,10},{10,1... | collective-permute-start | bytes 1572872 | tf_op jit(solution)/shard_map/while/body/eval_jaxpr/ppermute | solution.py:12
  386.3 12.6 %collective-permute-start = (f32[8,128,128]{2,1,0:T(8,128)}, f32[8,128,128]{2,1,0:T(8,128)S(1)}, u32[]{:S(2)}, u32[]{:S(2)}) collective-permute-start(f32[8,128,128]{2,1,0:T(8,128)} %get-tuple-element.685), channel_id=1, source_target_pairs={{0,1},{1,2},{2,3},{3,4},{4,5},{5,6},{6,7},{7,8},{8,9},{9,10},{10,1... | collective-permute-start | bytes 1572872 | tf_op jit(solution)/shard_map/while/body/eval_jaxpr/ppermute | solution.py:12
  399.9 11.8 %collective-permute-start = (f32[8,128,128]{2,1,0:T(8,128)}, f32[8,128,128]{2,1,0:T(8,128)S(1)}, u32[]{:S(2)}, u32[]{:S(2)}) collective-permute-start(f32[8,128,128]{2,1,0:T(8,128)} %get-tuple-element.685), channel_id=1, source_target_pairs={{0,1},{1,2},{2,3},{3,4},{4,5},{5,6},{6,7},{7,8},{8,9},{9,10},{10,1... | collective-permute-start | bytes 1572872 | tf_op jit(solution)/shard_map/while/body/eval_jaxpr/ppermute | solution.py:12
  411.7 1.0 copy-start.1
  412.7 13.2 %collective-permute-start = (f32[8,128,128]{2,1,0:T(8,128)}, f32[8,128,128]{2,1,0:T(8,128)S(1)}, u32[]{:S(2)}, u32[]{:S(2)}) collective-permute-start(f32[8,128,128]{2,1,0:T(8,128)} %get-tuple-element.685), channel_id=1, source_target_pairs={{0,1},{1,2},{2,3},{3,4},{4,5},{5,6},{6,7},{7,8},{8,9},{9,10},{10,1... | collective-permute-start | bytes 1572872 | tf_op jit(solution)/shard_map/while/body/eval_jaxpr/ppermute | solution.py:12
  426.9 12.6 %collective-permute-start = (f32[8,128,128]{2,1,0:T(8,128)}, f32[8,128,128]{2,1,0:T(8,128)S(1)}, u32[]{:S(2)}, u32[]{:S(2)}) collective-permute-start(f32[8,128,128]{2,1,0:T(8,128)} %get-tuple-element.685), channel_id=1, source_target_pairs={{0,1},{1,2},{2,3},{3,4},{4,5},{5,6},{6,7},{7,8},{8,9},{9,10},{10,1... | collective-permute-start | bytes 1572872 | tf_op jit(solution)/shard_map/while/body/eval_jaxpr/ppermute | solution.py:12
  440.5 13.4 %collective-permute-start = (f32[8,128,128]{2,1,0:T(8,128)}, f32[8,128,128]{2,1,0:T(8,128)S(1)}, u32[]{:S(2)}, u32[]{:S(2)}) collective-permute-start(f32[8,128,128]{2,1,0:T(8,128)} %get-tuple-element.685), channel_id=1, source_target_pairs={{0,1},{1,2},{2,3},{3,4},{4,5},{5,6},{6,7},{7,8},{8,9},{9,10},{10,1... | collective-permute-start | bytes 1572872 | tf_op jit(solution)/shard_map/while/body/eval_jaxpr/ppermute | solution.py:12
  454.9 14.2 %collective-permute-start = (f32[8,128,128]{2,1,0:T(8,128)}, f32[8,128,128]{2,1,0:T(8,128)S(1)}, u32[]{:S(2)}, u32[]{:S(2)}) collective-permute-start(f32[8,128,128]{2,1,0:T(8,128)} %get-tuple-element.685), channel_id=1, source_target_pairs={{0,1},{1,2},{2,3},{3,4},{4,5},{5,6},{6,7},{7,8},{8,9},{9,10},{10,1... | collective-permute-start | bytes 1572872 | tf_op jit(solution)/shard_map/while/body/eval_jaxpr/ppermute | solution.py:12
  470.1 15.0 %collective-permute-start = (f32[8,128,128]{2,1,0:T(8,128)}, f32[8,128,128]{2,1,0:T(8,128)S(1)}, u32[]{:S(2)}, u32[]{:S(2)}) collective-permute-start(f32[8,128,128]{2,1,0:T(8,128)} %get-tuple-element.685), channel_id=1, source_target_pairs={{0,1},{1,2},{2,3},{3,4},{4,5},{5,6},{6,7},{7,8},{8,9},{9,10},{10,1... | collective-permute-start | bytes 1572872 | tf_op jit(solution)/shard_map/while/body/eval_jaxpr/ppermute | solution.py:12
  486.1 15.8 %collective-permute-start = (f32[8,128,128]{2,1,0:T(8,128)}, f32[8,128,128]{2,1,0:T(8,128)S(1)}, u32[]{:S(2)}, u32[]{:S(2)}) collective-permute-start(f32[8,128,128]{2,1,0:T(8,128)} %get-tuple-element.685), channel_id=1, source_target_pairs={{0,1},{1,2},{2,3},{3,4},{4,5},{5,6},{6,7},{7,8},{8,9},{9,10},{10,1... | collective-permute-start | bytes 1572872 | tf_op jit(solution)/shard_map/while/body/eval_jaxpr/ppermute | solution.py:12
  502.8 18.0 %collective-permute-start = (f32[8,128,128]{2,1,0:T(8,128)}, f32[8,128,128]{2,1,0:T(8,128)S(1)}, u32[]{:S(2)}, u32[]{:S(2)}) collective-permute-start(f32[8,128,128]{2,1,0:T(8,128)} %get-tuple-element.685), channel_id=1, source_target_pairs={{0,1},{1,2},{2,3},{3,4},{4,5},{5,6},{6,7},{7,8},{8,9},{9,10},{10,1... | collective-permute-start | bytes 1572872 | tf_op jit(solution)/shard_map/while/body/eval_jaxpr/ppermute | solution.py:12
  521.9 19.5 %collective-permute-start = (f32[8,128,128]{2,1,0:T(8,128)}, f32[8,128,128]{2,1,0:T(8,128)S(1)}, u32[]{:S(2)}, u32[]{:S(2)}) collective-permute-start(f32[8,128,128]{2,1,0:T(8,128)} %get-tuple-element.685), channel_id=1, source_target_pairs={{0,1},{1,2},{2,3},{3,4},{4,5},{5,6},{6,7},{7,8},{8,9},{9,10},{10,1... | collective-permute-start | bytes 1572872 | tf_op jit(solution)/shard_map/while/body/eval_jaxpr/ppermute | solution.py:12
  542.3 18.5 %collective-permute-start = (f32[8,128,128]{2,1,0:T(8,128)}, f32[8,128,128]{2,1,0:T(8,128)S(1)}, u32[]{:S(2)}, u32[]{:S(2)}) collective-permute-start(f32[8,128,128]{2,1,0:T(8,128)} %get-tuple-element.685), channel_id=1, source_target_pairs={{0,1},{1,2},{2,3},{3,4},{4,5},{5,6},{6,7},{7,8},{8,9},{9,10},{10,1... | collective-permute-start | bytes 1572872 | tf_op jit(solution)/shard_map/while/body/eval_jaxpr/ppermute | solution.py:12
  617.6 167.1 %copy-start.7 = (s32[1,256]{1,0:T(1,128)S(1)}, s32[1,256]{1,0:T(1,128)}, u32[]{:S(2)}) copy-start(s32[1,256]{1,0:T(1,128)} %param.21) | copy-start | bytes 3076
  617.6 168.6 %copy-start.4 = (s32[1,2]{1,0:T(1,128)S(1)}, s32[1,2]{1,0:T(1,128)}, u32[]{:S(2)}) copy-start(s32[1,2]{1,0:T(1,128)} %param.20) | copy-start | bytes 28
  975.9 19.8 %copy-start.3 = (f32[2,512]{1,0:T(2,128)}, f32[2,512]{1,0:T(2,128)S(1)}, u32[]{:S(2)}) copy-start(f32[2,512]{1,0:T(2,128)S(1)} %divide_reduce_fusion) | copy-start | bytes 12292
  (22 other events, 21.6 us)
Sparse Core Ops, SparseCore 0:
  786.3 188.7 all-reduce.2
where the time goes:
time: 1010 us; the launch traced here: 1000 us
  waiting for transfers between devices  449 us (44%)
  starting transfers between devices  173 us (17%)
  blocking collectives  143 us (14%)
  matrix products  66.9 us (7%)
  loops' own time  57.3 us (6%)
  other arithmetic  53.2 us (5%)
  local copies, waits for them, and re-layouts  44.5 us (4%)
  between operations  16.6 us (2%)
    ppermute x31, waiting for transfers between devices, passed_along(): return lax.ppermute(x, axis, pairs)  263 us
    psum x1, waiting for transfers between devices, local(): lax.psum((mass_part * rescale, weighted * rescale, counts), 'ctx')  187 us
    ppermute x31, starting transfers between devices, passed_along(): return lax.ppermute(x, axis, pairs)  173 us
    pmax x1, blocking collectives, local(): top_score = lax.pmax(maxima, 'ctx')  126 us
    add x31, other arithmetic, relay(): return (carry_factor[:, None, None] * received + local_state, received)  30.3 us
    another operation x1, loops' own time, local(): lax.map(local_head, jnp.arange(head_count, dtype=jnp.int32))  30.3 us
    another operation x1, loops' own time, local(): lax.map(finish_head, (jnp.arange(head_count, dtype=jnp.int32), intra_all,...  21.1 us
  transfers between devices with their start and end apart: 32, of which 32 were waited for; matrix products, arithmetic and copies ran while one was open for 0% of the time, Pallas kernels for 0%

commit v1 on v0

v1 whole, which is shorter than its diff:
```python
import jax
import jax.numpy as jnp
from jax import lax
from jax.sharding import PartitionSpec as P

NEG_FILL = -1e30


def shifted(x, axis, by):
    count = lax.axis_size(axis)
    pairs = [(i, i + by) for i in range(count) if 0 <= i + by < count]
    return lax.ppermute(x, axis, pairs)


def swapped(x, axis, bit):
    count = lax.axis_size(axis)
    return lax.ppermute(x, axis, [(i, i ^ bit) for i in range(count)])


def butterfly_bits(axis):
    count = lax.axis_size(axis)
    assert count & (count - 1) == 0
    bits = []
    bit = 1
    while bit < count:
        bits.append(bit)
        bit *= 2
    return bits


def record_ids(length_row, positions):
    starts = jnp.cumsum(length_row) - length_row
    return jnp.sum((starts[:, None] <= positions[None, :]).astype(jnp.int32), axis=0) - 1


def exclusive_state_scan(local_state, carry, axis):
    head_count, head_dim, _ = local_state.shape
    count = lax.axis_size(axis)

    def pack(state, factor):
        rows = jnp.broadcast_to(factor[:, None, None], (head_count, 8, head_dim))
        return jnp.concatenate([state, rows], axis=1)

    state, factor = local_state, carry
    span = 1
    while 2 * span < count:
        got = shifted(pack(state, factor), axis, span)
        state = state + factor[:, None, None] * got[:, :head_dim, :]
        factor = factor * got[:, head_dim, 0]
        span *= 2
    near = shifted(pack(state, factor), axis, 1)
    far = shifted(state, axis, span + 1)
    near_state = near[:, :head_dim, :]
    near_factor = near[:, head_dim, 0]
    return near_state + near_factor[:, None, None] * far


def local(
    tokens,
    log_decay,
    lengths,
    label_ids,
    w_query,
    w_key,
    w_value,
    norm_gain,
    label_query,
    label_weight,
):
    tok_rows = tokens.shape[1]
    model_width = tokens.shape[2]
    head_count = log_decay.shape[1]
    head_dim = model_width // head_count
    qk_scale = head_dim ** (-0.5)
    record_count = lengths.shape[1]
    label_count = label_query.shape[0]
    shard_start = lax.axis_index("ctx") * tok_rows
    local_pos = jnp.arange(tok_rows, dtype=jnp.int32)
    record = record_ids(lengths[0], shard_start + local_pos)
    before_rec = record_ids(lengths[0], jnp.reshape(shard_start - 1, (1,)))[0]
    features = tokens[0]
    queries = jnp.dot(features, w_query, preferred_element_type=jnp.float32).astype(jnp.bfloat16)
    key_rows = jnp.dot(features, w_key, preferred_element_type=jnp.float32).astype(jnp.bfloat16)
    value_rows = jnp.dot(features, w_value, preferred_element_type=jnp.float32).astype(jnp.bfloat16)
    q3 = queries.reshape(tok_rows, head_count, head_dim)
    k3 = key_rows.reshape(tok_rows, head_count, head_dim)
    v3 = value_rows.reshape(tok_rows, head_count, head_dim)
    decay_cum = jnp.cumsum(log_decay[0], axis=1)
    pair_mask = (local_pos[:, None] >= local_pos[None, :]) & (record[:, None] == record[None, :])
    linked = record == before_rec
    tail_rec = record == record[tok_rows - 1]

    last_cum = decay_cum[:, tok_rows - 1]
    k_factor = jnp.where(tail_rec[None, :], jnp.exp(last_cum[:, None] - decay_cum), 0.0)
    k_decayed = (k3.astype(jnp.float32) * k_factor.T[:, :, None]).astype(jnp.bfloat16)
    local_state = jnp.einsum("thd,the->hde", k_decayed, v3, preferred_element_type=jnp.float32)
    carry = jnp.where(linked[tok_rows - 1], jnp.exp(last_cum), 0.0)
    incoming = exclusive_state_scan(local_state, carry, "ctx")

    scores = jnp.einsum("thd,shd->hts", q3, k3, preferred_element_type=jnp.float32) * qk_scale
    decay_pair = jnp.exp(jnp.minimum(decay_cum[:, :, None] - decay_cum[:, None, :], 0.0))
    weights = jnp.where(pair_mask[None], scores * decay_pair, 0.0).astype(jnp.bfloat16)
    intra = jnp.einsum("hts,shd->thd", weights, v3, preferred_element_type=jnp.float32)

    member = record[None, :] == jnp.arange(record_count, dtype=jnp.int32)[:, None]
    kf3 = features.reshape(tok_rows, head_count, head_dim)
    lq3 = label_query.reshape(label_count, head_count, head_dim)
    lw3 = label_weight.reshape(label_count, head_count, head_dim)
    pscore = jnp.einsum("lhd,thd->hlt", lq3, kf3, preferred_element_type=jnp.float32) * qk_scale
    maxima = jnp.max(
        jnp.where(member[None, :, None, :], pscore[:, None, :, :], NEG_FILL), axis=3
    )
    maxima_tok = jnp.sum(
        jnp.where(member[None, :, None, :], maxima[:, :, :, None], 0.0), axis=1
    )
    pool_weight = jnp.exp(pscore - maxima_tok)
    mass = jnp.sum(jnp.where(member[None, :, None, :], pool_weight[:, None], 0.0), axis=3)
    label_hot = (label_ids[0][:, None] == jnp.arange(label_count, dtype=jnp.int32)[None, :]).astype(
        jnp.bfloat16
    )
    counts = jnp.dot(member.astype(jnp.bfloat16), label_hot, preferred_element_type=jnp.float32)

    top, total_mass, total_counts = maxima, mass, counts
    for bit in butterfly_bits("ctx"):
        packed = jnp.concatenate([top, total_mass, total_counts[None]], axis=0)
        other = swapped(packed, "ctx", bit)
        o_top = other[:head_count]
        o_mass = other[head_count:2 * head_count]
        o_counts = other[2 * head_count]
        new_top = jnp.maximum(top, o_top)
        total_mass = total_mass * jnp.exp(top - new_top) + o_mass * jnp.exp(o_top - new_top)
        total_counts = total_counts + o_counts
        top = new_top
    rescale = jnp.exp(maxima - top) / total_mass

    q_decayed = q3.astype(jnp.float32) * jnp.where(linked[None, :], jnp.exp(decay_cum), 0.0).T[:, :, None]
    inter = jnp.einsum(
        "thd,hde->the", q_decayed, incoming, precision=lax.Precision.HIGH,
        preferred_element_type=jnp.float32,
    )
    total_out = intra + inter * qk_scale
    centred = total_out - jnp.mean(total_out, axis=2, keepdims=True)
    variance = jnp.mean(centred * centred, axis=2, keepdims=True)
    gain3 = norm_gain.reshape(head_count, head_dim)
    normed = centred * lax.rsqrt(variance + 1e-05) * gain3[None]
    out_rows = normed.reshape(tok_rows, model_width).astype(jnp.bfloat16)

    y3 = out_rows.reshape(tok_rows, head_count, head_dim)
    label_value = jnp.einsum("lhd,thd->hlt", lw3, y3, preferred_element_type=jnp.float32)
    weighted = jnp.sum(
        jnp.where(member[None, :, None, :], (pool_weight * label_value)[:, None], 0.0), axis=3
    )
    part = jnp.sum(weighted * rescale, axis=0)
    for bit in butterfly_bits("ctx"):
        part = part + swapped(part, "ctx", bit)
    logits = part
    target = (total_counts + 0.5) / (lengths[0].astype(jnp.float32)[:, None] + 1.0)
    rec_loss = jnp.mean(jax.nn.softplus(logits) - target * logits, axis=1)
    mean_loss = lax.psum(jnp.sum(rec_loss), "dp") / (lax.axis_size("dp") * record_count)
    return (out_rows[None], logits[None], rec_loss[None], mean_loss)


def solution(mesh):
    return jax.shard_map(
        local,
        mesh=mesh,
        in_specs=(
            P("dp", "ctx", None),
            P("dp", None, "ctx"),
            P("dp", None),
            P("dp", "ctx"),
            P(),
            P(),
            P(),
            P(),
            P(),
            P(),
        ),
        out_specs=(P("dp", "ctx", None), P("dp", None, None), P("dp", None), P()),
        check_vma=False,
    )
```

time: 1010 us -> 225 us (0.22)
  waiting for transfers between devices: 449 us -> 98.1 us
  blocking collectives: 143 us -> 24.7 us
  starting transfers between devices: 173 us -> 56.2 us
  loops' own time: 57.3 us -> 0 us
  matrix products: 66.9 us -> 14.4 us
  local copies, waits for them, and re-layouts: 44.5 us -> 5.1 us
  other arithmetic: 53.2 us -> 21.6 us
  between operations: 16.6 us -> 3.58 us
    psum x1 -> x0, waiting for transfers between devices: 187 us -> none  [local(): lax.psum((mass_part * rescale, weighted * rescale, counts), 'ctx')]
    ppermute x31 -> x16, waiting for transfers between devices: 263 us -> 98.1 us  [the longest x6 76.2 us: shifted(): return lax.ppermute(x, axis, pairs)]
    pmax x1 -> x0, blocking collectives: 126 us -> none  [local(): top_score = lax.pmax(maxima, 'ctx')]
    ppermute x31 -> x16, starting transfers between devices: 173 us -> 56.2 us  [the longest x6 31.7 us: shifted(): return lax.ppermute(x, axis, pairs)]
    another operation x4 -> x0, loops' own time: 57.3 us -> none  [the longest x1 30.3 us: local(): lax.map(local_head, jnp.arange(head_count, dtype=jnp.int32))]
    dot_general x56 -> x5, matrix products: 61.1 us -> 7.65 us  [the longest x1 3.15 us: local(): jnp.einsum('hts,shd->thd', weights, v3, preferred_element_type=jnp.float32)]
    add x31 -> x12, other arithmetic: 30.3 us -> 0.57 us  [the longest x4 0.48 us: exclusive_state_scan(): state = state + factor[:, None, None] * got[:, :head_dim, :]]
    dynamic_slice x56 -> x0, local copies, waits for them, and re-layouts: 28.5 us -> none  [the longest x24 14.2 us: local(): lax.map(local_head, jnp.arange(head_count, dtype=jnp.int32))]
  transfers between devices with their start and end apart: 32 -> 16, of which waited for: 32 -> 15; matrix products, arithmetic and copies ran while one was open for 0% -> 6% of each run, Pallas kernels for 0% -> 0%
where the time goes in v1:
time: 225 us; the launch traced here: 224 us
  waiting for transfers between devices  98.1 us (44%)
  starting transfers between devices  56.2 us (25%)
  blocking collectives  24.7 us (11%)
  other arithmetic  21.6 us (10%)
  matrix products  14.4 us (6%)
  local copies, waits for them, and re-layouts  5.1 us (2%)
  between operations  3.58 us (2%)
    ppermute x6, waiting for transfers between devices, shifted(): return lax.ppermute(x, axis, pairs)  76.2 us
    ppermute x6, starting transfers between devices, shifted(): return lax.ppermute(x, axis, pairs)  31.7 us
    psum x1, blocking collectives, local(): lax.psum(jnp.sum(rec_loss), 'dp') / (lax.axis_size('dp') * record_count)  24.7 us
    ppermute x10, starting transfers between devices, swapped(): return lax.ppermute(x, axis, [(i, i ^ bit) for i in range(count)])  24.6 us
    ppermute x10, waiting for transfers between devices, swapped(): return lax.ppermute(x, axis, [(i, i ^ bit) for i in range(count)])  21.9 us
    reduce_sum x1, other arithmetic, local(): jnp.sum(jnp.where(member[None, :, None, :], (pool_weight * label_value)[:...  4.52 us
  transfers between devices with their start and end apart: 16, of which 15 were waited for; matrix products, arithmetic and copies ran while one was open for 6% of the time, Pallas kernels for 0%

profile of v1, /device:TPU:1, one launch (start us, length us, event | category | flops | bytes accessed | tf_op | source)
XLA Modules:
  0.0 223.7 jit_solution(4718745508702200979)
XLA Ops:
  0.7 1.0 reduce-window.10
  3.0 1.3 fusion.58
  4.9 1.3 reduce-window.11
  7.7 0.8 slice_reduce_fusion.2
  9.3 2.5 %convolution_convert_fusion = bf16[256,1024]{1,0:T(8,128)(2,1)} fusion(bf16[1024,1024]{1,0:T(8,128)(2,1)S(1)} %copy-done, bf16[1,256,1024]{2,1,0:T(8,128)(2,1)} %param.10), kind=kOutput, calls=%fused_computation.12 | convolution fusion | flops 537133056 | bytes 3145728 | tf_op jit(solution)/shard_map/dot_general | solution.py:83
  11.8 1.2 copy.110
  13.1 2.4 %fusion.3 = bf16[32,8,8,128]{3,2,1,0:T(8,128)(2,1)S(1)} fusion(bf16[1024,1024]{1,0:T(8,128)(2,1)} %param.16, bf16[1,256,1024]{2,1,0:T(8,128)(2,1)S(1)} %copy-done.5), kind=kOutput, calls=%fused_computation.15 | convolution fusion | flops 537133056 | bytes 3145728 | tf_op jit(solution)/shard_map/dot_general | solution.py:84
  15.9 4.4 %collective-permute-start = (f32[8,136,128]{2,1,0:T(8,128)S(1)}, f32[8,136,128]{2,1,0:T(8,128)S(1)}, u32[]{:S(2)}, u32[]{:S(2)}) collective-permute-start(f32[8,136,128]{2,1,0:T(8,128)S(1)} %pad_maximum_fusion), channel_id=1, source_target_pairs={{0,1},{1,2},{2,3},{3,4},{4,5},{5,6},{6,7},{7,8},{8,9},{9,10},{10,1... | collective-permute-start | bytes 1671176 | tf_op jit(solution)/shard_map/ppermute | solution.py:12
  20.4 11.1 %collective-permute-done = f32[8,136,128]{2,1,0:T(8,128)S(1)} collective-permute-done((f32[8,136,128]{2,1,0:T(8,128)S(1)}, f32[8,136,128]{2,1,0:T(8,128)S(1)}, u32[]{:S(2)}, u32[]{:S(2)}) %collective-permute-start) | collective-permute-done | bytes 557088 | tf_op jit(solution)/shard_map/ppermute | solution.py:12
  32.0 5.5 %collective-permute-start.1 = (f32[8,136,128]{2,1,0:T(8,128)S(1)}, f32[8,136,128]{2,1,0:T(8,128)S(1)}, u32[]{:S(2)}, u32[]{:S(2)}) collective-permute-start(f32[8,136,128]{2,1,0:T(8,128)S(1)} %pad_maximum_fusion.1), channel_id=1, source_target_pairs={{0,2},{1,3},{2,4},{3,5},{4,6},{5,7},{6,8},{7,9},{8,10},{9,11},{10,... | collective-permute-start | bytes 1671176 | tf_op jit(solution)/shard_map/ppermute | solution.py:12
  38.2 21.6 %collective-permute-done.1 = f32[8,136,128]{2,1,0:T(8,128)S(1)} collective-permute-done((f32[8,136,128]{2,1,0:T(8,128)S(1)}, f32[8,136,128]{2,1,0:T(8,128)S(1)}, u32[]{:S(2)}, u32[]{:S(2)}) %collective-permute-start.1) | collective-permute-done | bytes 557088 | tf_op jit(solution)/shard_map/ppermute | solution.py:12
  60.3 12.4 %collective-permute-start.2 = (f32[8,136,128]{2,1,0:T(8,128)S(1)}, f32[8,136,128]{2,1,0:T(8,128)S(1)}, u32[]{:S(2)}, u32[]{:S(2)}) collective-permute-start(f32[8,136,128]{2,1,0:T(8,128)S(1)} %pad_maximum_fusion.2), channel_id=1, source_target_pairs={{0,4},{1,5},{2,6},{3,7},{4,8},{5,9},{6,10},{7,11},{8,12},{9,13},{1... | collective-permute-start | bytes 1671176 | tf_op jit(solution)/shard_map/ppermute | solution.py:12
  72.7 1.2 select_reduce_fusion.3
  73.9 1.5 select_reduce_fusion.2
  75.4 21.2 %collective-permute-done.2 = f32[8,136,128]{2,1,0:T(8,128)S(1)} collective-permute-done((f32[8,136,128]{2,1,0:T(8,128)S(1)}, f32[8,136,128]{2,1,0:T(8,128)S(1)}, u32[]{:S(2)}, u32[]{:S(2)}) %collective-permute-start.2) | collective-permute-done | bytes 557088 | tf_op jit(solution)/shard_map/ppermute | solution.py:12
  97.0 5.2 %collective-permute-start.3 = (f32[8,136,128]{2,1,0:T(8,128)S(1)}, f32[8,136,128]{2,1,0:T(8,128)S(1)}, u32[]{:S(2)}, u32[]{:S(2)}) collective-permute-start(f32[8,136,128]{2,1,0:T(8,128)S(1)} %pad_maximum_fusion.3), channel_id=1, source_target_pairs={{0,8},{1,9},{2,10},{3,11},{4,12},{5,13},{6,14},{7,15},{8,16},{9,17... | collective-permute-start | bytes 1671176 | tf_op jit(solution)/shard_map/ppermute | solution.py:12
  102.2 1.5 fusion.4
  103.8 2.7 %subtract_exponential_fusion = f32[8,512,256]{2,1,0:T(8,128)} fusion(f32[8,512,256]{2,1,0:T(8,128)S(1)} %convolution_multiply_fusion, f32[8,512,256]{2,1,0:T(8,128)S(1)} %select_reduce_fusion.2), kind=kLoop, calls=%fused_computation.5 | loop fusion | flops 1048576 | bytes 12582912 | tf_op jit(solution)/shard_map/exp | solution.py:116
  106.4 7.2 %collective-permute-done.3 = f32[8,136,128]{2,1,0:T(8,128)S(1)} collective-permute-done((f32[8,136,128]{2,1,0:T(8,128)S(1)}, f32[8,136,128]{2,1,0:T(8,128)S(1)}, u32[]{:S(2)}, u32[]{:S(2)}) %collective-permute-start.3) | collective-permute-done | bytes 557088 | tf_op jit(solution)/shard_map/ppermute | solution.py:12
  114.0 0.9 pad_maximum_fusion.4
  114.9 2.1 collective-permute-start.4
  117.1 2.1 collective-permute-start.5
  119.4 3.1 %fusion = f32[8,128,256]{2,1,0:T(8,128)} fusion(bf16[256,8,128]{0,2,1:T(8,128)(2,1)S(1)} %bitcast.130, f32[8,256]{1,0:T(8,128)S(1)} %get-tuple-element.33, pred[256,256]{1,0:T(8,128)(4,1)S(1)} %fusion.41, bf16[32,8,8,128]{3,2,1,0:T(8,128)(2,1)} %fusion.4, bf16[32,8,8,128]{3,2,1,0:T(8,128)(2,1)} %copy-done.4), kind=kOutput, calls=%fused_computation.8 | convolution fusion | flops 271581184 | bytes 2695168 | tf_op jit(solution)/shard_map/hts,shd->thd/dot_general | solution.py:103
  122.6 4.7 %collective-permute-done.4 = f32[8,136,128]{2,1,0:T(8,128)} collective-permute-done((f32[8,136,128]{2,1,0:T(8,128)}, f32[8,136,128]{2,1,0:T(8,128)}, u32[]{:S(2)}, u32[]{:S(2)}) %collective-permute-start.4) | collective-permute-done | bytes 557088 | tf_op jit(solution)/shard_map/ppermute | solution.py:12
  127.3 0.9 slice_reduce_fusion.1
  128.2 10.2 %collective-permute-done.5 = f32[8,128,128]{2,1,0:T(8,128)} collective-permute-done((f32[8,128,128]{2,1,0:T(8,128)S(1)}, f32[8,128,128]{2,1,0:T(8,128)}, u32[]{:S(2)}, u32[]{:S(2)}) %collective-permute-start.5) | collective-permute-done | bytes 524320 | tf_op jit(solution)/shard_map/ppermute | solution.py:12
  138.4 2.7 %fusion.69 = (f32[256,8]{0,1:T(8,128)S(1)}, f32[256,8,128]{0,2,1:T(8,128)S(1)}) fusion(f32[8,128,256]{2,1,0:T(8,128)} %fusion, f32[256,8]{0,1:T(8,128)S(1)} %get-tuple-element.32, bf16[32,8,8,128]{3,2,1,0:T(8,128)(2,1)} %fusion.4, f32[8,136,128]{2,1,0:T(8,128)} %collective-permute-done.4, f32[8,128,128]{2,1,0:T(8,128)} %collective-permute-done.5, ...), kind=kOutput, calls=%fused_computation.153 | convolution fusion | flops 202897408 | bytes 3686432 | tf_op jit(solution)/shard_map/thd,hde->the/dot_general | solution.py:137
  141.6 0.8 bitcast_multiply_fusion
  142.4 4.5 %select_reduce_fusion.1 = (f32[8,2,512]{2,1,0:T(2,128)S(1)}, f32[8,2,512]{2,1,0:T(2,128)S(1)}) fusion(f32[8,512,256]{2,1,0:T(8,128)S(1)} %bitcast_multiply_fusion, pred[2,256]{1,0:T(4,128)(4,1)S(1)} %iota_compare_fusion.3, f32[8,512,256]{2,1,0:T(8,128)S(1)} %copy-done.1), kind=kLoop, calls=%fused_computation.1 | loop fusion | flops 8372224 | bytes 8454656 | tf_op jit(solution)/shard_map/reduce_sum | solution.py:150
  147.0 3.1 %collective-permute-done.6 = f32[17,2,512]{2,1,0:T(2,128)S(1)} collective-permute-done((f32[17,2,512]{2,1,0:T(2,128)S(1)}, f32[17,2,512]{2,1,0:T(2,128)S(1)}, u32[]{:S(2)}, u32[]{:S(2)}) %collective-permute-start.6) | collective-permute-done | bytes 69664 | tf_op jit(solution)/shard_map/ppermute | solution.py:17
  150.3 3.7 %collective-permute-start.7 = (f32[17,2,512]{2,1,0:T(2,128)S(1)}, f32[17,2,512]{2,1,0:T(2,128)S(1)}, u32[]{:S(2)}, u32[]{:S(2)}) collective-permute-start(f32[17,2,512]{2,1,0:T(2,128)S(1)} %pad_maximum_fusion.6), channel_id=1, source_target_pairs={{0,2},{1,3},{2,0},{3,1},{4,6},{5,7},{6,4},{7,5},{8,10},{9,11},{10,... | collective-permute-start | bytes 208904 | tf_op jit(solution)/shard_map/ppermute | solution.py:17
  154.1 1.7 collective-permute-done.7
  155.9 3.6 %collective-permute-start.8 = (f32[17,2,512]{2,1,0:T(2,128)S(1)}, f32[17,2,512]{2,1,0:T(2,128)S(1)}, u32[]{:S(2)}, u32[]{:S(2)}) collective-permute-start(f32[17,2,512]{2,1,0:T(2,128)S(1)} %pad_maximum_fusion.7), channel_id=1, source_target_pairs={{0,4},{1,5},{2,6},{3,7},{4,0},{5,1},{6,2},{7,3},{8,12},{9,13},{10,... | collective-permute-start | bytes 208904 | tf_op jit(solution)/shard_map/ppermute | solution.py:17
  159.6 3.8 %collective-permute-done.8 = f32[17,2,512]{2,1,0:T(2,128)S(1)} collective-permute-done((f32[17,2,512]{2,1,0:T(2,128)S(1)}, f32[17,2,512]{2,1,0:T(2,128)S(1)}, u32[]{:S(2)}, u32[]{:S(2)}) %collective-permute-start.8) | collective-permute-done | bytes 69664 | tf_op jit(solution)/shard_map/ppermute | solution.py:17
  163.6 2.1 collective-permute-start.9
  165.6 2.0 collective-permute-done.9
  167.8 6.1 %collective-permute-start.10 = (f32[17,2,512]{2,0,1:T(8,128)S(1)}, f32[17,2,512]{2,0,1:T(8,128)S(1)}, u32[]{:S(2)}, u32[]{:S(2)}) collective-permute-start(f32[17,2,512]{2,0,1:T(8,128)S(1)} %copy.99), channel_id=1, source_target_pairs={{0,16},{1,17},{2,18},{3,19},{4,20},{5,21},{6,22},{7,23},{8,24},{9,... | collective-permute-start | bytes 208904 | tf_op jit(solution)/shard_map/ppermute | solution.py:17
  173.9 2.0 collective-permute-done.10
  176.2 2.4 %collective-permute-done.11 = f32[2,512]{1,0:T(2,128)S(1)} collective-permute-done((f32[2,512]{1,0:T(2,128)S(1)}, f32[2,512]{1,0:T(2,128)S(1)}, u32[]{:S(2)}, u32[]{:S(2)}) %collective-permute-start.11) | collective-permute-done | bytes 4128 | tf_op jit(solution)/shard_map/ppermute | solution.py:17
  178.6 3.6 %collective-permute-done.12 = f32[2,512]{1,0:T(2,128)S(1)} collective-permute-done((f32[2,512]{1,0:T(2,128)S(1)}, f32[2,512]{1,0:T(2,128)S(1)}, u32[]{:S(2)}, u32[]{:S(2)}) %collective-permute-start.12) | collective-permute-done | bytes 4128 | tf_op jit(solution)/shard_map/ppermute | solution.py:17
  182.3 4.4 %collective-permute-start.13 = (f32[2,512]{1,0:T(2,128)S(1)}, f32[2,512]{1,0:T(2,128)S(1)}, u32[]{:S(2)}, u32[]{:S(2)}) collective-permute-start(f32[2,512]{1,0:T(2,128)S(1)} %add.146), channel_id=1, source_target_pairs={{0,4},{1,5},{2,6},{3,7},{4,0},{5,1},{6,2},{7,3},{8,12},{9,13},{10,... | collective-permute-start | bytes 12296 | tf_op jit(solution)/shard_map/ppermute | solution.py:17
  186.7 2.0 collective-permute-done.13
  188.6 1.1 collective-permute-start.14
  189.8 1.3 collective-permute-done.14
  191.1 3.3 %collective-permute-start.15 = (f32[2,512]{1,0:T(2,128)S(1)}, f32[2,512]{1,0:T(2,128)S(1)}, u32[]{:S(2)}, u32[]{:S(2)}) collective-permute-start(f32[2,512]{1,0:T(2,128)S(1)} %add.148), channel_id=1, source_target_pairs={{0,16},{1,17},{2,18},{3,19},{4,20},{5,21},{6,22},{7,23},{8,24},{9,... | collective-permute-start | bytes 12296 | tf_op jit(solution)/shard_map/ppermute | solution.py:17
  194.4 1.0 copy.105
  196.1 1.1 multiply_reduce_fusion.1
  197.2 24.7 %psum.7 = f32[]{:T(128)} all-reduce(f32[]{:T(128)} %get-tuple-element.44), channel_id=1, replica_groups=mesh['dp'=8,'ctx'=32] {'dp'}, use_global_device_ids=true, to_apply=%region_14.15 | all-reduce | flops 1 | bytes 8 | tf_op jit(solution)/shard_map/psum | solution.py:159
  (98 shorter events, 8.8 us)
Async XLA Ops:
  0.6 8.6 %copy-start = (bf16[1024,1024]{1,0:T(8,128)(2,1)S(1)}, bf16[1024,1024]{1,0:T(8,128)(2,1)}, u32[]{:S(2)}) copy-start(bf16[1024,1024]{1,0:T(8,128)(2,1)} %param.15) | copy-start | bytes 6291460
  0.6 12.4 %copy-start.5 = (bf16[1,256,1024]{2,1,0:T(8,128)(2,1)S(1)}, bf16[1,256,1024]{2,1,0:T(8,128)(2,1)}, u32[]{:S(2)}) copy-start(bf16[1,256,1024]{2,1,0:T(8,128)(2,1)} %param.10) | copy-start | bytes 1572868
  13.1 24.4 %copy-start.3 = (bf16[512,1024]{1,0:T(8,128)(2,1)S(1)}, bf16[512,1024]{1,0:T(8,128)(2,1)}, u32[]{:S(2)}) copy-start(bf16[512,1024]{1,0:T(8,128)(2,1)} %param.18) | copy-start | bytes 3145732
  15.5 22.0 %copy-start.4 = (bf16[32,8,8,128]{3,2,1,0:T(8,128)(2,1)}, bf16[32,8,8,128]{3,2,1,0:T(8,128)(2,1)S(1)}, u32[]{:S(2)}) copy-start(bf16[32,8,8,128]{3,2,1,0:T(8,128)(2,1)S(1)} %fusion.3) | copy-start | bytes 1572868
  15.9 15.6 %collective-permute-start = (f32[8,136,128]{2,1,0:T(8,128)S(1)}, f32[8,136,128]{2,1,0:T(8,128)S(1)}, u32[]{:S(2)}, u32[]{:S(2)}) collective-permute-start(f32[8,136,128]{2,1,0:T(8,128)S(1)} %pad_maximum_fusion), channel_id=1, source_target_pairs={{0,1},{1,2},{2,3},{3,4},{4,5},{5,6},{6,7},{7,8},{8,9},{9,10},{10,1... | collective-permute-start | bytes 1671176 | tf_op jit(solution)/shard_map/ppermute | solution.py:12
  32.0 27.9 %collective-permute-start.1 = (f32[8,136,128]{2,1,0:T(8,128)S(1)}, f32[8,136,128]{2,1,0:T(8,128)S(1)}, u32[]{:S(2)}, u32[]{:S(2)}) collective-permute-start(f32[8,136,128]{2,1,0:T(8,128)S(1)} %pad_maximum_fusion.1), channel_id=1, source_target_pairs={{0,2},{1,3},{2,4},{3,5},{4,6},{5,7},{6,8},{7,9},{8,10},{9,11},{10,... | collective-permute-start | bytes 1671176 | tf_op jit(solution)/shard_map/ppermute | solution.py:12
  60.3 36.4 %collective-permute-start.2 = (f32[8,136,128]{2,1,0:T(8,128)S(1)}, f32[8,136,128]{2,1,0:T(8,128)S(1)}, u32[]{:S(2)}, u32[]{:S(2)}) collective-permute-start(f32[8,136,128]{2,1,0:T(8,128)S(1)} %pad_maximum_fusion.2), channel_id=1, source_target_pairs={{0,4},{1,5},{2,6},{3,7},{4,8},{5,9},{6,10},{7,11},{8,12},{9,13},{1... | collective-permute-start | bytes 1671176 | tf_op jit(solution)/shard_map/ppermute | solution.py:12
  73.8 28.4 %copy-start.8 = (bf16[1024,1024]{1,0:T(8,128)(2,1)S(1)}, bf16[1024,1024]{1,0:T(8,128)(2,1)}, u32[]{:S(2)}) copy-start(bf16[1024,1024]{1,0:T(8,128)(2,1)} %param.14) | copy-start | bytes 6291460
  97.0 16.6 %collective-permute-start.3 = (f32[8,136,128]{2,1,0:T(8,128)S(1)}, f32[8,136,128]{2,1,0:T(8,128)S(1)}, u32[]{:S(2)}, u32[]{:S(2)}) collective-permute-start(f32[8,136,128]{2,1,0:T(8,128)S(1)} %pad_maximum_fusion.3), channel_id=1, source_target_pairs={{0,8},{1,9},{2,10},{3,11},{4,12},{5,13},{6,14},{7,15},{8,16},{9,17... | collective-permute-start | bytes 1671176 | tf_op jit(solution)/shard_map/ppermute | solution.py:12
  103.8 15.4 %copy-start.9 = (s32[1,256]{1,0:T(1,128)S(1)}, s32[1,256]{1,0:T(1,128)}, u32[]{:S(2)}) copy-start(s32[1,256]{1,0:T(1,128)} %param.13) | copy-start | bytes 3076
  114.9 12.4 %collective-permute-start.4 = (f32[8,136,128]{2,1,0:T(8,128)}, f32[8,136,128]{2,1,0:T(8,128)}, u32[]{:S(2)}, u32[]{:S(2)}) collective-permute-start(f32[8,136,128]{2,1,0:T(8,128)} %pad_maximum_fusion.4), channel_id=1, source_target_pairs={{0,1},{1,2},{2,3},{3,4},{4,5},{5,6},{6,7},{7,8},{8,9},{9,10},{10,1... | collective-permute-start | bytes 1671176 | tf_op jit(solution)/shard_map/ppermute | solution.py:12
  117.1 21.4 %collective-permute-start.5 = (f32[8,128,128]{2,1,0:T(8,128)S(1)}, f32[8,128,128]{2,1,0:T(8,128)}, u32[]{:S(2)}, u32[]{:S(2)}) collective-permute-start(f32[8,128,128]{2,1,0:T(8,128)S(1)} %fusion.22), channel_id=1, source_target_pairs={{0,17},{1,18},{2,19},{3,20},{4,21},{5,22},{6,23},{7,24},{8,25},{9,... | collective-permute-start | bytes 1572872 | tf_op jit(solution)/shard_map/ppermute | solution.py:12
  119.4 21.9 %copy-start.6 = (f32[1024]{0:T(1024)S(1)}, f32[1024]{0:T(1024)}, u32[]{:S(2)}) copy-start(f32[1024]{0:T(1024)} %param.17) | copy-start | bytes 12292
  122.6 19.0 %copy-start.1 = (f32[8,512,256]{2,1,0:T(8,128)S(1)}, f32[8,512,256]{2,1,0:T(8,128)}, u32[]{:S(2)}) copy-start(f32[8,512,256]{2,1,0:T(8,128)} %subtract_exponential_fusion) | copy-start | bytes 12582916
  122.6 19.0 %copy-start.2 = (bf16[512,1024]{1,0:T(8,128)(2,1)S(1)}, bf16[512,1024]{1,0:T(8,128)(2,1)}, u32[]{:S(2)}) copy-start(bf16[512,1024]{1,0:T(8,128)(2,1)} %param.19) | copy-start | bytes 3145732
  142.4 52.0 %copy-start.7 = (s32[1,2]{1,0:T(1,128)S(1)}, s32[1,2]{1,0:T(1,128)}, u32[]{:S(2)}) copy-start(s32[1,2]{1,0:T(1,128)} %param.12) | copy-start | bytes 28
  146.9 3.2 %collective-permute-start.6 = (f32[17,2,512]{2,1,0:T(2,128)S(1)}, f32[17,2,512]{2,1,0:T(2,128)S(1)}, u32[]{:S(2)}, u32[]{:S(2)}) collective-permute-start(f32[17,2,512]{2,1,0:T(2,128)S(1)} %pad_maximum_fusion.5), channel_id=1, source_target_pairs={{0,1},{1,0},{2,3},{3,2},{4,5},{5,4},{6,7},{7,6},{8,9},{9,8},{10,11... | collective-permute-start | bytes 208904 | tf_op jit(solution)/shard_map/ppermute | solution.py:17
  150.3 5.4 %collective-permute-start.7 = (f32[17,2,512]{2,1,0:T(2,128)S(1)}, f32[17,2,512]{2,1,0:T(2,128)S(1)}, u32[]{:S(2)}, u32[]{:S(2)}) collective-permute-start(f32[17,2,512]{2,1,0:T(2,128)S(1)} %pad_maximum_fusion.6), channel_id=1, source_target_pairs={{0,2},{1,3},{2,0},{3,1},{4,6},{5,7},{6,4},{7,5},{8,10},{9,11},{10,... | collective-permute-start | bytes 208904 | tf_op jit(solution)/shard_map/ppermute | solution.py:17
  155.9 7.4 %collective-permute-start.8 = (f32[17,2,512]{2,1,0:T(2,128)S(1)}, f32[17,2,512]{2,1,0:T(2,128)S(1)}, u32[]{:S(2)}, u32[]{:S(2)}) collective-permute-start(f32[17,2,512]{2,1,0:T(2,128)S(1)} %pad_maximum_fusion.7), channel_id=1, source_target_pairs={{0,4},{1,5},{2,6},{3,7},{4,0},{5,1},{6,2},{7,3},{8,12},{9,13},{10,... | collective-permute-start | bytes 208904 | tf_op jit(solution)/shard_map/ppermute | solution.py:17
  163.6 4.1 %collective-permute-start.9 = (f32[17,2,512]{2,1,0:T(2,128)S(1)}, f32[17,2,512]{2,1,0:T(2,128)S(1)}, u32[]{:S(2)}, u32[]{:S(2)}) collective-permute-start(f32[17,2,512]{2,1,0:T(2,128)S(1)} %pad_maximum_fusion.8), channel_id=1, source_target_pairs={{0,8},{1,9},{2,10},{3,11},{4,12},{5,13},{6,14},{7,15},{8,0},{9,1},... | collective-permute-start | bytes 208904 | tf_op jit(solution)/shard_map/ppermute | solution.py:17
  167.8 8.1 %collective-permute-start.10 = (f32[17,2,512]{2,0,1:T(8,128)S(1)}, f32[17,2,512]{2,0,1:T(8,128)S(1)}, u32[]{:S(2)}, u32[]{:S(2)}) collective-permute-start(f32[17,2,512]{2,0,1:T(8,128)S(1)} %copy.99), channel_id=1, source_target_pairs={{0,16},{1,17},{2,18},{3,19},{4,20},{5,21},{6,22},{7,23},{8,24},{9,... | collective-permute-start | bytes 208904 | tf_op jit(solution)/shard_map/ppermute | solution.py:17
  176.1 2.5 %collective-permute-start.11 = (f32[2,512]{1,0:T(2,128)S(1)}, f32[2,512]{1,0:T(2,128)S(1)}, u32[]{:S(2)}, u32[]{:S(2)}) collective-permute-start(f32[2,512]{1,0:T(2,128)S(1)} %fusion.48), channel_id=1, source_target_pairs={{0,1},{1,0},{2,3},{3,2},{4,5},{5,4},{6,7},{7,6},{8,9},{9,8},{10,11... | collective-permute-start | bytes 12296 | tf_op jit(solution)/shard_map/ppermute | solution.py:17
  178.6 3.7 %collective-permute-start.12 = (f32[2,512]{1,0:T(2,128)S(1)}, f32[2,512]{1,0:T(2,128)S(1)}, u32[]{:S(2)}, u32[]{:S(2)}) collective-permute-start(f32[2,512]{1,0:T(2,128)S(1)} %add.145), channel_id=1, source_target_pairs={{0,2},{1,3},{2,0},{3,1},{4,6},{5,7},{6,4},{7,5},{8,10},{9,11},{10,... | collective-permute-start | bytes 12296 | tf_op jit(solution)/shard_map/ppermute | solution.py:17
  182.3 6.4 %collective-permute-start.13 = (f32[2,512]{1,0:T(2,128)S(1)}, f32[2,512]{1,0:T(2,128)S(1)}, u32[]{:S(2)}, u32[]{:S(2)}) collective-permute-start(f32[2,512]{1,0:T(2,128)S(1)} %add.146), channel_id=1, source_target_pairs={{0,4},{1,5},{2,6},{3,7},{4,0},{5,1},{6,2},{7,3},{8,12},{9,13},{10,... | collective-permute-start | bytes 12296 | tf_op jit(solution)/shard_map/ppermute | solution.py:17
  188.6 2.5 %collective-permute-start.14 = (f32[2,512]{1,0:T(2,128)S(1)}, f32[2,512]{1,0:T(2,128)S(1)}, u32[]{:S(2)}, u32[]{:S(2)}) collective-permute-start(f32[2,512]{1,0:T(2,128)S(1)} %add.147), channel_id=1, source_target_pairs={{0,8},{1,9},{2,10},{3,11},{4,12},{5,13},{6,14},{7,15},{8,0},{9,1},... | collective-permute-start | bytes 12296 | tf_op jit(solution)/shard_map/ppermute | solution.py:17
  191.1 4.3 %collective-permute-start.15 = (f32[2,512]{1,0:T(2,128)S(1)}, f32[2,512]{1,0:T(2,128)S(1)}, u32[]{:S(2)}, u32[]{:S(2)}) collective-permute-start(f32[2,512]{1,0:T(2,128)S(1)} %add.148), channel_id=1, source_target_pairs={{0,16},{1,17},{2,18},{3,19},{4,20},{5,21},{6,22},{7,23},{8,24},{9,... | collective-permute-start | bytes 12296 | tf_op jit(solution)/shard_map/ppermute | solution.py:17

commit v2 on v1

--- a/solution.py
+++ b/solution.py
@@ -36,23 +36,23 @@
 def exclusive_state_scan(local_state, carry, axis):
     head_count, head_dim, _ = local_state.shape
     count = lax.axis_size(axis)
-
-    def pack(state, factor):
-        rows = jnp.broadcast_to(factor[:, None, None], (head_count, 8, head_dim))
-        return jnp.concatenate([state, rows], axis=1)
-
-    state, factor = local_state, carry
-    span = 1
-    while 2 * span < count:
-        got = shifted(pack(state, factor), axis, span)
-        state = state + factor[:, None, None] * got[:, :head_dim, :]
-        factor = factor * got[:, head_dim, 0]
-        span *= 2
-    near = shifted(pack(state, factor), axis, 1)
-    far = shifted(state, axis, span + 1)
-    near_state = near[:, :head_dim, :]
-    near_factor = near[:, head_dim, 0]
-    return near_state + near_factor[:, None, None] * far
+    rows = head_count * head_dim // count
+    assert rows * count == head_count * head_dim and head_dim % rows == 0
+    owner_head = (jnp.arange(count) * rows) // head_dim
+    slices = local_state.reshape(count, rows, head_dim)
+    factor_rows = jnp.broadcast_to(carry[owner_head][:, None, None], (count, 8, head_dim))
+    sent = jnp.concatenate([slices, factor_rows], axis=1)
+    got = lax.all_to_all(sent, axis, 0, 0)
+    factors = got[:, rows, 0]
+    block = jnp.arange(count)
+    inside = (block[None, None, :] > block[None, :, None]) & (block[None, None, :] < block[:, None, None])
+    spans = jnp.prod(jnp.where(inside, factors[None, None, :], 1.0), axis=2)
+    mix = jnp.where(block[None, :] < block[:, None], spans, 0.0)
+    scanned = jnp.dot(
+        mix, got[:, :rows, :].reshape(count, rows * head_dim), precision=lax.Precision.HIGHEST
+    )
+    back = lax.all_to_all(scanned.reshape(count, rows, head_dim), axis, 0, 0)
+    return back.reshape(head_count, head_dim, head_dim)
 
 
 def local(

time: 225 us -> 160 us (0.71)
  waiting for transfers between devices: 98.1 us -> 39.1 us
  starting transfers between devices: 56.2 us -> 41.9 us
  local copies, waits for them, and re-layouts: 5.1 us -> 9.82 us
  matrix products: 14.4 us -> 17 us
    ppermute x6 -> x0, waiting for transfers between devices: 76.2 us -> none  [shifted(): return lax.ppermute(x, axis, pairs)]
    ppermute x6 -> x0, starting transfers between devices: 31.7 us -> none  [shifted(): return lax.ppermute(x, axis, pairs)]
    all_to_all x0 -> x2, starting transfers between devices: none -> 20.6 us  [the longest x1 12 us: exclusive_state_scan(): got = lax.all_to_all(sent, axis, 0, 0)]
    all_to_all x0 -> x2, waiting for transfers between devices: none -> 17.4 us  [the longest x1 8.7 us: exclusive_state_scan(): back = lax.all_to_all(scanned.reshape(count, rows, head_dim), axis, 0, 0)]
    unnamed x22 -> x26, local copies, waits for them, and re-layouts: 1.15 us -> 5.73 us
    ppermute x10, starting transfers between devices: 24.6 us -> 21.3 us  [swapped(): return lax.ppermute(x, axis, [(i, i ^ bit) for i in range(count)])]
    dot_general x1, matrix products: 0.76 us -> 3.34 us  [local(): jnp.einsum('lhd,thd->hlt', lw3, y3, preferred_element_type=jnp.float32)]
  transfers between devices with their start and end apart: 16 -> 12, of which waited for: 15 -> 12; matrix products, arithmetic and copies ran while one was open for 6% -> 7% of each run, Pallas kernels for 0% -> 0%
where the time goes in v2:
time: 160 us; the launch traced here: 159 us
  starting transfers between devices  41.9 us (26%)
  waiting for transfers between devices  39.1 us (24%)
  blocking collectives  26.7 us (17%)
  other arithmetic  21.5 us (13%)
  matrix products  17 us (11%)
  local copies, waits for them, and re-layouts  9.82 us (6%)
  between operations  3.56 us (2%)
    psum x1, blocking collectives, local(): lax.psum(jnp.sum(rec_loss), 'dp') / (lax.axis_size('dp') * record_count)  26.7 us
    ppermute x10, waiting for transfers between devices, swapped(): return lax.ppermute(x, axis, [(i, i ^ bit) for i in range(count)])  21.7 us
    ppermute x10, starting transfers between devices, swapped(): return lax.ppermute(x, axis, [(i, i ^ bit) for i in range(count)])  21.3 us
    all_to_all x1, starting transfers between devices, exclusive_state_scan(): got = lax.all_to_all(sent, axis, 0, 0)  12 us
    all_to_all x1, waiting for transfers between devices, exclusive_state_scan(): back = lax.all_to_all(scanned.reshape(count, rows, head_dim), axis, 0, 0)  8.7 us
    all_to_all x1, waiting for transfers between devices, exclusive_state_scan(): got = lax.all_to_all(sent, axis, 0, 0)  8.66 us
    all_to_all x1, starting transfers between devices, exclusive_state_scan(): back = lax.all_to_all(scanned.reshape(count, rows, head_dim), axis, 0, 0)  8.57 us
    unnamed x26, local copies, waits for them, and re-layouts  5.73 us
  transfers between devices with their start and end apart: 12, of which 12 were waited for; matrix products, arithmetic and copies ran while one was open for 7% of the time, Pallas kernels for 0%

profile of v2, /device:TPU:1, one launch (start us, length us, event | category | flops | bytes accessed | tf_op | source)
XLA Modules:
  0.0 159.5 jit_solution(11878068223243966234)
XLA Ops:
  0.7 1.0 reduce-window.10
  3.0 1.3 fusion.57
  4.9 1.3 reduce-window.11
  7.9 1.8 %convolution_convert_fusion = bf16[256,1024]{1,0:T(8,128)(2,1)S(1)} fusion(bf16[1024,1024]{1,0:T(8,128)(2,1)S(1)} %copy-done, bf16[1,256,1024]{2,1,0:T(8,128)(2,1)} %param.10), kind=kOutput, calls=%fused_computation.13 | convolution fusion | flops 537133056 | bytes 3145728 | tf_op jit(solution)/shard_map/dot_general | solution.py:83
  9.9 2.6 %fusion.3 = bf16[32,8,8,128]{3,2,1,0:T(8,128)(2,1)S(1)} fusion(bf16[1024,1024]{1,0:T(8,128)(2,1)} %param.16, bf16[1,256,1024]{2,1,0:T(8,128)(2,1)} %param.10), kind=kOutput, calls=%fused_computation.16 | convolution fusion | flops 537133056 | bytes 3145728 | tf_op jit(solution)/shard_map/dot_general | solution.py:84
  14.4 0.9 pad_maximum_fusion
  15.3 12.0 %all-to-all-start = ((f32[32,40,128]{2,1,0:T(8,128)}), f32[32,40,128]{2,1,0:T(8,128)S(1)}, u32[]{:S(2)}, u32[]{:S(2)}) async-start(f32[32,40,128]{2,1,0:T(8,128)} %pad_maximum_fusion), calls=%async_computation | async-start | bytes 1310720 | tf_op jit(solution)/shard_map/all_to_all | solution.py:45
  27.4 1.2 copy.154
  28.8 2.5 %fusion.4 = bf16[32,8,8,128]{3,2,1,0:T(8,128)(2,1)S(1)} fusion(bf16[1024,1024]{1,0:T(8,128)(2,1)} %param.14, bf16[1,256,1024]{2,1,0:T(8,128)(2,1)} %param.10), kind=kOutput, calls=%fused_computation.17 | convolution fusion | flops 537133056 | bytes 3145728 | tf_op jit(solution)/shard_map/dot_general | solution.py:82
  31.3 0.7 convolution_multiply_fusion
  32.0 1.9 %copy-done.2 = f32[8,512,256]{2,1,0:T(8,128)} copy-done((f32[8,512,256]{2,1,0:T(8,128)}, f32[8,512,256]{2,1,0:T(8,128)S(1)}, u32[]{:S(2)}) %copy-start.2) | copy-done | bytes 4194328
  33.9 1.2 select_reduce_fusion.3
  35.1 8.7 %all-to-all-done = f32[32,40,128]{2,1,0:T(8,128)S(1)} async-done(((f32[32,40,128]{2,1,0:T(8,128)}), f32[32,40,128]{2,1,0:T(8,128)S(1)}, u32[]{:S(2)}, u32[]{:S(2)}) %all-to-all-start) | async-done | bytes 655392 | tf_op jit(solution)/shard_map/all_to_all | solution.py:45
  44.8 0.9 fusion.17
  45.7 1.1 copy.112
  46.8 8.6 %all-to-all-start.1 = ((f32[32,32,128]{2,1,0:T(8,128)}), f32[32,32,128]{2,1,0:T(8,128)S(1)}, u32[]{:S(2)}, u32[]{:S(2)}) async-start(f32[32,32,128]{2,1,0:T(8,128)} %copy.112), calls=%async_computation.1 | async-start | bytes 1048576 | tf_op jit(solution)/shard_map/all_to_all | solution.py:54
  55.6 1.5 select_reduce_fusion.2
  57.5 2.7 %subtract_exponential_fusion = f32[8,512,256]{2,1,0:T(8,128)} fusion(f32[8,512,256]{2,1,0:T(8,128)S(1)} %copy-done.3, f32[8,512,256]{2,1,0:T(8,128)S(1)} %select_reduce_fusion.2), kind=kLoop, calls=%fused_computation.6 | loop fusion | flops 1048576 | bytes 12582912 | tf_op jit(solution)/shard_map/exp | solution.py:116
  60.2 8.7 %all-to-all-done.1 = f32[32,32,128]{2,1,0:T(8,128)S(1)} async-done(((f32[32,32,128]{2,1,0:T(8,128)}), f32[32,32,128]{2,1,0:T(8,128)S(1)}, u32[]{:S(2)}, u32[]{:S(2)}) %all-to-all-start.1) | async-done | bytes 524320 | tf_op jit(solution)/shard_map/all_to_all | solution.py:54
  68.9 1.9 %convolution_multiply_fusion.1 = f32[8,128,256]{2,1,0:T(8,128)} fusion(f32[8,128,128]{2,1,0:T(8,128)S(1)} %bitcast.155, f32[256,8]{0,1:T(8,128)S(1)} %get-tuple-element.40, bf16[32,8,8,128]{3,2,1,0:T(8,128)(2,1)S(1)} %fusion.4), kind=kOutput, calls=%fused_computation.12 | convolution fusion | flops 202113024 | bytes 2105344 | tf_op jit(solution)/shard_map/thd,hde->the/dot_general | solution.py:137
  70.8 2.7 %fusion.67 = (f32[256,8]{0,1:T(8,128)S(1)}, f32[256,8,128]{0,2,1:T(8,128)S(1)}) fusion(f32[8,128,256]{2,1,0:T(8,128)} %convolution_multiply_fusion.1, bf16[256,8,128]{0,2,1:T(8,128)(2,1)} %bitcast.152, f32[8,256]{1,0:T(8,128)S(1)} %get-tuple-element.41, pred[256,256]{1,0:T(8,128)(4,1)S(1)} %fusion.38, bf16[32,8,8,128]{3,2,1,0:T(8,128)(2,1)} %copy-done.8, ...), kind=kOutput, calls=%fused_computation.148 | convolution fusion | flops 272103424 | bytes 3751936 | tf_op jit(solution)/shard_map/hts,shd->thd/dot_general | solution.py:103
  73.7 0.8 copy-done.4
  74.5 1.4 multiply_convert_fusion
  75.9 3.3 %bitcast_multiply_fusion = f32[8,512,256]{2,1,0:T(8,128)S(1)} fusion(f32[8,512,256]{2,1,0:T(8,128)} %subtract_exponential_fusion, bf16[256,8,128]{0,2,1:T(8,128)(2,1)S(1)} %multiply_convert_fusion, bf16[512,1024]{1,0:T(8,128)(2,1)} %param.19), kind=kOutput, calls=%fused_computation.5 | convolution fusion | flops 269484032 | bytes 9961472 | tf_op jit(solution)/shard_map/lhd,thd->hlt/dot_general | solution.py:149
  79.7 4.5 %select_reduce_fusion.1 = (f32[8,2,512]{2,1,0:T(2,128)S(1)}, f32[8,2,512]{2,1,0:T(2,128)S(1)}) fusion(f32[8,512,256]{2,1,0:T(8,128)S(1)} %bitcast_multiply_fusion, pred[2,256]{1,0:T(4,128)(4,1)S(1)} %iota_compare_fusion.6, f32[8,512,256]{2,1,0:T(8,128)S(1)} %copy-done.1), kind=kLoop, calls=%fused_computation.2 | loop fusion | flops 8372224 | bytes 8454656 | tf_op jit(solution)/shard_map/reduce_sum | solution.py:150
  84.2 3.3 %collective-permute-start = (f32[17,2,512]{2,1,0:T(2,128)S(1)}, f32[17,2,512]{2,1,0:T(2,128)S(1)}, u32[]{:S(2)}, u32[]{:S(2)}) collective-permute-start(f32[17,2,512]{2,1,0:T(2,128)S(1)} %pad_maximum_fusion.1), channel_id=1, source_target_pairs={{0,1},{1,0},{2,3},{3,2},{4,5},{5,4},{6,7},{7,6},{8,9},{9,8},{10,11... | collective-permute-start | bytes 208904 | tf_op jit(solution)/shard_map/ppermute | solution.py:17
  87.5 1.7 %collective-permute-done = f32[17,2,512]{2,1,0:T(2,128)S(1)} collective-permute-done((f32[17,2,512]{2,1,0:T(2,128)S(1)}, f32[17,2,512]{2,1,0:T(2,128)S(1)}, u32[]{:S(2)}, u32[]{:S(2)}) %collective-permute-start) | collective-permute-done | bytes 69664 | tf_op jit(solution)/shard_map/ppermute | solution.py:17
  89.4 1.8 %collective-permute-start.1 = (f32[17,2,512]{2,1,0:T(2,128)S(1)}, f32[17,2,512]{2,1,0:T(2,128)S(1)}, u32[]{:S(2)}, u32[]{:S(2)}) collective-permute-start(f32[17,2,512]{2,1,0:T(2,128)S(1)} %pad_maximum_fusion.2), channel_id=1, source_target_pairs={{0,2},{1,3},{2,0},{3,1},{4,6},{5,7},{6,4},{7,5},{8,10},{9,11},{10,... | collective-permute-start | bytes 208904 | tf_op jit(solution)/shard_map/ppermute | solution.py:17
  91.2 2.4 %collective-permute-done.1 = f32[17,2,512]{2,1,0:T(2,128)S(1)} collective-permute-done((f32[17,2,512]{2,1,0:T(2,128)S(1)}, f32[17,2,512]{2,1,0:T(2,128)S(1)}, u32[]{:S(2)}, u32[]{:S(2)}) %collective-permute-start.1) | collective-permute-done | bytes 69664 | tf_op jit(solution)/shard_map/ppermute | solution.py:17
  93.7 2.4 %collective-permute-start.2 = (f32[17,2,512]{2,1,0:T(2,128)S(1)}, f32[17,2,512]{2,1,0:T(2,128)S(1)}, u32[]{:S(2)}, u32[]{:S(2)}) collective-permute-start(f32[17,2,512]{2,1,0:T(2,128)S(1)} %pad_maximum_fusion.3), channel_id=1, source_target_pairs={{0,4},{1,5},{2,6},{3,7},{4,0},{5,1},{6,2},{7,3},{8,12},{9,13},{10,... | collective-permute-start | bytes 208904 | tf_op jit(solution)/shard_map/ppermute | solution.py:17
  96.1 4.8 %collective-permute-done.2 = f32[17,2,512]{2,1,0:T(2,128)S(1)} collective-permute-done((f32[17,2,512]{2,1,0:T(2,128)S(1)}, f32[17,2,512]{2,1,0:T(2,128)S(1)}, u32[]{:S(2)}, u32[]{:S(2)}) %collective-permute-start.2) | collective-permute-done | bytes 69664 | tf_op jit(solution)/shard_map/ppermute | solution.py:17
  101.1 1.0 collective-permute-start.3
  102.1 2.2 %collective-permute-done.3 = f32[17,2,512]{2,1,0:T(2,128)S(1)} collective-permute-done((f32[17,2,512]{2,1,0:T(2,128)S(1)}, f32[17,2,512]{2,1,0:T(2,128)S(1)}, u32[]{:S(2)}, u32[]{:S(2)}) %collective-permute-start.3) | collective-permute-done | bytes 69664 | tf_op jit(solution)/shard_map/ppermute | solution.py:17
  104.6 2.6 %collective-permute-start.4 = (f32[17,2,512]{2,0,1:T(8,128)S(1)}, f32[17,2,512]{2,0,1:T(8,128)S(1)}, u32[]{:S(2)}, u32[]{:S(2)}) collective-permute-start(f32[17,2,512]{2,0,1:T(8,128)S(1)} %copy.136), channel_id=1, source_target_pairs={{0,16},{1,17},{2,18},{3,19},{4,20},{5,21},{6,22},{7,23},{8,24},{9,... | collective-permute-start | bytes 208904 | tf_op jit(solution)/shard_map/ppermute | solution.py:17
  107.1 2.5 %collective-permute-done.4 = f32[17,2,512]{2,0,1:T(8,128)S(1)} collective-permute-done((f32[17,2,512]{2,0,1:T(8,128)S(1)}, f32[17,2,512]{2,0,1:T(8,128)S(1)}, u32[]{:S(2)}, u32[]{:S(2)}) %collective-permute-start.4) | collective-permute-done | bytes 69664 | tf_op jit(solution)/shard_map/ppermute | solution.py:17
  109.8 2.2 %collective-permute-start.5 = (f32[2,512]{1,0:T(2,128)S(1)}, f32[2,512]{1,0:T(2,128)S(1)}, u32[]{:S(2)}, u32[]{:S(2)}) collective-permute-start(f32[2,512]{1,0:T(2,128)S(1)} %fusion.45), channel_id=1, source_target_pairs={{0,1},{1,0},{2,3},{3,2},{4,5},{5,4},{6,7},{7,6},{8,9},{9,8},{10,11... | collective-permute-start | bytes 12296 | tf_op jit(solution)/shard_map/ppermute | solution.py:17
  112.0 1.0 collective-permute-done.5
  113.0 2.1 %collective-permute-start.6 = (f32[2,512]{1,0:T(2,128)S(1)}, f32[2,512]{1,0:T(2,128)S(1)}, u32[]{:S(2)}, u32[]{:S(2)}) collective-permute-start(f32[2,512]{1,0:T(2,128)S(1)} %add.148), channel_id=1, source_target_pairs={{0,2},{1,3},{2,0},{3,1},{4,6},{5,7},{6,4},{7,5},{8,10},{9,11},{10,... | collective-permute-start | bytes 12296 | tf_op jit(solution)/shard_map/ppermute | solution.py:17
  115.1 1.3 collective-permute-done.6
  116.4 2.8 %collective-permute-start.7 = (f32[2,512]{1,0:T(2,128)S(1)}, f32[2,512]{1,0:T(2,128)S(1)}, u32[]{:S(2)}, u32[]{:S(2)}) collective-permute-start(f32[2,512]{1,0:T(2,128)S(1)} %add.149), channel_id=1, source_target_pairs={{0,4},{1,5},{2,6},{3,7},{4,0},{5,1},{6,2},{7,3},{8,12},{9,13},{10,... | collective-permute-start | bytes 12296 | tf_op jit(solution)/shard_map/ppermute | solution.py:17
  119.2 3.6 %collective-permute-done.7 = f32[2,512]{1,0:T(2,128)S(1)} collective-permute-done((f32[2,512]{1,0:T(2,128)S(1)}, f32[2,512]{1,0:T(2,128)S(1)}, u32[]{:S(2)}, u32[]{:S(2)}) %collective-permute-start.7) | collective-permute-done | bytes 4128 | tf_op jit(solution)/shard_map/ppermute | solution.py:17
  122.7 1.0 collective-permute-start.8
  123.7 1.5 collective-permute-done.8
  125.2 2.1 %collective-permute-start.9 = (f32[2,512]{1,0:T(2,128)S(1)}, f32[2,512]{1,0:T(2,128)S(1)}, u32[]{:S(2)}, u32[]{:S(2)}) collective-permute-start(f32[2,512]{1,0:T(2,128)S(1)} %add.151), channel_id=1, source_target_pairs={{0,16},{1,17},{2,18},{3,19},{4,20},{5,21},{6,22},{7,23},{8,24},{9,... | collective-permute-start | bytes 12296 | tf_op jit(solution)/shard_map/ppermute | solution.py:17
  127.3 1.0 copy.142
  128.3 0.8 collective-permute-done.9
  129.9 1.1 multiply_reduce_fusion.1
  131.0 26.7 %psum.7 = f32[]{:T(128)} all-reduce(f32[]{:T(128)} %get-tuple-element.48), channel_id=1, replica_groups=mesh['dp'=8,'ctx'=32] {'dp'}, use_global_device_ids=true, to_apply=%region_15.16 | all-reduce | flops 1 | bytes 8 | tf_op jit(solution)/shard_map/psum | solution.py:159
  (86 shorter events, 8.9 us)
Async XLA Ops:
  0.6 7.3 %copy-start = (bf16[1024,1024]{1,0:T(8,128)(2,1)S(1)}, bf16[1024,1024]{1,0:T(8,128)(2,1)}, u32[]{:S(2)}) copy-start(bf16[1024,1024]{1,0:T(8,128)(2,1)} %param.15) | copy-start | bytes 6291460
  9.9 5.5 %copy-start.5 = (bf16[256,1024]{0,1:T(8,128)(2,1)}, bf16[256,1024]{0,1:T(8,128)(2,1)S(1)}, u32[]{:S(2)}) copy-start(bf16[256,1024]{0,1:T(8,128)(2,1)S(1)} %copy.147) | copy-start | bytes 1572868
  12.5 2.8 %copy-start.7 = (bf16[32,8,8,128]{3,2,1,0:T(8,128)(2,1)}, bf16[32,8,8,128]{3,2,1,0:T(8,128)(2,1)S(1)}, u32[]{:S(2)}) copy-start(bf16[32,8,8,128]{3,2,1,0:T(8,128)(2,1)S(1)} %fusion.3) | copy-start | bytes 1572868
  15.3 28.4 %all-to-all-start = ((f32[32,40,128]{2,1,0:T(8,128)}), f32[32,40,128]{2,1,0:T(8,128)S(1)}, u32[]{:S(2)}, u32[]{:S(2)}) async-start(f32[32,40,128]{2,1,0:T(8,128)} %pad_maximum_fusion), calls=%async_computation | async-start | bytes 1310720 | tf_op jit(solution)/shard_map/all_to_all | solution.py:45
  27.4 3.9 %copy-start.6 = (bf16[512,1024]{1,0:T(8,128)(2,1)S(1)}, bf16[512,1024]{1,0:T(8,128)(2,1)}, u32[]{:S(2)}) copy-start(bf16[512,1024]{1,0:T(8,128)(2,1)} %param.18) | copy-start | bytes 3145732
  31.2 37.7 %copy-start.8 = (bf16[32,8,8,128]{3,2,1,0:T(8,128)(2,1)}, bf16[32,8,8,128]{3,2,1,0:T(8,128)(2,1)S(1)}, u32[]{:S(2)}) copy-start(bf16[32,8,8,128]{3,2,1,0:T(8,128)(2,1)S(1)} %fusion.4) | copy-start | bytes 1572868
  32.0 1.9 %copy-start.2 = (f32[8,512,256]{2,1,0:T(8,128)}, f32[8,512,256]{2,1,0:T(8,128)S(1)}, u32[]{:S(2)}) copy-start(f32[8,512,256]{2,1,0:T(8,128)S(1)} %convolution_multiply_fusion) | copy-start | bytes 12582916
  33.9 21.4 %copy-start.11 = (s32[1,256]{1,0:T(1,128)S(1)}, s32[1,256]{1,0:T(1,128)}, u32[]{:S(2)}) copy-start(s32[1,256]{1,0:T(1,128)} %param.13) | copy-start | bytes 3076
  46.8 22.1 %all-to-all-start.1 = ((f32[32,32,128]{2,1,0:T(8,128)}), f32[32,32,128]{2,1,0:T(8,128)S(1)}, u32[]{:S(2)}, u32[]{:S(2)}) async-start(f32[32,32,128]{2,1,0:T(8,128)} %copy.112), calls=%async_computation.1 | async-start | bytes 1048576 | tf_op jit(solution)/shard_map/all_to_all | solution.py:54
  55.3 2.2 %copy-start.3 = (f32[8,512,256]{2,1,0:T(8,128)S(1)}, f32[8,512,256]{2,1,0:T(8,128)}, u32[]{:S(2)}) copy-start(f32[8,512,256]{2,1,0:T(8,128)} %copy-done.2) | copy-start | bytes 12582916
  68.9 5.6 %copy-start.9 = (f32[1024]{0:T(1024)S(1)}, f32[1024]{0:T(1024)}, u32[]{:S(2)}) copy-start(f32[1024]{0:T(1024)} %param.17) | copy-start | bytes 12292
  73.5 1.0 copy-start.4
  75.9 3.7 %copy-start.1 = (f32[8,512,256]{2,1,0:T(8,128)S(1)}, f32[8,512,256]{2,1,0:T(8,128)}, u32[]{:S(2)}) copy-start(f32[8,512,256]{2,1,0:T(8,128)} %subtract_exponential_fusion) | copy-start | bytes 12582916
  79.7 47.7 %copy-start.10 = (s32[1,2]{1,0:T(1,128)S(1)}, s32[1,2]{1,0:T(1,128)}, u32[]{:S(2)}) copy-start(s32[1,2]{1,0:T(1,128)} %param.12) | copy-start | bytes 28
  84.2 5.0 %collective-permute-start = (f32[17,2,512]{2,1,0:T(2,128)S(1)}, f32[17,2,512]{2,1,0:T(2,128)S(1)}, u32[]{:S(2)}, u32[]{:S(2)}) collective-permute-start(f32[17,2,512]{2,1,0:T(2,128)S(1)} %pad_maximum_fusion.1), channel_id=1, source_target_pairs={{0,1},{1,0},{2,3},{3,2},{4,5},{5,4},{6,7},{7,6},{8,9},{9,8},{10,11... | collective-permute-start | bytes 208904 | tf_op jit(solution)/shard_map/ppermute | solution.py:17
  89.4 4.1 %collective-permute-start.1 = (f32[17,2,512]{2,1,0:T(2,128)S(1)}, f32[17,2,512]{2,1,0:T(2,128)S(1)}, u32[]{:S(2)}, u32[]{:S(2)}) collective-permute-start(f32[17,2,512]{2,1,0:T(2,128)S(1)} %pad_maximum_fusion.2), channel_id=1, source_target_pairs={{0,2},{1,3},{2,0},{3,1},{4,6},{5,7},{6,4},{7,5},{8,10},{9,11},{10,... | collective-permute-start | bytes 208904 | tf_op jit(solution)/shard_map/ppermute | solution.py:17
  93.7 7.2 %collective-permute-start.2 = (f32[17,2,512]{2,1,0:T(2,128)S(1)}, f32[17,2,512]{2,1,0:T(2,128)S(1)}, u32[]{:S(2)}, u32[]{:S(2)}) collective-permute-start(f32[17,2,512]{2,1,0:T(2,128)S(1)} %pad_maximum_fusion.3), channel_id=1, source_target_pairs={{0,4},{1,5},{2,6},{3,7},{4,0},{5,1},{6,2},{7,3},{8,12},{9,13},{10,... | collective-permute-start | bytes 208904 | tf_op jit(solution)/shard_map/ppermute | solution.py:17
  101.1 3.2 %collective-permute-start.3 = (f32[17,2,512]{2,1,0:T(2,128)S(1)}, f32[17,2,512]{2,1,0:T(2,128)S(1)}, u32[]{:S(2)}, u32[]{:S(2)}) collective-permute-start(f32[17,2,512]{2,1,0:T(2,128)S(1)} %pad_maximum_fusion.4), channel_id=1, source_target_pairs={{0,8},{1,9},{2,10},{3,11},{4,12},{5,13},{6,14},{7,15},{8,0},{9,1},... | collective-permute-start | bytes 208904 | tf_op jit(solution)/shard_map/ppermute | solution.py:17
  104.6 5.1 %collective-permute-start.4 = (f32[17,2,512]{2,0,1:T(8,128)S(1)}, f32[17,2,512]{2,0,1:T(8,128)S(1)}, u32[]{:S(2)}, u32[]{:S(2)}) collective-permute-start(f32[17,2,512]{2,0,1:T(8,128)S(1)} %copy.136), channel_id=1, source_target_pairs={{0,16},{1,17},{2,18},{3,19},{4,20},{5,21},{6,22},{7,23},{8,24},{9,... | collective-permute-start | bytes 208904 | tf_op jit(solution)/shard_map/ppermute | solution.py:17
  109.8 3.2 %collective-permute-start.5 = (f32[2,512]{1,0:T(2,128)S(1)}, f32[2,512]{1,0:T(2,128)S(1)}, u32[]{:S(2)}, u32[]{:S(2)}) collective-permute-start(f32[2,512]{1,0:T(2,128)S(1)} %fusion.45), channel_id=1, source_target_pairs={{0,1},{1,0},{2,3},{3,2},{4,5},{5,4},{6,7},{7,6},{8,9},{9,8},{10,11... | collective-permute-start | bytes 12296 | tf_op jit(solution)/shard_map/ppermute | solution.py:17
  113.0 3.4 %collective-permute-start.6 = (f32[2,512]{1,0:T(2,128)S(1)}, f32[2,512]{1,0:T(2,128)S(1)}, u32[]{:S(2)}, u32[]{:S(2)}) collective-permute-start(f32[2,512]{1,0:T(2,128)S(1)} %add.148), channel_id=1, source_target_pairs={{0,2},{1,3},{2,0},{3,1},{4,6},{5,7},{6,4},{7,5},{8,10},{9,11},{10,... | collective-permute-start | bytes 12296 | tf_op jit(solution)/shard_map/ppermute | solution.py:17
  116.4 6.4 %collective-permute-start.7 = (f32[2,512]{1,0:T(2,128)S(1)}, f32[2,512]{1,0:T(2,128)S(1)}, u32[]{:S(2)}, u32[]{:S(2)}) collective-permute-start(f32[2,512]{1,0:T(2,128)S(1)} %add.149), channel_id=1, source_target_pairs={{0,4},{1,5},{2,6},{3,7},{4,0},{5,1},{6,2},{7,3},{8,12},{9,13},{10,... | collective-permute-start | bytes 12296 | tf_op jit(solution)/shard_map/ppermute | solution.py:17
  122.7 2.5 %collective-permute-start.8 = (f32[2,512]{1,0:T(2,128)S(1)}, f32[2,512]{1,0:T(2,128)S(1)}, u32[]{:S(2)}, u32[]{:S(2)}) collective-permute-start(f32[2,512]{1,0:T(2,128)S(1)} %add.150), channel_id=1, source_target_pairs={{0,8},{1,9},{2,10},{3,11},{4,12},{5,13},{6,14},{7,15},{8,0},{9,1},... | collective-permute-start | bytes 12296 | tf_op jit(solution)/shard_map/ppermute | solution.py:17
  125.2 4.0 %collective-permute-start.9 = (f32[2,512]{1,0:T(2,128)S(1)}, f32[2,512]{1,0:T(2,128)S(1)}, u32[]{:S(2)}, u32[]{:S(2)}) collective-permute-start(f32[2,512]{1,0:T(2,128)S(1)} %add.151), channel_id=1, source_target_pairs={{0,16},{1,17},{2,18},{3,19},{4,20},{5,21},{6,22},{7,23},{8,24},{9,... | collective-permute-start | bytes 12296 | tf_op jit(solution)/shard_map/ppermute | solution.py:17

commit v3 on v2

--- a/solution.py
+++ b/solution.py
@@ -33,17 +33,34 @@
     return jnp.sum((starts[:, None] <= positions[None, :]).astype(jnp.int32), axis=0) - 1
 
 
-def exclusive_state_scan(local_state, carry, axis):
+def exclusive_state_scan(local_state, carry, stats, axis):
     head_count, head_dim, _ = local_state.shape
     count = lax.axis_size(axis)
     rows = head_count * head_dim // count
     assert rows * count == head_count * head_dim and head_dim % rows == 0
+    pair_count, fields = stats.shape
+    per_owner = pair_count // count
+    assert per_owner * count == pair_count and per_owner * fields < 8 * head_dim
+    pad = 8 * head_dim - per_owner * fields - 1
     owner_head = (jnp.arange(count) * rows) // head_dim
     slices = local_state.reshape(count, rows, head_dim)
-    factor_rows = jnp.broadcast_to(carry[owner_head][:, None, None], (count, 8, head_dim))
-    sent = jnp.concatenate([slices, factor_rows], axis=1)
-    got = lax.all_to_all(sent, axis, 0, 0)
-    factors = got[:, rows, 0]
+    extra = jnp.concatenate(
+        [
+            stats.reshape(count, per_owner * fields),
+            carry[owner_head][:, None],
+            jnp.zeros((count, pad), jnp.float32),
+        ],
+        axis=1,
+    ).reshape(count, 8, head_dim)
+    got = lax.all_to_all(jnp.concatenate([slices, extra], axis=1), axis, 0, 0)
+    got_extra = got[:, rows:, :].reshape(count, 8 * head_dim)
+    factors = got_extra[:, per_owner * fields]
+    part = got_extra[:, : per_owner * fields].reshape(count, per_owner, fields)
+    part_top = part[:, :, :head_count]
+    top = jnp.max(part_top, axis=0)
+    mass = jnp.sum(part[:, :, head_count:2 * head_count] * jnp.exp(part_top - top[None]), axis=0)
+    tally = jnp.sum(part[:, :, 2 * head_count:], axis=0)
+    combined = jnp.concatenate([top, mass, tally], axis=1).reshape(1, per_owner * fields)
     block = jnp.arange(count)
     inside = (block[None, None, :] > block[None, :, None]) & (block[None, None, :] < block[:, None, None])
     spans = jnp.prod(jnp.where(inside, factors[None, None, :], 1.0), axis=2)
@@ -51,8 +68,15 @@
     scanned = jnp.dot(
         mix, got[:, :rows, :].reshape(count, rows * head_dim), precision=lax.Precision.HIGHEST
     )
-    back = lax.all_to_all(scanned.reshape(count, rows, head_dim), axis, 0, 0)
-    return back.reshape(head_count, head_dim, head_dim)
+    back_extra = jnp.broadcast_to(
+        jnp.concatenate([combined, jnp.zeros((1, pad + 1), jnp.float32)], axis=1),
+        (count, 8 * head_dim),
+    ).reshape(count, 8, head_dim)
+    sent_back = jnp.concatenate([scanned.reshape(count, rows, head_dim), back_extra], axis=1)
+    back = lax.all_to_all(sent_back, axis, 0, 0)
+    state = back[:, :rows, :].reshape(head_count, head_dim, head_dim)
+    totals = back[:, rows:, :].reshape(count, 8 * head_dim)[:, : per_owner * fields]
+    return state, totals.reshape(pair_count, fields)
 
 
 def local(
@@ -95,7 +119,6 @@
     k_decayed = (k3.astype(jnp.float32) * k_factor.T[:, :, None]).astype(jnp.bfloat16)
     local_state = jnp.einsum("thd,the->hde", k_decayed, v3, preferred_element_type=jnp.float32)
     carry = jnp.where(linked[tok_rows - 1], jnp.exp(last_cum), 0.0)
-    incoming = exclusive_state_scan(local_state, carry, "ctx")
 
     scores = jnp.einsum("thd,shd->hts", q3, k3, preferred_element_type=jnp.float32) * qk_scale
     decay_pair = jnp.exp(jnp.minimum(decay_cum[:, :, None] - decay_cum[:, None, :], 0.0))
@@ -120,17 +143,19 @@
     )
     counts = jnp.dot(member.astype(jnp.bfloat16), label_hot, preferred_element_type=jnp.float32)
 
-    top, total_mass, total_counts = maxima, mass, counts
-    for bit in butterfly_bits("ctx"):
-        packed = jnp.concatenate([top, total_mass, total_counts[None]], axis=0)
-        other = swapped(packed, "ctx", bit)
-        o_top = other[:head_count]
-        o_mass = other[head_count:2 * head_count]
-        o_counts = other[2 * head_count]
-        new_top = jnp.maximum(top, o_top)
-        total_mass = total_mass * jnp.exp(top - new_top) + o_mass * jnp.exp(o_top - new_top)
-        total_counts = total_counts + o_counts
-        top = new_top
+    stats = jnp.concatenate(
+        [
+            jnp.transpose(maxima, (1, 2, 0)),
+            jnp.transpose(mass, (1, 2, 0)),
+            counts[:, :, None],
+        ],
+        axis=2,
+    ).reshape(record_count * label_count, 2 * head_count + 1)
+    incoming, totals = exclusive_state_scan(local_state, carry, stats, "ctx")
+    totals = totals.reshape(record_count, label_count, 2 * head_count + 1)
+    top = jnp.transpose(totals[:, :, :head_count], (2, 0, 1))
+    total_mass = jnp.transpose(totals[:, :, head_count:2 * head_count], (2, 0, 1))
+    total_counts = totals[:, :, 2 * head_count]
     rescale = jnp.exp(maxima - top) / total_mass
 
     q_decayed = q3.astype(jnp.float32) * jnp.where(linked[None, :], jnp.exp(decay_cum), 0.0).T[:, :, None]

time: 160 us -> 148 us (0.925)
  starting transfers between devices: 41.9 us -> 30.7 us
  local copies, waits for them, and re-layouts: 9.82 us -> 16.3 us
  blocking collectives: 26.7 us -> 21.5 us
  other arithmetic: 21.5 us -> 17.1 us
  matrix products: 17 us -> 19.5 us
    ppermute x10 -> x5, waiting for transfers between devices: 21.7 us -> 8.65 us  [swapped(): return lax.ppermute(x, axis, [(i, i ^ bit) for i in range(count)])]
    all_to_all x2, waiting for transfers between devices: 17.4 us -> 29.8 us  [the longest x1 16.4 us: exclusive_state_scan(): got = lax.all_to_all(jnp.concatenate([slices, extra], axis=1), axis, 0, 0)]
    ppermute x10 -> x5, starting transfers between devices: 21.3 us -> 10.1 us  [swapped(): return lax.ppermute(x, axis, [(i, i ^ bit) for i in range(count)])]
    psum x1, blocking collectives: 26.7 us -> 21.5 us  [local(): lax.psum(jnp.sum(rec_loss), 'dp') / (lax.axis_size('dp') * record_count)]
    reduce_sum x1, other arithmetic: 4.51 us -> 1.19 us  [local(): jnp.sum(jnp.where(member[None, :, None, :], (pool_weight * label_value)[:...]
    unnamed x26 -> x31, local copies, waits for them, and re-layouts: 5.73 us -> 8.21 us
    reduce_sum x0 -> x3, other arithmetic: none -> 1.7 us  [the longest x1 1.19 us: local(): jnp.sum(jnp.where(member[None, :, None, :], pool_weight[:, None], 0.0), a...]
  transfers between devices with their start and end apart: 12 -> 7, of which waited for: 12 -> 7; matrix products, arithmetic and copies ran while one was open for 7% -> 3% of each run, Pallas kernels for 0% -> 0%
where the time goes in v3:
time: 148 us; the launch traced here: 147 us
  waiting for transfers between devices  38.4 us (26%)
  starting transfers between devices  30.7 us (21%)
  blocking collectives  21.5 us (15%)
  matrix products  19.5 us (13%)
  other arithmetic  17.1 us (12%)
  local copies, waits for them, and re-layouts  16.3 us (11%)
  between operations  3.5 us (2%)
    psum x1, blocking collectives, local(): lax.psum(jnp.sum(rec_loss), 'dp') / (lax.axis_size('dp') * record_count)  21.5 us
    all_to_all x1, waiting for transfers between devices, exclusive_state_scan(): got = lax.all_to_all(jnp.concatenate([slices, extra], axis=1), axis, 0, 0)  16.4 us
    all_to_all x1, waiting for transfers between devices, exclusive_state_scan(): back = lax.all_to_all(sent_back, axis, 0, 0)  13.4 us
    all_to_all x1, starting transfers between devices, exclusive_state_scan(): got = lax.all_to_all(jnp.concatenate([slices, extra], axis=1), axis, 0, 0)  12 us
    ppermute x5, starting transfers between devices, swapped(): return lax.ppermute(x, axis, [(i, i ^ bit) for i in range(count)])  10.1 us
    ppermute x5, waiting for transfers between devices, swapped(): return lax.ppermute(x, axis, [(i, i ^ bit) for i in range(count)])  8.65 us
    all_to_all x1, starting transfers between devices, exclusive_state_scan(): back = lax.all_to_all(sent_back, axis, 0, 0)  8.57 us
    unnamed x31, local copies, waits for them, and re-layouts  8.21 us
  transfers between devices with their start and end apart: 7, of which 7 were waited for; matrix products, arithmetic and copies ran while one was open for 3% of the time, Pallas kernels for 0%

profile of v3, /device:TPU:1, one launch (start us, length us, event | category | flops | bytes accessed | tf_op | source)
XLA Modules:
  0.0 147.0 jit_solution(15901839097047175490)
XLA Ops:
  0.7 1.0 reduce-window.10
  1.6 0.7 bitcast_subtract_fusion.1
  3.0 1.1 copy.120
  4.1 1.9 %convolution_multiply_fusion = f32[8,512,256]{2,1,0:T(8,128)S(1)} fusion(bf16[256,8,128]{2,1,0:T(8,128)(2,1)S(1)} %bitcast.141, bf16[512,1024]{1,0:T(8,128)(2,1)} %param.18), kind=kOutput, calls=%fused_computation.7 | convolution fusion | flops 269484032 | bytes 5767168 | tf_op jit(solution)/shard_map/lhd,thd->hlt/dot_general | solution.py:132
  6.1 1.2 select_reduce_fusion.3
  7.3 1.5 %select_reduce_fusion.2 = f32[8,512,256]{2,1,0:T(8,128)S(1)} fusion(f32[8,2,512]{2,1,0:T(2,128)S(1)} %select_reduce_fusion.3, pred[2,256]{1,0:T(4,128)(4,1)S(1)} %iota_compare_fusion.6), kind=kLoop, calls=%fused_computation.3 | loop fusion | flops 3145728 | bytes 4227584 | tf_op jit(solution)/shard_map/reduce_sum | solution.py:136
  8.8 1.2 subtract_exponential_fusion
  10.1 1.9 %copy-done.1 = f32[8,512,256]{2,1,0:T(8,128)} copy-done((f32[8,512,256]{2,1,0:T(8,128)}, f32[8,512,256]{2,1,0:T(8,128)S(1)}, u32[]{:S(2)}) %copy-start.1) | copy-done | bytes 4194328
  12.0 1.2 select_reduce_fusion.1
  14.0 0.6 fusion.49
  16.1 0.7 broadcast_compare_fusion.1
  17.6 0.7 broadcast_select_fusion
  18.3 0.7 gather_fusion
  19.3 1.5 %convolution_convert_fusion = bf16[256,1024]{1,0:T(8,128)(2,1)} fusion(bf16[1024,1024]{1,0:T(8,128)(2,1)S(1)} %copy-done, bf16[1,256,1024]{2,1,0:T(8,128)(2,1)S(1)} %copy-done.6), kind=kOutput, calls=%fused_computation.13 | convolution fusion | flops 537133056 | bytes 3145728 | tf_op jit(solution)/shard_map/dot_general | solution.py:107
  20.8 1.2 copy.114
  22.1 2.6 %fusion.3 = bf16[32,8,8,128]{3,2,1,0:T(8,128)(2,1)S(1)} fusion(bf16[1024,1024]{1,0:T(8,128)(2,1)} %param.16, bf16[1,256,1024]{2,1,0:T(8,128)(2,1)} %param.10), kind=kOutput, calls=%fused_computation.16 | convolution fusion | flops 537133056 | bytes 3145728 | tf_op jit(solution)/shard_map/dot_general | solution.py:108
  25.1 0.9 pad_maximum_fusion
  25.9 12.0 %all-to-all-start = ((f32[32,40,128]{2,1,0:T(8,128)}), f32[32,40,128]{2,1,0:T(8,128)S(1)}, u32[]{:S(2)}, u32[]{:S(2)}) async-start(f32[32,40,128]{2,1,0:T(8,128)} %pad_maximum_fusion), calls=%async_computation | async-start | bytes 1310720 | tf_op jit(solution)/shard_map/all_to_all | solution.py:55
  38.0 16.4 %all-to-all-done = f32[32,40,128]{2,1,0:T(8,128)S(1)} async-done(((f32[32,40,128]{2,1,0:T(8,128)}), f32[32,40,128]{2,1,0:T(8,128)S(1)}, u32[]{:S(2)}, u32[]{:S(2)}) %all-to-all-start) | async-done | bytes 655392 | tf_op jit(solution)/shard_map/all_to_all | solution.py:55
  56.8 0.9 fusion.17
  57.7 1.2 copy.100
  59.0 8.6 %all-to-all-start.1 = ((f32[32,40,128]{2,1,0:T(8,128)}), f32[32,40,128]{2,1,0:T(8,128)S(1)}, u32[]{:S(2)}, u32[]{:S(2)}) async-start(f32[32,40,128]{2,1,0:T(8,128)} %copy.100), calls=%async_computation.1 | async-start | bytes 1310720 | tf_op jit(solution)/shard_map/all_to_all | solution.py:76
  67.7 3.1 %fusion.4 = bf16[32,8,8,128]{3,2,1,0:T(8,128)(2,1)} fusion(bf16[1024,1024]{1,0:T(8,128)(2,1)} %param.14, bf16[1,256,1024]{2,1,0:T(8,128)(2,1)S(1)} %copy-done.7), kind=kOutput, calls=%fused_computation.17 | convolution fusion | flops 537133056 | bytes 3145728 | tf_op jit(solution)/shard_map/dot_general | solution.py:106
  70.8 13.4 %all-to-all-done.1 = f32[32,40,128]{2,1,0:T(8,128)S(1)} async-done(((f32[32,40,128]{2,1,0:T(8,128)}), f32[32,40,128]{2,1,0:T(8,128)S(1)}, u32[]{:S(2)}, u32[]{:S(2)}) %all-to-all-start.1) | async-done | bytes 655392 | tf_op jit(solution)/shard_map/all_to_all | solution.py:76
  84.2 0.8 copy-done.3
  85.0 2.9 %convolution_multiply_fusion.1 = f32[8,128,256]{2,1,0:T(8,128)} fusion(f32[8,128,128]{2,1,0:T(8,128)S(1)} %bitcast.140, f32[256,8]{0,1:T(8,128)S(1)} %get-tuple-element.24, bf16[32,8,8,128]{3,2,1,0:T(8,128)(2,1)} %fusion.4), kind=kOutput, calls=%fused_computation.12 | convolution fusion | flops 202113024 | bytes 2105344 | tf_op jit(solution)/shard_map/thd,hde->the/dot_general | solution.py:162
  88.0 2.7 %fusion.56 = (f32[256,8]{0,1:T(8,128)S(1)}, f32[256,8,128]{0,2,1:T(8,128)S(1)}) fusion(f32[8,128,256]{2,1,0:T(8,128)} %convolution_multiply_fusion.1, bf16[256,8,128]{0,2,1:T(8,128)(2,1)} %bitcast.137, f32[8,256]{1,0:T(8,128)S(1)} %get-tuple-element.25, pred[256,256]{1,0:T(8,128)(4,1)S(1)} %fusion.39, bf16[32,8,8,128]{3,2,1,0:T(8,128)(2,1)} %fusion.4, ...), kind=kOutput, calls=%fused_computation.119 | convolution fusion | flops 272103424 | bytes 3751936 | tf_op jit(solution)/shard_map/hts,shd->thd/dot_general | solution.py:126
  90.8 0.8 copy-done.2
  91.7 1.4 multiply_convert_fusion
  93.1 3.2 %bitcast_multiply_fusion = f32[8,512,256]{2,1,0:T(8,128)S(1)} fusion(f32[8,512,256]{2,1,0:T(8,128)} %copy-done.1, bf16[256,8,128]{0,2,1:T(8,128)(2,1)S(1)} %multiply_convert_fusion, bf16[512,1024]{1,0:T(8,128)(2,1)} %param.19), kind=kOutput, calls=%fused_computation.5 | convolution fusion | flops 269484032 | bytes 9961472 | tf_op jit(solution)/shard_map/lhd,thd->hlt/dot_general | solution.py:174
  96.3 1.2 select_reduce_fusion
  98.1 1.1 fusion.55
  99.2 1.2 copy.112
  100.5 1.2 copy.113
  101.7 2.8 %collective-permute-start = (f32[2,512]{1,0:T(2,128)S(1)}, f32[2,512]{1,0:T(2,128)S(1)}, u32[]{:S(2)}, u32[]{:S(2)}) collective-permute-start(f32[2,512]{1,0:T(2,128)S(1)} %fusion.42), channel_id=1, source_target_pairs={{0,1},{1,0},{2,3},{3,2},{4,5},{5,4},{6,7},{7,6},{8,9},{9,8},{10,11... | collective-permute-start | bytes 12296 | tf_op jit(solution)/shard_map/ppermute | solution.py:17
  104.5 1.0 collective-permute-done
  105.5 1.7 %collective-permute-start.1 = (f32[2,512]{1,0:T(2,128)S(1)}, f32[2,512]{1,0:T(2,128)S(1)}, u32[]{:S(2)}, u32[]{:S(2)}) collective-permute-start(f32[2,512]{1,0:T(2,128)S(1)} %add.114), channel_id=1, source_target_pairs={{0,2},{1,3},{2,0},{3,1},{4,6},{5,7},{6,4},{7,5},{8,10},{9,11},{10,... | collective-permute-start | bytes 12296 | tf_op jit(solution)/shard_map/ppermute | solution.py:17
  107.3 1.6 %collective-permute-done.1 = f32[2,512]{1,0:T(2,128)S(1)} collective-permute-done((f32[2,512]{1,0:T(2,128)S(1)}, f32[2,512]{1,0:T(2,128)S(1)}, u32[]{:S(2)}, u32[]{:S(2)}) %collective-permute-start.1) | collective-permute-done | bytes 4128 | tf_op jit(solution)/shard_map/ppermute | solution.py:17
  108.9 2.7 %collective-permute-start.2 = (f32[2,512]{1,0:T(2,128)S(1)}, f32[2,512]{1,0:T(2,128)S(1)}, u32[]{:S(2)}, u32[]{:S(2)}) collective-permute-start(f32[2,512]{1,0:T(2,128)S(1)} %add.115), channel_id=1, source_target_pairs={{0,4},{1,5},{2,6},{3,7},{4,0},{5,1},{6,2},{7,3},{8,12},{9,13},{10,... | collective-permute-start | bytes 12296 | tf_op jit(solution)/shard_map/ppermute | solution.py:17
  111.6 3.6 %collective-permute-done.2 = f32[2,512]{1,0:T(2,128)S(1)} collective-permute-done((f32[2,512]{1,0:T(2,128)S(1)}, f32[2,512]{1,0:T(2,128)S(1)}, u32[]{:S(2)}, u32[]{:S(2)}) %collective-permute-start.2) | collective-permute-done | bytes 4128 | tf_op jit(solution)/shard_map/ppermute | solution.py:17
  115.2 0.8 collective-permute-start.3
  116.1 1.6 %collective-permute-done.3 = f32[2,512]{1,0:T(2,128)S(1)} collective-permute-done((f32[2,512]{1,0:T(2,128)S(1)}, f32[2,512]{1,0:T(2,128)S(1)}, u32[]{:S(2)}, u32[]{:S(2)}) %collective-permute-start.3) | collective-permute-done | bytes 4128 | tf_op jit(solution)/shard_map/ppermute | solution.py:17
  117.7 2.1 %collective-permute-start.4 = (f32[2,512]{1,0:T(2,128)S(1)}, f32[2,512]{1,0:T(2,128)S(1)}, u32[]{:S(2)}, u32[]{:S(2)}) collective-permute-start(f32[2,512]{1,0:T(2,128)S(1)} %add.117), channel_id=1, source_target_pairs={{0,16},{1,17},{2,18},{3,19},{4,20},{5,21},{6,22},{7,23},{8,24},{9,... | collective-permute-start | bytes 12296 | tf_op jit(solution)/shard_map/ppermute | solution.py:17
  120.1 1.0 copy.108
  121.2 0.7 collective-permute-done.4
  121.9 0.7 fusion.47
  122.6 1.1 multiply_reduce_fusion.1
  123.7 21.5 %psum.7 = f32[]{:T(128)} all-reduce(f32[]{:T(128)} %get-tuple-element.32), channel_id=1, replica_groups=mesh['dp'=8,'ctx'=32] {'dp'}, use_global_device_ids=true, to_apply=%region_18.19 | all-reduce | flops 1 | bytes 8 | tf_op jit(solution)/shard_map/psum | solution.py:184
  (80 shorter events, 7.6 us)
Async XLA Ops:
  0.6 18.7 %copy-start = (bf16[1024,1024]{1,0:T(8,128)(2,1)S(1)}, bf16[1024,1024]{1,0:T(8,128)(2,1)}, u32[]{:S(2)}) copy-start(bf16[1024,1024]{1,0:T(8,128)(2,1)} %param.15) | copy-start | bytes 6291460
  10.0 1.9 %copy-start.1 = (f32[8,512,256]{2,1,0:T(8,128)}, f32[8,512,256]{2,1,0:T(8,128)S(1)}, u32[]{:S(2)}) copy-start(f32[8,512,256]{2,1,0:T(8,128)S(1)} %subtract_exponential_fusion) | copy-start | bytes 12582916
  12.0 1.2 copy-start.11
  12.0 2.0 %copy-start.10 = (s32[1,2]{1,0:T(1,128)S(1)}, s32[1,2]{1,0:T(1,128)}, u32[]{:S(2)}) copy-start(s32[1,2]{1,0:T(1,128)} %param.12) | copy-start | bytes 28
  12.0 3.3 %copy-start.8 = (f32[1,8,256]{2,1,0:T(8,128)S(1)}, f32[1,8,256]{2,1,0:T(8,128)}, u32[]{:S(2)}) copy-start(f32[1,8,256]{2,1,0:T(8,128)} %param.11) | copy-start | bytes 24580
  12.0 7.3 %copy-start.6 = (bf16[1,256,1024]{2,1,0:T(8,128)(2,1)S(1)}, bf16[1,256,1024]{2,1,0:T(8,128)(2,1)}, u32[]{:S(2)}) copy-start(bf16[1,256,1024]{2,1,0:T(8,128)(2,1)} %param.10) | copy-start | bytes 1572868
  22.1 32.5 %copy-start.4 = (bf16[256,1024]{0,1:T(8,128)(2,1)}, bf16[256,1024]{0,1:T(8,128)(2,1)S(1)}, u32[]{:S(2)}) copy-start(bf16[256,1024]{0,1:T(8,128)(2,1)S(1)} %copy.114) | copy-start | bytes 1572868
  24.7 1.2 copy-start.5
  25.9 28.4 %all-to-all-start = ((f32[32,40,128]{2,1,0:T(8,128)}), f32[32,40,128]{2,1,0:T(8,128)S(1)}, u32[]{:S(2)}, u32[]{:S(2)}) async-start(f32[32,40,128]{2,1,0:T(8,128)} %pad_maximum_fusion), calls=%async_computation | async-start | bytes 1310720 | tf_op jit(solution)/shard_map/all_to_all | solution.py:55
  56.8 10.9 %copy-start.7 = (bf16[1,256,1024]{2,1,0:T(8,128)(2,1)S(1)}, bf16[1,256,1024]{2,1,0:T(8,128)(2,1)}, u32[]{:S(2)}) copy-start(bf16[1,256,1024]{2,1,0:T(8,128)(2,1)} %param.10) | copy-start | bytes 1572868
  59.0 25.2 %all-to-all-start.1 = ((f32[32,40,128]{2,1,0:T(8,128)}), f32[32,40,128]{2,1,0:T(8,128)S(1)}, u32[]{:S(2)}, u32[]{:S(2)}) async-start(f32[32,40,128]{2,1,0:T(8,128)} %copy.100), calls=%async_computation.1 | async-start | bytes 1310720 | tf_op jit(solution)/shard_map/all_to_all | solution.py:76
  84.2 0.9 copy-start.3
  85.0 6.6 %copy-start.9 = (f32[1024]{0:T(1024)S(1)}, f32[1024]{0:T(1024)}, u32[]{:S(2)}) copy-start(f32[1024]{0:T(1024)} %param.17) | copy-start | bytes 12292
  90.7 1.0 copy-start.2
  96.3 1.2 slice-start
  101.7 3.8 %collective-permute-start = (f32[2,512]{1,0:T(2,128)S(1)}, f32[2,512]{1,0:T(2,128)S(1)}, u32[]{:S(2)}, u32[]{:S(2)}) collective-permute-start(f32[2,512]{1,0:T(2,128)S(1)} %fusion.42), channel_id=1, source_target_pairs={{0,1},{1,0},{2,3},{3,2},{4,5},{5,4},{6,7},{7,6},{8,9},{9,8},{10,11... | collective-permute-start | bytes 12296 | tf_op jit(solution)/shard_map/ppermute | solution.py:17
  105.5 3.4 %collective-permute-start.1 = (f32[2,512]{1,0:T(2,128)S(1)}, f32[2,512]{1,0:T(2,128)S(1)}, u32[]{:S(2)}, u32[]{:S(2)}) collective-permute-start(f32[2,512]{1,0:T(2,128)S(1)} %add.114), channel_id=1, source_target_pairs={{0,2},{1,3},{2,0},{3,1},{4,6},{5,7},{6,4},{7,5},{8,10},{9,11},{10,... | collective-permute-start | bytes 12296 | tf_op jit(solution)/shard_map/ppermute | solution.py:17
  108.9 6.4 %collective-permute-start.2 = (f32[2,512]{1,0:T(2,128)S(1)}, f32[2,512]{1,0:T(2,128)S(1)}, u32[]{:S(2)}, u32[]{:S(2)}) collective-permute-start(f32[2,512]{1,0:T(2,128)S(1)} %add.115), channel_id=1, source_target_pairs={{0,4},{1,5},{2,6},{3,7},{4,0},{5,1},{6,2},{7,3},{8,12},{9,13},{10,... | collective-permute-start | bytes 12296 | tf_op jit(solution)/shard_map/ppermute | solution.py:17
  115.2 2.5 %collective-permute-start.3 = (f32[2,512]{1,0:T(2,128)S(1)}, f32[2,512]{1,0:T(2,128)S(1)}, u32[]{:S(2)}, u32[]{:S(2)}) collective-permute-start(f32[2,512]{1,0:T(2,128)S(1)} %add.116), channel_id=1, source_target_pairs={{0,8},{1,9},{2,10},{3,11},{4,12},{5,13},{6,14},{7,15},{8,0},{9,1},... | collective-permute-start | bytes 12296 | tf_op jit(solution)/shard_map/ppermute | solution.py:17
  117.7 4.2 %collective-permute-start.4 = (f32[2,512]{1,0:T(2,128)S(1)}, f32[2,512]{1,0:T(2,128)S(1)}, u32[]{:S(2)}, u32[]{:S(2)}) collective-permute-start(f32[2,512]{1,0:T(2,128)S(1)} %add.117), channel_id=1, source_target_pairs={{0,16},{1,17},{2,18},{3,19},{4,20},{5,21},{6,22},{7,23},{8,24},{9,... | collective-permute-start | bytes 12296 | tf_op jit(solution)/shard_map/ppermute | solution.py:17

commit v4 on v3

--- a/solution.py
+++ b/solution.py
@@ -15,6 +15,13 @@
 def swapped(x, axis, bit):
     count = lax.axis_size(axis)
     return lax.ppermute(x, axis, [(i, i ^ bit) for i in range(count)])
+
+
+def group_sum(x, axis, stride, size):
+    values = [x] + [swapped(x, axis, stride * d) for d in range(1, size)]
+    while len(values) > 1:
+        values = [values[i] + values[i + 1] for i in range(0, len(values), 2)]
+    return values[0]
 
 
 def butterfly_bits(axis):
@@ -176,12 +183,18 @@
         jnp.where(member[None, :, None, :], (pool_weight * label_value)[:, None], 0.0), axis=3
     )
     part = jnp.sum(weighted * rescale, axis=0)
-    for bit in butterfly_bits("ctx"):
-        part = part + swapped(part, "ctx", bit)
+    count = lax.axis_size("ctx")
+    inner = min(count, 8)
+    assert count % inner == 0 and inner & (inner - 1) == 0
+    part = group_sum(part, "ctx", 1, inner)
+    if count > inner:
+        part = group_sum(part, "ctx", inner, count // inner)
     logits = part
     target = (total_counts + 0.5) / (lengths[0].astype(jnp.float32)[:, None] + 1.0)
     rec_loss = jnp.mean(jax.nn.softplus(logits) - target * logits, axis=1)
-    mean_loss = lax.psum(jnp.sum(rec_loss), "dp") / (lax.axis_size("dp") * record_count)
+    mean_loss = group_sum(jnp.sum(rec_loss), "dp", 1, lax.axis_size("dp")) / (
+        lax.axis_size("dp") * record_count
+    )
     return (out_rows[None], logits[None], rec_loss[None], mean_loss)
 
 

time: 148 us -> 147 us (level)
  starting transfers between devices: 30.7 us -> 52.2 us
  blocking collectives: 21.5 us -> 0 us
  waiting for transfers between devices: 38.4 us -> 33.4 us
  between operations: 3.5 us -> 7.85 us
    ppermute x5 -> x17, starting transfers between devices: 10.1 us -> 31.6 us  [swapped(): return lax.ppermute(x, axis, [(i, i ^ bit) for i in range(count)])]
    psum x1 -> x0, blocking collectives: 21.5 us -> none  [local(): lax.psum(jnp.sum(rec_loss), 'dp') / (lax.axis_size('dp') * record_count)]
    ppermute x5 -> x17, waiting for transfers between devices: 8.65 us -> 3.61 us  [swapped(): return lax.ppermute(x, axis, [(i, i ^ bit) for i in range(count)])]
  transfers between devices with their start and end apart: 7 -> 19, of which waited for: 7 -> 5; matrix products, arithmetic and copies ran while one was open for 3% -> 3% of each run, Pallas kernels for 0% -> 0%
where the time goes in v4:
time: 147 us; the launch traced here: 146 us
  starting transfers between devices  52.2 us (36%)
  waiting for transfers between devices  33.4 us (23%)
  matrix products  19.5 us (13%)
  other arithmetic  17.1 us (12%)
  local copies, waits for them, and re-layouts  16.3 us (11%)
  between operations  7.85 us (5%)
    ppermute x17, starting transfers between devices, swapped(): return lax.ppermute(x, axis, [(i, i ^ bit) for i in range(count)])  31.6 us
    all_to_all x1, waiting for transfers between devices, exclusive_state_scan(): got = lax.all_to_all(jnp.concatenate([slices, extra], axis=1), axis, 0, 0)  16.4 us
    all_to_all x1, waiting for transfers between devices, exclusive_state_scan(): back = lax.all_to_all(sent_back, axis, 0, 0)  13.4 us
    all_to_all x1, starting transfers between devices, exclusive_state_scan(): got = lax.all_to_all(jnp.concatenate([slices, extra], axis=1), axis, 0, 0)  12 us
    all_to_all x1, starting transfers between devices, exclusive_state_scan(): back = lax.all_to_all(sent_back, axis, 0, 0)  8.57 us
    unnamed x31, local copies, waits for them, and re-layouts  8.21 us
    ppermute x17, waiting for transfers between devices, swapped(): return lax.ppermute(x, axis, [(i, i ^ bit) for i in range(count)])  3.61 us
    dot_general x1, matrix products, local(): jnp.einsum('lhd,thd->hlt', lw3, y3, preferred_element_type=jnp.float32)  3.2 us
  transfers between devices with their start and end apart: 19, of which 5 were waited for; matrix products, arithmetic and copies ran while one was open for 3% of the time, Pallas kernels for 0%

profile of v4, /device:TPU:1, one launch (start us, length us, event | category | flops | bytes accessed | tf_op | source)
XLA Modules:
  0.0 146.3 jit_solution(17298581674890882184)
XLA Ops:
  0.7 1.0 reduce-window.10
  3.0 1.1 copy.120
  4.1 1.9 %convolution_multiply_fusion = f32[8,512,256]{2,1,0:T(8,128)S(1)} fusion(bf16[256,8,128]{2,1,0:T(8,128)(2,1)S(1)} %bitcast.140, bf16[512,1024]{1,0:T(8,128)(2,1)} %param.18), kind=kOutput, calls=%fused_computation.7 | convolution fusion | flops 269484032 | bytes 5767168 | tf_op jit(solution)/shard_map/lhd,thd->hlt/dot_general | solution.py:139
  6.1 1.2 select_reduce_fusion.3
  7.3 1.5 %select_reduce_fusion.2 = f32[8,512,256]{2,1,0:T(8,128)S(1)} fusion(f32[8,2,512]{2,1,0:T(2,128)S(1)} %select_reduce_fusion.3, pred[2,256]{1,0:T(4,128)(4,1)S(1)} %iota_compare_fusion.6), kind=kLoop, calls=%fused_computation.3 | loop fusion | flops 3145728 | bytes 4227584 | tf_op jit(solution)/shard_map/reduce_sum | solution.py:143
  8.8 1.2 subtract_exponential_fusion
  10.1 1.9 %copy-done.1 = f32[8,512,256]{2,1,0:T(8,128)} copy-done((f32[8,512,256]{2,1,0:T(8,128)}, f32[8,512,256]{2,1,0:T(8,128)S(1)}, u32[]{:S(2)}) %copy-start.1) | copy-done | bytes 4194328
  12.0 1.2 select_reduce_fusion.1
  19.3 1.5 %convolution_convert_fusion = bf16[256,1024]{1,0:T(8,128)(2,1)} fusion(bf16[1024,1024]{1,0:T(8,128)(2,1)S(1)} %copy-done, bf16[1,256,1024]{2,1,0:T(8,128)(2,1)S(1)} %copy-done.6), kind=kOutput, calls=%fused_computation.13 | convolution fusion | flops 537133056 | bytes 3145728 | tf_op jit(solution)/shard_map/dot_general | solution.py:114
  20.8 1.2 copy.114
  22.1 2.6 %fusion.3 = bf16[32,8,8,128]{3,2,1,0:T(8,128)(2,1)S(1)} fusion(bf16[1024,1024]{1,0:T(8,128)(2,1)} %param.16, bf16[1,256,1024]{2,1,0:T(8,128)(2,1)} %param.10), kind=kOutput, calls=%fused_computation.16 | convolution fusion | flops 537133056 | bytes 3145728 | tf_op jit(solution)/shard_map/dot_general | solution.py:115
  25.1 0.9 pad_maximum_fusion
  25.9 12.0 %all-to-all-start = ((f32[32,40,128]{2,1,0:T(8,128)}), f32[32,40,128]{2,1,0:T(8,128)S(1)}, u32[]{:S(2)}, u32[]{:S(2)}) async-start(f32[32,40,128]{2,1,0:T(8,128)} %pad_maximum_fusion), calls=%async_computation | async-start | bytes 1310720 | tf_op jit(solution)/shard_map/all_to_all | solution.py:62
  38.0 16.4 %all-to-all-done = f32[32,40,128]{2,1,0:T(8,128)S(1)} async-done(((f32[32,40,128]{2,1,0:T(8,128)}), f32[32,40,128]{2,1,0:T(8,128)S(1)}, u32[]{:S(2)}, u32[]{:S(2)}) %all-to-all-start) | async-done | bytes 655392 | tf_op jit(solution)/shard_map/all_to_all | solution.py:62
  56.8 0.9 fusion.17
  57.7 1.2 copy.100
  59.0 8.6 %all-to-all-start.1 = ((f32[32,40,128]{2,1,0:T(8,128)}), f32[32,40,128]{2,1,0:T(8,128)S(1)}, u32[]{:S(2)}, u32[]{:S(2)}) async-start(f32[32,40,128]{2,1,0:T(8,128)} %copy.100), calls=%async_computation.1 | async-start | bytes 1310720 | tf_op jit(solution)/shard_map/all_to_all | solution.py:83
  67.7 3.1 %fusion.4 = bf16[32,8,8,128]{3,2,1,0:T(8,128)(2,1)} fusion(bf16[1024,1024]{1,0:T(8,128)(2,1)} %param.14, bf16[1,256,1024]{2,1,0:T(8,128)(2,1)S(1)} %copy-done.7), kind=kOutput, calls=%fused_computation.17 | convolution fusion | flops 537133056 | bytes 3145728 | tf_op jit(solution)/shard_map/dot_general | solution.py:113
  70.8 13.4 %all-to-all-done.1 = f32[32,40,128]{2,1,0:T(8,128)S(1)} async-done(((f32[32,40,128]{2,1,0:T(8,128)}), f32[32,40,128]{2,1,0:T(8,128)S(1)}, u32[]{:S(2)}, u32[]{:S(2)}) %all-to-all-start.1) | async-done | bytes 655392 | tf_op jit(solution)/shard_map/all_to_all | solution.py:83
  84.2 0.8 copy-done.3
  85.0 2.9 %convolution_multiply_fusion.1 = f32[8,128,256]{2,1,0:T(8,128)} fusion(f32[8,128,128]{2,1,0:T(8,128)S(1)} %bitcast.139, f32[256,8]{0,1:T(8,128)S(1)} %get-tuple-element.26, bf16[32,8,8,128]{3,2,1,0:T(8,128)(2,1)} %fusion.4), kind=kOutput, calls=%fused_computation.12 | convolution fusion | flops 202113024 | bytes 2105344 | tf_op jit(solution)/shard_map/thd,hde->the/dot_general | solution.py:169
  88.0 2.7 %fusion.56 = (f32[256,8]{0,1:T(8,128)S(1)}, f32[256,8,128]{0,2,1:T(8,128)S(1)}) fusion(f32[8,128,256]{2,1,0:T(8,128)} %convolution_multiply_fusion.1, bf16[256,8,128]{0,2,1:T(8,128)(2,1)} %bitcast.136, f32[8,256]{1,0:T(8,128)S(1)} %get-tuple-element.27, pred[256,256]{1,0:T(8,128)(4,1)S(1)} %fusion.39, bf16[32,8,8,128]{3,2,1,0:T(8,128)(2,1)} %fusion.4, ...), kind=kOutput, calls=%fused_computation.120 | convolution fusion | flops 272103424 | bytes 3751936 | tf_op jit(solution)/shard_map/hts,shd->thd/dot_general | solution.py:133
  90.8 0.8 copy-done.2
  91.7 1.4 multiply_convert_fusion
  93.1 3.2 %bitcast_multiply_fusion = f32[8,512,256]{2,1,0:T(8,128)S(1)} fusion(f32[8,512,256]{2,1,0:T(8,128)} %copy-done.1, bf16[256,8,128]{0,2,1:T(8,128)(2,1)S(1)} %multiply_convert_fusion, bf16[512,1024]{1,0:T(8,128)(2,1)} %param.19), kind=kOutput, calls=%fused_computation.5 | convolution fusion | flops 269484032 | bytes 9961472 | tf_op jit(solution)/shard_map/lhd,thd->hlt/dot_general | solution.py:181
  96.3 1.2 select_reduce_fusion
  98.1 1.1 fusion.55
  99.2 1.2 copy.112
  100.5 1.2 copy.113
  101.7 2.8 %collective-permute-start = (f32[2,512]{1,0:T(2,128)S(1)}, f32[2,512]{1,0:T(2,128)S(1)}, u32[]{:S(2)}, u32[]{:S(2)}) collective-permute-start(f32[2,512]{1,0:T(2,128)S(1)} %fusion.42), channel_id=1, source_target_pairs={{0,1},{1,0},{2,3},{3,2},{4,5},{5,4},{6,7},{7,6},{8,9},{9,8},{10,11... | collective-permute-start | bytes 12296 | tf_op jit(solution)/shard_map/ppermute | solution.py:17
  104.5 0.9 collective-permute-start.1
  105.4 1.3 collective-permute-start.2
  106.7 2.6 %collective-permute-start.3 = (f32[2,512]{1,0:T(2,128)S(1)}, f32[2,512]{1,0:T(2,128)S(1)}, u32[]{:S(2)}, u32[]{:S(2)}) collective-permute-start(f32[2,512]{1,0:T(2,128)S(1)} %fusion.42), channel_id=1, source_target_pairs={{0,4},{1,5},{2,6},{3,7},{4,0},{5,1},{6,2},{7,3},{8,12},{9,13},{10,... | collective-permute-start | bytes 12296 | tf_op jit(solution)/shard_map/ppermute | solution.py:17
  109.3 2.0 %collective-permute-start.4 = (f32[2,512]{1,0:T(2,128)S(1)}, f32[2,512]{1,0:T(2,128)S(1)}, u32[]{:S(2)}, u32[]{:S(2)}) collective-permute-start(f32[2,512]{1,0:T(2,128)S(1)} %fusion.42), channel_id=1, source_target_pairs={{0,5},{1,4},{2,7},{3,6},{4,1},{5,0},{6,3},{7,2},{8,13},{9,12},{10,... | collective-permute-start | bytes 12296 | tf_op jit(solution)/shard_map/ppermute | solution.py:17
  111.4 1.3 collective-permute-start.5
  112.7 2.0 %collective-permute-start.6 = (f32[2,512]{1,0:T(2,128)S(1)}, f32[2,512]{1,0:T(2,128)S(1)}, u32[]{:S(2)}, u32[]{:S(2)}) collective-permute-start(f32[2,512]{1,0:T(2,128)S(1)} %fusion.42), channel_id=1, source_target_pairs={{0,7},{1,6},{2,5},{3,4},{4,3},{5,2},{6,1},{7,0},{8,15},{9,14},{10,... | collective-permute-start | bytes 12296 | tf_op jit(solution)/shard_map/ppermute | solution.py:17
  114.8 1.1 collective-permute-done.5
  116.4 1.3 collective-permute-start.7
  117.7 2.3 %collective-permute-start.8 = (f32[2,512]{1,0:T(2,128)S(1)}, f32[2,512]{1,0:T(2,128)S(1)}, u32[]{:S(2)}, u32[]{:S(2)}) collective-permute-start(f32[2,512]{1,0:T(2,128)S(1)} %add_add_fusion.1), channel_id=1, source_target_pairs={{0,16},{1,17},{2,18},{3,19},{4,20},{5,21},{6,22},{7,23},{8,24},{9,... | collective-permute-start | bytes 12296 | tf_op jit(solution)/shard_map/ppermute | solution.py:17
  120.7 1.0 copy.108
  121.7 2.0 %collective-permute-done.9 = f32[2,512]{1,0:T(2,128)S(1)} collective-permute-done((f32[2,512]{1,0:T(2,128)S(1)}, f32[2,512]{1,0:T(2,128)S(1)}, u32[]{:S(2)}, u32[]{:S(2)}) %collective-permute-start.9) | collective-permute-done | bytes 4128 | tf_op jit(solution)/shard_map/ppermute | solution.py:17
  123.7 0.7 fusion.47
  124.4 1.1 multiply_reduce_fusion.1
  125.5 2.5 %collective-permute-start.15 = (f32[]{:T(128)}, f32[]{:T(128)}, u32[]{:S(2)}, u32[]{:S(2)}) collective-permute-start(f32[]{:T(128)} %get-tuple-element.32), channel_id=1, source_target_pairs={{0,192},{32,224},{64,128},{96,160},{128,64},{160,96},{192,0},{224,... | collective-permute-start | bytes 20 | tf_op jit(solution)/shard_map/ppermute | solution.py:17
  128.0 7.2 %collective-permute-start.16 = (f32[]{:T(128)}, f32[]{:T(128)}, u32[]{:S(2)}, u32[]{:S(2)}) collective-permute-start(f32[]{:T(128)} %get-tuple-element.32), channel_id=1, source_target_pairs={{0,224},{32,192},{64,160},{96,128},{128,96},{160,64},{192,32},{224... | collective-permute-start | bytes 20 | tf_op jit(solution)/shard_map/ppermute | solution.py:17
  135.2 1.5 %collective-permute-start.13 = (f32[]{:T(128)}, f32[]{:T(128)}, u32[]{:S(2)}, u32[]{:S(2)}) collective-permute-start(f32[]{:T(128)} %get-tuple-element.32), channel_id=1, source_target_pairs={{0,128},{32,160},{64,192},{96,224},{128,0},{160,32},{192,64},{224,... | collective-permute-start | bytes 20 | tf_op jit(solution)/shard_map/ppermute | solution.py:17
  136.7 1.5 %collective-permute-start.14 = (f32[]{:T(128)}, f32[]{:T(128)}, u32[]{:S(2)}, u32[]{:S(2)}) collective-permute-start(f32[]{:T(128)} %get-tuple-element.32), channel_id=1, source_target_pairs={{0,160},{32,128},{64,224},{96,192},{128,32},{160,0},{192,96},{224,... | collective-permute-start | bytes 20 | tf_op jit(solution)/shard_map/ppermute | solution.py:17
  138.3 1.9 %collective-permute-start.12 = (f32[]{:T(128)}, f32[]{:T(128)}, u32[]{:S(2)}, u32[]{:S(2)}) collective-permute-start(f32[]{:T(128)} %get-tuple-element.32), channel_id=1, source_target_pairs={{0,96},{32,64},{64,32},{96,0},{128,224},{160,192},{192,160},{224,1... | collective-permute-start | bytes 20 | tf_op jit(solution)/shard_map/ppermute | solution.py:17
  (100 shorter events, 11.7 us)
Async XLA Ops:
  0.6 18.7 %copy-start = (bf16[1024,1024]{1,0:T(8,128)(2,1)S(1)}, bf16[1024,1024]{1,0:T(8,128)(2,1)}, u32[]{:S(2)}) copy-start(bf16[1024,1024]{1,0:T(8,128)(2,1)} %param.15) | copy-start | bytes 6291460
  10.0 1.9 %copy-start.1 = (f32[8,512,256]{2,1,0:T(8,128)}, f32[8,512,256]{2,1,0:T(8,128)S(1)}, u32[]{:S(2)}) copy-start(f32[8,512,256]{2,1,0:T(8,128)S(1)} %subtract_exponential_fusion) | copy-start | bytes 12582916
  12.0 1.2 copy-start.11
  12.0 2.0 %copy-start.10 = (s32[1,2]{1,0:T(1,128)S(1)}, s32[1,2]{1,0:T(1,128)}, u32[]{:S(2)}) copy-start(s32[1,2]{1,0:T(1,128)} %param.12) | copy-start | bytes 28
  12.0 3.3 %copy-start.8 = (f32[1,8,256]{2,1,0:T(8,128)S(1)}, f32[1,8,256]{2,1,0:T(8,128)}, u32[]{:S(2)}) copy-start(f32[1,8,256]{2,1,0:T(8,128)} %param.11) | copy-start | bytes 24580
  12.0 7.3 %copy-start.6 = (bf16[1,256,1024]{2,1,0:T(8,128)(2,1)S(1)}, bf16[1,256,1024]{2,1,0:T(8,128)(2,1)}, u32[]{:S(2)}) copy-start(bf16[1,256,1024]{2,1,0:T(8,128)(2,1)} %param.10) | copy-start | bytes 1572868
  22.1 32.5 %copy-start.4 = (bf16[256,1024]{0,1:T(8,128)(2,1)}, bf16[256,1024]{0,1:T(8,128)(2,1)S(1)}, u32[]{:S(2)}) copy-start(bf16[256,1024]{0,1:T(8,128)(2,1)S(1)} %copy.114) | copy-start | bytes 1572868
  24.7 1.2 copy-start.5
  25.9 28.4 %all-to-all-start = ((f32[32,40,128]{2,1,0:T(8,128)}), f32[32,40,128]{2,1,0:T(8,128)S(1)}, u32[]{:S(2)}, u32[]{:S(2)}) async-start(f32[32,40,128]{2,1,0:T(8,128)} %pad_maximum_fusion), calls=%async_computation | async-start | bytes 1310720 | tf_op jit(solution)/shard_map/all_to_all | solution.py:62
  56.8 10.9 %copy-start.7 = (bf16[1,256,1024]{2,1,0:T(8,128)(2,1)S(1)}, bf16[1,256,1024]{2,1,0:T(8,128)(2,1)}, u32[]{:S(2)}) copy-start(bf16[1,256,1024]{2,1,0:T(8,128)(2,1)} %param.10) | copy-start | bytes 1572868
  59.0 25.2 %all-to-all-start.1 = ((f32[32,40,128]{2,1,0:T(8,128)}), f32[32,40,128]{2,1,0:T(8,128)S(1)}, u32[]{:S(2)}, u32[]{:S(2)}) async-start(f32[32,40,128]{2,1,0:T(8,128)} %copy.100), calls=%async_computation.1 | async-start | bytes 1310720 | tf_op jit(solution)/shard_map/all_to_all | solution.py:83
  84.2 0.9 copy-start.3
  85.0 6.6 %copy-start.9 = (f32[1024]{0:T(1024)S(1)}, f32[1024]{0:T(1024)}, u32[]{:S(2)}) copy-start(f32[1024]{0:T(1024)} %param.17) | copy-start | bytes 12292
  90.7 1.0 copy-start.2
  96.3 1.2 slice-start
  101.7 9.6 %collective-permute-start = (f32[2,512]{1,0:T(2,128)S(1)}, f32[2,512]{1,0:T(2,128)S(1)}, u32[]{:S(2)}, u32[]{:S(2)}) collective-permute-start(f32[2,512]{1,0:T(2,128)S(1)} %fusion.42), channel_id=1, source_target_pairs={{0,1},{1,0},{2,3},{3,2},{4,5},{5,4},{6,7},{7,6},{8,9},{9,8},{10,11... | collective-permute-start | bytes 12296 | tf_op jit(solution)/shard_map/ppermute | solution.py:17
  104.5 8.2 %collective-permute-start.1 = (f32[2,512]{1,0:T(2,128)S(1)}, f32[2,512]{1,0:T(2,128)S(1)}, u32[]{:S(2)}, u32[]{:S(2)}) collective-permute-start(f32[2,512]{1,0:T(2,128)S(1)} %fusion.42), channel_id=1, source_target_pairs={{0,2},{1,3},{2,0},{3,1},{4,6},{5,7},{6,4},{7,5},{8,10},{9,11},{10,... | collective-permute-start | bytes 12296 | tf_op jit(solution)/shard_map/ppermute | solution.py:17
  105.4 9.4 %collective-permute-start.2 = (f32[2,512]{1,0:T(2,128)S(1)}, f32[2,512]{1,0:T(2,128)S(1)}, u32[]{:S(2)}, u32[]{:S(2)}) collective-permute-start(f32[2,512]{1,0:T(2,128)S(1)} %fusion.42), channel_id=1, source_target_pairs={{0,3},{1,2},{2,1},{3,0},{4,7},{5,6},{6,5},{7,4},{8,11},{9,10},{10,... | collective-permute-start | bytes 12296 | tf_op jit(solution)/shard_map/ppermute | solution.py:17
  106.7 8.1 %collective-permute-start.3 = (f32[2,512]{1,0:T(2,128)S(1)}, f32[2,512]{1,0:T(2,128)S(1)}, u32[]{:S(2)}, u32[]{:S(2)}) collective-permute-start(f32[2,512]{1,0:T(2,128)S(1)} %fusion.42), channel_id=1, source_target_pairs={{0,4},{1,5},{2,6},{3,7},{4,0},{5,1},{6,2},{7,3},{8,12},{9,13},{10,... | collective-permute-start | bytes 12296 | tf_op jit(solution)/shard_map/ppermute | solution.py:17
  109.3 5.5 %collective-permute-start.4 = (f32[2,512]{1,0:T(2,128)S(1)}, f32[2,512]{1,0:T(2,128)S(1)}, u32[]{:S(2)}, u32[]{:S(2)}) collective-permute-start(f32[2,512]{1,0:T(2,128)S(1)} %fusion.42), channel_id=1, source_target_pairs={{0,5},{1,4},{2,7},{3,6},{4,1},{5,0},{6,3},{7,2},{8,13},{9,12},{10,... | collective-permute-start | bytes 12296 | tf_op jit(solution)/shard_map/ppermute | solution.py:17
  111.4 4.6 %collective-permute-start.5 = (f32[2,512]{1,0:T(2,128)S(1)}, f32[2,512]{1,0:T(2,128)S(1)}, u32[]{:S(2)}, u32[]{:S(2)}) collective-permute-start(f32[2,512]{1,0:T(2,128)S(1)} %fusion.42), channel_id=1, source_target_pairs={{0,6},{1,7},{2,4},{3,5},{4,2},{5,3},{6,0},{7,1},{8,14},{9,15},{10,... | collective-permute-start | bytes 12296 | tf_op jit(solution)/shard_map/ppermute | solution.py:17
  112.7 3.7 %collective-permute-start.6 = (f32[2,512]{1,0:T(2,128)S(1)}, f32[2,512]{1,0:T(2,128)S(1)}, u32[]{:S(2)}, u32[]{:S(2)}) collective-permute-start(f32[2,512]{1,0:T(2,128)S(1)} %fusion.42), channel_id=1, source_target_pairs={{0,7},{1,6},{2,5},{3,4},{4,3},{5,2},{6,1},{7,0},{8,15},{9,14},{10,... | collective-permute-start | bytes 12296 | tf_op jit(solution)/shard_map/ppermute | solution.py:17
  116.4 5.3 %collective-permute-start.7 = (f32[2,512]{1,0:T(2,128)S(1)}, f32[2,512]{1,0:T(2,128)S(1)}, u32[]{:S(2)}, u32[]{:S(2)}) collective-permute-start(f32[2,512]{1,0:T(2,128)S(1)} %add_add_fusion.1), channel_id=1, source_target_pairs={{0,8},{1,9},{2,10},{3,11},{4,12},{5,13},{6,14},{7,15},{8,0},{9,1},... | collective-permute-start | bytes 12296 | tf_op jit(solution)/shard_map/ppermute | solution.py:17
  117.7 4.0 %collective-permute-start.8 = (f32[2,512]{1,0:T(2,128)S(1)}, f32[2,512]{1,0:T(2,128)S(1)}, u32[]{:S(2)}, u32[]{:S(2)}) collective-permute-start(f32[2,512]{1,0:T(2,128)S(1)} %add_add_fusion.1), channel_id=1, source_target_pairs={{0,16},{1,17},{2,18},{3,19},{4,20},{5,21},{6,22},{7,23},{8,24},{9,... | collective-permute-start | bytes 12296 | tf_op jit(solution)/shard_map/ppermute | solution.py:17
  120.0 3.7 %collective-permute-start.9 = (f32[2,512]{1,0:T(2,128)S(1)}, f32[2,512]{1,0:T(2,128)S(1)}, u32[]{:S(2)}, u32[]{:S(2)}) collective-permute-start(f32[2,512]{1,0:T(2,128)S(1)} %add_add_fusion.1), channel_id=1, source_target_pairs={{0,24},{1,25},{2,26},{3,27},{4,28},{5,29},{6,30},{7,31},{8,16},{9,... | collective-permute-start | bytes 12296 | tf_op jit(solution)/shard_map/ppermute | solution.py:17
  125.5 12.8 %collective-permute-start.15 = (f32[]{:T(128)}, f32[]{:T(128)}, u32[]{:S(2)}, u32[]{:S(2)}) collective-permute-start(f32[]{:T(128)} %get-tuple-element.32), channel_id=1, source_target_pairs={{0,192},{32,224},{64,128},{96,160},{128,64},{160,96},{192,0},{224,... | collective-permute-start | bytes 20 | tf_op jit(solution)/shard_map/ppermute | solution.py:17
  128.0 12.2 %collective-permute-start.16 = (f32[]{:T(128)}, f32[]{:T(128)}, u32[]{:S(2)}, u32[]{:S(2)}) collective-permute-start(f32[]{:T(128)} %get-tuple-element.32), channel_id=1, source_target_pairs={{0,224},{32,192},{64,160},{96,128},{128,96},{160,64},{192,32},{224... | collective-permute-start | bytes 20 | tf_op jit(solution)/shard_map/ppermute | solution.py:17
  135.2 6.2 %collective-permute-start.13 = (f32[]{:T(128)}, f32[]{:T(128)}, u32[]{:S(2)}, u32[]{:S(2)}) collective-permute-start(f32[]{:T(128)} %get-tuple-element.32), channel_id=1, source_target_pairs={{0,128},{32,160},{64,192},{96,224},{128,0},{160,32},{192,64},{224,... | collective-permute-start | bytes 20 | tf_op jit(solution)/shard_map/ppermute | solution.py:17
  136.7 4.7 %collective-permute-start.14 = (f32[]{:T(128)}, f32[]{:T(128)}, u32[]{:S(2)}, u32[]{:S(2)}) collective-permute-start(f32[]{:T(128)} %get-tuple-element.32), channel_id=1, source_target_pairs={{0,160},{32,128},{64,224},{96,192},{128,32},{160,0},{192,96},{224,... | collective-permute-start | bytes 20 | tf_op jit(solution)/shard_map/ppermute | solution.py:17
  138.3 5.7 %collective-permute-start.11 = (f32[]{:T(128)}, f32[]{:T(128)}, u32[]{:S(2)}, u32[]{:S(2)}) collective-permute-start(f32[]{:T(128)} %get-tuple-element.32), channel_id=1, source_target_pairs={{0,64},{32,96},{64,0},{96,32},{128,192},{160,224},{192,128},{224,1... | collective-permute-start | bytes 20 | tf_op jit(solution)/shard_map/ppermute | solution.py:17
  138.3 5.7 %collective-permute-start.12 = (f32[]{:T(128)}, f32[]{:T(128)}, u32[]{:S(2)}, u32[]{:S(2)}) collective-permute-start(f32[]{:T(128)} %get-tuple-element.32), channel_id=1, source_target_pairs={{0,96},{32,64},{64,32},{96,0},{128,224},{160,192},{192,160},{224,1... | collective-permute-start | bytes 20 | tf_op jit(solution)/shard_map/ppermute | solution.py:17
  140.2 2.5 %collective-permute-start.10 = (f32[]{:T(128)}, f32[]{:T(128)}, u32[]{:S(2)}, u32[]{:S(2)}) collective-permute-start(f32[]{:T(128)} %get-tuple-element.32), channel_id=1, source_target_pairs={{0,32},{32,0},{64,96},{96,64},{128,160},{160,128},{192,224},{224,1... | collective-permute-start | bytes 20 | tf_op jit(solution)/shard_map/ppermute | solution.py:17

commit v5 on v4

--- a/solution.py
+++ b/solution.py
@@ -1,6 +1,9 @@
+import functools
+
 import jax
 import jax.numpy as jnp
 from jax import lax
+from jax.experimental import pallas as pl
 from jax.sharding import PartitionSpec as P
 
 NEG_FILL = -1e30
@@ -33,6 +36,67 @@
         bits.append(bit)
         bit *= 2
     return bits
+
+
+def split_dot(a, b):
+    a_hi = a.astype(jnp.bfloat16)
+    a_lo = (a - a_hi.astype(jnp.float32)).astype(jnp.bfloat16)
+    b_hi = b.astype(jnp.bfloat16)
+    b_lo = (b - b_hi.astype(jnp.float32)).astype(jnp.bfloat16)
+    out = jnp.dot(a_hi, b_hi, preferred_element_type=jnp.float32)
+    out = out + jnp.dot(a_hi, b_lo, preferred_element_type=jnp.float32)
+    return out + jnp.dot(a_lo, b_hi, preferred_element_type=jnp.float32)
+
+
+def finish_kernel(qd_ref, state_ref, intra_ref, gain_ref, lw_ref, pw_ref, member_ref, rescale_ref,
+                  out_ref, part_ref, *, qk_scale):
+    inter = split_dot(qd_ref[...], state_ref[0])
+    total = intra_ref[...] + inter * qk_scale
+    centred = total - jnp.mean(total, axis=1, keepdims=True)
+    variance = jnp.mean(centred * centred, axis=1, keepdims=True)
+    normed = centred * lax.rsqrt(variance + 1e-05) * gain_ref[...]
+    y = normed.astype(jnp.bfloat16)
+    out_ref[...] = y
+    label_value = lax.dot_general(
+        lw_ref[...], y, (((1,), (1,)), ((), ())), preferred_element_type=jnp.float32
+    )
+    prod = pw_ref[0] * label_value
+    weighted = lax.dot_general(
+        member_ref[...], prod, (((1,), (1,)), ((), ())),
+        precision=lax.Precision.HIGHEST, preferred_element_type=jnp.float32,
+    )
+    part_ref[0] = weighted * rescale_ref[0]
+
+
+def finish_call(q_decayed, incoming, intra, norm_gain, label_weight, pool_weight, member, rescale,
+                qk_scale):
+    tok_rows, model_width = q_decayed.shape
+    head_count, head_dim, _ = incoming.shape
+    label_count = label_weight.shape[0]
+    record_count = member.shape[0]
+    return pl.pallas_call(
+        functools.partial(finish_kernel, qk_scale=qk_scale),
+        grid=(head_count,),
+        in_specs=[
+            pl.BlockSpec((tok_rows, head_dim), lambda h: (0, h)),
+            pl.BlockSpec((1, head_dim, head_dim), lambda h: (h, 0, 0)),
+            pl.BlockSpec((tok_rows, head_dim), lambda h: (0, h)),
+            pl.BlockSpec((1, head_dim), lambda h: (0, h)),
+            pl.BlockSpec((label_count, head_dim), lambda h: (0, h)),
+            pl.BlockSpec((1, label_count, tok_rows), lambda h: (h, 0, 0)),
+            pl.BlockSpec((record_count, tok_rows), lambda h: (0, 0)),
+            pl.BlockSpec((1, record_count, label_count), lambda h: (h, 0, 0)),
+        ],
+        out_specs=[
+            pl.BlockSpec((tok_rows, head_dim), lambda h: (0, h)),
+            pl.BlockSpec((1, record_count, label_count), lambda h: (h, 0, 0)),
+        ],
+        out_shape=[
+            jax.ShapeDtypeStruct((tok_rows, model_width), jnp.bfloat16),
+            jax.ShapeDtypeStruct((head_count, record_count, label_count), jnp.float32),
+        ],
+    )(q_decayed, incoming, intra, norm_gain.reshape(1, model_width), label_weight, pool_weight,
+      member, rescale)
 
 
 def record_ids(length_row, positions):
@@ -165,24 +229,14 @@
     total_counts = totals[:, :, 2 * head_count]
     rescale = jnp.exp(maxima - top) / total_mass
 
-    q_decayed = q3.astype(jnp.float32) * jnp.where(linked[None, :], jnp.exp(decay_cum), 0.0).T[:, :, None]
-    inter = jnp.einsum(
-        "thd,hde->the", q_decayed, incoming, precision=lax.Precision.HIGH,
-        preferred_element_type=jnp.float32,
-    )
-    total_out = intra + inter * qk_scale
-    centred = total_out - jnp.mean(total_out, axis=2, keepdims=True)
-    variance = jnp.mean(centred * centred, axis=2, keepdims=True)
-    gain3 = norm_gain.reshape(head_count, head_dim)
-    normed = centred * lax.rsqrt(variance + 1e-05) * gain3[None]
-    out_rows = normed.reshape(tok_rows, model_width).astype(jnp.bfloat16)
-
-    y3 = out_rows.reshape(tok_rows, head_count, head_dim)
-    label_value = jnp.einsum("lhd,thd->hlt", lw3, y3, preferred_element_type=jnp.float32)
-    weighted = jnp.sum(
-        jnp.where(member[None, :, None, :], (pool_weight * label_value)[:, None], 0.0), axis=3
-    )
-    part = jnp.sum(weighted * rescale, axis=0)
+    q_decayed = (
+        q3.astype(jnp.float32) * jnp.where(linked[None, :], jnp.exp(decay_cum), 0.0).T[:, :, None]
+    ).reshape(tok_rows, model_width)
+    out_rows, head_parts = finish_call(
+        q_decayed, incoming, intra.reshape(tok_rows, model_width), norm_gain, label_weight,
+        pool_weight, member.astype(jnp.float32), rescale, qk_scale,
+    )
+    part = jnp.sum(head_parts, axis=0)
     count = lax.axis_size("ctx")
     inner = min(count, 8)
     assert count % inner == 0 and inner & (inner - 1) == 0

time: 147 us -> 150 us (1.020)
  Pallas kernels: 0 us -> 11.2 us
  matrix products: 19.5 us -> 14.9 us
  waiting for transfers between devices: 33.4 us -> 29.2 us
    pallas_call x0 -> x1, Pallas kernels: none -> 11.2 us  [finish_call(): pl.pallas_call(functools.partial(finish_kernel, qk_scale=qk_scale), grid=...]
    dot_general x2 -> x0, matrix products: 6.15 us -> none  [the longest x1 3.2 us: local(): jnp.einsum('lhd,thd->hlt', lw3, y3, preferred_element_type=jnp.float32)]
    all_to_all x1, waiting for transfers between devices: 13.4 us -> 8.24 us  [exclusive_state_scan(): back = lax.all_to_all(sent_back, axis, 0, 0)]
    unnamed x31 -> x24, local copies, waits for them, and re-layouts: 8.21 us -> 4.38 us
    reshape x0 -> x2, local copies, waits for them, and re-layouts: none -> 3.82 us  [the longest x1 2.58 us: local(): intra.reshape(tok_rows, model_width)]
    dot_general x1, matrix products: 1.51 us -> 3.1 us  [local(): jnp.dot(features, w_key, preferred_element_type=jnp.float32)]
  transfers between devices with their start and end apart: 19 -> 19, of which waited for: 5 -> 6; matrix products, arithmetic and copies ran while one was open for 3% -> 6% of each run, Pallas kernels for 0% -> 0%
where the time goes in v5:
time: 150 us; the launch traced here: 149 us
  starting transfers between devices  52.3 us (35%)
  waiting for transfers between devices  29.2 us (19%)
  local copies, waits for them, and re-layouts  17.6 us (12%)
  other arithmetic  16.3 us (11%)
  matrix products  14.9 us (10%)
  Pallas kernels  11.2 us (7%)
  between operations  7.8 us (5%)
    ppermute x17, starting transfers between devices, swapped(): return lax.ppermute(x, axis, [(i, i ^ bit) for i in range(count)])  31.6 us
    all_to_all x1, waiting for transfers between devices, exclusive_state_scan(): got = lax.all_to_all(jnp.concatenate([slices, extra], axis=1), axis, 0, 0)  16.4 us
    all_to_all x1, starting transfers between devices, exclusive_state_scan(): got = lax.all_to_all(jnp.concatenate([slices, extra], axis=1), axis, 0, 0)  12 us
    pallas_call x1, Pallas kernels, finish_call(): pl.pallas_call(functools.partial(finish_kernel, qk_scale=qk_scale), grid=...  11.2 us
    all_to_all x1, starting transfers between devices, exclusive_state_scan(): back = lax.all_to_all(sent_back, axis, 0, 0)  8.59 us
    all_to_all x1, waiting for transfers between devices, exclusive_state_scan(): back = lax.all_to_all(sent_back, axis, 0, 0)  8.24 us
    ppermute x17, waiting for transfers between devices, swapped(): return lax.ppermute(x, axis, [(i, i ^ bit) for i in range(count)])  4.6 us
    unnamed x24, local copies, waits for them, and re-layouts  4.38 us
  transfers between devices with their start and end apart: 19, of which 6 were waited for; matrix products, arithmetic and copies ran while one was open for 6% of the time, Pallas kernels for 0%

profile of v5, /device:TPU:1, one launch (start us, length us, event | category | flops | bytes accessed | tf_op | source)
XLA Modules:
  0.0 149.3 jit_solution(201548581952557939)
XLA Ops:
  0.7 1.0 reduce-window.10
  3.6 1.1 copy.100
  4.7 1.9 %convolution_multiply_fusion = f32[8,512,256]{2,1,0:T(8,128)S(1)} fusion(bf16[256,8,128]{2,1,0:T(8,128)(2,1)S(1)} %bitcast.122, bf16[512,1024]{1,0:T(8,128)(2,1)} %param.18), kind=kOutput, calls=%fused_computation.5 | convolution fusion | flops 269484032 | bytes 5767168 | tf_op jit(solution)/shard_map/lhd,thd->hlt/dot_general | solution.py:203
  6.6 1.2 select_reduce_fusion.2
  7.8 1.5 %select_reduce_fusion.1 = f32[8,512,256]{2,1,0:T(8,128)S(1)} fusion(f32[8,2,512]{2,1,0:T(2,128)S(1)} %select_reduce_fusion.2, pred[2,256]{1,0:T(4,128)(4,1)S(1)} %get-tuple-element.15), kind=kLoop, calls=%fused_computation.2 | loop fusion | flops 3145728 | bytes 4227584 | tf_op jit(solution)/shard_map/reduce_sum | solution.py:207
  9.4 1.2 subtract_exponential_fusion.pw_ref
  10.7 1.2 select_reduce_fusion
  11.9 0.7 copy-done.1
  17.6 0.7 gather_fusion
  18.7 3.1 %convolution_convert_fusion.1 = bf16[256,1024]{1,0:T(8,128)(2,1)} fusion(bf16[1024,1024]{1,0:T(8,128)(2,1)} %param.15, bf16[1,256,1024]{2,1,0:T(8,128)(2,1)S(1)} %copy-done.2), kind=kOutput, calls=%fused_computation.9 | convolution fusion | flops 537133056 | bytes 3145728 | tf_op jit(solution)/shard_map/dot_general | solution.py:178
  21.8 1.2 copy.94
  23.0 3.3 %convolution_convert_fusion = bf16[256,1024]{1,0:T(8,128)(2,1)} fusion(bf16[1024,1024]{1,0:T(8,128)(2,1)} %param.16, bf16[1,256,1024]{2,1,0:T(8,128)(2,1)S(1)} %copy-done.2), kind=kOutput, calls=%fused_computation.8 | convolution fusion | flops 537133056 | bytes 3145728 | tf_op jit(solution)/shard_map/dot_general | solution.py:179
  26.3 1.2 copy.95
  27.9 0.9 pad_maximum_fusion
  28.8 12.0 %all-to-all-start = ((f32[32,40,128]{2,1,0:T(8,128)}), f32[32,40,128]{2,1,0:T(8,128)S(1)}, u32[]{:S(2)}, u32[]{:S(2)}) async-start(f32[32,40,128]{2,1,0:T(8,128)} %pad_maximum_fusion), calls=%async_computation | async-start | bytes 1310720 | tf_op jit(solution)/shard_map/all_to_all | solution.py:126
  40.9 16.4 %all-to-all-done = f32[32,40,128]{2,1,0:T(8,128)S(1)} async-done(((f32[32,40,128]{2,1,0:T(8,128)}), f32[32,40,128]{2,1,0:T(8,128)S(1)}, u32[]{:S(2)}, u32[]{:S(2)}) %all-to-all-start) | async-done | bytes 655392 | tf_op jit(solution)/shard_map/all_to_all | solution.py:126
  59.6 0.9 fusion.13
  60.6 1.2 copy.84
  61.8 8.6 %all-to-all-start.1 = ((f32[32,40,128]{2,1,0:T(8,128)}), f32[32,40,128]{2,1,0:T(8,128)S(1)}, u32[]{:S(2)}, u32[]{:S(2)}) async-start(f32[32,40,128]{2,1,0:T(8,128)} %copy.84), calls=%async_computation.1 | async-start | bytes 1310720 | tf_op jit(solution)/shard_map/all_to_all | solution.py:147
  71.0 1.9 %bitcast_multiply_fusion = (f32[256,1024]{1,0:T(8,128)}, bf16[256,1024]{1,0:T(8,128)(2,1)}) fusion(f32[32,8,8,128]{3,2,1,0:T(8,128)S(1)} %bitcast.113, bf16[1024,1024]{1,0:T(8,128)(2,1)S(1)} %copy-done, bf16[1,256,1024]{2,1,0:T(8,128)(2,1)S(1)} %copy-done.3), kind=kOutput, calls=%fused_computation.12 | convolution fusion | flops 537657344 | bytes 5242880 | tf_op jit(solution)/shard_map/dot_general | solution.py:177
  72.9 3.3 %fusion = f32[8,128,256]{2,1,0:T(8,128)} fusion(bf16[256,8,128]{0,2,1:T(8,128)(2,1)} %bitcast.118, bf16[256,8,128]{0,2,1:T(8,128)(2,1)} %bitcast.116, f32[8,256]{1,0:T(8,128)S(1)} %get-tuple-element.11, pred[256,256]{1,0:T(8,128)(4,1)S(1)} %fusion.24, bf16[256,1024]{1,0:T(8,128)(2,1)} %get-tuple-element.21), kind=kOutput, calls=%fused_computation.7 | convolution fusion | flops 271581184 | bytes 2695168 | tf_op jit(solution)/shard_map/hts,shd->thd/dot_general | solution.py:197
  76.2 2.6 %copy.91.intra_ref = f32[256,1024]{1,0:T(8,128)} copy(f32[256,1024]{0,1:T(8,128)} %bitcast.123) | data formatting | bytes 2097152 | tf_op jit(solution)/shard_map/reshape | solution.py:236
  78.7 8.2 %all-to-all-done.1 = f32[32,40,128]{2,1,0:T(8,128)S(1)} async-done(((f32[32,40,128]{2,1,0:T(8,128)}), f32[32,40,128]{2,1,0:T(8,128)S(1)}, u32[]{:S(2)}, u32[]{:S(2)}) %all-to-all-start.1) | async-done | bytes 655392 | tf_op jit(solution)/shard_map/all_to_all | solution.py:147
  87.6 1.1 fusion.39
  88.8 1.2 copy.92
  90.0 1.2 copy.93
  91.8 0.9 slice.83
  92.7 11.2 %shard_map.129 = (bf16[256,1024]{1,0:T(8,128)(2,1)}, f32[8,2,512]{2,1,0:T(2,128)}) custom-call(f32[256,1024]{1,0:T(8,128)} %get-tuple-element.20.qd_ref, f32[8,128,128]{2,1,0:T(8,128)} %bitcast.119, f32[256,1024]{1,0:T(8,128)} %copy.91.intra_ref, f32[1,1024]{1,0:T(1,128)} %bitcast.134, bf16[512,1024]{1,0:T(8,128)(2,1)} %lw_ref.1, f32[8,512,256]{2,1,0:T(8,128)} %copy-done.1, ...), custom_call_target="tpu_custom_call" | custom-call | tf_op jit(solution)/shard_map/pallas_call | solution.py:77
  103.9 0.8 reduce_sum.90
  104.7 2.8 %collective-permute-start = (f32[2,512]{1,0:T(2,128)S(1)}, f32[2,512]{1,0:T(2,128)S(1)}, u32[]{:S(2)}, u32[]{:S(2)}) collective-permute-start(f32[2,512]{1,0:T(2,128)S(1)} %reduce_sum.90), channel_id=1, source_target_pairs={{0,1},{1,0},{2,3},{3,2},{4,5},{5,4},{6,7},{7,6},{8,9},{9,8},{10,11... | collective-permute-start | bytes 12296 | tf_op jit(solution)/shard_map/ppermute | solution.py:20
  107.5 0.9 collective-permute-start.1
  108.3 1.3 collective-permute-start.2
  109.6 2.6 %collective-permute-start.3 = (f32[2,512]{1,0:T(2,128)S(1)}, f32[2,512]{1,0:T(2,128)S(1)}, u32[]{:S(2)}, u32[]{:S(2)}) collective-permute-start(f32[2,512]{1,0:T(2,128)S(1)} %reduce_sum.90), channel_id=1, source_target_pairs={{0,4},{1,5},{2,6},{3,7},{4,0},{5,1},{6,2},{7,3},{8,12},{9,13},{10,... | collective-permute-start | bytes 12296 | tf_op jit(solution)/shard_map/ppermute | solution.py:20
  112.3 2.0 %collective-permute-start.4 = (f32[2,512]{1,0:T(2,128)S(1)}, f32[2,512]{1,0:T(2,128)S(1)}, u32[]{:S(2)}, u32[]{:S(2)}) collective-permute-start(f32[2,512]{1,0:T(2,128)S(1)} %reduce_sum.90), channel_id=1, source_target_pairs={{0,5},{1,4},{2,7},{3,6},{4,1},{5,0},{6,3},{7,2},{8,13},{9,12},{10,... | collective-permute-start | bytes 12296 | tf_op jit(solution)/shard_map/ppermute | solution.py:20
  114.3 1.3 collective-permute-start.5
  115.7 2.0 %collective-permute-start.6 = (f32[2,512]{1,0:T(2,128)S(1)}, f32[2,512]{1,0:T(2,128)S(1)}, u32[]{:S(2)}, u32[]{:S(2)}) collective-permute-start(f32[2,512]{1,0:T(2,128)S(1)} %reduce_sum.90), channel_id=1, source_target_pairs={{0,7},{1,6},{2,5},{3,4},{4,3},{5,2},{6,1},{7,0},{8,15},{9,14},{10,... | collective-permute-start | bytes 12296 | tf_op jit(solution)/shard_map/ppermute | solution.py:20
  117.7 1.1 collective-permute-done.5
  119.3 1.3 collective-permute-start.7
  120.7 2.3 %collective-permute-start.8 = (f32[2,512]{1,0:T(2,128)S(1)}, f32[2,512]{1,0:T(2,128)S(1)}, u32[]{:S(2)}, u32[]{:S(2)}) collective-permute-start(f32[2,512]{1,0:T(2,128)S(1)} %add_add_fusion.1), channel_id=1, source_target_pairs={{0,16},{1,17},{2,18},{3,19},{4,20},{5,21},{6,22},{7,23},{8,24},{9,... | collective-permute-start | bytes 12296 | tf_op jit(solution)/shard_map/ppermute | solution.py:20
  123.7 1.0 collective-permute-done.8
  124.6 2.0 %collective-permute-done.9 = f32[2,512]{1,0:T(2,128)S(1)} collective-permute-done((f32[2,512]{1,0:T(2,128)S(1)}, f32[2,512]{1,0:T(2,128)S(1)}, u32[]{:S(2)}, u32[]{:S(2)}) %collective-permute-start.9) | collective-permute-done | bytes 4128 | tf_op jit(solution)/shard_map/ppermute | solution.py:20
  126.6 0.7 fusion.30
  127.3 1.1 multiply_reduce_fusion
  128.4 2.5 %collective-permute-start.15 = (f32[]{:T(128)}, f32[]{:T(128)}, u32[]{:S(2)}, u32[]{:S(2)}) collective-permute-start(f32[]{:T(128)} %get-tuple-element.18), channel_id=1, source_target_pairs={{0,192},{32,224},{64,128},{96,160},{128,64},{160,96},{192,0},{224,... | collective-permute-start | bytes 20 | tf_op jit(solution)/shard_map/ppermute | solution.py:20
  130.9 7.2 %collective-permute-start.16 = (f32[]{:T(128)}, f32[]{:T(128)}, u32[]{:S(2)}, u32[]{:S(2)}) collective-permute-start(f32[]{:T(128)} %get-tuple-element.18), channel_id=1, source_target_pairs={{0,224},{32,192},{64,160},{96,128},{128,96},{160,64},{192,32},{224... | collective-permute-start | bytes 20 | tf_op jit(solution)/shard_map/ppermute | solution.py:20
  138.1 1.5 %collective-permute-start.13 = (f32[]{:T(128)}, f32[]{:T(128)}, u32[]{:S(2)}, u32[]{:S(2)}) collective-permute-start(f32[]{:T(128)} %get-tuple-element.18), channel_id=1, source_target_pairs={{0,128},{32,160},{64,192},{96,224},{128,0},{160,32},{192,64},{224,... | collective-permute-start | bytes 20 | tf_op jit(solution)/shard_map/ppermute | solution.py:20
  139.7 1.5 %collective-permute-start.14 = (f32[]{:T(128)}, f32[]{:T(128)}, u32[]{:S(2)}, u32[]{:S(2)}) collective-permute-start(f32[]{:T(128)} %get-tuple-element.18), channel_id=1, source_target_pairs={{0,160},{32,128},{64,224},{96,192},{128,32},{160,0},{192,96},{224,... | collective-permute-start | bytes 20 | tf_op jit(solution)/shard_map/ppermute | solution.py:20
  141.2 1.9 %collective-permute-start.12 = (f32[]{:T(128)}, f32[]{:T(128)}, u32[]{:S(2)}, u32[]{:S(2)}) collective-permute-start(f32[]{:T(128)} %get-tuple-element.18), channel_id=1, source_target_pairs={{0,96},{32,64},{64,32},{96,0},{128,224},{160,192},{192,160},{224,1... | collective-permute-start | bytes 20 | tf_op jit(solution)/shard_map/ppermute | solution.py:20
  (91 shorter events, 12.4 us)
Async XLA Ops:
  0.6 70.3 %copy-start = (bf16[1024,1024]{1,0:T(8,128)(2,1)S(1)}, bf16[1024,1024]{1,0:T(8,128)(2,1)}, u32[]{:S(2)}) copy-start(bf16[1024,1024]{1,0:T(8,128)(2,1)} %param.14) | copy-start | bytes 6291460
  10.6 1.9 %copy-start.1 = (f32[8,512,256]{2,1,0:T(8,128)}, f32[8,512,256]{2,1,0:T(8,128)S(1)}, u32[]{:S(2)}) copy-start(f32[8,512,256]{2,1,0:T(8,128)S(1)} %subtract_exponential_fusion.pw_ref) | copy-start | bytes 12582916
  10.6 1.9 %copy-start.8 = (s32[1,256]{1,0:T(1,128)S(1)}, s32[1,256]{1,0:T(1,128)}, u32[]{:S(2)}) copy-start(s32[1,256]{1,0:T(1,128)} %param.13) | copy-start | bytes 3076
  10.6 2.7 %copy-start.7 = (s32[1,2]{1,0:T(1,128)S(1)}, s32[1,2]{1,0:T(1,128)}, u32[]{:S(2)}) copy-start(s32[1,2]{1,0:T(1,128)} %param.12) | copy-start | bytes 28
  10.7 4.0 %copy-start.6 = (f32[1,8,256]{2,1,0:T(8,128)S(1)}, f32[1,8,256]{2,1,0:T(8,128)}, u32[]{:S(2)}) copy-start(f32[1,8,256]{2,1,0:T(8,128)} %param.11) | copy-start | bytes 24580
  12.5 6.1 %copy-start.2 = (bf16[1,256,1024]{2,1,0:T(8,128)(2,1)S(1)}, bf16[1,256,1024]{2,1,0:T(8,128)(2,1)}, u32[]{:S(2)}) copy-start(bf16[1,256,1024]{2,1,0:T(8,128)(2,1)} %param.10) | copy-start | bytes 1572868
  23.0 4.6 %copy-start.4 = (bf16[256,1024]{0,1:T(8,128)(2,1)}, bf16[256,1024]{0,1:T(8,128)(2,1)S(1)}, u32[]{:S(2)}) copy-start(bf16[256,1024]{0,1:T(8,128)(2,1)S(1)} %copy.94) | copy-start | bytes 1572868
  27.6 1.2 copy-start.5
  28.8 28.4 %all-to-all-start = ((f32[32,40,128]{2,1,0:T(8,128)}), f32[32,40,128]{2,1,0:T(8,128)S(1)}, u32[]{:S(2)}, u32[]{:S(2)}) async-start(f32[32,40,128]{2,1,0:T(8,128)} %pad_maximum_fusion), calls=%async_computation | async-start | bytes 1310720 | tf_op jit(solution)/shard_map/all_to_all | solution.py:126
  60.6 10.4 %copy-start.3 = (bf16[1,256,1024]{2,1,0:T(8,128)(2,1)S(1)}, bf16[1,256,1024]{2,1,0:T(8,128)(2,1)}, u32[]{:S(2)}) copy-start(bf16[1,256,1024]{2,1,0:T(8,128)(2,1)} %param.10) | copy-start | bytes 1572868
  61.8 25.2 %all-to-all-start.1 = ((f32[32,40,128]{2,1,0:T(8,128)}), f32[32,40,128]{2,1,0:T(8,128)S(1)}, u32[]{:S(2)}, u32[]{:S(2)}) async-start(f32[32,40,128]{2,1,0:T(8,128)} %copy.84), calls=%async_computation.1 | async-start | bytes 1310720 | tf_op jit(solution)/shard_map/all_to_all | solution.py:147
  104.7 9.6 %collective-permute-start = (f32[2,512]{1,0:T(2,128)S(1)}, f32[2,512]{1,0:T(2,128)S(1)}, u32[]{:S(2)}, u32[]{:S(2)}) collective-permute-start(f32[2,512]{1,0:T(2,128)S(1)} %reduce_sum.90), channel_id=1, source_target_pairs={{0,1},{1,0},{2,3},{3,2},{4,5},{5,4},{6,7},{7,6},{8,9},{9,8},{10,11... | collective-permute-start | bytes 12296 | tf_op jit(solution)/shard_map/ppermute | solution.py:20
  107.5 8.2 %collective-permute-start.1 = (f32[2,512]{1,0:T(2,128)S(1)}, f32[2,512]{1,0:T(2,128)S(1)}, u32[]{:S(2)}, u32[]{:S(2)}) collective-permute-start(f32[2,512]{1,0:T(2,128)S(1)} %reduce_sum.90), channel_id=1, source_target_pairs={{0,2},{1,3},{2,0},{3,1},{4,6},{5,7},{6,4},{7,5},{8,10},{9,11},{10,... | collective-permute-start | bytes 12296 | tf_op jit(solution)/shard_map/ppermute | solution.py:20
  108.3 9.4 %collective-permute-start.2 = (f32[2,512]{1,0:T(2,128)S(1)}, f32[2,512]{1,0:T(2,128)S(1)}, u32[]{:S(2)}, u32[]{:S(2)}) collective-permute-start(f32[2,512]{1,0:T(2,128)S(1)} %reduce_sum.90), channel_id=1, source_target_pairs={{0,3},{1,2},{2,1},{3,0},{4,7},{5,6},{6,5},{7,4},{8,11},{9,10},{10,... | collective-permute-start | bytes 12296 | tf_op jit(solution)/shard_map/ppermute | solution.py:20
  109.6 8.1 %collective-permute-start.3 = (f32[2,512]{1,0:T(2,128)S(1)}, f32[2,512]{1,0:T(2,128)S(1)}, u32[]{:S(2)}, u32[]{:S(2)}) collective-permute-start(f32[2,512]{1,0:T(2,128)S(1)} %reduce_sum.90), channel_id=1, source_target_pairs={{0,4},{1,5},{2,6},{3,7},{4,0},{5,1},{6,2},{7,3},{8,12},{9,13},{10,... | collective-permute-start | bytes 12296 | tf_op jit(solution)/shard_map/ppermute | solution.py:20
  112.3 5.5 %collective-permute-start.4 = (f32[2,512]{1,0:T(2,128)S(1)}, f32[2,512]{1,0:T(2,128)S(1)}, u32[]{:S(2)}, u32[]{:S(2)}) collective-permute-start(f32[2,512]{1,0:T(2,128)S(1)} %reduce_sum.90), channel_id=1, source_target_pairs={{0,5},{1,4},{2,7},{3,6},{4,1},{5,0},{6,3},{7,2},{8,13},{9,12},{10,... | collective-permute-start | bytes 12296 | tf_op jit(solution)/shard_map/ppermute | solution.py:20
  114.3 4.6 %collective-permute-start.5 = (f32[2,512]{1,0:T(2,128)S(1)}, f32[2,512]{1,0:T(2,128)S(1)}, u32[]{:S(2)}, u32[]{:S(2)}) collective-permute-start(f32[2,512]{1,0:T(2,128)S(1)} %reduce_sum.90), channel_id=1, source_target_pairs={{0,6},{1,7},{2,4},{3,5},{4,2},{5,3},{6,0},{7,1},{8,14},{9,15},{10,... | collective-permute-start | bytes 12296 | tf_op jit(solution)/shard_map/ppermute | solution.py:20
  115.7 3.7 %collective-permute-start.6 = (f32[2,512]{1,0:T(2,128)S(1)}, f32[2,512]{1,0:T(2,128)S(1)}, u32[]{:S(2)}, u32[]{:S(2)}) collective-permute-start(f32[2,512]{1,0:T(2,128)S(1)} %reduce_sum.90), channel_id=1, source_target_pairs={{0,7},{1,6},{2,5},{3,4},{4,3},{5,2},{6,1},{7,0},{8,15},{9,14},{10,... | collective-permute-start | bytes 12296 | tf_op jit(solution)/shard_map/ppermute | solution.py:20
  119.3 4.3 %collective-permute-start.7 = (f32[2,512]{1,0:T(2,128)S(1)}, f32[2,512]{1,0:T(2,128)S(1)}, u32[]{:S(2)}, u32[]{:S(2)}) collective-permute-start(f32[2,512]{1,0:T(2,128)S(1)} %add_add_fusion.1), channel_id=1, source_target_pairs={{0,8},{1,9},{2,10},{3,11},{4,12},{5,13},{6,14},{7,15},{8,0},{9,1},... | collective-permute-start | bytes 12296 | tf_op jit(solution)/shard_map/ppermute | solution.py:20
  120.7 4.0 %collective-permute-start.8 = (f32[2,512]{1,0:T(2,128)S(1)}, f32[2,512]{1,0:T(2,128)S(1)}, u32[]{:S(2)}, u32[]{:S(2)}) collective-permute-start(f32[2,512]{1,0:T(2,128)S(1)} %add_add_fusion.1), channel_id=1, source_target_pairs={{0,16},{1,17},{2,18},{3,19},{4,20},{5,21},{6,22},{7,23},{8,24},{9,... | collective-permute-start | bytes 12296 | tf_op jit(solution)/shard_map/ppermute | solution.py:20
  123.0 3.7 %collective-permute-start.9 = (f32[2,512]{1,0:T(2,128)S(1)}, f32[2,512]{1,0:T(2,128)S(1)}, u32[]{:S(2)}, u32[]{:S(2)}) collective-permute-start(f32[2,512]{1,0:T(2,128)S(1)} %add_add_fusion.1), channel_id=1, source_target_pairs={{0,24},{1,25},{2,26},{3,27},{4,28},{5,29},{6,30},{7,31},{8,16},{9,... | collective-permute-start | bytes 12296 | tf_op jit(solution)/shard_map/ppermute | solution.py:20
  128.4 12.8 %collective-permute-start.15 = (f32[]{:T(128)}, f32[]{:T(128)}, u32[]{:S(2)}, u32[]{:S(2)}) collective-permute-start(f32[]{:T(128)} %get-tuple-element.18), channel_id=1, source_target_pairs={{0,192},{32,224},{64,128},{96,160},{128,64},{160,96},{192,0},{224,... | collective-permute-start | bytes 20 | tf_op jit(solution)/shard_map/ppermute | solution.py:20
  130.9 12.2 %collective-permute-start.16 = (f32[]{:T(128)}, f32[]{:T(128)}, u32[]{:S(2)}, u32[]{:S(2)}) collective-permute-start(f32[]{:T(128)} %get-tuple-element.18), channel_id=1, source_target_pairs={{0,224},{32,192},{64,160},{96,128},{128,96},{160,64},{192,32},{224... | collective-permute-start | bytes 20 | tf_op jit(solution)/shard_map/ppermute | solution.py:20
  138.1 6.2 %collective-permute-start.13 = (f32[]{:T(128)}, f32[]{:T(128)}, u32[]{:S(2)}, u32[]{:S(2)}) collective-permute-start(f32[]{:T(128)} %get-tuple-element.18), channel_id=1, source_target_pairs={{0,128},{32,160},{64,192},{96,224},{128,0},{160,32},{192,64},{224,... | collective-permute-start | bytes 20 | tf_op jit(solution)/shard_map/ppermute | solution.py:20
  139.7 4.7 %collective-permute-start.14 = (f32[]{:T(128)}, f32[]{:T(128)}, u32[]{:S(2)}, u32[]{:S(2)}) collective-permute-start(f32[]{:T(128)} %get-tuple-element.18), channel_id=1, source_target_pairs={{0,160},{32,128},{64,224},{96,192},{128,32},{160,0},{192,96},{224,... | collective-permute-start | bytes 20 | tf_op jit(solution)/shard_map/ppermute | solution.py:20
  141.2 5.7 %collective-permute-start.11 = (f32[]{:T(128)}, f32[]{:T(128)}, u32[]{:S(2)}, u32[]{:S(2)}) collective-permute-start(f32[]{:T(128)} %get-tuple-element.18), channel_id=1, source_target_pairs={{0,64},{32,96},{64,0},{96,32},{128,192},{160,224},{192,128},{224,1... | collective-permute-start | bytes 20 | tf_op jit(solution)/shard_map/ppermute | solution.py:20
  141.2 5.7 %collective-permute-start.12 = (f32[]{:T(128)}, f32[]{:T(128)}, u32[]{:S(2)}, u32[]{:S(2)}) collective-permute-start(f32[]{:T(128)} %get-tuple-element.18), channel_id=1, source_target_pairs={{0,96},{32,64},{64,32},{96,0},{128,224},{160,192},{192,160},{224,1... | collective-permute-start | bytes 20 | tf_op jit(solution)/shard_map/ppermute | solution.py:20
  143.1 2.5 %collective-permute-start.10 = (f32[]{:T(128)}, f32[]{:T(128)}, u32[]{:S(2)}, u32[]{:S(2)}) collective-permute-start(f32[]{:T(128)} %get-tuple-element.18), channel_id=1, source_target_pairs={{0,32},{32,0},{64,96},{96,64},{128,160},{160,128},{192,224},{224,1... | collective-permute-start | bytes 20 | tf_op jit(solution)/shard_map/ppermute | solution.py:20

commit v6 on v5

--- a/solution.py
+++ b/solution.py
@@ -48,9 +48,11 @@
     return out + jnp.dot(a_lo, b_hi, preferred_element_type=jnp.float32)
 
 
-def finish_kernel(qd_ref, state_ref, intra_ref, gain_ref, lw_ref, pw_ref, member_ref, rescale_ref,
+def finish_kernel(qd_ref, back_ref, intra_ref, gain_ref, lw_ref, pw_ref, member_ref,
                   out_ref, part_ref, *, qk_scale):
-    inter = split_dot(qd_ref[...], state_ref[0])
+    block = back_ref[...]
+    state = block.reshape(block.shape[0] * block.shape[1], block.shape[2])
+    inter = split_dot(qd_ref[...], state)
     total = intra_ref[...] + inter * qk_scale
     centred = total - jnp.mean(total, axis=1, keepdims=True)
     variance = jnp.mean(centred * centred, axis=1, keepdims=True)
@@ -61,42 +63,47 @@
         lw_ref[...], y, (((1,), (1,)), ((), ())), preferred_element_type=jnp.float32
     )
     prod = pw_ref[0] * label_value
-    weighted = lax.dot_general(
-        member_ref[...], prod, (((1,), (1,)), ((), ())),
-        precision=lax.Precision.HIGHEST, preferred_element_type=jnp.float32,
-    )
-    part_ref[0] = weighted * rescale_ref[0]
-
-
-def finish_call(q_decayed, incoming, intra, norm_gain, label_weight, pool_weight, member, rescale,
-                qk_scale):
+    member = member_ref[...]
+    hi = prod.astype(jnp.bfloat16)
+    rest = prod - hi.astype(jnp.float32)
+    mid = rest.astype(jnp.bfloat16)
+    lo = (rest - mid.astype(jnp.float32)).astype(jnp.bfloat16)
+    weighted = jnp.dot(hi, member, preferred_element_type=jnp.float32)
+    weighted = weighted + jnp.dot(mid, member, preferred_element_type=jnp.float32)
+    part_ref[0] = weighted + jnp.dot(lo, member, preferred_element_type=jnp.float32)
+
+
+def finish_call(q_decayed, back, intra, norm_gain, label_weight, pool_weight, member_cols,
+                head_count, qk_scale):
     tok_rows, model_width = q_decayed.shape
-    head_count, head_dim, _ = incoming.shape
+    head_dim = model_width // head_count
+    owners, _, lanes = back.shape
+    per_head = owners // head_count
+    rows = head_dim // per_head
     label_count = label_weight.shape[0]
-    record_count = member.shape[0]
+    width = member_cols.shape[1]
     return pl.pallas_call(
         functools.partial(finish_kernel, qk_scale=qk_scale),
         grid=(head_count,),
         in_specs=[
             pl.BlockSpec((tok_rows, head_dim), lambda h: (0, h)),
-            pl.BlockSpec((1, head_dim, head_dim), lambda h: (h, 0, 0)),
+            pl.BlockSpec((per_head, rows, lanes), lambda h: (h, 0, 0)),
             pl.BlockSpec((tok_rows, head_dim), lambda h: (0, h)),
             pl.BlockSpec((1, head_dim), lambda h: (0, h)),
             pl.BlockSpec((label_count, head_dim), lambda h: (0, h)),
             pl.BlockSpec((1, label_count, tok_rows), lambda h: (h, 0, 0)),
-            pl.BlockSpec((record_count, tok_rows), lambda h: (0, 0)),
-            pl.BlockSpec((1, record_count, label_count), lambda h: (h, 0, 0)),
+            pl.BlockSpec((tok_rows, width), lambda h: (0, 0)),
         ],
         out_specs=[
             pl.BlockSpec((tok_rows, head_dim), lambda h: (0, h)),
-            pl.BlockSpec((1, record_count, label_count), lambda h: (h, 0, 0)),
+            pl.BlockSpec((1, label_count, width), lambda h: (h, 0, 0)),
         ],
         out_shape=[
             jax.ShapeDtypeStruct((tok_rows, model_width), jnp.bfloat16),
-            jax.ShapeDtypeStruct((head_count, record_count, label_count), jnp.float32),
-        ],
-    )(q_decayed, incoming, intra, norm_gain.reshape(1, model_width), label_weight, pool_weight,
-      member, rescale)
+            jax.ShapeDtypeStruct((head_count, label_count, width), jnp.float32),
+        ],
+    )(q_decayed, back, intra, norm_gain.reshape(1, model_width), label_weight, pool_weight,
+      member_cols)
 
 
 def record_ids(length_row, positions):
@@ -145,9 +152,8 @@
     ).reshape(count, 8, head_dim)
     sent_back = jnp.concatenate([scanned.reshape(count, rows, head_dim), back_extra], axis=1)
     back = lax.all_to_all(sent_back, axis, 0, 0)
-    state = back[:, :rows, :].reshape(head_count, head_dim, head_dim)
     totals = back[:, rows:, :].reshape(count, 8 * head_dim)[:, : per_owner * fields]
-    return state, totals.reshape(pair_count, fields)
+    return back, totals.reshape(pair_count, fields)
 
 
 def local(
@@ -232,11 +238,14 @@
     q_decayed = (
         q3.astype(jnp.float32) * jnp.where(linked[None, :], jnp.exp(decay_cum), 0.0).T[:, :, None]
     ).reshape(tok_rows, model_width)
+    member_cols = jnp.zeros((tok_rows, 128), jnp.bfloat16).at[:, :record_count].set(
+        member.T.astype(jnp.bfloat16)
+    )
     out_rows, head_parts = finish_call(
         q_decayed, incoming, intra.reshape(tok_rows, model_width), norm_gain, label_weight,
-        pool_weight, member.astype(jnp.float32), rescale, qk_scale,
-    )
-    part = jnp.sum(head_parts, axis=0)
+        pool_weight, member_cols, head_count, qk_scale,
+    )
+    part = jnp.sum(jnp.transpose(head_parts[:, :, :record_count], (0, 2, 1)) * rescale, axis=0)
     count = lax.axis_size("ctx")
     inner = min(count, 8)
     assert count % inner == 0 and inner & (inner - 1) == 0

time: 150 us -> 204 us (1.36)
  waiting for transfers between devices: 29.2 us -> 73.9 us
  local copies, waits for them, and re-layouts: 17.6 us -> 26.5 us
  starting transfers between devices: 52.3 us -> 46.3 us
  other arithmetic: 16.3 us -> 21.7 us
    ppermute x17, waiting for transfers between devices: 4.6 us -> 51.3 us  [swapped(): return lax.ppermute(x, axis, [(i, i ^ bit) for i in range(count)])]
    ppermute x17, starting transfers between devices: 31.6 us -> 25.7 us  [swapped(): return lax.ppermute(x, axis, [(i, i ^ bit) for i in range(count)])]
    unnamed x24 -> x25, local copies, waits for them, and re-layouts: 4.38 us -> 9.36 us
    add x0 -> x1, local copies, waits for them, and re-layouts: none -> 3.11 us  [local(): total_counts + 0.5]
    reduce_sum x1, other arithmetic: 0.78 us -> 3.25 us  [local(): jnp.sum(jnp.transpose(head_parts[:, :, :record_count], (0, 2, 1)) * resca...]
    another operation x3 -> x5, other arithmetic: 1.59 us -> 3.67 us
  transfers between devices with their start and end apart: 19 -> 19, of which waited for: 6 -> 10; matrix products, arithmetic and copies ran while one was open for 6% -> 7% of each run, Pallas kernels for 0% -> 0%
where the time goes in v6:
time: 204 us; the launch traced here: 201 us
  waiting for transfers between devices  73.9 us (36%)
  starting transfers between devices  46.3 us (23%)
  local copies, waits for them, and re-layouts  26.5 us (13%)
  other arithmetic  21.7 us (11%)
  matrix products  14.4 us (7%)
  Pallas kernels  10.7 us (5%)
  between operations  7.92 us (4%)
    ppermute x17, waiting for transfers between devices, swapped(): return lax.ppermute(x, axis, [(i, i ^ bit) for i in range(count)])  51.3 us
    ppermute x17, starting transfers between devices, swapped(): return lax.ppermute(x, axis, [(i, i ^ bit) for i in range(count)])  25.7 us
    all_to_all x1, waiting for transfers between devices, exclusive_state_scan(): got = lax.all_to_all(jnp.concatenate([slices, extra], axis=1), axis, 0, 0)  16.4 us
    all_to_all x1, starting transfers between devices, exclusive_state_scan(): got = lax.all_to_all(jnp.concatenate([slices, extra], axis=1), axis, 0, 0)  12 us
    pallas_call x1, Pallas kernels, finish_call(): pl.pallas_call(functools.partial(finish_kernel, qk_scale=qk_scale), grid=...  10.7 us
    unnamed x25, local copies, waits for them, and re-layouts  9.36 us
    all_to_all x1, starting transfers between devices, exclusive_state_scan(): back = lax.all_to_all(sent_back, axis, 0, 0)  8.58 us
    all_to_all x1, waiting for transfers between devices, exclusive_state_scan(): back = lax.all_to_all(sent_back, axis, 0, 0)  6.27 us
  transfers between devices with their start and end apart: 19, of which 10 were waited for; matrix products, arithmetic and copies ran while one was open for 7% of the time, Pallas kernels for 0%

profile of v6, /device:TPU:1, one launch (start us, length us, event | category | flops | bytes accessed | tf_op | source)
XLA Modules:
  0.0 201.5 jit_solution(8368328847780525013)
XLA Ops:
  0.7 1.0 reduce-window.10
  3.0 1.3 fusion.36
  5.0 1.3 reduce-window.11
  9.4 0.9 convolution_bitcast_fusion
  10.3 1.1 copy.133
  12.2 1.2 select_reduce_fusion.2
  13.4 1.5 select_reduce_fusion.1
  15.0 1.2 subtract_exponential_fusion.pw_ref
  16.2 1.2 select_reduce_fusion
  18.9 3.1 %convolution_convert_fusion = bf16[256,1024]{1,0:T(8,128)(2,1)} fusion(bf16[1024,1024]{1,0:T(8,128)(2,1)} %param.18, bf16[1,256,1024]{2,1,0:T(8,128)(2,1)S(1)} %copy-done.3), kind=kOutput, calls=%fused_computation.11 | convolution fusion | flops 537133056 | bytes 3145728 | tf_op jit(solution)/shard_map/dot_general | solution.py:185
  22.0 1.2 copy.128
  23.2 3.3 %convolution_convert_fusion.1 = bf16[256,1024]{1,0:T(8,128)(2,1)} fusion(bf16[1024,1024]{1,0:T(8,128)(2,1)} %param.17, bf16[1,256,1024]{2,1,0:T(8,128)(2,1)S(1)} %copy-done.3), kind=kOutput, calls=%fused_computation.12 | convolution fusion | flops 537133056 | bytes 3145728 | tf_op jit(solution)/shard_map/dot_general | solution.py:184
  26.5 1.2 copy.127
  29.0 12.0 %all-to-all-start = ((f32[32,40,128]{2,1,0:T(8,128)}), f32[32,40,128]{2,1,0:T(8,128)S(1)}, u32[]{:S(2)}, u32[]{:S(2)}) async-start(f32[32,40,128]{2,1,0:T(8,128)} %pad_maximum_fusion), calls=%async_computation | async-start | bytes 1310720 | tf_op jit(solution)/shard_map/all_to_all | solution.py:133
  41.1 16.4 %all-to-all-done = f32[32,40,128]{2,1,0:T(8,128)S(1)} async-done(((f32[32,40,128]{2,1,0:T(8,128)}), f32[32,40,128]{2,1,0:T(8,128)S(1)}, u32[]{:S(2)}, u32[]{:S(2)}) %all-to-all-start) | async-done | bytes 655392 | tf_op jit(solution)/shard_map/all_to_all | solution.py:133
  62.0 8.6 %all-to-all-start.1 = ((f32[32,40,128]{2,1,0:T(8,128)}), f32[32,40,128]{2,1,0:T(8,128)S(1)}, u32[]{:S(2)}, u32[]{:S(2)}) async-start(f32[32,40,128]{2,1,0:T(8,128)} %pad_maximum_fusion.1), calls=%async_computation.1 | async-start | bytes 1310720 | tf_op jit(solution)/shard_map/all_to_all | solution.py:154
  71.2 2.0 bitcast_multiply_fusion
  73.1 3.2 %fusion.2 = f32[8,128,256]{2,1,0:T(8,128)} fusion(bf16[256,8,128]{0,2,1:T(8,128)(2,1)} %bitcast.127, bf16[256,8,128]{0,2,1:T(8,128)(2,1)} %bitcast.129, f32[8,256]{1,0:T(8,128)S(1)} %get-tuple-element.39, pred[256,256]{1,0:T(8,128)(4,1)S(1)} %fusion.28, bf16[256,1024]{1,0:T(8,128)(2,1)} %get-tuple-element.47), kind=kOutput, calls=%fused_computation.10 | convolution fusion | flops 271581184 | bytes 2695168 | tf_op jit(solution)/shard_map/hts,shd->thd/dot_general | solution.py:203
  76.4 2.5 %copy.123.intra_ref = f32[256,1024]{1,0:T(8,128)} copy(f32[256,1024]{0,1:T(8,128)} %bitcast.133) | data formatting | bytes 2097152 | tf_op jit(solution)/shard_map/reshape | solution.py:245
  80.9 6.3 %all-to-all-done.1.back_ref = f32[32,40,128]{2,1,0:T(8,128)S(1)} async-done(((f32[32,40,128]{2,1,0:T(8,128)}), f32[32,40,128]{2,1,0:T(8,128)S(1)}, u32[]{:S(2)}, u32[]{:S(2)}) %all-to-all-start.1) | async-done | bytes 655392 | tf_op jit(solution)/shard_map/all_to_all | solution.py:154
  87.8 1.1 fusion.42
  89.0 1.2 copy.125
  90.2 2.0 copy.120
  92.2 5.5 %copy.126 = f32[2,512,8]{0,1,2:T(8,128)} copy(f32[2,512,8]{2,1,0:T(8,128)} %get-tuple-element.40) | data formatting | bytes 65536
  97.7 10.7 %shard_map.129 = (bf16[256,1024]{1,0:T(8,128)(2,1)}, f32[8,512,128]{2,1,0:T(8,128)}) custom-call(f32[256,1024]{1,0:T(8,128)} %get-tuple-element.46.qd_ref, f32[32,40,128]{2,1,0:T(8,128)} %copy-done.2, f32[256,1024]{1,0:T(8,128)} %copy.123.intra_ref, f32[1,1024]{1,0:T(1,128)} %bitcast.145, bf16[512,1024]{1,0:T(8,128)(2,1)} %lw_ref.1, ...), custom_call_target="tpu_custom_call" | custom-call | tf_op jit(solution)/shard_map/pallas_call | solution.py:85
  108.4 3.3 %fusion.1 = f32[2,512]{0,1:T(8,128)S(1)} fusion(f32[8,2,512]{1,2,0:T(8,128)} %copy.120, f32[2,512,8]{0,1,2:T(8,128)} %copy.126, f32[8,512,128]{2,1,0:T(8,128)} %get-tuple-element.19), kind=kLoop, calls=%fused_computation.9 | loop fusion | flops 23552 | bytes 102400 | tf_op jit(solution)/shard_map/reduce_sum | solution.py:248
  111.7 3.1 %collective-permute-start.5 = (f32[2,512]{0,1:T(8,128)S(1)}, f32[2,512]{0,1:T(8,128)S(1)}, u32[]{:S(2)}, u32[]{:S(2)}) collective-permute-start(f32[2,512]{0,1:T(8,128)S(1)} %fusion.1), channel_id=1, source_target_pairs={{0,6},{1,7},{2,4},{3,5},{4,2},{5,3},{6,0},{7,1},{8,14},{9,15},{10,... | collective-permute-start | bytes 12296 | tf_op jit(solution)/shard_map/ppermute | solution.py:20
  114.8 2.0 %collective-permute-start.6 = (f32[2,512]{0,1:T(8,128)S(1)}, f32[2,512]{0,1:T(8,128)S(1)}, u32[]{:S(2)}, u32[]{:S(2)}) collective-permute-start(f32[2,512]{0,1:T(8,128)S(1)} %fusion.1), channel_id=1, source_target_pairs={{0,7},{1,6},{2,5},{3,4},{4,3},{5,2},{6,1},{7,0},{8,15},{9,14},{10,... | collective-permute-start | bytes 12296 | tf_op jit(solution)/shard_map/ppermute | solution.py:20
  116.8 2.3 %collective-permute-start.3 = (f32[2,512]{0,1:T(8,128)S(1)}, f32[2,512]{0,1:T(8,128)S(1)}, u32[]{:S(2)}, u32[]{:S(2)}) collective-permute-start(f32[2,512]{0,1:T(8,128)S(1)} %fusion.1), channel_id=1, source_target_pairs={{0,4},{1,5},{2,6},{3,7},{4,0},{5,1},{6,2},{7,3},{8,12},{9,13},{10,... | collective-permute-start | bytes 12296 | tf_op jit(solution)/shard_map/ppermute | solution.py:20
  119.1 1.6 collective-permute-start.4
  120.7 2.1 %collective-permute-start.1 = (f32[2,512]{0,1:T(8,128)S(1)}, f32[2,512]{0,1:T(8,128)S(1)}, u32[]{:S(2)}, u32[]{:S(2)}) collective-permute-start(f32[2,512]{0,1:T(8,128)S(1)} %fusion.1), channel_id=1, source_target_pairs={{0,2},{1,3},{2,0},{3,1},{4,6},{5,7},{6,4},{7,5},{8,10},{9,11},{10,... | collective-permute-start | bytes 12296 | tf_op jit(solution)/shard_map/ppermute | solution.py:20
  122.8 25.8 %collective-permute-done.5 = f32[2,512]{0,1:T(8,128)S(1)} collective-permute-done((f32[2,512]{0,1:T(8,128)S(1)}, f32[2,512]{0,1:T(8,128)S(1)}, u32[]{:S(2)}, u32[]{:S(2)}) %collective-permute-start.5) | collective-permute-done | bytes 4128 | tf_op jit(solution)/shard_map/ppermute | solution.py:20
  148.6 2.1 %collective-permute-start.2 = (f32[2,512]{0,1:T(8,128)S(1)}, f32[2,512]{0,1:T(8,128)S(1)}, u32[]{:S(2)}, u32[]{:S(2)}) collective-permute-start(f32[2,512]{0,1:T(8,128)S(1)} %fusion.1), channel_id=1, source_target_pairs={{0,3},{1,2},{2,1},{3,0},{4,7},{5,6},{6,5},{7,4},{8,11},{9,10},{10,... | collective-permute-start | bytes 12296 | tf_op jit(solution)/shard_map/ppermute | solution.py:20
  150.7 5.1 %collective-permute-done.6 = f32[2,512]{0,1:T(8,128)S(1)} collective-permute-done((f32[2,512]{0,1:T(8,128)S(1)}, f32[2,512]{0,1:T(8,128)S(1)}, u32[]{:S(2)}, u32[]{:S(2)}) %collective-permute-start.6) | collective-permute-done | bytes 4128 | tf_op jit(solution)/shard_map/ppermute | solution.py:20
  155.8 4.0 %collective-permute-done.4 = f32[2,512]{0,1:T(8,128)S(1)} collective-permute-done((f32[2,512]{0,1:T(8,128)S(1)}, f32[2,512]{0,1:T(8,128)S(1)}, u32[]{:S(2)}, u32[]{:S(2)}) %collective-permute-start.4) | collective-permute-done | bytes 4128 | tf_op jit(solution)/shard_map/ppermute | solution.py:20
  159.8 1.1 collective-permute-done.2
  160.9 5.8 %collective-permute-done = f32[2,512]{0,1:T(8,128)S(1)} collective-permute-done((f32[2,512]{0,1:T(8,128)S(1)}, f32[2,512]{0,1:T(8,128)S(1)}, u32[]{:S(2)}, u32[]{:S(2)}) %collective-permute-start) | collective-permute-done | bytes 4128 | tf_op jit(solution)/shard_map/ppermute | solution.py:20
  166.8 2.5 %collective-permute-start.8 = (f32[2,512]{0,1:T(8,128)S(1)}, f32[2,512]{0,1:T(8,128)}, u32[]{:S(2)}, u32[]{:S(2)}) collective-permute-start(f32[2,512]{0,1:T(8,128)S(1)} %add_add_fusion.1), channel_id=1, source_target_pairs={{0,16},{1,17},{2,18},{3,19},{4,20},{5,21},{6,22},{7,23},{8,24},{9,... | collective-permute-start | bytes 12296 | tf_op jit(solution)/shard_map/ppermute | solution.py:20
  169.3 1.1 collective-permute-start.9
  170.6 3.1 %copy.124 = f32[2,512,1]{0,1,2:T(8,128)S(1)} copy(f32[2,512,1]{2,1,0:T(8,128)S(1)} %slice_add_fusion) | data formatting | bytes 8192 | tf_op jit(solution)/shard_map/add | solution.py:256
  174.5 7.4 %collective-permute-done.9 = f32[2,512]{0,1:T(8,128)} collective-permute-done((f32[2,512]{0,1:T(8,128)S(1)}, f32[2,512]{0,1:T(8,128)}, u32[]{:S(2)}, u32[]{:S(2)}) %collective-permute-start.9) | collective-permute-done | bytes 4128 | tf_op jit(solution)/shard_map/ppermute | solution.py:20
  181.9 1.3 fusion.25
  183.2 1.1 multiply_reduce_fusion
  184.3 0.9 collective-permute-start.10
  185.3 1.2 collective-permute-start.11
  186.9 2.7 %collective-permute-start.13 = (f32[]{:T(128)}, f32[]{:T(128)}, u32[]{:S(2)}, u32[]{:S(2)}) collective-permute-start(f32[]{:T(128)} %get-tuple-element.44), channel_id=1, source_target_pairs={{0,128},{32,160},{64,192},{96,224},{128,0},{160,32},{192,64},{224,... | collective-permute-start | bytes 20 | tf_op jit(solution)/shard_map/ppermute | solution.py:20
  191.0 2.5 %collective-permute-start.15 = (f32[]{:T(128)}, f32[]{:T(128)}, u32[]{:S(2)}, u32[]{:S(2)}) collective-permute-start(f32[]{:T(128)} %get-tuple-element.44), channel_id=1, source_target_pairs={{0,192},{32,224},{64,128},{96,160},{128,64},{160,96},{192,0},{224,... | collective-permute-start | bytes 20 | tf_op jit(solution)/shard_map/ppermute | solution.py:20
  197.8 1.3 collective-permute-done.16
  (96 shorter events, 18.9 us)
Async XLA Ops:
  0.6 70.5 %copy-start = (bf16[1024,1024]{1,0:T(8,128)(2,1)S(1)}, bf16[1024,1024]{1,0:T(8,128)(2,1)}, u32[]{:S(2)}) copy-start(bf16[1024,1024]{1,0:T(8,128)(2,1)} %param.16) | copy-start | bytes 6291460
  0.6 10.8 %copy-start.7 = (bf16[512,1024]{1,0:T(8,128)(2,1)S(1)}, bf16[512,1024]{1,0:T(8,128)(2,1)}, u32[]{:S(2)}) copy-start(bf16[512,1024]{1,0:T(8,128)(2,1)} %param.20) | copy-start | bytes 3145732
  16.2 1.9 copy-start.1
  16.2 2.7 %copy-start.3 = (bf16[1,256,1024]{2,1,0:T(8,128)(2,1)S(1)}, bf16[1,256,1024]{2,1,0:T(8,128)(2,1)}, u32[]{:S(2)}) copy-start(bf16[1,256,1024]{2,1,0:T(8,128)(2,1)} %param.12) | copy-start | bytes 1572868
  23.2 4.6 %copy-start.5 = (bf16[256,1024]{0,1:T(8,128)(2,1)}, bf16[256,1024]{0,1:T(8,128)(2,1)S(1)}, u32[]{:S(2)}) copy-start(bf16[256,1024]{0,1:T(8,128)(2,1)S(1)} %copy.128) | copy-start | bytes 1572868
  27.7 1.3 copy-start.6
  29.0 28.4 %all-to-all-start = ((f32[32,40,128]{2,1,0:T(8,128)}), f32[32,40,128]{2,1,0:T(8,128)S(1)}, u32[]{:S(2)}, u32[]{:S(2)}) async-start(f32[32,40,128]{2,1,0:T(8,128)} %pad_maximum_fusion), calls=%async_computation | async-start | bytes 1310720 | tf_op jit(solution)/shard_map/all_to_all | solution.py:133
  61.1 10.1 %copy-start.4 = (bf16[1,256,1024]{2,1,0:T(8,128)(2,1)S(1)}, bf16[1,256,1024]{2,1,0:T(8,128)(2,1)}, u32[]{:S(2)}) copy-start(bf16[1,256,1024]{2,1,0:T(8,128)(2,1)} %param.12) | copy-start | bytes 1572868
  62.0 25.2 %all-to-all-start.1 = ((f32[32,40,128]{2,1,0:T(8,128)}), f32[32,40,128]{2,1,0:T(8,128)S(1)}, u32[]{:S(2)}, u32[]{:S(2)}) async-start(f32[32,40,128]{2,1,0:T(8,128)} %pad_maximum_fusion.1), calls=%async_computation.1 | async-start | bytes 1310720 | tf_op jit(solution)/shard_map/all_to_all | solution.py:154
  87.2 5.0 %copy-start.2 = (f32[32,40,128]{2,1,0:T(8,128)}, f32[32,40,128]{2,1,0:T(8,128)S(1)}, u32[]{:S(2)}) copy-start(f32[32,40,128]{2,1,0:T(8,128)S(1)} %all-to-all-done.1.back_ref) | copy-start | bytes 1966084
  108.4 47.4 %copy-start.8 = (s32[1,2]{1,0:T(1,128)S(1)}, s32[1,2]{1,0:T(1,128)}, u32[]{:S(2)}) copy-start(s32[1,2]{1,0:T(1,128)} %param.14) | copy-start | bytes 28
  111.7 36.9 %collective-permute-start.5 = (f32[2,512]{0,1:T(8,128)S(1)}, f32[2,512]{0,1:T(8,128)S(1)}, u32[]{:S(2)}, u32[]{:S(2)}) collective-permute-start(f32[2,512]{0,1:T(8,128)S(1)} %fusion.1), channel_id=1, source_target_pairs={{0,6},{1,7},{2,4},{3,5},{4,2},{5,3},{6,0},{7,1},{8,14},{9,15},{10,... | collective-permute-start | bytes 12296 | tf_op jit(solution)/shard_map/ppermute | solution.py:20
  114.8 41.0 %collective-permute-start.6 = (f32[2,512]{0,1:T(8,128)S(1)}, f32[2,512]{0,1:T(8,128)S(1)}, u32[]{:S(2)}, u32[]{:S(2)}) collective-permute-start(f32[2,512]{0,1:T(8,128)S(1)} %fusion.1), channel_id=1, source_target_pairs={{0,7},{1,6},{2,5},{3,4},{4,3},{5,2},{6,1},{7,0},{8,15},{9,14},{10,... | collective-permute-start | bytes 12296 | tf_op jit(solution)/shard_map/ppermute | solution.py:20
  116.8 39.0 %collective-permute-start.3 = (f32[2,512]{0,1:T(8,128)S(1)}, f32[2,512]{0,1:T(8,128)S(1)}, u32[]{:S(2)}, u32[]{:S(2)}) collective-permute-start(f32[2,512]{0,1:T(8,128)S(1)} %fusion.1), channel_id=1, source_target_pairs={{0,4},{1,5},{2,6},{3,7},{4,0},{5,1},{6,2},{7,3},{8,12},{9,13},{10,... | collective-permute-start | bytes 12296 | tf_op jit(solution)/shard_map/ppermute | solution.py:20
  119.1 40.7 %collective-permute-start.4 = (f32[2,512]{0,1:T(8,128)S(1)}, f32[2,512]{0,1:T(8,128)S(1)}, u32[]{:S(2)}, u32[]{:S(2)}) collective-permute-start(f32[2,512]{0,1:T(8,128)S(1)} %fusion.1), channel_id=1, source_target_pairs={{0,5},{1,4},{2,7},{3,6},{4,1},{5,0},{6,3},{7,2},{8,13},{9,12},{10,... | collective-permute-start | bytes 12296 | tf_op jit(solution)/shard_map/ppermute | solution.py:20
  120.7 39.1 %collective-permute-start.1 = (f32[2,512]{0,1:T(8,128)S(1)}, f32[2,512]{0,1:T(8,128)S(1)}, u32[]{:S(2)}, u32[]{:S(2)}) collective-permute-start(f32[2,512]{0,1:T(8,128)S(1)} %fusion.1), channel_id=1, source_target_pairs={{0,2},{1,3},{2,0},{3,1},{4,6},{5,7},{6,4},{7,5},{8,10},{9,11},{10,... | collective-permute-start | bytes 12296 | tf_op jit(solution)/shard_map/ppermute | solution.py:20
  148.6 12.3 %collective-permute-start.2 = (f32[2,512]{0,1:T(8,128)S(1)}, f32[2,512]{0,1:T(8,128)S(1)}, u32[]{:S(2)}, u32[]{:S(2)}) collective-permute-start(f32[2,512]{0,1:T(8,128)S(1)} %fusion.1), channel_id=1, source_target_pairs={{0,3},{1,2},{2,1},{3,0},{4,7},{5,6},{6,5},{7,4},{8,11},{9,10},{10,... | collective-permute-start | bytes 12296 | tf_op jit(solution)/shard_map/ppermute | solution.py:20
  155.8 10.9 %collective-permute-start = (f32[2,512]{0,1:T(8,128)S(1)}, f32[2,512]{0,1:T(8,128)S(1)}, u32[]{:S(2)}, u32[]{:S(2)}) collective-permute-start(f32[2,512]{0,1:T(8,128)S(1)} %fusion.1), channel_id=1, source_target_pairs={{0,1},{1,0},{2,3},{3,2},{4,5},{5,4},{6,7},{7,6},{8,9},{9,8},{10,11... | collective-permute-start | bytes 12296 | tf_op jit(solution)/shard_map/ppermute | solution.py:20
  166.8 7.7 %collective-permute-start.8 = (f32[2,512]{0,1:T(8,128)S(1)}, f32[2,512]{0,1:T(8,128)}, u32[]{:S(2)}, u32[]{:S(2)}) collective-permute-start(f32[2,512]{0,1:T(8,128)S(1)} %add_add_fusion.1), channel_id=1, source_target_pairs={{0,16},{1,17},{2,18},{3,19},{4,20},{5,21},{6,22},{7,23},{8,24},{9,... | collective-permute-start | bytes 12296 | tf_op jit(solution)/shard_map/ppermute | solution.py:20
  169.3 12.6 %collective-permute-start.9 = (f32[2,512]{0,1:T(8,128)S(1)}, f32[2,512]{0,1:T(8,128)}, u32[]{:S(2)}, u32[]{:S(2)}) collective-permute-start(f32[2,512]{0,1:T(8,128)S(1)} %add_add_fusion.1), channel_id=1, source_target_pairs={{0,24},{1,25},{2,26},{3,27},{4,28},{5,29},{6,30},{7,31},{8,16},{9,... | collective-permute-start | bytes 12296 | tf_op jit(solution)/shard_map/ppermute | solution.py:20
  170.4 11.5 %collective-permute-start.7 = (f32[2,512]{0,1:T(8,128)S(1)}, f32[2,512]{0,1:T(8,128)}, u32[]{:S(2)}, u32[]{:S(2)}) collective-permute-start(f32[2,512]{0,1:T(8,128)S(1)} %add_add_fusion.1), channel_id=1, source_target_pairs={{0,8},{1,9},{2,10},{3,11},{4,12},{5,13},{6,14},{7,15},{8,0},{9,1},... | collective-permute-start | bytes 12296 | tf_op jit(solution)/shard_map/ppermute | solution.py:20
  184.3 6.6 %collective-permute-start.10 = (f32[]{:T(128)}, f32[]{:T(128)}, u32[]{:S(2)}, u32[]{:S(2)}) collective-permute-start(f32[]{:T(128)} %get-tuple-element.44), channel_id=1, source_target_pairs={{0,32},{32,0},{64,96},{96,64},{128,160},{160,128},{192,224},{224,1... | collective-permute-start | bytes 20 | tf_op jit(solution)/shard_map/ppermute | solution.py:20
  185.3 9.5 %collective-permute-start.11 = (f32[]{:T(128)}, f32[]{:T(128)}, u32[]{:S(2)}, u32[]{:S(2)}) collective-permute-start(f32[]{:T(128)} %get-tuple-element.44), channel_id=1, source_target_pairs={{0,64},{32,96},{64,0},{96,32},{128,192},{160,224},{192,128},{224,1... | collective-permute-start | bytes 20 | tf_op jit(solution)/shard_map/ppermute | solution.py:20
  186.5 8.7 %collective-permute-start.12 = (f32[]{:T(128)}, f32[]{:T(128)}, u32[]{:S(2)}, u32[]{:S(2)}) collective-permute-start(f32[]{:T(128)} %get-tuple-element.44), channel_id=1, source_target_pairs={{0,96},{32,64},{64,32},{96,0},{128,224},{160,192},{192,160},{224,1... | collective-permute-start | bytes 20 | tf_op jit(solution)/shard_map/ppermute | solution.py:20
  186.9 9.6 %collective-permute-start.13 = (f32[]{:T(128)}, f32[]{:T(128)}, u32[]{:S(2)}, u32[]{:S(2)}) collective-permute-start(f32[]{:T(128)} %get-tuple-element.44), channel_id=1, source_target_pairs={{0,128},{32,160},{64,192},{96,224},{128,0},{160,32},{192,64},{224,... | collective-permute-start | bytes 20 | tf_op jit(solution)/shard_map/ppermute | solution.py:20
  189.6 6.8 %collective-permute-start.14 = (f32[]{:T(128)}, f32[]{:T(128)}, u32[]{:S(2)}, u32[]{:S(2)}) collective-permute-start(f32[]{:T(128)} %get-tuple-element.44), channel_id=1, source_target_pairs={{0,160},{32,128},{64,224},{96,192},{128,32},{160,0},{192,96},{224,... | collective-permute-start | bytes 20 | tf_op jit(solution)/shard_map/ppermute | solution.py:20
  191.0 6.8 %collective-permute-start.15 = (f32[]{:T(128)}, f32[]{:T(128)}, u32[]{:S(2)}, u32[]{:S(2)}) collective-permute-start(f32[]{:T(128)} %get-tuple-element.44), channel_id=1, source_target_pairs={{0,192},{32,224},{64,128},{96,160},{128,64},{160,96},{192,0},{224,... | collective-permute-start | bytes 20 | tf_op jit(solution)/shard_map/ppermute | solution.py:20
  194.7 4.3 %collective-permute-start.16 = (f32[]{:T(128)}, f32[]{:T(128)}, u32[]{:S(2)}, u32[]{:S(2)}) collective-permute-start(f32[]{:T(128)} %get-tuple-element.44), channel_id=1, source_target_pairs={{0,224},{32,192},{64,160},{96,128},{128,96},{160,64},{192,32},{224... | collective-permute-start | bytes 20 | tf_op jit(solution)/shard_map/ppermute | solution.py:20

commit v7 on v4

--- a/solution.py
+++ b/solution.py
@@ -192,9 +192,10 @@
     logits = part
     target = (total_counts + 0.5) / (lengths[0].astype(jnp.float32)[:, None] + 1.0)
     rec_loss = jnp.mean(jax.nn.softplus(logits) - target * logits, axis=1)
-    mean_loss = group_sum(jnp.sum(rec_loss), "dp", 1, lax.axis_size("dp")) / (
-        lax.axis_size("dp") * record_count
-    )
+    loss_sum = jnp.sum(rec_loss)
+    for bit in butterfly_bits("dp"):
+        loss_sum = loss_sum + swapped(loss_sum, "dp", bit)
+    mean_loss = loss_sum / (lax.axis_size("dp") * record_count)
     return (out_rows[None], logits[None], rec_loss[None], mean_loss)
 
 

time: 147 us -> 145 us (0.986)
  between operations: 7.85 us -> 5.59 us
  starting transfers between devices: 52.2 us -> 50 us
  waiting for transfers between devices: 33.4 us -> 35.4 us
    ppermute x17 -> x13, starting transfers between devices: 31.6 us -> 29.4 us  [swapped(): return lax.ppermute(x, axis, [(i, i ^ bit) for i in range(count)])]
    ppermute x17 -> x13, waiting for transfers between devices: 3.61 us -> 5.63 us  [swapped(): return lax.ppermute(x, axis, [(i, i ^ bit) for i in range(count)])]
  transfers between devices with their start and end apart: 19 -> 15, of which waited for: 5 -> 8; matrix products, arithmetic and copies ran while one was open for 3% -> 3% of each run, Pallas kernels for 0% -> 0%
where the time goes in v7:
time: 145 us; the launch traced here: 144 us
  starting transfers between devices  50 us (34%)
  waiting for transfers between devices  35.4 us (24%)
  matrix products  19.5 us (13%)
  other arithmetic  17.1 us (12%)
  local copies, waits for them, and re-layouts  16.3 us (11%)
  between operations  5.59 us (4%)
    ppermute x13, starting transfers between devices, swapped(): return lax.ppermute(x, axis, [(i, i ^ bit) for i in range(count)])  29.4 us
    all_to_all x1, waiting for transfers between devices, exclusive_state_scan(): got = lax.all_to_all(jnp.concatenate([slices, extra], axis=1), axis, 0, 0)  16.4 us
    all_to_all x1, waiting for transfers between devices, exclusive_state_scan(): back = lax.all_to_all(sent_back, axis, 0, 0)  13.4 us
    all_to_all x1, starting transfers between devices, exclusive_state_scan(): got = lax.all_to_all(jnp.concatenate([slices, extra], axis=1), axis, 0, 0)  12 us
    all_to_all x1, starting transfers between devices, exclusive_state_scan(): back = lax.all_to_all(sent_back, axis, 0, 0)  8.57 us
    unnamed x31, local copies, waits for them, and re-layouts  8.21 us
    ppermute x13, waiting for transfers between devices, swapped(): return lax.ppermute(x, axis, [(i, i ^ bit) for i in range(count)])  5.63 us
    dot_general x1, matrix products, local(): jnp.einsum('lhd,thd->hlt', lw3, y3, preferred_element_type=jnp.float32)  3.2 us
  transfers between devices with their start and end apart: 15, of which 8 were waited for; matrix products, arithmetic and copies ran while one was open for 3% of the time, Pallas kernels for 0%

profile of v7, /device:TPU:1, one launch (start us, length us, event | category | flops | bytes accessed | tf_op | source)
XLA Modules:
  0.0 143.8 jit_solution(9701745019217523121)
XLA Ops:
  0.7 1.0 reduce-window.10
  3.0 1.1 copy.120
  4.1 1.9 %convolution_multiply_fusion = f32[8,512,256]{2,1,0:T(8,128)S(1)} fusion(bf16[256,8,128]{2,1,0:T(8,128)(2,1)S(1)} %bitcast.140, bf16[512,1024]{1,0:T(8,128)(2,1)} %param.18), kind=kOutput, calls=%fused_computation.7 | convolution fusion | flops 269484032 | bytes 5767168 | tf_op jit(solution)/shard_map/lhd,thd->hlt/dot_general | solution.py:139
  6.1 1.2 select_reduce_fusion.3
  7.3 1.5 %select_reduce_fusion.2 = f32[8,512,256]{2,1,0:T(8,128)S(1)} fusion(f32[8,2,512]{2,1,0:T(2,128)S(1)} %select_reduce_fusion.3, pred[2,256]{1,0:T(4,128)(4,1)S(1)} %iota_compare_fusion.6), kind=kLoop, calls=%fused_computation.3 | loop fusion | flops 3145728 | bytes 4227584 | tf_op jit(solution)/shard_map/reduce_sum | solution.py:143
  8.8 1.2 subtract_exponential_fusion
  10.1 1.9 %copy-done.1 = f32[8,512,256]{2,1,0:T(8,128)} copy-done((f32[8,512,256]{2,1,0:T(8,128)}, f32[8,512,256]{2,1,0:T(8,128)S(1)}, u32[]{:S(2)}) %copy-start.1) | copy-done | bytes 4194328
  12.0 1.2 select_reduce_fusion.1
  18.3 0.7 gather_fusion
  19.3 1.5 %convolution_convert_fusion = bf16[256,1024]{1,0:T(8,128)(2,1)} fusion(bf16[1024,1024]{1,0:T(8,128)(2,1)S(1)} %copy-done, bf16[1,256,1024]{2,1,0:T(8,128)(2,1)S(1)} %copy-done.6), kind=kOutput, calls=%fused_computation.13 | convolution fusion | flops 537133056 | bytes 3145728 | tf_op jit(solution)/shard_map/dot_general | solution.py:114
  20.8 1.2 copy.114
  22.1 2.6 %fusion.3 = bf16[32,8,8,128]{3,2,1,0:T(8,128)(2,1)S(1)} fusion(bf16[1024,1024]{1,0:T(8,128)(2,1)} %param.16, bf16[1,256,1024]{2,1,0:T(8,128)(2,1)} %param.10), kind=kOutput, calls=%fused_computation.16 | convolution fusion | flops 537133056 | bytes 3145728 | tf_op jit(solution)/shard_map/dot_general | solution.py:115
  25.1 0.9 pad_maximum_fusion
  25.9 12.0 %all-to-all-start = ((f32[32,40,128]{2,1,0:T(8,128)}), f32[32,40,128]{2,1,0:T(8,128)S(1)}, u32[]{:S(2)}, u32[]{:S(2)}) async-start(f32[32,40,128]{2,1,0:T(8,128)} %pad_maximum_fusion), calls=%async_computation | async-start | bytes 1310720 | tf_op jit(solution)/shard_map/all_to_all | solution.py:62
  38.0 16.4 %all-to-all-done = f32[32,40,128]{2,1,0:T(8,128)S(1)} async-done(((f32[32,40,128]{2,1,0:T(8,128)}), f32[32,40,128]{2,1,0:T(8,128)S(1)}, u32[]{:S(2)}, u32[]{:S(2)}) %all-to-all-start) | async-done | bytes 655392 | tf_op jit(solution)/shard_map/all_to_all | solution.py:62
  56.8 0.9 fusion.17
  57.7 1.2 copy.100
  59.0 8.6 %all-to-all-start.1 = ((f32[32,40,128]{2,1,0:T(8,128)}), f32[32,40,128]{2,1,0:T(8,128)S(1)}, u32[]{:S(2)}, u32[]{:S(2)}) async-start(f32[32,40,128]{2,1,0:T(8,128)} %copy.100), calls=%async_computation.1 | async-start | bytes 1310720 | tf_op jit(solution)/shard_map/all_to_all | solution.py:83
  67.7 3.1 %fusion.4 = bf16[32,8,8,128]{3,2,1,0:T(8,128)(2,1)} fusion(bf16[1024,1024]{1,0:T(8,128)(2,1)} %param.14, bf16[1,256,1024]{2,1,0:T(8,128)(2,1)S(1)} %copy-done.7), kind=kOutput, calls=%fused_computation.17 | convolution fusion | flops 537133056 | bytes 3145728 | tf_op jit(solution)/shard_map/dot_general | solution.py:113
  70.8 13.4 %all-to-all-done.1 = f32[32,40,128]{2,1,0:T(8,128)S(1)} async-done(((f32[32,40,128]{2,1,0:T(8,128)}), f32[32,40,128]{2,1,0:T(8,128)S(1)}, u32[]{:S(2)}, u32[]{:S(2)}) %all-to-all-start.1) | async-done | bytes 655392 | tf_op jit(solution)/shard_map/all_to_all | solution.py:83
  84.2 0.8 copy-done.3
  85.0 2.9 %convolution_multiply_fusion.1 = f32[8,128,256]{2,1,0:T(8,128)} fusion(f32[8,128,128]{2,1,0:T(8,128)S(1)} %bitcast.139, f32[256,8]{0,1:T(8,128)S(1)} %get-tuple-element.26, bf16[32,8,8,128]{3,2,1,0:T(8,128)(2,1)} %fusion.4), kind=kOutput, calls=%fused_computation.12 | convolution fusion | flops 202113024 | bytes 2105344 | tf_op jit(solution)/shard_map/thd,hde->the/dot_general | solution.py:169
  88.0 2.7 %fusion.56 = (f32[256,8]{0,1:T(8,128)S(1)}, f32[256,8,128]{0,2,1:T(8,128)S(1)}) fusion(f32[8,128,256]{2,1,0:T(8,128)} %convolution_multiply_fusion.1, bf16[256,8,128]{0,2,1:T(8,128)(2,1)} %bitcast.136, f32[8,256]{1,0:T(8,128)S(1)} %get-tuple-element.27, pred[256,256]{1,0:T(8,128)(4,1)S(1)} %fusion.39, bf16[32,8,8,128]{3,2,1,0:T(8,128)(2,1)} %fusion.4, ...), kind=kOutput, calls=%fused_computation.120 | convolution fusion | flops 272103424 | bytes 3751936 | tf_op jit(solution)/shard_map/hts,shd->thd/dot_general | solution.py:133
  90.8 0.8 copy-done.2
  91.7 1.4 multiply_convert_fusion
  93.1 3.2 %bitcast_multiply_fusion = f32[8,512,256]{2,1,0:T(8,128)S(1)} fusion(f32[8,512,256]{2,1,0:T(8,128)} %copy-done.1, bf16[256,8,128]{0,2,1:T(8,128)(2,1)S(1)} %multiply_convert_fusion, bf16[512,1024]{1,0:T(8,128)(2,1)} %param.19), kind=kOutput, calls=%fused_computation.5 | convolution fusion | flops 269484032 | bytes 9961472 | tf_op jit(solution)/shard_map/lhd,thd->hlt/dot_general | solution.py:181
  96.3 1.2 select_reduce_fusion
  98.1 1.1 fusion.55
  99.2 1.2 copy.112
  100.5 1.2 copy.113
  101.7 2.8 %collective-permute-start = (f32[2,512]{1,0:T(2,128)S(1)}, f32[2,512]{1,0:T(2,128)S(1)}, u32[]{:S(2)}, u32[]{:S(2)}) collective-permute-start(f32[2,512]{1,0:T(2,128)S(1)} %fusion.42), channel_id=1, source_target_pairs={{0,1},{1,0},{2,3},{3,2},{4,5},{5,4},{6,7},{7,6},{8,9},{9,8},{10,11... | collective-permute-start | bytes 12296 | tf_op jit(solution)/shard_map/ppermute | solution.py:17
  104.5 0.9 collective-permute-start.1
  105.4 1.3 collective-permute-start.2
  106.7 2.6 %collective-permute-start.3 = (f32[2,512]{1,0:T(2,128)S(1)}, f32[2,512]{1,0:T(2,128)S(1)}, u32[]{:S(2)}, u32[]{:S(2)}) collective-permute-start(f32[2,512]{1,0:T(2,128)S(1)} %fusion.42), channel_id=1, source_target_pairs={{0,4},{1,5},{2,6},{3,7},{4,0},{5,1},{6,2},{7,3},{8,12},{9,13},{10,... | collective-permute-start | bytes 12296 | tf_op jit(solution)/shard_map/ppermute | solution.py:17
  109.3 2.0 %collective-permute-start.4 = (f32[2,512]{1,0:T(2,128)S(1)}, f32[2,512]{1,0:T(2,128)S(1)}, u32[]{:S(2)}, u32[]{:S(2)}) collective-permute-start(f32[2,512]{1,0:T(2,128)S(1)} %fusion.42), channel_id=1, source_target_pairs={{0,5},{1,4},{2,7},{3,6},{4,1},{5,0},{6,3},{7,2},{8,13},{9,12},{10,... | collective-permute-start | bytes 12296 | tf_op jit(solution)/shard_map/ppermute | solution.py:17
  111.4 1.3 collective-permute-start.5
  112.7 2.0 %collective-permute-start.6 = (f32[2,512]{1,0:T(2,128)S(1)}, f32[2,512]{1,0:T(2,128)S(1)}, u32[]{:S(2)}, u32[]{:S(2)}) collective-permute-start(f32[2,512]{1,0:T(2,128)S(1)} %fusion.42), channel_id=1, source_target_pairs={{0,7},{1,6},{2,5},{3,4},{4,3},{5,2},{6,1},{7,0},{8,15},{9,14},{10,... | collective-permute-start | bytes 12296 | tf_op jit(solution)/shard_map/ppermute | solution.py:17
  114.8 1.1 collective-permute-done.5
  116.4 1.3 collective-permute-start.7
  117.7 2.3 %collective-permute-start.8 = (f32[2,512]{1,0:T(2,128)S(1)}, f32[2,512]{1,0:T(2,128)S(1)}, u32[]{:S(2)}, u32[]{:S(2)}) collective-permute-start(f32[2,512]{1,0:T(2,128)S(1)} %add_add_fusion.1), channel_id=1, source_target_pairs={{0,16},{1,17},{2,18},{3,19},{4,20},{5,21},{6,22},{7,23},{8,24},{9,... | collective-permute-start | bytes 12296 | tf_op jit(solution)/shard_map/ppermute | solution.py:17
  120.7 1.0 copy.108
  121.7 2.0 %collective-permute-done.9 = f32[2,512]{1,0:T(2,128)S(1)} collective-permute-done((f32[2,512]{1,0:T(2,128)S(1)}, f32[2,512]{1,0:T(2,128)S(1)}, u32[]{:S(2)}, u32[]{:S(2)}) %collective-permute-start.9) | collective-permute-done | bytes 4128 | tf_op jit(solution)/shard_map/ppermute | solution.py:17
  123.7 0.7 fusion.47
  124.4 1.1 multiply_reduce_fusion.1
  125.5 6.8 %collective-permute-start.10 = (f32[]{:T(128)}, f32[]{:T(128)}, u32[]{:S(2)}, u32[]{:S(2)}) collective-permute-start(f32[]{:T(128)} %get-tuple-element.32), channel_id=1, source_target_pairs={{0,32},{32,0},{64,96},{96,64},{128,160},{160,128},{192,224},{224,1... | collective-permute-start | bytes 20 | tf_op jit(solution)/shard_map/ppermute | solution.py:17
  132.4 1.0 collective-permute-done.10
  134.7 2.0 %collective-permute-start.11 = (f32[]{:T(128)}, f32[]{:T(128)}, u32[]{:S(2)}, u32[]{:S(2)}) collective-permute-start(f32[]{:T(128)} %add.151), channel_id=1, source_target_pairs={{0,64},{32,96},{64,0},{96,32},{128,192},{160,224},{192,128},{224,1... | collective-permute-start | bytes 20 | tf_op jit(solution)/shard_map/ppermute | solution.py:17
  137.9 3.6 %collective-permute-start.12 = (f32[]{:T(128)}, f32[]{:T(128)}, u32[]{:S(2)}, u32[]{:S(2)}) collective-permute-start(f32[]{:T(128)} %add.152), channel_id=1, source_target_pairs={{0,128},{32,160},{64,192},{96,224},{128,0},{160,32},{192,64},{224,... | collective-permute-start | bytes 20 | tf_op jit(solution)/shard_map/ppermute | solution.py:17
  (92 shorter events, 12.0 us)
Async XLA Ops:
  0.6 18.7 %copy-start = (bf16[1024,1024]{1,0:T(8,128)(2,1)S(1)}, bf16[1024,1024]{1,0:T(8,128)(2,1)}, u32[]{:S(2)}) copy-start(bf16[1024,1024]{1,0:T(8,128)(2,1)} %param.15) | copy-start | bytes 6291460
  10.0 1.9 %copy-start.1 = (f32[8,512,256]{2,1,0:T(8,128)}, f32[8,512,256]{2,1,0:T(8,128)S(1)}, u32[]{:S(2)}) copy-start(f32[8,512,256]{2,1,0:T(8,128)S(1)} %subtract_exponential_fusion) | copy-start | bytes 12582916
  12.0 1.2 copy-start.11
  12.0 2.0 %copy-start.10 = (s32[1,2]{1,0:T(1,128)S(1)}, s32[1,2]{1,0:T(1,128)}, u32[]{:S(2)}) copy-start(s32[1,2]{1,0:T(1,128)} %param.12) | copy-start | bytes 28
  12.0 3.3 %copy-start.8 = (f32[1,8,256]{2,1,0:T(8,128)S(1)}, f32[1,8,256]{2,1,0:T(8,128)}, u32[]{:S(2)}) copy-start(f32[1,8,256]{2,1,0:T(8,128)} %param.11) | copy-start | bytes 24580
  12.0 7.3 %copy-start.6 = (bf16[1,256,1024]{2,1,0:T(8,128)(2,1)S(1)}, bf16[1,256,1024]{2,1,0:T(8,128)(2,1)}, u32[]{:S(2)}) copy-start(bf16[1,256,1024]{2,1,0:T(8,128)(2,1)} %param.10) | copy-start | bytes 1572868
  22.1 32.5 %copy-start.4 = (bf16[256,1024]{0,1:T(8,128)(2,1)}, bf16[256,1024]{0,1:T(8,128)(2,1)S(1)}, u32[]{:S(2)}) copy-start(bf16[256,1024]{0,1:T(8,128)(2,1)S(1)} %copy.114) | copy-start | bytes 1572868
  24.7 1.2 copy-start.5
  25.9 28.4 %all-to-all-start = ((f32[32,40,128]{2,1,0:T(8,128)}), f32[32,40,128]{2,1,0:T(8,128)S(1)}, u32[]{:S(2)}, u32[]{:S(2)}) async-start(f32[32,40,128]{2,1,0:T(8,128)} %pad_maximum_fusion), calls=%async_computation | async-start | bytes 1310720 | tf_op jit(solution)/shard_map/all_to_all | solution.py:62
  56.8 10.9 %copy-start.7 = (bf16[1,256,1024]{2,1,0:T(8,128)(2,1)S(1)}, bf16[1,256,1024]{2,1,0:T(8,128)(2,1)}, u32[]{:S(2)}) copy-start(bf16[1,256,1024]{2,1,0:T(8,128)(2,1)} %param.10) | copy-start | bytes 1572868
  59.0 25.2 %all-to-all-start.1 = ((f32[32,40,128]{2,1,0:T(8,128)}), f32[32,40,128]{2,1,0:T(8,128)S(1)}, u32[]{:S(2)}, u32[]{:S(2)}) async-start(f32[32,40,128]{2,1,0:T(8,128)} %copy.100), calls=%async_computation.1 | async-start | bytes 1310720 | tf_op jit(solution)/shard_map/all_to_all | solution.py:83
  84.2 0.9 copy-start.3
  85.0 6.6 %copy-start.9 = (f32[1024]{0:T(1024)S(1)}, f32[1024]{0:T(1024)}, u32[]{:S(2)}) copy-start(f32[1024]{0:T(1024)} %param.17) | copy-start | bytes 12292
  90.7 1.0 copy-start.2
  96.3 1.2 slice-start
  101.7 9.6 %collective-permute-start = (f32[2,512]{1,0:T(2,128)S(1)}, f32[2,512]{1,0:T(2,128)S(1)}, u32[]{:S(2)}, u32[]{:S(2)}) collective-permute-start(f32[2,512]{1,0:T(2,128)S(1)} %fusion.42), channel_id=1, source_target_pairs={{0,1},{1,0},{2,3},{3,2},{4,5},{5,4},{6,7},{7,6},{8,9},{9,8},{10,11... | collective-permute-start | bytes 12296 | tf_op jit(solution)/shard_map/ppermute | solution.py:17
  104.5 8.2 %collective-permute-start.1 = (f32[2,512]{1,0:T(2,128)S(1)}, f32[2,512]{1,0:T(2,128)S(1)}, u32[]{:S(2)}, u32[]{:S(2)}) collective-permute-start(f32[2,512]{1,0:T(2,128)S(1)} %fusion.42), channel_id=1, source_target_pairs={{0,2},{1,3},{2,0},{3,1},{4,6},{5,7},{6,4},{7,5},{8,10},{9,11},{10,... | collective-permute-start | bytes 12296 | tf_op jit(solution)/shard_map/ppermute | solution.py:17
  105.4 9.4 %collective-permute-start.2 = (f32[2,512]{1,0:T(2,128)S(1)}, f32[2,512]{1,0:T(2,128)S(1)}, u32[]{:S(2)}, u32[]{:S(2)}) collective-permute-start(f32[2,512]{1,0:T(2,128)S(1)} %fusion.42), channel_id=1, source_target_pairs={{0,3},{1,2},{2,1},{3,0},{4,7},{5,6},{6,5},{7,4},{8,11},{9,10},{10,... | collective-permute-start | bytes 12296 | tf_op jit(solution)/shard_map/ppermute | solution.py:17
  106.7 8.1 %collective-permute-start.3 = (f32[2,512]{1,0:T(2,128)S(1)}, f32[2,512]{1,0:T(2,128)S(1)}, u32[]{:S(2)}, u32[]{:S(2)}) collective-permute-start(f32[2,512]{1,0:T(2,128)S(1)} %fusion.42), channel_id=1, source_target_pairs={{0,4},{1,5},{2,6},{3,7},{4,0},{5,1},{6,2},{7,3},{8,12},{9,13},{10,... | collective-permute-start | bytes 12296 | tf_op jit(solution)/shard_map/ppermute | solution.py:17
  109.3 5.5 %collective-permute-start.4 = (f32[2,512]{1,0:T(2,128)S(1)}, f32[2,512]{1,0:T(2,128)S(1)}, u32[]{:S(2)}, u32[]{:S(2)}) collective-permute-start(f32[2,512]{1,0:T(2,128)S(1)} %fusion.42), channel_id=1, source_target_pairs={{0,5},{1,4},{2,7},{3,6},{4,1},{5,0},{6,3},{7,2},{8,13},{9,12},{10,... | collective-permute-start | bytes 12296 | tf_op jit(solution)/shard_map/ppermute | solution.py:17
  111.4 4.6 %collective-permute-start.5 = (f32[2,512]{1,0:T(2,128)S(1)}, f32[2,512]{1,0:T(2,128)S(1)}, u32[]{:S(2)}, u32[]{:S(2)}) collective-permute-start(f32[2,512]{1,0:T(2,128)S(1)} %fusion.42), channel_id=1, source_target_pairs={{0,6},{1,7},{2,4},{3,5},{4,2},{5,3},{6,0},{7,1},{8,14},{9,15},{10,... | collective-permute-start | bytes 12296 | tf_op jit(solution)/shard_map/ppermute | solution.py:17
  112.7 3.7 %collective-permute-start.6 = (f32[2,512]{1,0:T(2,128)S(1)}, f32[2,512]{1,0:T(2,128)S(1)}, u32[]{:S(2)}, u32[]{:S(2)}) collective-permute-start(f32[2,512]{1,0:T(2,128)S(1)} %fusion.42), channel_id=1, source_target_pairs={{0,7},{1,6},{2,5},{3,4},{4,3},{5,2},{6,1},{7,0},{8,15},{9,14},{10,... | collective-permute-start | bytes 12296 | tf_op jit(solution)/shard_map/ppermute | solution.py:17
  116.4 5.3 %collective-permute-start.7 = (f32[2,512]{1,0:T(2,128)S(1)}, f32[2,512]{1,0:T(2,128)S(1)}, u32[]{:S(2)}, u32[]{:S(2)}) collective-permute-start(f32[2,512]{1,0:T(2,128)S(1)} %add_add_fusion.1), channel_id=1, source_target_pairs={{0,8},{1,9},{2,10},{3,11},{4,12},{5,13},{6,14},{7,15},{8,0},{9,1},... | collective-permute-start | bytes 12296 | tf_op jit(solution)/shard_map/ppermute | solution.py:17
  117.7 4.0 %collective-permute-start.8 = (f32[2,512]{1,0:T(2,128)S(1)}, f32[2,512]{1,0:T(2,128)S(1)}, u32[]{:S(2)}, u32[]{:S(2)}) collective-permute-start(f32[2,512]{1,0:T(2,128)S(1)} %add_add_fusion.1), channel_id=1, source_target_pairs={{0,16},{1,17},{2,18},{3,19},{4,20},{5,21},{6,22},{7,23},{8,24},{9,... | collective-permute-start | bytes 12296 | tf_op jit(solution)/shard_map/ppermute | solution.py:17
  120.0 3.7 %collective-permute-start.9 = (f32[2,512]{1,0:T(2,128)S(1)}, f32[2,512]{1,0:T(2,128)S(1)}, u32[]{:S(2)}, u32[]{:S(2)}) collective-permute-start(f32[2,512]{1,0:T(2,128)S(1)} %add_add_fusion.1), channel_id=1, source_target_pairs={{0,24},{1,25},{2,26},{3,27},{4,28},{5,29},{6,30},{7,31},{8,16},{9,... | collective-permute-start | bytes 12296 | tf_op jit(solution)/shard_map/ppermute | solution.py:17
  125.5 7.8 %collective-permute-start.10 = (f32[]{:T(128)}, f32[]{:T(128)}, u32[]{:S(2)}, u32[]{:S(2)}) collective-permute-start(f32[]{:T(128)} %get-tuple-element.32), channel_id=1, source_target_pairs={{0,32},{32,0},{64,96},{96,64},{128,160},{160,128},{192,224},{224,1... | collective-permute-start | bytes 20 | tf_op jit(solution)/shard_map/ppermute | solution.py:17
  134.7 2.6 %collective-permute-start.11 = (f32[]{:T(128)}, f32[]{:T(128)}, u32[]{:S(2)}, u32[]{:S(2)}) collective-permute-start(f32[]{:T(128)} %add.151), channel_id=1, source_target_pairs={{0,64},{32,96},{64,0},{96,32},{128,192},{160,224},{192,128},{224,1... | collective-permute-start | bytes 20 | tf_op jit(solution)/shard_map/ppermute | solution.py:17
  137.9 4.1 %collective-permute-start.12 = (f32[]{:T(128)}, f32[]{:T(128)}, u32[]{:S(2)}, u32[]{:S(2)}) collective-permute-start(f32[]{:T(128)} %add.152), channel_id=1, source_target_pairs={{0,128},{32,160},{64,192},{96,224},{128,0},{160,32},{192,64},{224,... | collective-permute-start | bytes 20 | tf_op jit(solution)/shard_map/ppermute | solution.py:17

commit v8 on v7

--- a/solution.py
+++ b/solution.py
@@ -1,6 +1,9 @@
+import functools
+
 import jax
 import jax.numpy as jnp
 from jax import lax
+from jax.experimental import pallas as pl
 from jax.sharding import PartitionSpec as P
 
 NEG_FILL = -1e30
@@ -35,12 +38,52 @@
     return bits
 
 
+def pool_stats_kernel(lq_ref, kf_ref, member_ref, weight_ref, stats_ref, *, qk_scale, record_count):
+    score = lax.dot_general(
+        lq_ref[...], kf_ref[...], (((1,), (1,)), ((), ())), preferred_element_type=jnp.float32
+    ) * qk_scale
+    member = member_ref[...]
+    masks = [member[r:r + 1, :] > 0.5 for r in range(record_count)]
+    tops = [jnp.max(jnp.where(m, score, NEG_FILL), axis=1, keepdims=True) for m in masks]
+    top_tok = jnp.zeros_like(score)
+    for m, t in zip(masks, tops):
+        top_tok = top_tok + jnp.where(m, t, 0.0)
+    weight = jnp.exp(score - top_tok)
+    weight_ref[0] = weight
+    masses = [jnp.sum(jnp.where(m, weight, 0.0), axis=1, keepdims=True) for m in masks]
+    stats_ref[0] = jnp.concatenate(tops + masses, axis=1)
+
+
+def pool_stats_call(label_query, features, member_rows, head_count, qk_scale):
+    label_count, model_width = label_query.shape
+    tok_rows = features.shape[0]
+    head_dim = model_width // head_count
+    record_count = member_rows.shape[0]
+    return pl.pallas_call(
+        functools.partial(pool_stats_kernel, qk_scale=qk_scale, record_count=record_count),
+        grid=(head_count,),
+        in_specs=[
+            pl.BlockSpec((label_count, head_dim), lambda h: (0, h)),
+            pl.BlockSpec((tok_rows, head_dim), lambda h: (0, h)),
+            pl.BlockSpec((record_count, tok_rows), lambda h: (0, 0)),
+        ],
+        out_specs=[
+            pl.BlockSpec((1, label_count, tok_rows), lambda h: (h, 0, 0)),
+            pl.BlockSpec((1, label_count, 2 * record_count), lambda h: (h, 0, 0)),
+        ],
+        out_shape=[
+            jax.ShapeDtypeStruct((head_count, label_count, tok_rows), jnp.float32),
+            jax.ShapeDtypeStruct((head_count, label_count, 2 * record_count), jnp.float32),
+        ],
+    )(label_query, features, member_rows)
+
+
 def record_ids(length_row, positions):
     starts = jnp.cumsum(length_row) - length_row
     return jnp.sum((starts[:, None] <= positions[None, :]).astype(jnp.int32), axis=0) - 1
 
 
-def exclusive_state_scan(local_state, carry, stats, axis):
+def exclusive_state_scan(local_state, carry, stats, passenger, axis):
     head_count, head_dim, _ = local_state.shape
     count = lax.axis_size(axis)
     rows = head_count * head_dim // count
@@ -60,6 +103,7 @@
         axis=1,
     ).reshape(count, 8, head_dim)
     got = lax.all_to_all(jnp.concatenate([slices, extra], axis=1), axis, 0, 0)
+    got, passenger = lax.optimization_barrier((got, passenger))
     got_extra = got[:, rows:, :].reshape(count, 8 * head_dim)
     factors = got_extra[:, per_owner * fields]
     part = got_extra[:, : per_owner * fields].reshape(count, per_owner, fields)
@@ -83,7 +127,7 @@
     back = lax.all_to_all(sent_back, axis, 0, 0)
     state = back[:, :rows, :].reshape(head_count, head_dim, head_dim)
     totals = back[:, rows:, :].reshape(count, 8 * head_dim)[:, : per_owner * fields]
-    return state, totals.reshape(pair_count, fields)
+    return state, totals.reshape(pair_count, fields), passenger
 
 
 def local(
@@ -136,15 +180,11 @@
     kf3 = features.reshape(tok_rows, head_count, head_dim)
     lq3 = label_query.reshape(label_count, head_count, head_dim)
     lw3 = label_weight.reshape(label_count, head_count, head_dim)
-    pscore = jnp.einsum("lhd,thd->hlt", lq3, kf3, preferred_element_type=jnp.float32) * qk_scale
-    maxima = jnp.max(
-        jnp.where(member[None, :, None, :], pscore[:, None, :, :], NEG_FILL), axis=3
-    )
-    maxima_tok = jnp.sum(
-        jnp.where(member[None, :, None, :], maxima[:, :, :, None], 0.0), axis=1
-    )
-    pool_weight = jnp.exp(pscore - maxima_tok)
-    mass = jnp.sum(jnp.where(member[None, :, None, :], pool_weight[:, None], 0.0), axis=3)
+    pool_weight, head_stats = pool_stats_call(
+        label_query, features, member.astype(jnp.float32), head_count, qk_scale
+    )
+    maxima = jnp.transpose(head_stats[:, :, :record_count], (0, 2, 1))
+    mass = jnp.transpose(head_stats[:, :, record_count:], (0, 2, 1))
     label_hot = (label_ids[0][:, None] == jnp.arange(label_count, dtype=jnp.int32)[None, :]).astype(
         jnp.bfloat16
     )
@@ -158,7 +198,7 @@
         ],
         axis=2,
     ).reshape(record_count * label_count, 2 * head_count + 1)
-    incoming, totals = exclusive_state_scan(local_state, carry, stats, "ctx")
+    incoming, totals, intra = exclusive_state_scan(local_state, carry, stats, intra, "ctx")
     totals = totals.reshape(record_count, label_count, 2 * head_count + 1)
     top = jnp.transpose(totals[:, :, :head_count], (2, 0, 1))
     total_mass = jnp.transpose(totals[:, :, head_count:2 * head_count], (2, 0, 1))

time: 145 us -> 210 us (1.45)
  blocking collectives: 0 us -> 25 us
  local copies, waits for them, and re-layouts: 16.3 us -> 36.5 us
  waiting for transfers between devices: 35.4 us -> 54.6 us
  starting transfers between devices: 50 us -> 41.3 us
  Pallas kernels: 0 us -> 7.86 us
  other arithmetic: 17.1 us -> 22 us
  matrix products: 19.5 us -> 15.8 us
    ppermute x13, waiting for transfers between devices: 5.63 us -> 44.7 us  [swapped(): return lax.ppermute(x, axis, [(i, i ^ bit) for i in range(count)])]
    all_to_all x0 -> x1, blocking collectives: none -> 25 us  [exclusive_state_scan(): back = lax.all_to_all(sent_back, axis, 0, 0)]
    all_to_all x1 -> x0, waiting for transfers between devices: 13.4 us -> none  [exclusive_state_scan(): back = lax.all_to_all(sent_back, axis, 0, 0)]
    all_to_all x1 -> x0, starting transfers between devices: 8.57 us -> none  [exclusive_state_scan(): back = lax.all_to_all(sent_back, axis, 0, 0)]
    pallas_call x0 -> x1, Pallas kernels: none -> 7.86 us  [pool_stats_call(): pl.pallas_call(functools.partial(pool_stats_kernel, qk_scale=qk_scale, re...]
    all_to_all x1, waiting for transfers between devices: 16.4 us -> 9.88 us  [exclusive_state_scan(): got = lax.all_to_all(jnp.concatenate([slices, extra], axis=1), axis, 0, 0)]
    unnamed x31 -> x26, local copies, waits for them, and re-layouts: 8.21 us -> 13.7 us
    concatenate x1, local copies, waits for them, and re-layouts: 0.22 us -> 5.17 us  [local(): jnp.concatenate([jnp.transpose(maxima, (1, 2, 0)), jnp.transpose(mass, (1...]
  transfers between devices with their start and end apart: 15 -> 14, of which waited for: 8 -> 10; matrix products, arithmetic and copies ran while one was open for 3% -> 6% of each run, Pallas kernels for 0% -> 0%
where the time goes in v8:
time: 210 us; the launch traced here: 209 us
  waiting for transfers between devices  54.6 us (26%)
  starting transfers between devices  41.3 us (20%)
  local copies, waits for them, and re-layouts  36.5 us (17%)
  blocking collectives  25 us (12%)
  other arithmetic  22 us (10%)
  matrix products  15.8 us (8%)
  Pallas kernels  7.86 us (4%)
  between operations  5.55 us (3%)
    ppermute x13, waiting for transfers between devices, swapped(): return lax.ppermute(x, axis, [(i, i ^ bit) for i in range(count)])  44.7 us
    ppermute x13, starting transfers between devices, swapped(): return lax.ppermute(x, axis, [(i, i ^ bit) for i in range(count)])  29.3 us
    all_to_all x1, blocking collectives, exclusive_state_scan(): back = lax.all_to_all(sent_back, axis, 0, 0)  25 us
    unnamed x26, local copies, waits for them, and re-layouts  13.7 us
    all_to_all x1, starting transfers between devices, exclusive_state_scan(): got = lax.all_to_all(jnp.concatenate([slices, extra], axis=1), axis, 0, 0)  12 us
    all_to_all x1, waiting for transfers between devices, exclusive_state_scan(): got = lax.all_to_all(jnp.concatenate([slices, extra], axis=1), axis, 0, 0)  9.88 us
    pallas_call x1, Pallas kernels, pool_stats_call(): pl.pallas_call(functools.partial(pool_stats_kernel, qk_scale=qk_scale, re...  7.86 us
    concatenate x1, local copies, waits for them, and re-layouts, local(): jnp.concatenate([jnp.transpose(maxima, (1, 2, 0)), jnp.transpose(mass, (1...  5.17 us
  transfers between devices with their start and end apart: 14, of which 10 were waited for; matrix products, arithmetic and copies ran while one was open for 6% of the time, Pallas kernels for 0%

profile of v8, /device:TPU:1, one launch (start us, length us, event | category | flops | bytes accessed | tf_op | source)
XLA Modules:
  0.0 208.6 jit_solution(12647604631954308326)
XLA Ops:
  0.7 1.0 reduce-window.10
  3.6 1.3 fusion.37
  5.5 1.3 reduce-window.11
  9.9 7.9 %shard_map.129 = (f32[8,512,256]{2,1,0:T(8,128)}, f32[8,512,4]{2,1,0:T(8,128)}) custom-call(bf16[512,1024]{1,0:T(8,128)(2,1)} %lq_ref.1, bf16[256,1024]{1,0:T(8,128)(2,1)} %bitcast.135, f32[2,256]{1,0:T(2,128)} %get-tuple-element.45.member_ref), custom_call_target="tpu_custom_call" | custom-call | tf_op jit(solution)/shard_map/pallas_call | solution.py:62
  17.8 2.9 %slice_bitcast_fusion.1 = (f32[2,512,8]{0,1,2:T(8,128)S(1)}, f32[2,512,8]{0,1,2:T(8,128)S(1)}) fusion(f32[8,512,4]{2,1,0:T(8,128)} %get-tuple-element.8), kind=kLoop, calls=%fused_computation.9 | loop fusion | bytes 131072 | tf_op jit(solution)/shard_map/transpose;transpose | solution.py:195
  21.1 2.6 %pad_maximum_fusion = f32[2,512,17]{0,1,2:T(8,128)} fusion(f32[2,512,1]{0,1,2:T(8,128)S(1)} %convolution_bitcast_fusion, f32[2,512,8]{0,1,2:T(8,128)S(1)} %get-tuple-element.41, f32[2,512,8]{0,1,2:T(8,128)S(1)} %get-tuple-element.40), kind=kLoop, calls=%fused_computation.2 | loop fusion | flops 34816 | bytes 139264 | tf_op jit(solution)/shard_map/concatenate | solution.py:193
  23.7 5.2 %copy.117 = f32[2,512,17]{2,1,0:T(8,128)S(1)} copy(f32[2,512,17]{0,1,2:T(8,128)} %pad_maximum_fusion) | data formatting | bytes 139264 | tf_op jit(solution)/shard_map/concatenate | solution.py:193
  29.5 1.5 convolution_convert_fusion.2
  31.0 1.2 copy.145
  32.2 3.1 %convolution_convert_fusion.1 = bf16[256,1024]{1,0:T(8,128)(2,1)} fusion(bf16[1024,1024]{1,0:T(8,128)(2,1)} %param.16, bf16[1,256,1024]{2,1,0:T(8,128)(2,1)S(1)} %copy-done.5), kind=kOutput, calls=%fused_computation.16 | convolution fusion | flops 537133056 | bytes 3145728 | tf_op jit(solution)/shard_map/dot_general | solution.py:159
  35.3 1.2 copy.146
  36.9 0.9 pad_maximum_fusion.1
  37.8 12.0 %all-to-all-start = ((f32[32,40,128]{2,1,0:T(8,128)}), f32[32,40,128]{2,1,0:T(8,128)S(1)}, u32[]{:S(2)}, u32[]{:S(2)}) async-start(f32[32,40,128]{2,1,0:T(8,128)} %pad_maximum_fusion.1), calls=%async_computation | async-start | bytes 1310720 | tf_op jit(solution)/shard_map/all_to_all | solution.py:105
  50.0 3.3 %fusion.5 = bf16[32,8,8,128]{3,2,1,0:T(8,128)(2,1)} fusion(bf16[1024,1024]{1,0:T(8,128)(2,1)} %param.14, bf16[1,256,1024]{2,1,0:T(8,128)(2,1)} %param.10), kind=kOutput, calls=%fused_computation.18 | convolution fusion | flops 537133056 | bytes 3145728 | tf_op jit(solution)/shard_map/dot_general | solution.py:157
  53.3 3.1 %fusion.2 = f32[256,8,128]{0,2,1:T(8,128)} fusion(bf16[256,8,128]{0,2,1:T(8,128)(2,1)} %bitcast.129, bf16[256,8,128]{0,2,1:T(8,128)(2,1)S(1)} %bitcast.127, f32[8,256]{1,0:T(8,128)S(1)} %get-tuple-element.39, pred[256,256]{1,0:T(8,128)(4,1)S(1)} %fusion.32, bf16[32,8,8,128]{3,2,1,0:T(8,128)(2,1)} %fusion.5), kind=kOutput, calls=%fused_computation.11 | convolution fusion | flops 271581184 | bytes 2695168 | tf_op jit(solution)/shard_map/hts,shd->thd/dot_general | solution.py:177
  56.4 9.9 %all-to-all-done = f32[32,40,128]{2,1,0:T(8,128)S(1)} async-done(((f32[32,40,128]{2,1,0:T(8,128)}), f32[32,40,128]{2,1,0:T(8,128)S(1)}, u32[]{:S(2)}, u32[]{:S(2)}) %all-to-all-start) | async-done | bytes 655392 | tf_op jit(solution)/shard_map/all_to_all | solution.py:105
  68.6 0.9 fusion.16
  70.0 25.0 %all_to_all.10 = f32[32,40,128]{2,1,0:T(8,128)S(1)} all-to-all(f32[32,40,128]{2,1,0:T(8,128)S(1)} %copy.124), channel_id=1, replica_groups=mesh['dp'=8,'ctx'=32] {'ctx'}, dimensions={0} | all-to-all | bytes 1310720 | tf_op jit(solution)/shard_map/all_to_all | solution.py:127
  95.6 1.1 fusion.47
  96.7 5.4 %copy.143 = f32[2,512,8]{0,1,2:T(8,128)} copy(f32[2,512,8]{2,1,0:T(8,128)} %get-tuple-element.42) | data formatting | bytes 65536
  102.1 5.5 %copy.144 = f32[2,512,8]{0,1,2:T(8,128)} copy(f32[2,512,8]{2,1,0:T(8,128)} %get-tuple-element.43) | data formatting | bytes 65536
  107.6 4.8 %bitcast_divide_fusion = f32[8,2,512]{1,2,0:T(8,128)} fusion(f32[2,512,8]{0,1,2:T(8,128)} %copy.144, f32[2,512,8]{0,1,2:T(8,128)} %copy.143, f32[8,512,4]{2,1,0:T(8,128)} %get-tuple-element.8), kind=kLoop, calls=%fused_computation.4 | loop fusion | flops 16384 | bytes 131072 | tf_op jit(solution)/shard_map/div | solution.py:206
  112.4 2.2 %copy.132 = f32[8,2,512]{2,1,0:T(2,128)S(1)} copy(f32[8,2,512]{1,2,0:T(8,128)} %bitcast_divide_fusion) | data formatting | bytes 65536 | tf_op jit(solution)/shard_map/div | solution.py:206
  114.7 2.5 %fusion.48 = (f32[256,8]{0,1:T(8,128)S(1)}, f32[256,8,128]{0,2,1:T(8,128)S(1)}) fusion(f32[256,8,128]{0,2,1:T(8,128)} %fusion.2, f32[8,128,128]{2,1,0:T(8,128)S(1)} %bitcast.132, f32[256,8]{0,1:T(8,128)S(1)} %get-tuple-element.38, bf16[32,8,8,128]{3,2,1,0:T(8,128)(2,1)} %fusion.5), kind=kOutput, calls=%fused_computation.110 | convolution fusion | flops 202635264 | bytes 3162112 | tf_op jit(solution)/shard_map/thd,hde->the/dot_general | solution.py:209
  117.6 0.9 copy-done.3
  119.2 1.2 select_reduce_fusion
  120.6 2.8 %collective-permute-start = (f32[2,512]{0,1:T(8,128)S(1)}, f32[2,512]{0,1:T(8,128)S(1)}, u32[]{:S(2)}, u32[]{:S(2)}) collective-permute-start(f32[2,512]{0,1:T(8,128)S(1)} %copy.142), channel_id=1, source_target_pairs={{0,1},{1,0},{2,3},{3,2},{4,5},{5,4},{6,7},{7,6},{8,9},{9,8},{10,11... | collective-permute-start | bytes 12296 | tf_op jit(solution)/shard_map/ppermute | solution.py:20
  123.4 0.9 collective-permute-start.1
  124.3 1.3 collective-permute-start.2
  125.6 2.6 %collective-permute-start.3 = (f32[2,512]{0,1:T(8,128)S(1)}, f32[2,512]{0,1:T(8,128)S(1)}, u32[]{:S(2)}, u32[]{:S(2)}) collective-permute-start(f32[2,512]{0,1:T(8,128)S(1)} %copy.142), channel_id=1, source_target_pairs={{0,4},{1,5},{2,6},{3,7},{4,0},{5,1},{6,2},{7,3},{8,12},{9,13},{10,... | collective-permute-start | bytes 12296 | tf_op jit(solution)/shard_map/ppermute | solution.py:20
  128.2 2.0 collective-permute-start.4
  130.2 1.4 collective-permute-start.5
  131.6 5.8 %collective-permute-done.1 = f32[2,512]{0,1:T(8,128)S(1)} collective-permute-done((f32[2,512]{0,1:T(8,128)S(1)}, f32[2,512]{0,1:T(8,128)S(1)}, u32[]{:S(2)}, u32[]{:S(2)}) %collective-permute-start.1) | collective-permute-done | bytes 4128 | tf_op jit(solution)/shard_map/ppermute | solution.py:20
  137.4 20.0 %collective-permute-done.2 = f32[2,512]{0,1:T(8,128)S(1)} collective-permute-done((f32[2,512]{0,1:T(8,128)S(1)}, f32[2,512]{0,1:T(8,128)S(1)}, u32[]{:S(2)}, u32[]{:S(2)}) %collective-permute-start.2) | collective-permute-done | bytes 4128 | tf_op jit(solution)/shard_map/ppermute | solution.py:20
  157.4 9.0 %collective-permute-done.3 = f32[2,512]{0,1:T(8,128)S(1)} collective-permute-done((f32[2,512]{0,1:T(8,128)S(1)}, f32[2,512]{0,1:T(8,128)S(1)}, u32[]{:S(2)}, u32[]{:S(2)}) %collective-permute-start.3) | collective-permute-done | bytes 4128 | tf_op jit(solution)/shard_map/ppermute | solution.py:20
  166.4 1.0 collective-permute-done.4
  168.2 1.5 collective-permute-start.7
  169.7 9.1 %collective-permute-start.8 = (f32[2,512]{0,1:T(8,128)}, f32[2,512]{0,1:T(8,128)}, u32[]{:S(2)}, u32[]{:S(2)}) collective-permute-start(f32[2,512]{0,1:T(8,128)} %add_add_fusion.1), channel_id=1, source_target_pairs={{0,16},{1,17},{2,18},{3,19},{4,20},{5,21},{6,22},{7,23},{8,24},{9,... | collective-permute-start | bytes 12296 | tf_op jit(solution)/shard_map/ppermute | solution.py:20
  178.8 1.0 slice_add_fusion
  179.8 4.1 %copy.141 = f32[2,512,1]{0,1,2:T(8,128)S(1)} copy(f32[2,512,1]{2,1,0:T(8,128)} %slice_add_fusion) | data formatting | bytes 8192 | tf_op jit(solution)/shard_map/add | solution.py:233
  183.9 1.0 copy.135
  184.9 3.4 %collective-permute-done.8 = f32[2,512]{0,1:T(8,128)} collective-permute-done((f32[2,512]{0,1:T(8,128)}, f32[2,512]{0,1:T(8,128)}, u32[]{:S(2)}, u32[]{:S(2)}) %collective-permute-start.8) | collective-permute-done | bytes 4128 | tf_op jit(solution)/shard_map/ppermute | solution.py:20
  188.3 4.1 %collective-permute-done.9 = f32[2,512]{0,1:T(8,128)} collective-permute-done((f32[2,512]{0,1:T(8,128)}, f32[2,512]{0,1:T(8,128)}, u32[]{:S(2)}, u32[]{:S(2)}) %collective-permute-start.9) | collective-permute-done | bytes 4128 | tf_op jit(solution)/shard_map/ppermute | solution.py:20
  192.5 1.3 fusion.29
  193.8 1.1 multiply_reduce_fusion.2
  194.9 2.2 %collective-permute-start.10 = (f32[]{:T(128)}, f32[]{:T(128)}, u32[]{:S(2)}, u32[]{:S(2)}) collective-permute-start(f32[]{:T(128)} %get-tuple-element.48), channel_id=1, source_target_pairs={{0,32},{32,0},{64,96},{96,64},{128,160},{160,128},{192,224},{224,1... | collective-permute-start | bytes 20 | tf_op jit(solution)/shard_map/ppermute | solution.py:20
  199.4 2.0 collective-permute-start.11
  202.7 3.5 %collective-permute-start.12 = (f32[]{:T(128)}, f32[]{:T(128)}, u32[]{:S(2)}, u32[]{:S(2)}) collective-permute-start(f32[]{:T(128)} %add.148), channel_id=1, source_target_pairs={{0,128},{32,160},{64,192},{96,224},{128,0},{160,32},{192,64},{224,... | collective-permute-start | bytes 20 | tf_op jit(solution)/shard_map/ppermute | solution.py:20
  (86 shorter events, 14.1 us)
Async XLA Ops:
  0.6 28.8 %copy-start = (bf16[1024,1024]{1,0:T(8,128)(2,1)S(1)}, bf16[1024,1024]{1,0:T(8,128)(2,1)}, u32[]{:S(2)}) copy-start(bf16[1024,1024]{1,0:T(8,128)(2,1)} %param.15) | copy-start | bytes 6291460
  17.8 2.9 %copy-start.7 = (s32[1,256]{1,0:T(1,128)S(1)}, s32[1,256]{1,0:T(1,128)}, u32[]{:S(2)}) copy-start(s32[1,256]{1,0:T(1,128)} %param.13) | copy-start | bytes 3076
  23.7 5.7 %copy-start.4 = (bf16[1,256,1024]{2,1,0:T(8,128)(2,1)S(1)}, bf16[1,256,1024]{2,1,0:T(8,128)(2,1)}, u32[]{:S(2)}) copy-start(bf16[1,256,1024]{2,1,0:T(8,128)(2,1)} %param.10) | copy-start | bytes 1572868
  29.4 2.8 %copy-start.5 = (bf16[1,256,1024]{2,1,0:T(8,128)(2,1)S(1)}, bf16[1,256,1024]{2,1,0:T(8,128)(2,1)}, u32[]{:S(2)}) copy-start(bf16[1,256,1024]{2,1,0:T(8,128)(2,1)} %param.10) | copy-start | bytes 1572868
  36.6 1.3 copy-start.2
  37.8 28.4 %all-to-all-start = ((f32[32,40,128]{2,1,0:T(8,128)}), f32[32,40,128]{2,1,0:T(8,128)S(1)}, u32[]{:S(2)}, u32[]{:S(2)}) async-start(f32[32,40,128]{2,1,0:T(8,128)} %pad_maximum_fusion.1), calls=%async_computation | async-start | bytes 1310720 | tf_op jit(solution)/shard_map/all_to_all | solution.py:105
  114.7 2.7 %copy-start.6 = (f32[1024]{0:T(1024)S(1)}, f32[1024]{0:T(1024)}, u32[]{:S(2)}) copy-start(f32[1024]{0:T(1024)} %param.17) | copy-start | bytes 12292
  114.7 2.9 %copy-start.1 = (f32[8,512,256]{2,1,0:T(8,128)S(1)}, f32[8,512,256]{2,1,0:T(8,128)}, u32[]{:S(2)}) copy-start(f32[8,512,256]{2,1,0:T(8,128)} %get-tuple-element.11) | copy-start | bytes 12582916
  117.2 1.3 copy-start.3
  119.2 18.2 %copy-start.8 = (s32[1,2]{1,0:T(1,128)S(1)}, s32[1,2]{1,0:T(1,128)}, u32[]{:S(2)}) copy-start(s32[1,2]{1,0:T(1,128)} %param.12) | copy-start | bytes 28
  120.6 9.6 %collective-permute-start = (f32[2,512]{0,1:T(8,128)S(1)}, f32[2,512]{0,1:T(8,128)S(1)}, u32[]{:S(2)}, u32[]{:S(2)}) collective-permute-start(f32[2,512]{0,1:T(8,128)S(1)} %copy.142), channel_id=1, source_target_pairs={{0,1},{1,0},{2,3},{3,2},{4,5},{5,4},{6,7},{7,6},{8,9},{9,8},{10,11... | collective-permute-start | bytes 12296 | tf_op jit(solution)/shard_map/ppermute | solution.py:20
  123.4 14.0 %collective-permute-start.1 = (f32[2,512]{0,1:T(8,128)S(1)}, f32[2,512]{0,1:T(8,128)S(1)}, u32[]{:S(2)}, u32[]{:S(2)}) collective-permute-start(f32[2,512]{0,1:T(8,128)S(1)} %copy.142), channel_id=1, source_target_pairs={{0,2},{1,3},{2,0},{3,1},{4,6},{5,7},{6,4},{7,5},{8,10},{9,11},{10,... | collective-permute-start | bytes 12296 | tf_op jit(solution)/shard_map/ppermute | solution.py:20
  124.3 33.2 %collective-permute-start.2 = (f32[2,512]{0,1:T(8,128)S(1)}, f32[2,512]{0,1:T(8,128)S(1)}, u32[]{:S(2)}, u32[]{:S(2)}) collective-permute-start(f32[2,512]{0,1:T(8,128)S(1)} %copy.142), channel_id=1, source_target_pairs={{0,3},{1,2},{2,1},{3,0},{4,7},{5,6},{6,5},{7,4},{8,11},{9,10},{10,... | collective-permute-start | bytes 12296 | tf_op jit(solution)/shard_map/ppermute | solution.py:20
  125.6 40.8 %collective-permute-start.3 = (f32[2,512]{0,1:T(8,128)S(1)}, f32[2,512]{0,1:T(8,128)S(1)}, u32[]{:S(2)}, u32[]{:S(2)}) collective-permute-start(f32[2,512]{0,1:T(8,128)S(1)} %copy.142), channel_id=1, source_target_pairs={{0,4},{1,5},{2,6},{3,7},{4,0},{5,1},{6,2},{7,3},{8,12},{9,13},{10,... | collective-permute-start | bytes 12296 | tf_op jit(solution)/shard_map/ppermute | solution.py:20
  128.2 39.2 %collective-permute-start.4 = (f32[2,512]{0,1:T(8,128)S(1)}, f32[2,512]{0,1:T(8,128)S(1)}, u32[]{:S(2)}, u32[]{:S(2)}) collective-permute-start(f32[2,512]{0,1:T(8,128)S(1)} %copy.142), channel_id=1, source_target_pairs={{0,5},{1,4},{2,7},{3,6},{4,1},{5,0},{6,3},{7,2},{8,13},{9,12},{10,... | collective-permute-start | bytes 12296 | tf_op jit(solution)/shard_map/ppermute | solution.py:20
  130.2 37.1 %collective-permute-start.5 = (f32[2,512]{0,1:T(8,128)S(1)}, f32[2,512]{0,1:T(8,128)S(1)}, u32[]{:S(2)}, u32[]{:S(2)}) collective-permute-start(f32[2,512]{0,1:T(8,128)S(1)} %copy.142), channel_id=1, source_target_pairs={{0,6},{1,7},{2,4},{3,5},{4,2},{5,3},{6,0},{7,1},{8,14},{9,15},{10,... | collective-permute-start | bytes 12296 | tf_op jit(solution)/shard_map/ppermute | solution.py:20
  137.4 30.0 %collective-permute-start.6 = (f32[2,512]{0,1:T(8,128)S(1)}, f32[2,512]{0,1:T(8,128)S(1)}, u32[]{:S(2)}, u32[]{:S(2)}) collective-permute-start(f32[2,512]{0,1:T(8,128)S(1)} %copy.142), channel_id=1, source_target_pairs={{0,7},{1,6},{2,5},{3,4},{4,3},{5,2},{6,1},{7,0},{8,15},{9,14},{10,... | collective-permute-start | bytes 12296 | tf_op jit(solution)/shard_map/ppermute | solution.py:20
  168.2 16.7 %collective-permute-start.7 = (f32[2,512]{0,1:T(8,128)}, f32[2,512]{0,1:T(8,128)S(1)}, u32[]{:S(2)}, u32[]{:S(2)}) collective-permute-start(f32[2,512]{0,1:T(8,128)} %add_add_fusion.1), channel_id=1, source_target_pairs={{0,8},{1,9},{2,10},{3,11},{4,12},{5,13},{6,14},{7,15},{8,0},{9,1},... | collective-permute-start | bytes 12296 | tf_op jit(solution)/shard_map/ppermute | solution.py:20
  169.7 18.7 %collective-permute-start.8 = (f32[2,512]{0,1:T(8,128)}, f32[2,512]{0,1:T(8,128)}, u32[]{:S(2)}, u32[]{:S(2)}) collective-permute-start(f32[2,512]{0,1:T(8,128)} %add_add_fusion.1), channel_id=1, source_target_pairs={{0,16},{1,17},{2,18},{3,19},{4,20},{5,21},{6,22},{7,23},{8,24},{9,... | collective-permute-start | bytes 12296 | tf_op jit(solution)/shard_map/ppermute | solution.py:20
  178.8 13.7 %collective-permute-start.9 = (f32[2,512]{0,1:T(8,128)}, f32[2,512]{0,1:T(8,128)}, u32[]{:S(2)}, u32[]{:S(2)}) collective-permute-start(f32[2,512]{0,1:T(8,128)} %add_add_fusion.1), channel_id=1, source_target_pairs={{0,24},{1,25},{2,26},{3,27},{4,28},{5,29},{6,30},{7,31},{8,16},{9,... | collective-permute-start | bytes 12296 | tf_op jit(solution)/shard_map/ppermute | solution.py:20
  194.9 3.1 %collective-permute-start.10 = (f32[]{:T(128)}, f32[]{:T(128)}, u32[]{:S(2)}, u32[]{:S(2)}) collective-permute-start(f32[]{:T(128)} %get-tuple-element.48), channel_id=1, source_target_pairs={{0,32},{32,0},{64,96},{96,64},{128,160},{160,128},{192,224},{224,1... | collective-permute-start | bytes 20 | tf_op jit(solution)/shard_map/ppermute | solution.py:20
  199.4 2.6 %collective-permute-start.11 = (f32[]{:T(128)}, f32[]{:T(128)}, u32[]{:S(2)}, u32[]{:S(2)}) collective-permute-start(f32[]{:T(128)} %add.147), channel_id=1, source_target_pairs={{0,64},{32,96},{64,0},{96,32},{128,192},{160,224},{192,128},{224,1... | collective-permute-start | bytes 20 | tf_op jit(solution)/shard_map/ppermute | solution.py:20
  202.7 4.1 %collective-permute-start.12 = (f32[]{:T(128)}, f32[]{:T(128)}, u32[]{:S(2)}, u32[]{:S(2)}) collective-permute-start(f32[]{:T(128)} %add.148), channel_id=1, source_target_pairs={{0,128},{32,160},{64,192},{96,224},{128,0},{160,32},{192,64},{224,... | collective-permute-start | bytes 20 | tf_op jit(solution)/shard_map/ppermute | solution.py:20

commit v9 on v7

--- a/solution.py
+++ b/solution.py
@@ -40,7 +40,7 @@
     return jnp.sum((starts[:, None] <= positions[None, :]).astype(jnp.int32), axis=0) - 1
 
 
-def exclusive_state_scan(local_state, carry, stats, axis):
+def exclusive_state_scan(local_state, carry, stats, passenger, axis):
     head_count, head_dim, _ = local_state.shape
     count = lax.axis_size(axis)
     rows = head_count * head_dim // count
@@ -60,6 +60,7 @@
         axis=1,
     ).reshape(count, 8, head_dim)
     got = lax.all_to_all(jnp.concatenate([slices, extra], axis=1), axis, 0, 0)
+    got, passenger = lax.optimization_barrier((got, passenger))
     got_extra = got[:, rows:, :].reshape(count, 8 * head_dim)
     factors = got_extra[:, per_owner * fields]
     part = got_extra[:, : per_owner * fields].reshape(count, per_owner, fields)
@@ -83,7 +84,7 @@
     back = lax.all_to_all(sent_back, axis, 0, 0)
     state = back[:, :rows, :].reshape(head_count, head_dim, head_dim)
     totals = back[:, rows:, :].reshape(count, 8 * head_dim)[:, : per_owner * fields]
-    return state, totals.reshape(pair_count, fields)
+    return state, totals.reshape(pair_count, fields), passenger
 
 
 def local(
@@ -158,7 +159,7 @@
         ],
         axis=2,
     ).reshape(record_count * label_count, 2 * head_count + 1)
-    incoming, totals = exclusive_state_scan(local_state, carry, stats, "ctx")
+    incoming, totals, intra = exclusive_state_scan(local_state, carry, stats, intra, "ctx")
     totals = totals.reshape(record_count, label_count, 2 * head_count + 1)
     top = jnp.transpose(totals[:, :, :head_count], (2, 0, 1))
     total_mass = jnp.transpose(totals[:, :, head_count:2 * head_count], (2, 0, 1))

time: 145 us -> 138 us (0.952)
  blocking collectives: 0 us -> 25.2 us
  waiting for transfers between devices: 35.4 us -> 15.3 us
  starting transfers between devices: 50 us -> 41.6 us
  matrix products: 19.5 us -> 17.1 us
    all_to_all x0 -> x1, blocking collectives: none -> 25.2 us  [exclusive_state_scan(): back = lax.all_to_all(sent_back, axis, 0, 0)]
    all_to_all x1 -> x0, waiting for transfers between devices: 13.4 us -> none  [exclusive_state_scan(): back = lax.all_to_all(sent_back, axis, 0, 0)]
    all_to_all x1 -> x0, starting transfers between devices: 8.57 us -> none  [exclusive_state_scan(): back = lax.all_to_all(sent_back, axis, 0, 0)]
    all_to_all x1, waiting for transfers between devices: 16.4 us -> 9.72 us  [exclusive_state_scan(): got = lax.all_to_all(jnp.concatenate([slices, extra], axis=1), axis, 0, 0)]
    dot_general x1, matrix products: 3.2 us -> 0.71 us  [local(): jnp.einsum('lhd,thd->hlt', lw3, y3, preferred_element_type=jnp.float32)]
    dot_general x1, matrix products: 2.95 us -> 0.99 us  [local(): jnp.einsum('thd,hde->the', q_decayed, incoming, precision=lax.Precision.H...]
    unnamed x31, local copies, waits for them, and re-layouts: 8.21 us -> 6.62 us
  transfers between devices with their start and end apart: 15 -> 14, of which waited for: 8 -> 7; matrix products, arithmetic and copies ran while one was open for 3% -> 6% of each run, Pallas kernels for 0% -> 0%
where the time goes in v9:
time: 138 us; the launch traced here: 137 us
  starting transfers between devices  41.6 us (30%)
  blocking collectives  25.2 us (18%)
  matrix products  17.1 us (12%)
  local copies, waits for them, and re-layouts  16 us (12%)
  other arithmetic  15.9 us (12%)
  waiting for transfers between devices  15.3 us (11%)
  between operations  5.6 us (4%)
    ppermute x13, starting transfers between devices, swapped(): return lax.ppermute(x, axis, [(i, i ^ bit) for i in range(count)])  29.4 us
    all_to_all x1, blocking collectives, exclusive_state_scan(): back = lax.all_to_all(sent_back, axis, 0, 0)  25.2 us
    all_to_all x1, starting transfers between devices, exclusive_state_scan(): got = lax.all_to_all(jnp.concatenate([slices, extra], axis=1), axis, 0, 0)  12.2 us
    all_to_all x1, waiting for transfers between devices, exclusive_state_scan(): got = lax.all_to_all(jnp.concatenate([slices, extra], axis=1), axis, 0, 0)  9.72 us
    unnamed x31, local copies, waits for them, and re-layouts  6.62 us
    ppermute x13, waiting for transfers between devices, swapped(): return lax.ppermute(x, axis, [(i, i ^ bit) for i in range(count)])  5.6 us
    dot_general x1, matrix products, local(): jnp.dot(features, w_query, preferred_element_type=jnp.float32)  3.27 us
    dot_general x1, matrix products, local(): jnp.dot(features, w_value, preferred_element_type=jnp.float32)  3.1 us
  transfers between devices with their start and end apart: 14, of which 7 were waited for; matrix products, arithmetic and copies ran while one was open for 6% of the time, Pallas kernels for 0%

profile of v9, /device:TPU:1, one launch (start us, length us, event | category | flops | bytes accessed | tf_op | source)
XLA Modules:
  0.0 136.7 jit_solution(3590514397468606144)
XLA Ops:
  0.7 1.0 reduce-window.10
  1.6 0.7 bitcast_subtract_fusion.1
  3.0 1.1 copy.120
  4.1 1.9 %convolution_multiply_fusion = f32[8,512,256]{2,1,0:T(8,128)S(1)} fusion(bf16[256,8,128]{2,1,0:T(8,128)(2,1)S(1)} %bitcast.139, bf16[512,1024]{1,0:T(8,128)(2,1)} %param.18), kind=kOutput, calls=%fused_computation.7 | convolution fusion | flops 269484032 | bytes 5767168 | tf_op jit(solution)/shard_map/lhd,thd->hlt/dot_general | solution.py:140
  6.1 1.2 select_reduce_fusion.3
  7.3 1.5 %select_reduce_fusion.2 = f32[8,512,256]{2,1,0:T(8,128)S(1)} fusion(f32[8,2,512]{2,1,0:T(2,128)S(1)} %select_reduce_fusion.3, pred[2,256]{1,0:T(4,128)(4,1)S(1)} %iota_compare_fusion.6), kind=kLoop, calls=%fused_computation.3 | loop fusion | flops 3145728 | bytes 4227584 | tf_op jit(solution)/shard_map/reduce_sum | solution.py:144
  8.8 1.2 subtract_exponential_fusion
  10.1 1.9 %copy-done.1 = f32[8,512,256]{2,1,0:T(8,128)} copy-done((f32[8,512,256]{2,1,0:T(8,128)}, f32[8,512,256]{2,1,0:T(8,128)S(1)}, u32[]{:S(2)}) %copy-start.1) | copy-done | bytes 4194328
  12.0 1.2 select_reduce_fusion.1
  16.1 0.7 broadcast_compare_fusion.1
  17.6 0.7 broadcast_select_fusion
  18.3 0.7 gather_fusion
  19.3 1.5 %convolution_convert_fusion.2 = bf16[256,1024]{1,0:T(8,128)(2,1)} fusion(bf16[1024,1024]{1,0:T(8,128)(2,1)S(1)} %copy-done, bf16[1,256,1024]{2,1,0:T(8,128)(2,1)S(1)} %copy-done.6), kind=kOutput, calls=%fused_computation.16 | convolution fusion | flops 537133056 | bytes 3145728 | tf_op jit(solution)/shard_map/dot_general | solution.py:115
  20.8 1.2 copy.114
  22.1 3.1 %convolution_convert_fusion.1 = bf16[256,1024]{1,0:T(8,128)(2,1)} fusion(bf16[1024,1024]{1,0:T(8,128)(2,1)} %param.16, bf16[1,256,1024]{2,1,0:T(8,128)(2,1)S(1)} %copy-done.6), kind=kOutput, calls=%fused_computation.15 | convolution fusion | flops 537133056 | bytes 3145728 | tf_op jit(solution)/shard_map/dot_general | solution.py:116
  25.2 1.2 copy.115
  26.7 0.9 pad_maximum_fusion
  27.6 12.2 %all-to-all-start = ((f32[32,40,128]{2,1,0:T(8,128)}), f32[32,40,128]{2,1,0:T(8,128)S(1)}, u32[]{:S(2)}, u32[]{:S(2)}) async-start(f32[32,40,128]{2,1,0:T(8,128)} %pad_maximum_fusion), calls=%async_computation | async-start | bytes 1310720 | tf_op jit(solution)/shard_map/all_to_all | solution.py:62
  40.0 3.3 %fusion.4 = bf16[32,8,8,128]{3,2,1,0:T(8,128)(2,1)} fusion(bf16[1024,1024]{1,0:T(8,128)(2,1)} %param.14, bf16[1,256,1024]{2,1,0:T(8,128)(2,1)} %param.10), kind=kOutput, calls=%fused_computation.17 | convolution fusion | flops 537133056 | bytes 3145728 | tf_op jit(solution)/shard_map/dot_general | solution.py:114
  43.3 3.1 %fusion.1 = f32[256,8,128]{0,2,1:T(8,128)} fusion(bf16[256,8,128]{0,2,1:T(8,128)(2,1)} %bitcast.135, bf16[256,8,128]{0,2,1:T(8,128)(2,1)S(1)} %bitcast.133, f32[8,256]{1,0:T(8,128)S(1)} %get-tuple-element.31, pred[256,256]{1,0:T(8,128)(4,1)S(1)} %fusion.35, bf16[32,8,8,128]{3,2,1,0:T(8,128)(2,1)} %fusion.4), kind=kOutput, calls=%fused_computation.10 | convolution fusion | flops 271581184 | bytes 2695168 | tf_op jit(solution)/shard_map/hts,shd->thd/dot_general | solution.py:134
  46.4 9.7 %all-to-all-done = f32[32,40,128]{2,1,0:T(8,128)S(1)} async-done(((f32[32,40,128]{2,1,0:T(8,128)}), f32[32,40,128]{2,1,0:T(8,128)S(1)}, u32[]{:S(2)}, u32[]{:S(2)}) %all-to-all-start) | async-done | bytes 655392 | tf_op jit(solution)/shard_map/all_to_all | solution.py:62
  56.1 0.9 slice.61
  59.3 1.9 %fusion.17 = f32[32,32,128]{2,0,1:T(8,128)S(1)} fusion(f32[32,32]{1,0:T(8,128)S(1)} %select_reduce_fusion.4, f32[4,8,32,128]{3,2,1,0:T(8,128)} %bitcast.137), kind=kOutput, calls=%fused_computation.37 | convolution fusion | flops 50333696 | bytes 1052672 | tf_op jit(solution)/shard_map/dot_general | solution.py:76
  61.7 25.2 %all_to_all.10 = f32[32,40,128]{2,1,0:T(8,128)S(1)} all-to-all(f32[32,40,128]{2,1,0:T(8,128)S(1)} %copy.100), channel_id=1, replica_groups=mesh['dp'=8,'ctx'=32] {'ctx'}, dimensions={0} | all-to-all | bytes 1310720 | tf_op jit(solution)/shard_map/all_to_all | solution.py:84
  87.0 1.0 fusion.52
  88.4 0.7 bitcast_multiply_fusion
  89.1 1.2 select_reduce_fusion
  91.0 1.1 fusion.51
  92.1 1.2 copy.112
  93.3 1.2 copy.113
  94.6 2.8 %collective-permute-start = (f32[2,512]{1,0:T(2,128)S(1)}, f32[2,512]{1,0:T(2,128)S(1)}, u32[]{:S(2)}, u32[]{:S(2)}) collective-permute-start(f32[2,512]{1,0:T(2,128)S(1)} %fusion.38), channel_id=1, source_target_pairs={{0,1},{1,0},{2,3},{3,2},{4,5},{5,4},{6,7},{7,6},{8,9},{9,8},{10,11... | collective-permute-start | bytes 12296 | tf_op jit(solution)/shard_map/ppermute | solution.py:17
  97.4 0.9 collective-permute-start.1
  98.2 1.3 collective-permute-start.2
  99.5 2.6 %collective-permute-start.3 = (f32[2,512]{1,0:T(2,128)S(1)}, f32[2,512]{1,0:T(2,128)S(1)}, u32[]{:S(2)}, u32[]{:S(2)}) collective-permute-start(f32[2,512]{1,0:T(2,128)S(1)} %fusion.38), channel_id=1, source_target_pairs={{0,4},{1,5},{2,6},{3,7},{4,0},{5,1},{6,2},{7,3},{8,12},{9,13},{10,... | collective-permute-start | bytes 12296 | tf_op jit(solution)/shard_map/ppermute | solution.py:17
  102.2 2.0 %collective-permute-start.4 = (f32[2,512]{1,0:T(2,128)S(1)}, f32[2,512]{1,0:T(2,128)S(1)}, u32[]{:S(2)}, u32[]{:S(2)}) collective-permute-start(f32[2,512]{1,0:T(2,128)S(1)} %fusion.38), channel_id=1, source_target_pairs={{0,5},{1,4},{2,7},{3,6},{4,1},{5,0},{6,3},{7,2},{8,13},{9,12},{10,... | collective-permute-start | bytes 12296 | tf_op jit(solution)/shard_map/ppermute | solution.py:17
  104.2 1.4 collective-permute-start.5
  105.6 2.0 %collective-permute-start.6 = (f32[2,512]{1,0:T(2,128)S(1)}, f32[2,512]{1,0:T(2,128)S(1)}, u32[]{:S(2)}, u32[]{:S(2)}) collective-permute-start(f32[2,512]{1,0:T(2,128)S(1)} %fusion.38), channel_id=1, source_target_pairs={{0,7},{1,6},{2,5},{3,4},{4,3},{5,2},{6,1},{7,0},{8,15},{9,14},{10,... | collective-permute-start | bytes 12296 | tf_op jit(solution)/shard_map/ppermute | solution.py:17
  107.6 1.1 collective-permute-done.5
  109.2 1.3 collective-permute-start.7
  110.6 2.3 %collective-permute-start.8 = (f32[2,512]{1,0:T(2,128)S(1)}, f32[2,512]{1,0:T(2,128)S(1)}, u32[]{:S(2)}, u32[]{:S(2)}) collective-permute-start(f32[2,512]{1,0:T(2,128)S(1)} %add_add_fusion.1), channel_id=1, source_target_pairs={{0,16},{1,17},{2,18},{3,19},{4,20},{5,21},{6,22},{7,23},{8,24},{9,... | collective-permute-start | bytes 12296 | tf_op jit(solution)/shard_map/ppermute | solution.py:17
  113.6 1.0 copy.108
  114.6 1.9 %collective-permute-done.9 = f32[2,512]{1,0:T(2,128)S(1)} collective-permute-done((f32[2,512]{1,0:T(2,128)S(1)}, f32[2,512]{1,0:T(2,128)S(1)}, u32[]{:S(2)}, u32[]{:S(2)}) %collective-permute-start.9) | collective-permute-done | bytes 4128 | tf_op jit(solution)/shard_map/ppermute | solution.py:17
  116.5 0.7 fusion.43
  117.2 1.1 multiply_reduce_fusion.1
  118.3 6.9 %collective-permute-start.10 = (f32[]{:T(128)}, f32[]{:T(128)}, u32[]{:S(2)}, u32[]{:S(2)}) collective-permute-start(f32[]{:T(128)} %get-tuple-element.36), channel_id=1, source_target_pairs={{0,32},{32,0},{64,96},{96,64},{128,160},{160,128},{192,224},{224,1... | collective-permute-start | bytes 20 | tf_op jit(solution)/shard_map/ppermute | solution.py:17
  125.2 1.0 collective-permute-done.10
  127.5 2.0 %collective-permute-start.11 = (f32[]{:T(128)}, f32[]{:T(128)}, u32[]{:S(2)}, u32[]{:S(2)}) collective-permute-start(f32[]{:T(128)} %add.147), channel_id=1, source_target_pairs={{0,64},{32,96},{64,0},{96,32},{128,192},{160,224},{192,128},{224,1... | collective-permute-start | bytes 20 | tf_op jit(solution)/shard_map/ppermute | solution.py:17
  130.8 3.6 %collective-permute-start.12 = (f32[]{:T(128)}, f32[]{:T(128)}, u32[]{:S(2)}, u32[]{:S(2)}) collective-permute-start(f32[]{:T(128)} %add.148), channel_id=1, source_target_pairs={{0,128},{32,160},{64,192},{96,224},{128,0},{160,32},{192,64},{224,... | collective-permute-start | bytes 20 | tf_op jit(solution)/shard_map/ppermute | solution.py:17
  (91 shorter events, 10.7 us)
Async XLA Ops:
  0.6 18.7 %copy-start = (bf16[1024,1024]{1,0:T(8,128)(2,1)S(1)}, bf16[1024,1024]{1,0:T(8,128)(2,1)}, u32[]{:S(2)}) copy-start(bf16[1024,1024]{1,0:T(8,128)(2,1)} %param.15) | copy-start | bytes 6291460
  10.0 1.9 %copy-start.1 = (f32[8,512,256]{2,1,0:T(8,128)}, f32[8,512,256]{2,1,0:T(8,128)S(1)}, u32[]{:S(2)}) copy-start(f32[8,512,256]{2,1,0:T(8,128)S(1)} %subtract_exponential_fusion) | copy-start | bytes 12582916
  12.0 1.2 copy-start.11
  12.0 2.0 %copy-start.10 = (s32[1,2]{1,0:T(1,128)S(1)}, s32[1,2]{1,0:T(1,128)}, u32[]{:S(2)}) copy-start(s32[1,2]{1,0:T(1,128)} %param.12) | copy-start | bytes 28
  12.0 3.3 %copy-start.8 = (f32[1,8,256]{2,1,0:T(8,128)S(1)}, f32[1,8,256]{2,1,0:T(8,128)}, u32[]{:S(2)}) copy-start(f32[1,8,256]{2,1,0:T(8,128)} %param.11) | copy-start | bytes 24580
  12.0 7.3 %copy-start.6 = (bf16[1,256,1024]{2,1,0:T(8,128)(2,1)S(1)}, bf16[1,256,1024]{2,1,0:T(8,128)(2,1)}, u32[]{:S(2)}) copy-start(bf16[1,256,1024]{2,1,0:T(8,128)(2,1)} %param.10) | copy-start | bytes 1572868
  26.4 1.2 copy-start.3
  27.6 28.4 %all-to-all-start = ((f32[32,40,128]{2,1,0:T(8,128)}), f32[32,40,128]{2,1,0:T(8,128)S(1)}, u32[]{:S(2)}, u32[]{:S(2)}) async-start(f32[32,40,128]{2,1,0:T(8,128)} %pad_maximum_fusion), calls=%async_computation | async-start | bytes 1310720 | tf_op jit(solution)/shard_map/all_to_all | solution.py:62
  58.3 28.6 %copy-start.5 = (f32[256,8,128]{0,2,1:T(8,128)S(1)}, f32[256,8,128]{0,2,1:T(8,128)}, u32[]{:S(2)}) copy-start(f32[256,8,128]{0,2,1:T(8,128)} %fusion.1) | copy-start | bytes 3145732
  58.6 28.4 %copy-start.7 = (bf16[32,8,8,128]{3,2,1,0:T(8,128)(2,1)S(1)}, bf16[32,8,8,128]{3,2,1,0:T(8,128)(2,1)}, u32[]{:S(2)}) copy-start(bf16[32,8,8,128]{3,2,1,0:T(8,128)(2,1)} %fusion.4) | copy-start | bytes 1572868
  61.2 26.9 %copy-start.9 = (f32[1024]{0:T(1024)S(1)}, f32[1024]{0:T(1024)}, u32[]{:S(2)}) copy-start(f32[1024]{0:T(1024)} %param.17) | copy-start | bytes 12292
  61.6 26.7 %copy-start.2 = (f32[8,512,256]{2,1,0:T(8,128)S(1)}, f32[8,512,256]{2,1,0:T(8,128)}, u32[]{:S(2)}) copy-start(f32[8,512,256]{2,1,0:T(8,128)} %copy-done.1) | copy-start | bytes 12582916
  61.7 26.7 %copy-start.4 = (bf16[512,1024]{1,0:T(8,128)(2,1)S(1)}, bf16[512,1024]{1,0:T(8,128)(2,1)}, u32[]{:S(2)}) copy-start(bf16[512,1024]{1,0:T(8,128)(2,1)} %param.19) | copy-start | bytes 3145732
  94.6 9.6 %collective-permute-start = (f32[2,512]{1,0:T(2,128)S(1)}, f32[2,512]{1,0:T(2,128)S(1)}, u32[]{:S(2)}, u32[]{:S(2)}) collective-permute-start(f32[2,512]{1,0:T(2,128)S(1)} %fusion.38), channel_id=1, source_target_pairs={{0,1},{1,0},{2,3},{3,2},{4,5},{5,4},{6,7},{7,6},{8,9},{9,8},{10,11... | collective-permute-start | bytes 12296 | tf_op jit(solution)/shard_map/ppermute | solution.py:17
  97.4 8.2 %collective-permute-start.1 = (f32[2,512]{1,0:T(2,128)S(1)}, f32[2,512]{1,0:T(2,128)S(1)}, u32[]{:S(2)}, u32[]{:S(2)}) collective-permute-start(f32[2,512]{1,0:T(2,128)S(1)} %fusion.38), channel_id=1, source_target_pairs={{0,2},{1,3},{2,0},{3,1},{4,6},{5,7},{6,4},{7,5},{8,10},{9,11},{10,... | collective-permute-start | bytes 12296 | tf_op jit(solution)/shard_map/ppermute | solution.py:17
  98.2 9.4 %collective-permute-start.2 = (f32[2,512]{1,0:T(2,128)S(1)}, f32[2,512]{1,0:T(2,128)S(1)}, u32[]{:S(2)}, u32[]{:S(2)}) collective-permute-start(f32[2,512]{1,0:T(2,128)S(1)} %fusion.38), channel_id=1, source_target_pairs={{0,3},{1,2},{2,1},{3,0},{4,7},{5,6},{6,5},{7,4},{8,11},{9,10},{10,... | collective-permute-start | bytes 12296 | tf_op jit(solution)/shard_map/ppermute | solution.py:17
  99.5 8.1 %collective-permute-start.3 = (f32[2,512]{1,0:T(2,128)S(1)}, f32[2,512]{1,0:T(2,128)S(1)}, u32[]{:S(2)}, u32[]{:S(2)}) collective-permute-start(f32[2,512]{1,0:T(2,128)S(1)} %fusion.38), channel_id=1, source_target_pairs={{0,4},{1,5},{2,6},{3,7},{4,0},{5,1},{6,2},{7,3},{8,12},{9,13},{10,... | collective-permute-start | bytes 12296 | tf_op jit(solution)/shard_map/ppermute | solution.py:17
  102.2 5.5 %collective-permute-start.4 = (f32[2,512]{1,0:T(2,128)S(1)}, f32[2,512]{1,0:T(2,128)S(1)}, u32[]{:S(2)}, u32[]{:S(2)}) collective-permute-start(f32[2,512]{1,0:T(2,128)S(1)} %fusion.38), channel_id=1, source_target_pairs={{0,5},{1,4},{2,7},{3,6},{4,1},{5,0},{6,3},{7,2},{8,13},{9,12},{10,... | collective-permute-start | bytes 12296 | tf_op jit(solution)/shard_map/ppermute | solution.py:17
  104.2 4.6 %collective-permute-start.5 = (f32[2,512]{1,0:T(2,128)S(1)}, f32[2,512]{1,0:T(2,128)S(1)}, u32[]{:S(2)}, u32[]{:S(2)}) collective-permute-start(f32[2,512]{1,0:T(2,128)S(1)} %fusion.38), channel_id=1, source_target_pairs={{0,6},{1,7},{2,4},{3,5},{4,2},{5,3},{6,0},{7,1},{8,14},{9,15},{10,... | collective-permute-start | bytes 12296 | tf_op jit(solution)/shard_map/ppermute | solution.py:17
  105.6 3.7 %collective-permute-start.6 = (f32[2,512]{1,0:T(2,128)S(1)}, f32[2,512]{1,0:T(2,128)S(1)}, u32[]{:S(2)}, u32[]{:S(2)}) collective-permute-start(f32[2,512]{1,0:T(2,128)S(1)} %fusion.38), channel_id=1, source_target_pairs={{0,7},{1,6},{2,5},{3,4},{4,3},{5,2},{6,1},{7,0},{8,15},{9,14},{10,... | collective-permute-start | bytes 12296 | tf_op jit(solution)/shard_map/ppermute | solution.py:17
  109.2 5.3 %collective-permute-start.7 = (f32[2,512]{1,0:T(2,128)S(1)}, f32[2,512]{1,0:T(2,128)S(1)}, u32[]{:S(2)}, u32[]{:S(2)}) collective-permute-start(f32[2,512]{1,0:T(2,128)S(1)} %add_add_fusion.1), channel_id=1, source_target_pairs={{0,8},{1,9},{2,10},{3,11},{4,12},{5,13},{6,14},{7,15},{8,0},{9,1},... | collective-permute-start | bytes 12296 | tf_op jit(solution)/shard_map/ppermute | solution.py:17
  110.6 4.0 %collective-permute-start.8 = (f32[2,512]{1,0:T(2,128)S(1)}, f32[2,512]{1,0:T(2,128)S(1)}, u32[]{:S(2)}, u32[]{:S(2)}) collective-permute-start(f32[2,512]{1,0:T(2,128)S(1)} %add_add_fusion.1), channel_id=1, source_target_pairs={{0,16},{1,17},{2,18},{3,19},{4,20},{5,21},{6,22},{7,23},{8,24},{9,... | collective-permute-start | bytes 12296 | tf_op jit(solution)/shard_map/ppermute | solution.py:17
  112.8 3.7 %collective-permute-start.9 = (f32[2,512]{1,0:T(2,128)S(1)}, f32[2,512]{1,0:T(2,128)S(1)}, u32[]{:S(2)}, u32[]{:S(2)}) collective-permute-start(f32[2,512]{1,0:T(2,128)S(1)} %add_add_fusion.1), channel_id=1, source_target_pairs={{0,24},{1,25},{2,26},{3,27},{4,28},{5,29},{6,30},{7,31},{8,16},{9,... | collective-permute-start | bytes 12296 | tf_op jit(solution)/shard_map/ppermute | solution.py:17
  118.3 7.8 %collective-permute-start.10 = (f32[]{:T(128)}, f32[]{:T(128)}, u32[]{:S(2)}, u32[]{:S(2)}) collective-permute-start(f32[]{:T(128)} %get-tuple-element.36), channel_id=1, source_target_pairs={{0,32},{32,0},{64,96},{96,64},{128,160},{160,128},{192,224},{224,1... | collective-permute-start | bytes 20 | tf_op jit(solution)/shard_map/ppermute | solution.py:17
  127.5 2.6 %collective-permute-start.11 = (f32[]{:T(128)}, f32[]{:T(128)}, u32[]{:S(2)}, u32[]{:S(2)}) collective-permute-start(f32[]{:T(128)} %add.147), channel_id=1, source_target_pairs={{0,64},{32,96},{64,0},{96,32},{128,192},{160,224},{192,128},{224,1... | collective-permute-start | bytes 20 | tf_op jit(solution)/shard_map/ppermute | solution.py:17
  130.8 4.1 %collective-permute-start.12 = (f32[]{:T(128)}, f32[]{:T(128)}, u32[]{:S(2)}, u32[]{:S(2)}) collective-permute-start(f32[]{:T(128)} %add.148), channel_id=1, source_target_pairs={{0,128},{32,160},{64,192},{96,224},{128,0},{160,32},{192,64},{224,... | collective-permute-start | bytes 20 | tf_op jit(solution)/shard_map/ppermute | solution.py:17

commit v10 on v9

--- a/solution.py
+++ b/solution.py
@@ -184,18 +184,10 @@
         jnp.where(member[None, :, None, :], (pool_weight * label_value)[:, None], 0.0), axis=3
     )
     part = jnp.sum(weighted * rescale, axis=0)
-    count = lax.axis_size("ctx")
-    inner = min(count, 8)
-    assert count % inner == 0 and inner & (inner - 1) == 0
-    part = group_sum(part, "ctx", 1, inner)
-    if count > inner:
-        part = group_sum(part, "ctx", inner, count // inner)
-    logits = part
+    logits = jnp.sum(lax.all_gather(part, "ctx"), axis=0)
     target = (total_counts + 0.5) / (lengths[0].astype(jnp.float32)[:, None] + 1.0)
     rec_loss = jnp.mean(jax.nn.softplus(logits) - target * logits, axis=1)
-    loss_sum = jnp.sum(rec_loss)
-    for bit in butterfly_bits("dp"):
-        loss_sum = loss_sum + swapped(loss_sum, "dp", bit)
+    loss_sum = jnp.sum(lax.all_gather(jnp.sum(rec_loss), "dp"))
     mean_loss = loss_sum / (lax.axis_size("dp") * record_count)
     return (out_rows[None], logits[None], rec_loss[None], mean_loss)
 

time: 138 us -> 161 us (1.17)
  blocking collectives: 25.2 us -> 58 us
  starting transfers between devices: 41.6 us -> 20.6 us
  waiting for transfers between devices: 15.3 us -> 26 us
  between operations: 5.6 us -> 3.52 us
  local copies, waits for them, and re-layouts: 16 us -> 17.7 us
    all_gather x0 -> x1, blocking collectives: none -> 33.1 us  [local(): logits = jnp.sum(lax.all_gather(part, 'ctx'), axis=0)]
    ppermute x13 -> x0, starting transfers between devices: 29.4 us -> none  [swapped(): return lax.ppermute(x, axis, [(i, i ^ bit) for i in range(count)])]
    all_to_all x1 -> x0, blocking collectives: 25.2 us -> none  [exclusive_state_scan(): back = lax.all_to_all(sent_back, axis, 0, 0)]
    unnamed x0 -> x1, blocking collectives: none -> 24.9 us
    all_to_all x0 -> x1, waiting for transfers between devices: none -> 16.2 us  [exclusive_state_scan(): back = lax.all_to_all(sent_back, axis, 0, 0)]
    all_to_all x0 -> x1, starting transfers between devices: none -> 8.4 us  [exclusive_state_scan(): back = lax.all_to_all(sent_back, axis, 0, 0)]
    ppermute x13 -> x0, waiting for transfers between devices: 5.6 us -> none  [swapped(): return lax.ppermute(x, axis, [(i, i ^ bit) for i in range(count)])]
    unnamed x31 -> x37, local copies, waits for them, and re-layouts: 6.62 us -> 7.48 us
  transfers between devices with their start and end apart: 14 -> 2, of which waited for: 7 -> 2; matrix products, arithmetic and copies ran while one was open for 6% -> 4% of each run, Pallas kernels for 0% -> 0%
where the time goes in v10:
time: 161 us; the launch traced here: 160 us
  blocking collectives  58 us (36%)
  waiting for transfers between devices  26 us (16%)
  starting transfers between devices  20.6 us (13%)
  matrix products  18.3 us (11%)
  local copies, waits for them, and re-layouts  17.7 us (11%)
  other arithmetic  16 us (10%)
  between operations  3.52 us (2%)
    all_gather x1, blocking collectives, local(): logits = jnp.sum(lax.all_gather(part, 'ctx'), axis=0)  33.1 us
    unnamed x1, blocking collectives  24.9 us
    all_to_all x1, waiting for transfers between devices, exclusive_state_scan(): back = lax.all_to_all(sent_back, axis, 0, 0)  16.2 us
    all_to_all x1, starting transfers between devices, exclusive_state_scan(): got = lax.all_to_all(jnp.concatenate([slices, extra], axis=1), axis, 0, 0)  12.2 us
    all_to_all x1, waiting for transfers between devices, exclusive_state_scan(): got = lax.all_to_all(jnp.concatenate([slices, extra], axis=1), axis, 0, 0)  9.73 us
    all_to_all x1, starting transfers between devices, exclusive_state_scan(): back = lax.all_to_all(sent_back, axis, 0, 0)  8.4 us
    unnamed x37, local copies, waits for them, and re-layouts  7.48 us
    dot_general x1, matrix products, local(): jnp.dot(features, w_query, preferred_element_type=jnp.float32)  3.27 us
  transfers between devices with their start and end apart: 2, of which 2 were waited for; matrix products, arithmetic and copies ran while one was open for 4% of the time, Pallas kernels for 0%

profile of v10, /device:TPU:1, one launch (start us, length us, event | category | flops | bytes accessed | tf_op | source)
XLA Modules:
  0.0 160.1 jit_solution(5690157890810088656)
XLA Ops:
  0.7 1.0 reduce-window.10
  1.6 0.7 bitcast_subtract_fusion.1
  2.4 0.6 slice.54
  3.0 1.1 copy.120
  4.1 1.9 %convolution_multiply_fusion = f32[8,512,256]{2,1,0:T(8,128)S(1)} fusion(bf16[256,8,128]{2,1,0:T(8,128)(2,1)S(1)} %bitcast.142, bf16[512,1024]{1,0:T(8,128)(2,1)} %param.18), kind=kOutput, calls=%fused_computation.7 | convolution fusion | flops 269484032 | bytes 5767168 | tf_op jit(solution)/shard_map/lhd,thd->hlt/dot_general | solution.py:140
  6.1 1.2 select_reduce_fusion.3
  7.3 1.5 select_reduce_fusion.2
  8.8 1.2 subtract_exponential_fusion
  10.1 1.9 %copy-done.1 = f32[8,512,256]{2,1,0:T(8,128)} copy-done((f32[8,512,256]{2,1,0:T(8,128)}, f32[8,512,256]{2,1,0:T(8,128)S(1)}, u32[]{:S(2)}) %copy-start.1) | copy-done | bytes 4194328
  12.0 1.2 select_reduce_fusion.1
  14.0 0.6 fusion.45
  15.3 0.6 reduce-window.11
  16.1 0.7 broadcast_compare_fusion.1
  16.7 0.6 slice.58
  17.6 0.7 broadcast_select_fusion
  18.3 0.7 gather_fusion
  19.3 1.5 convolution_convert_fusion.2
  20.8 1.2 copy.114
  22.1 3.1 %convolution_convert_fusion.1 = bf16[256,1024]{1,0:T(8,128)(2,1)} fusion(bf16[1024,1024]{1,0:T(8,128)(2,1)} %param.16, bf16[1,256,1024]{2,1,0:T(8,128)(2,1)S(1)} %copy-done.7), kind=kOutput, calls=%fused_computation.15 | convolution fusion | flops 537133056 | bytes 3145728 | tf_op jit(solution)/shard_map/dot_general | solution.py:116
  25.2 1.2 copy.115
  26.4 0.3 fusion.16
  26.8 0.9 pad_maximum_fusion
  27.7 12.2 %all-to-all-start = ((f32[32,40,128]{2,1,0:T(8,128)}), f32[32,40,128]{2,1,0:T(8,128)S(1)}, u32[]{:S(2)}, u32[]{:S(2)}) async-start(f32[32,40,128]{2,1,0:T(8,128)} %pad_maximum_fusion), calls=%async_computation | async-start | bytes 1310720 | tf_op jit(solution)/shard_map/all_to_all | solution.py:62
  40.0 3.3 %fusion.4 = bf16[32,8,8,128]{3,2,1,0:T(8,128)(2,1)} fusion(bf16[1024,1024]{1,0:T(8,128)(2,1)} %param.14, bf16[1,256,1024]{2,1,0:T(8,128)(2,1)} %param.10), kind=kOutput, calls=%fused_computation.17 | convolution fusion | flops 537133056 | bytes 3145728 | tf_op jit(solution)/shard_map/dot_general | solution.py:114
  43.3 3.1 %fusion.1 = f32[256,8,128]{0,2,1:T(8,128)} fusion(bf16[256,8,128]{0,2,1:T(8,128)(2,1)} %bitcast.138, bf16[256,8,128]{0,2,1:T(8,128)(2,1)S(1)} %bitcast.136, f32[8,256]{1,0:T(8,128)S(1)} %get-tuple-element.29, pred[256,256]{1,0:T(8,128)(4,1)S(1)} %fusion.35, bf16[32,8,8,128]{3,2,1,0:T(8,128)(2,1)} %fusion.4), kind=kOutput, calls=%fused_computation.10 | convolution fusion | flops 271581184 | bytes 2695168 | tf_op jit(solution)/shard_map/hts,shd->thd/dot_general | solution.py:134
  46.4 9.7 %all-to-all-done = f32[32,40,128]{2,1,0:T(8,128)S(1)} async-done(((f32[32,40,128]{2,1,0:T(8,128)}), f32[32,40,128]{2,1,0:T(8,128)S(1)}, u32[]{:S(2)}, u32[]{:S(2)}) %all-to-all-start) | async-done | bytes 655392 | tf_op jit(solution)/shard_map/all_to_all | solution.py:62
  56.1 0.9 slice.61
  57.2 0.6 reshape.364
  57.8 0.3 slice_reduce_fusion
  58.6 0.6 select_reduce_fusion.4
  59.3 1.9 %fusion.17 = f32[32,32,128]{2,0,1:T(8,128)S(1)} fusion(f32[32,32]{1,0:T(8,128)S(1)} %select_reduce_fusion.4, f32[4,8,32,128]{3,2,1,0:T(8,128)} %bitcast.140), kind=kOutput, calls=%fused_computation.37 | convolution fusion | flops 50333696 | bytes 1052672 | tf_op jit(solution)/shard_map/dot_general | solution.py:76
  61.2 1.2 copy.100
  62.5 8.4 %all-to-all-start.1 = ((f32[32,40,128]{2,1,0:T(8,128)}), f32[32,40,128]{2,1,0:T(8,128)S(1)}, u32[]{:S(2)}, u32[]{:S(2)}) async-start(f32[32,40,128]{2,1,0:T(8,128)} %copy.100), calls=%async_computation.1 | async-start | bytes 1310720 | tf_op jit(solution)/shard_map/all_to_all | solution.py:84
  70.9 0.6 dynamic-slice
  71.5 16.2 %all-to-all-done.1 = f32[32,40,128]{2,1,0:T(8,128)S(1)} async-done(((f32[32,40,128]{2,1,0:T(8,128)}), f32[32,40,128]{2,1,0:T(8,128)S(1)}, u32[]{:S(2)}, u32[]{:S(2)}) %all-to-all-start.1) | async-done | bytes 655392 | tf_op jit(solution)/shard_map/all_to_all | solution.py:84
  87.8 0.6 reshape_reshape.7
  88.4 1.1 fusion.51
  89.5 0.4 fusion.23
  90.0 2.3 %fusion.52 = (f32[256,8]{0,1:T(8,128)S(1)}, f32[256,8,128]{0,2,1:T(8,128)S(1)}) fusion(f32[256,8,128]{0,2,1:T(8,128)S(1)} %copy-done.6, f32[8,128,128]{2,1,0:T(8,128)S(1)} %bitcast.141, f32[256,8]{0,1:T(8,128)S(1)} %get-tuple-element.28, bf16[32,8,8,128]{3,2,1,0:T(8,128)(2,1)} %fusion.4), kind=kOutput, calls=%fused_computation.114 | convolution fusion | flops 202635264 | bytes 3162112 | tf_op jit(solution)/shard_map/thd,hde->the/dot_general | solution.py:170
  92.7 0.7 bitcast_multiply_fusion
  93.4 1.2 select_reduce_fusion
  94.6 1.2 copy.112
  96.1 33.1 %all-gather.1 = f32[32,2,512]{2,1,0:T(2,128)S(1)} all-gather(f32[1,2,512]{2,1,0:T(2,128)S(1)} %bitcast.152), channel_id=2, replica_groups=mesh['dp'=8,'ctx'=32] {'ctx'}, dimensions={0}, use_global_device_ids=true | all-gather | bytes 135168 | tf_op jit(solution)/shard_map/all_gather | solution.py:187
  129.4 1.1 multiply_reduce_fusion.1
  130.6 1.3 dynamic-update-slice
  131.9 24.9 %all-reduce.1 = f32[8]{0:T(128)S(1)} all-reduce(f32[8]{0:T(128)S(1)} %dynamic-update-slice), channel_id=1, replica_groups=mesh['dp'=8,'ctx'=32] {'dp'}, use_global_device_ids=true, to_apply=%add.1 | all-reduce | flops 8 | bytes 64
  156.7 0.6 reduce_sum.142
  157.3 1.0 copy.108
  (76 shorter events, 3.7 us)
Async XLA Ops:
  0.6 18.7 %copy-start = (bf16[1024,1024]{1,0:T(8,128)(2,1)S(1)}, bf16[1024,1024]{1,0:T(8,128)(2,1)}, u32[]{:S(2)}) copy-start(bf16[1024,1024]{1,0:T(8,128)(2,1)} %param.15) | copy-start | bytes 6291460
  10.0 1.9 %copy-start.1 = (f32[8,512,256]{2,1,0:T(8,128)}, f32[8,512,256]{2,1,0:T(8,128)S(1)}, u32[]{:S(2)}) copy-start(f32[8,512,256]{2,1,0:T(8,128)S(1)} %subtract_exponential_fusion) | copy-start | bytes 12582916
  12.0 1.2 copy-start.12
  12.0 2.0 %copy-start.11 = (s32[1,2]{1,0:T(1,128)S(1)}, s32[1,2]{1,0:T(1,128)}, u32[]{:S(2)}) copy-start(s32[1,2]{1,0:T(1,128)} %param.12) | copy-start | bytes 28
  12.0 3.3 %copy-start.9 = (f32[1,8,256]{2,1,0:T(8,128)S(1)}, f32[1,8,256]{2,1,0:T(8,128)}, u32[]{:S(2)}) copy-start(f32[1,8,256]{2,1,0:T(8,128)} %param.11) | copy-start | bytes 24580
  12.0 7.3 %copy-start.7 = (bf16[1,256,1024]{2,1,0:T(8,128)(2,1)S(1)}, bf16[1,256,1024]{2,1,0:T(8,128)(2,1)}, u32[]{:S(2)}) copy-start(bf16[1,256,1024]{2,1,0:T(8,128)(2,1)} %param.10) | copy-start | bytes 1572868
  26.4 1.2 copy-start.3
  27.7 28.4 %all-to-all-start = ((f32[32,40,128]{2,1,0:T(8,128)}), f32[32,40,128]{2,1,0:T(8,128)S(1)}, u32[]{:S(2)}, u32[]{:S(2)}) async-start(f32[32,40,128]{2,1,0:T(8,128)} %pad_maximum_fusion), calls=%async_computation | async-start | bytes 1310720 | tf_op jit(solution)/shard_map/all_to_all | solution.py:62
  56.9 13.9 %copy-start.13 = (u32[256]{0:T(256)S(1)}, u32[256]{0:T(256)}, u32[]{:S(2)}) copy-start(u32[256]{0:T(256)} %constant.82) | copy-start | bytes 3076
  62.5 25.2 %all-to-all-start.1 = ((f32[32,40,128]{2,1,0:T(8,128)}), f32[32,40,128]{2,1,0:T(8,128)S(1)}, u32[]{:S(2)}, u32[]{:S(2)}) async-start(f32[32,40,128]{2,1,0:T(8,128)} %copy.100), calls=%async_computation.1 | async-start | bytes 1310720 | tf_op jit(solution)/shard_map/all_to_all | solution.py:84
  87.8 4.7 %copy-start.10 = (f32[1024]{0:T(1024)S(1)}, f32[1024]{0:T(1024)}, u32[]{:S(2)}) copy-start(f32[1024]{0:T(1024)} %param.17) | copy-start | bytes 12292
  88.4 1.6 %copy-start.6 = (f32[256,8,128]{0,2,1:T(8,128)S(1)}, f32[256,8,128]{0,2,1:T(8,128)}, u32[]{:S(2)}) copy-start(f32[256,8,128]{0,2,1:T(8,128)} %fusion.1) | copy-start | bytes 3145732
  89.5 3.1 %copy-start.2 = (f32[8,512,256]{2,1,0:T(8,128)S(1)}, f32[8,512,256]{2,1,0:T(8,128)}, u32[]{:S(2)}) copy-start(f32[8,512,256]{2,1,0:T(8,128)} %copy-done.1) | copy-start | bytes 12582916
  89.5 3.2 %copy-start.5 = (bf16[512,1024]{1,0:T(8,128)(2,1)S(1)}, bf16[512,1024]{1,0:T(8,128)(2,1)}, u32[]{:S(2)}) copy-start(bf16[512,1024]{1,0:T(8,128)(2,1)} %param.19) | copy-start | bytes 3145732
  93.4 2.4 %copy-start.4 = (f32[2,512,8]{2,1,0:T(8,128)S(1)}, f32[2,512,8]{2,1,0:T(8,128)}, u32[]{:S(2)}) copy-start(f32[2,512,8]{2,1,0:T(8,128)} %get-tuple-element.31) | copy-start | bytes 98308
  129.2 29.7 %copy-start.8 = (f32[2,512]{1,0:T(2,128)}, f32[2,512]{1,0:T(2,128)S(1)}, u32[]{:S(2)}) copy-start(f32[2,512]{1,0:T(2,128)S(1)} %reduce_sum.139) | copy-start | bytes 12292

commit v11 on v9

--- a/solution.py
+++ b/solution.py
@@ -36,7 +36,8 @@
 
 
 def record_ids(length_row, positions):
-    starts = jnp.cumsum(length_row) - length_row
+    order = jnp.arange(length_row.shape[0])
+    starts = jnp.sum(jnp.where(order[None, :] < order[:, None], length_row[None, :], 0), axis=1)
     return jnp.sum((starts[:, None] <= positions[None, :]).astype(jnp.int32), axis=0) - 1
 
 
@@ -49,12 +50,11 @@
     per_owner = pair_count // count
     assert per_owner * count == pair_count and per_owner * fields < 8 * head_dim
     pad = 8 * head_dim - per_owner * fields - 1
-    owner_head = (jnp.arange(count) * rows) // head_dim
     slices = local_state.reshape(count, rows, head_dim)
     extra = jnp.concatenate(
         [
             stats.reshape(count, per_owner * fields),
-            carry[owner_head][:, None],
+            jnp.repeat(carry, count // head_count)[:, None],
             jnp.zeros((count, pad), jnp.float32),
         ],
         axis=1,
@@ -141,9 +141,9 @@
     maxima = jnp.max(
         jnp.where(member[None, :, None, :], pscore[:, None, :, :], NEG_FILL), axis=3
     )
-    maxima_tok = jnp.sum(
-        jnp.where(member[None, :, None, :], maxima[:, :, :, None], 0.0), axis=1
-    )
+    maxima_tok = maxima[:, record_count - 1, :, None]
+    for r in range(record_count - 2, -1, -1):
+        maxima_tok = jnp.where(record[None, None, :] == r, maxima[:, r, :, None], maxima_tok)
     pool_weight = jnp.exp(pscore - maxima_tok)
     mass = jnp.sum(jnp.where(member[None, :, None, :], pool_weight[:, None], 0.0), axis=3)
     label_hot = (label_ids[0][:, None] == jnp.arange(label_count, dtype=jnp.int32)[None, :]).astype(

time: 138 us -> 139 us (level)
  matrix products: 17.1 us -> 18.8 us
  other arithmetic: 15.9 us -> 14.5 us
  local copies, waits for them, and re-layouts: 16 us -> 17.4 us
    unnamed x31 -> x28, local copies, waits for them, and re-layouts: 6.62 us -> 6.81 us
  transfers between devices with their start and end apart: 14 -> 14, of which waited for: 7 -> 9; matrix products, arithmetic and copies ran while one was open for 6% -> 6% of each run, Pallas kernels for 0% -> 0%
where the time goes in v11:
time: 139 us; the launch traced here: 138 us
  starting transfers between devices  40.7 us (29%)
  blocking collectives  25.3 us (18%)
  matrix products  18.8 us (14%)
  local copies, waits for them, and re-layouts  17.4 us (13%)
  waiting for transfers between devices  15.4 us (11%)
  other arithmetic  14.5 us (10%)
  between operations  5.61 us (4%)
    ppermute x13, starting transfers between devices, swapped(): return lax.ppermute(x, axis, [(i, i ^ bit) for i in range(count)])  28.7 us
    all_to_all x1, blocking collectives, exclusive_state_scan(): back = lax.all_to_all(sent_back, axis, 0, 0)  25.3 us
    all_to_all x1, starting transfers between devices, exclusive_state_scan(): got = lax.all_to_all(jnp.concatenate([slices, extra], axis=1), axis, 0, 0)  12 us
    all_to_all x1, waiting for transfers between devices, exclusive_state_scan(): got = lax.all_to_all(jnp.concatenate([slices, extra], axis=1), axis, 0, 0)  9.91 us
    unnamed x28, local copies, waits for them, and re-layouts  6.81 us
    ppermute x13, waiting for transfers between devices, swapped(): return lax.ppermute(x, axis, [(i, i ^ bit) for i in range(count)])  5.46 us
    dot_general x1, matrix products, local(): jnp.dot(features, w_query, preferred_element_type=jnp.float32)  3.27 us
    dot_general x1, matrix products, local(): jnp.dot(features, w_value, preferred_element_type=jnp.float32)  3.1 us
  transfers between devices with their start and end apart: 14, of which 9 were waited for; matrix products, arithmetic and copies ran while one was open for 6% of the time, Pallas kernels for 0%

profile of v11, /device:TPU:1, one launch (start us, length us, event | category | flops | bytes accessed | tf_op | source)
XLA Modules:
  0.0 137.5 jit_solution(11027300609848461599)
XLA Ops:
  0.7 0.9 fusion.45
  3.6 0.7 broadcast_compare_fusion.2
  4.8 0.9 convolution_bitcast_fusion
  5.7 1.3 reduce-window.6
  7.5 0.7 broadcast_select_fusion
  8.3 2.6 %convolution_convert_fusion.2 = bf16[256,1024]{1,0:T(8,128)(2,1)} fusion(bf16[1024,1024]{1,0:T(8,128)(2,1)S(1)} %copy-done, bf16[1,256,1024]{2,1,0:T(8,128)(2,1)} %param.10), kind=kOutput, calls=%fused_computation.14 | convolution fusion | flops 537133056 | bytes 3145728 | tf_op jit(solution)/shard_map/dot_general | solution.py:115
  10.9 1.2 copy.119
  12.1 3.1 %convolution_convert_fusion.1 = bf16[256,1024]{1,0:T(8,128)(2,1)} fusion(bf16[1024,1024]{1,0:T(8,128)(2,1)} %param.16, bf16[1,256,1024]{2,1,0:T(8,128)(2,1)S(1)} %copy-done.6), kind=kOutput, calls=%fused_computation.13 | convolution fusion | flops 537133056 | bytes 3145728 | tf_op jit(solution)/shard_map/dot_general | solution.py:116
  15.2 1.2 copy.120
  16.5 1.3 copy.125
  17.8 1.9 %convolution_multiply_fusion = f32[8,512,256]{2,1,0:T(8,128)S(1)} fusion(bf16[256,8,128]{2,1,0:T(8,128)(2,1)S(1)} %bitcast.133, bf16[512,1024]{1,0:T(8,128)(2,1)} %param.18), kind=kOutput, calls=%fused_computation.5 | convolution fusion | flops 269484032 | bytes 5767168 | tf_op jit(solution)/shard_map/lhd,thd->hlt/dot_general | solution.py:140
  19.8 1.2 select_reduce_fusion.2
  21.0 1.4 %subtract_exponential_fusion = f32[8,512,256]{2,1,0:T(8,128)S(1)} fusion(f32[8,512,256]{2,1,0:T(8,128)S(1)} %convolution_multiply_fusion, f32[8,512]{1,0:T(8,128)S(1)} %get-tuple-element.43, f32[8,512]{1,0:T(8,128)S(1)} %get-tuple-element.44, pred[256]{0:T(512)(128)(4,1)S(1)} %get-tuple-element.37), kind=kLoop, calls=%fused_computation.4 | loop fusion | flops 2097152 | bytes 8421632 | tf_op jit(solution)/shard_map/exp | solution.py:147
  22.5 1.9 %copy-done.1 = f32[8,512,256]{2,1,0:T(8,128)} copy-done((f32[8,512,256]{2,1,0:T(8,128)}, f32[8,512,256]{2,1,0:T(8,128)S(1)}, u32[]{:S(2)}) %copy-start.1) | copy-done | bytes 4194328
  24.4 1.2 select_reduce_fusion.1
  25.6 1.0 copy.96
  26.6 1.3 reshape_reshape.6
  28.5 0.9 pad_maximum_fusion
  29.4 12.0 %all-to-all-start = ((f32[32,40,128]{2,1,0:T(8,128)}), f32[32,40,128]{2,1,0:T(8,128)S(1)}, u32[]{:S(2)}, u32[]{:S(2)}) async-start(f32[32,40,128]{2,1,0:T(8,128)} %pad_maximum_fusion), calls=%async_computation | async-start | bytes 1310720 | tf_op jit(solution)/shard_map/all_to_all | solution.py:62
  41.5 3.3 %fusion.4 = bf16[32,8,8,128]{3,2,1,0:T(8,128)(2,1)} fusion(bf16[1024,1024]{1,0:T(8,128)(2,1)} %param.14, bf16[1,256,1024]{2,1,0:T(8,128)(2,1)} %param.10), kind=kOutput, calls=%fused_computation.15 | convolution fusion | flops 537133056 | bytes 3145728 | tf_op jit(solution)/shard_map/dot_general | solution.py:114
  44.8 3.1 %fusion.1 = f32[256,8,128]{0,2,1:T(8,128)} fusion(bf16[256,8,128]{0,2,1:T(8,128)(2,1)} %bitcast.129, bf16[256,8,128]{0,2,1:T(8,128)(2,1)S(1)} %bitcast.127, f32[8,256]{1,0:T(8,128)S(1)} %get-tuple-element.31, pred[256,256]{1,0:T(8,128)(4,1)S(1)} %fusion.35, bf16[32,8,8,128]{3,2,1,0:T(8,128)(2,1)} %fusion.4), kind=kOutput, calls=%fused_computation.8 | convolution fusion | flops 271581184 | bytes 2695168 | tf_op jit(solution)/shard_map/hts,shd->thd/dot_general | solution.py:134
  47.9 9.9 %all-to-all-done = f32[32,40,128]{2,1,0:T(8,128)S(1)} async-done(((f32[32,40,128]{2,1,0:T(8,128)}), f32[32,40,128]{2,1,0:T(8,128)S(1)}, u32[]{:S(2)}, u32[]{:S(2)}) %all-to-all-start) | async-done | bytes 655392 | tf_op jit(solution)/shard_map/all_to_all | solution.py:62
  57.8 0.9 slice.69
  61.0 1.9 %fusion.17 = f32[32,32,128]{2,0,1:T(8,128)S(1)} fusion(f32[32,32]{1,0:T(8,128)S(1)} %select_reduce_fusion.3, f32[4,8,32,128]{3,2,1,0:T(8,128)} %bitcast.131), kind=kOutput, calls=%fused_computation.35 | convolution fusion | flops 50333696 | bytes 1052672 | tf_op jit(solution)/shard_map/dot_general | solution.py:76
  63.4 25.3 %all_to_all.10 = f32[32,40,128]{2,1,0:T(8,128)S(1)} all-to-all(f32[32,40,128]{2,1,0:T(8,128)S(1)} %copy.103), channel_id=1, replica_groups=mesh['dp'=8,'ctx'=32] {'ctx'}, dimensions={0} | all-to-all | bytes 1310720 | tf_op jit(solution)/shard_map/all_to_all | solution.py:84
  88.7 1.0 fusion.52
  90.2 0.7 bitcast_multiply_fusion
  90.9 1.2 select_reduce_fusion
  92.7 1.1 fusion.50
  93.8 1.2 copy.117
  95.0 1.2 copy.118
  96.3 1.9 %collective-permute-start.6 = (f32[2,512]{1,0:T(2,128)S(1)}, f32[2,512]{1,0:T(2,128)S(1)}, u32[]{:S(2)}, u32[]{:S(2)}) collective-permute-start(f32[2,512]{1,0:T(2,128)S(1)} %fusion.38), channel_id=1, source_target_pairs={{0,7},{1,6},{2,5},{3,4},{4,3},{5,2},{6,1},{7,0},{8,15},{9,14},{10,... | collective-permute-start | bytes 12296 | tf_op jit(solution)/shard_map/ppermute | solution.py:17
  98.2 4.2 %collective-permute-start.5 = (f32[2,512]{1,0:T(2,128)S(1)}, f32[2,512]{1,0:T(2,128)S(1)}, u32[]{:S(2)}, u32[]{:S(2)}) collective-permute-start(f32[2,512]{1,0:T(2,128)S(1)} %fusion.38), channel_id=1, source_target_pairs={{0,6},{1,7},{2,4},{3,5},{4,2},{5,3},{6,0},{7,1},{8,14},{9,15},{10,... | collective-permute-start | bytes 12296 | tf_op jit(solution)/shard_map/ppermute | solution.py:17
  103.0 1.8 %collective-permute-start.3 = (f32[2,512]{1,0:T(2,128)S(1)}, f32[2,512]{1,0:T(2,128)S(1)}, u32[]{:S(2)}, u32[]{:S(2)}) collective-permute-start(f32[2,512]{1,0:T(2,128)S(1)} %fusion.38), channel_id=1, source_target_pairs={{0,4},{1,5},{2,6},{3,7},{4,0},{5,1},{6,2},{7,3},{8,12},{9,13},{10,... | collective-permute-start | bytes 12296 | tf_op jit(solution)/shard_map/ppermute | solution.py:17
  104.8 2.9 %collective-permute-start.2 = (f32[2,512]{1,0:T(2,128)S(1)}, f32[2,512]{1,0:T(2,128)S(1)}, u32[]{:S(2)}, u32[]{:S(2)}) collective-permute-start(f32[2,512]{1,0:T(2,128)S(1)} %fusion.38), channel_id=1, source_target_pairs={{0,3},{1,2},{2,1},{3,0},{4,7},{5,6},{6,5},{7,4},{8,11},{9,10},{10,... | collective-permute-start | bytes 12296 | tf_op jit(solution)/shard_map/ppermute | solution.py:17
  107.7 1.5 %collective-permute-start.1 = (f32[2,512]{1,0:T(2,128)S(1)}, f32[2,512]{1,0:T(2,128)S(1)}, u32[]{:S(2)}, u32[]{:S(2)}) collective-permute-start(f32[2,512]{1,0:T(2,128)S(1)} %fusion.38), channel_id=1, source_target_pairs={{0,2},{1,3},{2,0},{3,1},{4,6},{5,7},{6,4},{7,5},{8,10},{9,11},{10,... | collective-permute-start | bytes 12296 | tf_op jit(solution)/shard_map/ppermute | solution.py:17
  109.4 1.7 %collective-permute-done.1 = f32[2,512]{1,0:T(2,128)S(1)} collective-permute-done((f32[2,512]{1,0:T(2,128)S(1)}, f32[2,512]{1,0:T(2,128)S(1)}, u32[]{:S(2)}, u32[]{:S(2)}) %collective-permute-start.1) | collective-permute-done | bytes 4128 | tf_op jit(solution)/shard_map/ppermute | solution.py:17
  111.1 0.9 collective-permute-done
  112.0 0.9 collective-permute-start.9
  112.9 1.7 %collective-permute-start.8 = (f32[2,512]{1,0:T(2,128)S(1)}, f32[2,512]{1,0:T(2,128)S(1)}, u32[]{:S(2)}, u32[]{:S(2)}) collective-permute-start(f32[2,512]{1,0:T(2,128)S(1)} %add_add_fusion.1), channel_id=1, source_target_pairs={{0,16},{1,17},{2,18},{3,19},{4,20},{5,21},{6,22},{7,23},{8,24},{9,... | collective-permute-start | bytes 12296 | tf_op jit(solution)/shard_map/ppermute | solution.py:17
  114.7 0.7 collective-permute-start.7
  115.7 1.0 copy.111
  117.4 0.7 fusion.43
  118.1 1.1 multiply_reduce_fusion.1
  119.2 6.8 %collective-permute-start.10 = (f32[]{:T(128)}, f32[]{:T(128)}, u32[]{:S(2)}, u32[]{:S(2)}) collective-permute-start(f32[]{:T(128)} %get-tuple-element.39), channel_id=1, source_target_pairs={{0,32},{32,0},{64,96},{96,64},{128,160},{160,128},{192,224},{224,1... | collective-permute-start | bytes 20 | tf_op jit(solution)/shard_map/ppermute | solution.py:17
  126.1 1.0 collective-permute-done.10
  128.4 2.0 %collective-permute-start.11 = (f32[]{:T(128)}, f32[]{:T(128)}, u32[]{:S(2)}, u32[]{:S(2)}) collective-permute-start(f32[]{:T(128)} %add.128), channel_id=1, source_target_pairs={{0,64},{32,96},{64,0},{96,32},{128,192},{160,224},{192,128},{224,1... | collective-permute-start | bytes 20 | tf_op jit(solution)/shard_map/ppermute | solution.py:17
  131.6 3.6 %collective-permute-start.12 = (f32[]{:T(128)}, f32[]{:T(128)}, u32[]{:S(2)}, u32[]{:S(2)}) collective-permute-start(f32[]{:T(128)} %add.129), channel_id=1, source_target_pairs={{0,128},{32,160},{64,192},{96,224},{128,0},{160,32},{192,64},{224,... | collective-permute-start | bytes 20 | tf_op jit(solution)/shard_map/ppermute | solution.py:17
  (85 shorter events, 10.1 us)
Async XLA Ops:
  0.6 7.7 %copy-start = (bf16[1024,1024]{1,0:T(8,128)(2,1)S(1)}, bf16[1024,1024]{1,0:T(8,128)(2,1)}, u32[]{:S(2)}) copy-start(bf16[1024,1024]{1,0:T(8,128)(2,1)} %param.15) | copy-start | bytes 6291460
  0.6 11.5 %copy-start.6 = (bf16[1,256,1024]{2,1,0:T(8,128)(2,1)S(1)}, bf16[1,256,1024]{2,1,0:T(8,128)(2,1)}, u32[]{:S(2)}) copy-start(bf16[1,256,1024]{2,1,0:T(8,128)(2,1)} %param.10) | copy-start | bytes 1572868
  16.5 11.7 %copy-start.3 = (bf16[256,1024]{0,1:T(8,128)(2,1)}, bf16[256,1024]{0,1:T(8,128)(2,1)S(1)}, u32[]{:S(2)}) copy-start(bf16[256,1024]{0,1:T(8,128)(2,1)S(1)} %copy.120) | copy-start | bytes 1572868
  22.5 1.9 %copy-start.1 = (f32[8,512,256]{2,1,0:T(8,128)}, f32[8,512,256]{2,1,0:T(8,128)S(1)}, u32[]{:S(2)}) copy-start(f32[8,512,256]{2,1,0:T(8,128)S(1)} %subtract_exponential_fusion) | copy-start | bytes 12582916
  29.4 28.4 %all-to-all-start = ((f32[32,40,128]{2,1,0:T(8,128)}), f32[32,40,128]{2,1,0:T(8,128)S(1)}, u32[]{:S(2)}, u32[]{:S(2)}) async-start(f32[32,40,128]{2,1,0:T(8,128)} %pad_maximum_fusion), calls=%async_computation | async-start | bytes 1310720 | tf_op jit(solution)/shard_map/all_to_all | solution.py:62
  60.2 28.6 %copy-start.5 = (f32[256,8,128]{0,2,1:T(8,128)S(1)}, f32[256,8,128]{0,2,1:T(8,128)}, u32[]{:S(2)}) copy-start(f32[256,8,128]{0,2,1:T(8,128)} %fusion.1) | copy-start | bytes 3145732
  60.4 28.4 %copy-start.7 = (bf16[32,8,8,128]{3,2,1,0:T(8,128)(2,1)S(1)}, bf16[32,8,8,128]{3,2,1,0:T(8,128)(2,1)}, u32[]{:S(2)}) copy-start(bf16[32,8,8,128]{3,2,1,0:T(8,128)(2,1)} %fusion.4) | copy-start | bytes 1572868
  63.0 27.0 %copy-start.8 = (f32[1024]{0:T(1024)S(1)}, f32[1024]{0:T(1024)}, u32[]{:S(2)}) copy-start(f32[1024]{0:T(1024)} %param.17) | copy-start | bytes 12292
  63.4 26.8 %copy-start.2 = (f32[8,512,256]{2,1,0:T(8,128)S(1)}, f32[8,512,256]{2,1,0:T(8,128)}, u32[]{:S(2)}) copy-start(f32[8,512,256]{2,1,0:T(8,128)} %copy-done.1) | copy-start | bytes 12582916
  63.4 26.8 %copy-start.4 = (bf16[512,1024]{1,0:T(8,128)(2,1)S(1)}, bf16[512,1024]{1,0:T(8,128)(2,1)}, u32[]{:S(2)}) copy-start(bf16[512,1024]{1,0:T(8,128)(2,1)} %param.19) | copy-start | bytes 3145732
  90.9 18.3 %copy-start.9 = (s32[1,2]{1,0:T(1,128)S(1)}, s32[1,2]{1,0:T(1,128)}, u32[]{:S(2)}) copy-start(s32[1,2]{1,0:T(1,128)} %param.12) | copy-start | bytes 28
  96.3 11.4 %collective-permute-start.6 = (f32[2,512]{1,0:T(2,128)S(1)}, f32[2,512]{1,0:T(2,128)S(1)}, u32[]{:S(2)}, u32[]{:S(2)}) collective-permute-start(f32[2,512]{1,0:T(2,128)S(1)} %fusion.38), channel_id=1, source_target_pairs={{0,7},{1,6},{2,5},{3,4},{4,3},{5,2},{6,1},{7,0},{8,15},{9,14},{10,... | collective-permute-start | bytes 12296 | tf_op jit(solution)/shard_map/ppermute | solution.py:17
  98.2 11.0 %collective-permute-start.5 = (f32[2,512]{1,0:T(2,128)S(1)}, f32[2,512]{1,0:T(2,128)S(1)}, u32[]{:S(2)}, u32[]{:S(2)}) collective-permute-start(f32[2,512]{1,0:T(2,128)S(1)} %fusion.38), channel_id=1, source_target_pairs={{0,6},{1,7},{2,4},{3,5},{4,2},{5,3},{6,0},{7,1},{8,14},{9,15},{10,... | collective-permute-start | bytes 12296 | tf_op jit(solution)/shard_map/ppermute | solution.py:17
  102.4 6.9 %collective-permute-start.4 = (f32[2,512]{1,0:T(2,128)S(1)}, f32[2,512]{1,0:T(2,128)S(1)}, u32[]{:S(2)}, u32[]{:S(2)}) collective-permute-start(f32[2,512]{1,0:T(2,128)S(1)} %fusion.38), channel_id=1, source_target_pairs={{0,5},{1,4},{2,7},{3,6},{4,1},{5,0},{6,3},{7,2},{8,13},{9,12},{10,... | collective-permute-start | bytes 12296 | tf_op jit(solution)/shard_map/ppermute | solution.py:17
  103.0 6.4 %collective-permute-start.3 = (f32[2,512]{1,0:T(2,128)S(1)}, f32[2,512]{1,0:T(2,128)S(1)}, u32[]{:S(2)}, u32[]{:S(2)}) collective-permute-start(f32[2,512]{1,0:T(2,128)S(1)} %fusion.38), channel_id=1, source_target_pairs={{0,4},{1,5},{2,6},{3,7},{4,0},{5,1},{6,2},{7,3},{8,12},{9,13},{10,... | collective-permute-start | bytes 12296 | tf_op jit(solution)/shard_map/ppermute | solution.py:17
  104.8 4.6 %collective-permute-start.2 = (f32[2,512]{1,0:T(2,128)S(1)}, f32[2,512]{1,0:T(2,128)S(1)}, u32[]{:S(2)}, u32[]{:S(2)}) collective-permute-start(f32[2,512]{1,0:T(2,128)S(1)} %fusion.38), channel_id=1, source_target_pairs={{0,3},{1,2},{2,1},{3,0},{4,7},{5,6},{6,5},{7,4},{8,11},{9,10},{10,... | collective-permute-start | bytes 12296 | tf_op jit(solution)/shard_map/ppermute | solution.py:17
  107.7 3.4 %collective-permute-start.1 = (f32[2,512]{1,0:T(2,128)S(1)}, f32[2,512]{1,0:T(2,128)S(1)}, u32[]{:S(2)}, u32[]{:S(2)}) collective-permute-start(f32[2,512]{1,0:T(2,128)S(1)} %fusion.38), channel_id=1, source_target_pairs={{0,2},{1,3},{2,0},{3,1},{4,6},{5,7},{6,4},{7,5},{8,10},{9,11},{10,... | collective-permute-start | bytes 12296 | tf_op jit(solution)/shard_map/ppermute | solution.py:17
  109.2 2.8 %collective-permute-start = (f32[2,512]{1,0:T(2,128)S(1)}, f32[2,512]{1,0:T(2,128)S(1)}, u32[]{:S(2)}, u32[]{:S(2)}) collective-permute-start(f32[2,512]{1,0:T(2,128)S(1)} %fusion.38), channel_id=1, source_target_pairs={{0,1},{1,0},{2,3},{3,2},{4,5},{5,4},{6,7},{7,6},{8,9},{9,8},{10,11... | collective-permute-start | bytes 12296 | tf_op jit(solution)/shard_map/ppermute | solution.py:17
  112.0 4.7 %collective-permute-start.9 = (f32[2,512]{1,0:T(2,128)S(1)}, f32[2,512]{1,0:T(2,128)S(1)}, u32[]{:S(2)}, u32[]{:S(2)}) collective-permute-start(f32[2,512]{1,0:T(2,128)S(1)} %add_add_fusion.1), channel_id=1, source_target_pairs={{0,24},{1,25},{2,26},{3,27},{4,28},{5,29},{6,30},{7,31},{8,16},{9,... | collective-permute-start | bytes 12296 | tf_op jit(solution)/shard_map/ppermute | solution.py:17
  112.9 4.0 %collective-permute-start.8 = (f32[2,512]{1,0:T(2,128)S(1)}, f32[2,512]{1,0:T(2,128)S(1)}, u32[]{:S(2)}, u32[]{:S(2)}) collective-permute-start(f32[2,512]{1,0:T(2,128)S(1)} %add_add_fusion.1), channel_id=1, source_target_pairs={{0,16},{1,17},{2,18},{3,19},{4,20},{5,21},{6,22},{7,23},{8,24},{9,... | collective-permute-start | bytes 12296 | tf_op jit(solution)/shard_map/ppermute | solution.py:17
  114.7 2.7 %collective-permute-start.7 = (f32[2,512]{1,0:T(2,128)S(1)}, f32[2,512]{1,0:T(2,128)S(1)}, u32[]{:S(2)}, u32[]{:S(2)}) collective-permute-start(f32[2,512]{1,0:T(2,128)S(1)} %add_add_fusion.1), channel_id=1, source_target_pairs={{0,8},{1,9},{2,10},{3,11},{4,12},{5,13},{6,14},{7,15},{8,0},{9,1},... | collective-permute-start | bytes 12296 | tf_op jit(solution)/shard_map/ppermute | solution.py:17
  119.2 7.8 %collective-permute-start.10 = (f32[]{:T(128)}, f32[]{:T(128)}, u32[]{:S(2)}, u32[]{:S(2)}) collective-permute-start(f32[]{:T(128)} %get-tuple-element.39), channel_id=1, source_target_pairs={{0,32},{32,0},{64,96},{96,64},{128,160},{160,128},{192,224},{224,1... | collective-permute-start | bytes 20 | tf_op jit(solution)/shard_map/ppermute | solution.py:17
  128.4 2.6 %collective-permute-start.11 = (f32[]{:T(128)}, f32[]{:T(128)}, u32[]{:S(2)}, u32[]{:S(2)}) collective-permute-start(f32[]{:T(128)} %add.128), channel_id=1, source_target_pairs={{0,64},{32,96},{64,0},{96,32},{128,192},{160,224},{192,128},{224,1... | collective-permute-start | bytes 20 | tf_op jit(solution)/shard_map/ppermute | solution.py:17
  131.6 4.1 %collective-permute-start.12 = (f32[]{:T(128)}, f32[]{:T(128)}, u32[]{:S(2)}, u32[]{:S(2)}) collective-permute-start(f32[]{:T(128)} %add.129), channel_id=1, source_target_pairs={{0,128},{32,160},{64,192},{96,224},{128,0},{160,32},{192,64},{224,... | collective-permute-start | bytes 20 | tf_op jit(solution)/shard_map/ppermute | solution.py:17

commit v12 on v9

--- a/solution.py
+++ b/solution.py
@@ -124,8 +124,18 @@
 
     last_cum = decay_cum[:, tok_rows - 1]
     k_factor = jnp.where(tail_rec[None, :], jnp.exp(last_cum[:, None] - decay_cum), 0.0)
-    k_decayed = (k3.astype(jnp.float32) * k_factor.T[:, :, None]).astype(jnp.bfloat16)
-    local_state = jnp.einsum("thd,the->hde", k_decayed, v3, preferred_element_type=jnp.float32)
+    k_decayed = (
+        key_rows.astype(jnp.float32) * jnp.repeat(k_factor.T, head_dim, axis=1)
+    ).astype(jnp.bfloat16)
+    full_state = lax.dot_general(
+        k_decayed, value_rows, (((0,), (0,)), ((), ())), preferred_element_type=jnp.float32
+    )
+    local_state = jnp.stack(
+        [
+            full_state[h * head_dim:(h + 1) * head_dim, h * head_dim:(h + 1) * head_dim]
+            for h in range(head_count)
+        ]
+    )
     carry = jnp.where(linked[tok_rows - 1], jnp.exp(last_cum), 0.0)
 
     scores = jnp.einsum("thd,shd->hts", q3, k3, preferred_element_type=jnp.float32) * qk_scale

time: 138 us -> 134 us (0.971)
  waiting for transfers between devices: 15.3 us -> 13.3 us
  matrix products: 17.1 us -> 15.2 us
  local copies, waits for them, and re-layouts: 16 us -> 14.5 us
    all_to_all x1, waiting for transfers between devices: 9.72 us -> 7.64 us  [exclusive_state_scan(): got = lax.all_to_all(jnp.concatenate([slices, extra], axis=1), axis, 0, 0)]
    unnamed x31 -> x42, local copies, waits for them, and re-layouts: 6.62 us -> 5.87 us
  transfers between devices with their start and end apart: 14 -> 14, of which waited for: 7 -> 7; matrix products, arithmetic and copies ran while one was open for 6% -> 7% of each run, Pallas kernels for 0% -> 0%
where the time goes in v12:
time: 134 us; the launch traced here: 133 us
  starting transfers between devices  41.5 us (31%)
  blocking collectives  25.3 us (19%)
  other arithmetic  17.2 us (13%)
  matrix products  15.2 us (11%)
  local copies, waits for them, and re-layouts  14.5 us (11%)
  waiting for transfers between devices  13.3 us (10%)
  between operations  5.76 us (4%)
    ppermute x13, starting transfers between devices, swapped(): return lax.ppermute(x, axis, [(i, i ^ bit) for i in range(count)])  29.3 us
    all_to_all x1, blocking collectives, exclusive_state_scan(): back = lax.all_to_all(sent_back, axis, 0, 0)  25.3 us
    all_to_all x1, starting transfers between devices, exclusive_state_scan(): got = lax.all_to_all(jnp.concatenate([slices, extra], axis=1), axis, 0, 0)  12.2 us
    all_to_all x1, waiting for transfers between devices, exclusive_state_scan(): got = lax.all_to_all(jnp.concatenate([slices, extra], axis=1), axis, 0, 0)  7.64 us
    unnamed x42, local copies, waits for them, and re-layouts  5.87 us
    ppermute x13, waiting for transfers between devices, swapped(): return lax.ppermute(x, axis, [(i, i ^ bit) for i in range(count)])  5.64 us
    dot_general x1, matrix products, local(): jnp.einsum('hts,shd->thd', weights, v3, preferred_element_type=jnp.float32)  3.26 us
    dot_general x1, matrix products, local(): jnp.dot(features, w_query, preferred_element_type=jnp.float32)  3.1 us
  transfers between devices with their start and end apart: 14, of which 7 were waited for; matrix products, arithmetic and copies ran while one was open for 7% of the time, Pallas kernels for 0%

profile of v12, /device:TPU:1, one launch (start us, length us, event | category | flops | bytes accessed | tf_op | source)
XLA Modules:
  0.0 132.7 jit_solution(1316256578530841544)
XLA Ops:
  0.7 1.0 reduce-window.10
  1.6 0.7 bitcast_subtract_fusion.1
  3.0 1.3 fusion.58
  4.9 1.3 reduce-window.11
  6.4 0.7 broadcast_compare_fusion.1
  8.1 1.8 %convolution_convert_fusion.1 = bf16[256,1024]{1,0:T(8,128)(2,1)S(1)} fusion(bf16[1024,1024]{1,0:T(8,128)(2,1)S(1)} %copy-done, bf16[1,256,1024]{2,1,0:T(8,128)(2,1)} %param.10), kind=kOutput, calls=%fused_computation.15 | convolution fusion | flops 537133056 | bytes 3145728 | tf_op jit(solution)/shard_map/dot_general | solution.py:116
  9.9 2.6 %convolution_convert_fusion.2 = bf16[256,1024]{1,0:T(8,128)(2,1)S(1)} fusion(bf16[1024,1024]{1,0:T(8,128)(2,1)} %param.15, bf16[1,256,1024]{2,1,0:T(8,128)(2,1)} %param.10), kind=kOutput, calls=%fused_computation.16 | convolution fusion | flops 537133056 | bytes 3145728 | tf_op jit(solution)/shard_map/dot_general | solution.py:115
  12.9 0.9 fusion.17
  14.3 0.7 convolution_multiply_fusion
  15.0 1.2 select_reduce_fusion.3
  16.2 1.5 %select_reduce_fusion.2 = f32[8,512,256]{2,1,0:T(8,128)S(1)} fusion(f32[8,2,512]{2,1,0:T(2,128)S(1)} %select_reduce_fusion.3, pred[2,256]{1,0:T(4,128)(4,1)S(1)} %iota_compare_fusion.6), kind=kLoop, calls=%fused_computation.3 | loop fusion | flops 3145728 | bytes 4227584 | tf_op jit(solution)/shard_map/reduce_sum | solution.py:154
  17.8 1.2 subtract_exponential_fusion
  19.0 1.9 %copy-done.1 = f32[8,512,256]{2,1,0:T(8,128)} copy-done((f32[8,512,256]{2,1,0:T(8,128)}, f32[8,512,256]{2,1,0:T(8,128)S(1)}, u32[]{:S(2)}) %copy-start.1) | copy-done | bytes 4194328
  20.9 1.2 select_reduce_fusion.1
  22.9 0.7 broadcast_select_fusion
  23.6 0.7 gather_fusion
  24.6 0.9 pad_maximum_fusion
  25.5 12.2 %all-to-all-start = ((f32[32,40,128]{2,1,0:T(8,128)}), f32[32,40,128]{2,1,0:T(8,128)S(1)}, u32[]{:S(2)}, u32[]{:S(2)}) async-start(f32[32,40,128]{2,1,0:T(8,128)} %pad_maximum_fusion), calls=%async_computation | async-start | bytes 1310720 | tf_op jit(solution)/shard_map/all_to_all | solution.py:62
  37.7 2.1 %copy.105 = bf16[256,1024]{0,1:T(8,128)(2,1)} copy(bf16[256,1024]{1,0:T(8,128)(2,1)} %copy-done.3) | data formatting | bytes 1048576 | tf_op jit(solution)/shard_map/reshape | solution.py:119
  39.9 3.1 %fusion.4 = bf16[32,8,8,128]{3,2,1,0:T(8,128)(2,1)} fusion(bf16[1024,1024]{1,0:T(8,128)(2,1)} %param.14, bf16[1,256,1024]{2,1,0:T(8,128)(2,1)S(1)} %copy-done.9), kind=kOutput, calls=%fused_computation.17 | convolution fusion | flops 537133056 | bytes 3145728 | tf_op jit(solution)/shard_map/dot_general | solution.py:114
  43.0 3.3 %fusion.1 = f32[256,8,128]{0,2,1:T(8,128)} fusion(bf16[256,8,128]{0,2,1:T(8,128)(2,1)} %bitcast.185, f32[8,256]{1,0:T(8,128)S(1)} %get-tuple-element.31, pred[256,256]{1,0:T(8,128)(4,1)S(1)} %fusion.40, bf16[32,8,8,128]{3,2,1,0:T(8,128)(2,1)} %fusion.4, bf16[256,1024]{1,0:T(8,128)(2,1)} %copy-done.4), kind=kOutput, calls=%fused_computation.10 | convolution fusion | flops 271581184 | bytes 2695168 | tf_op jit(solution)/shard_map/hts,shd->thd/dot_general | solution.py:144
  46.3 7.6 %all-to-all-done = f32[32,40,128]{2,1,0:T(8,128)S(1)} async-done(((f32[32,40,128]{2,1,0:T(8,128)}), f32[32,40,128]{2,1,0:T(8,128)S(1)}, u32[]{:S(2)}, u32[]{:S(2)}) %all-to-all-start) | async-done | bytes 655392 | tf_op jit(solution)/shard_map/all_to_all | solution.py:62
  56.3 0.9 fusion.19
  57.7 25.3 %all_to_all.10 = f32[32,40,128]{2,1,0:T(8,128)S(1)} all-to-all(f32[32,40,128]{2,1,0:T(8,128)S(1)} %copy.93), channel_id=1, replica_groups=mesh['dp'=8,'ctx'=32] {'ctx'}, dimensions={0} | all-to-all | bytes 1310720 | tf_op jit(solution)/shard_map/all_to_all | solution.py:84
  83.1 1.0 fusion.65
  84.5 0.7 bitcast_multiply_fusion
  85.2 1.2 select_reduce_fusion
  87.1 1.1 fusion.64
  88.2 1.2 copy.106
  89.4 1.2 copy.107
  90.7 2.7 %collective-permute-start = (f32[2,512]{1,0:T(2,128)S(1)}, f32[2,512]{1,0:T(2,128)S(1)}, u32[]{:S(2)}, u32[]{:S(2)}) collective-permute-start(f32[2,512]{1,0:T(2,128)S(1)} %fusion.51), channel_id=1, source_target_pairs={{0,1},{1,0},{2,3},{3,2},{4,5},{5,4},{6,7},{7,6},{8,9},{9,8},{10,11... | collective-permute-start | bytes 12296 | tf_op jit(solution)/shard_map/ppermute | solution.py:17
  93.4 0.9 collective-permute-start.1
  94.3 1.3 collective-permute-start.2
  95.6 2.6 %collective-permute-start.3 = (f32[2,512]{1,0:T(2,128)S(1)}, f32[2,512]{1,0:T(2,128)S(1)}, u32[]{:S(2)}, u32[]{:S(2)}) collective-permute-start(f32[2,512]{1,0:T(2,128)S(1)} %fusion.51), channel_id=1, source_target_pairs={{0,4},{1,5},{2,6},{3,7},{4,0},{5,1},{6,2},{7,3},{8,12},{9,13},{10,... | collective-permute-start | bytes 12296 | tf_op jit(solution)/shard_map/ppermute | solution.py:17
  98.2 2.0 %collective-permute-start.4 = (f32[2,512]{1,0:T(2,128)S(1)}, f32[2,512]{1,0:T(2,128)S(1)}, u32[]{:S(2)}, u32[]{:S(2)}) collective-permute-start(f32[2,512]{1,0:T(2,128)S(1)} %fusion.51), channel_id=1, source_target_pairs={{0,5},{1,4},{2,7},{3,6},{4,1},{5,0},{6,3},{7,2},{8,13},{9,12},{10,... | collective-permute-start | bytes 12296 | tf_op jit(solution)/shard_map/ppermute | solution.py:17
  100.2 1.3 %collective-permute-start.5 = (f32[2,512]{1,0:T(2,128)S(1)}, f32[2,512]{1,0:T(2,128)S(1)}, u32[]{:S(2)}, u32[]{:S(2)}) collective-permute-start(f32[2,512]{1,0:T(2,128)S(1)} %fusion.51), channel_id=1, source_target_pairs={{0,6},{1,7},{2,4},{3,5},{4,2},{5,3},{6,0},{7,1},{8,14},{9,15},{10,... | collective-permute-start | bytes 12296 | tf_op jit(solution)/shard_map/ppermute | solution.py:17
  101.6 2.1 %collective-permute-start.6 = (f32[2,512]{1,0:T(2,128)S(1)}, f32[2,512]{1,0:T(2,128)S(1)}, u32[]{:S(2)}, u32[]{:S(2)}) collective-permute-start(f32[2,512]{1,0:T(2,128)S(1)} %fusion.51), channel_id=1, source_target_pairs={{0,7},{1,6},{2,5},{3,4},{4,3},{5,2},{6,1},{7,0},{8,15},{9,14},{10,... | collective-permute-start | bytes 12296 | tf_op jit(solution)/shard_map/ppermute | solution.py:17
  103.7 1.1 collective-permute-done.5
  105.3 1.3 collective-permute-start.7
  106.6 2.3 %collective-permute-start.8 = (f32[2,512]{1,0:T(2,128)S(1)}, f32[2,512]{1,0:T(2,128)S(1)}, u32[]{:S(2)}, u32[]{:S(2)}) collective-permute-start(f32[2,512]{1,0:T(2,128)S(1)} %add_add_fusion.1), channel_id=1, source_target_pairs={{0,16},{1,17},{2,18},{3,19},{4,20},{5,21},{6,22},{7,23},{8,24},{9,... | collective-permute-start | bytes 12296 | tf_op jit(solution)/shard_map/ppermute | solution.py:17
  109.6 1.0 copy.101
  110.6 2.0 %collective-permute-done.9 = f32[2,512]{1,0:T(2,128)S(1)} collective-permute-done((f32[2,512]{1,0:T(2,128)S(1)}, f32[2,512]{1,0:T(2,128)S(1)}, u32[]{:S(2)}, u32[]{:S(2)}) %collective-permute-start.9) | collective-permute-done | bytes 4128 | tf_op jit(solution)/shard_map/ppermute | solution.py:17
  112.6 0.7 fusion.56
  113.3 1.1 multiply_reduce_fusion.1
  114.4 6.8 %collective-permute-start.10 = (f32[]{:T(128)}, f32[]{:T(128)}, u32[]{:S(2)}, u32[]{:S(2)}) collective-permute-start(f32[]{:T(128)} %get-tuple-element.36), channel_id=1, source_target_pairs={{0,32},{32,0},{64,96},{96,64},{128,160},{160,128},{192,224},{224,1... | collective-permute-start | bytes 20 | tf_op jit(solution)/shard_map/ppermute | solution.py:17
  121.2 1.0 collective-permute-done.10
  123.5 2.0 %collective-permute-start.11 = (f32[]{:T(128)}, f32[]{:T(128)}, u32[]{:S(2)}, u32[]{:S(2)}) collective-permute-start(f32[]{:T(128)} %add.147), channel_id=1, source_target_pairs={{0,64},{32,96},{64,0},{96,32},{128,192},{160,224},{192,128},{224,1... | collective-permute-start | bytes 20 | tf_op jit(solution)/shard_map/ppermute | solution.py:17
  126.8 3.6 %collective-permute-start.12 = (f32[]{:T(128)}, f32[]{:T(128)}, u32[]{:S(2)}, u32[]{:S(2)}) collective-permute-start(f32[]{:T(128)} %add.148), channel_id=1, source_target_pairs={{0,128},{32,160},{64,192},{96,224},{128,0},{160,32},{192,64},{224,... | collective-permute-start | bytes 20 | tf_op jit(solution)/shard_map/ppermute | solution.py:17
  (104 shorter events, 10.0 us)
Async XLA Ops:
  0.6 7.5 %copy-start = (bf16[1024,1024]{1,0:T(8,128)(2,1)S(1)}, bf16[1024,1024]{1,0:T(8,128)(2,1)}, u32[]{:S(2)}) copy-start(bf16[1024,1024]{1,0:T(8,128)(2,1)} %param.16) | copy-start | bytes 6291460
  9.9 3.9 %copy-start.3 = (bf16[256,1024]{1,0:T(8,128)(2,1)}, bf16[256,1024]{1,0:T(8,128)(2,1)S(1)}, u32[]{:S(2)}) copy-start(bf16[256,1024]{1,0:T(8,128)(2,1)S(1)} %convolution_convert_fusion.1) | copy-start | bytes 1572868
  12.6 1.3 copy-start.4
  12.9 1.1 copy-start.8
  12.9 1.4 %copy-start.7 = (bf16[512,1024]{1,0:T(8,128)(2,1)S(1)}, bf16[512,1024]{1,0:T(8,128)(2,1)}, u32[]{:S(2)}) copy-start(bf16[512,1024]{1,0:T(8,128)(2,1)} %param.18) | copy-start | bytes 3145732
  19.0 1.9 %copy-start.1 = (f32[8,512,256]{2,1,0:T(8,128)}, f32[8,512,256]{2,1,0:T(8,128)S(1)}, u32[]{:S(2)}) copy-start(f32[8,512,256]{2,1,0:T(8,128)S(1)} %subtract_exponential_fusion) | copy-start | bytes 12582916
  20.9 1.2 copy-start.13
  24.3 15.6 %copy-start.9 = (bf16[1,256,1024]{2,1,0:T(8,128)(2,1)S(1)}, bf16[1,256,1024]{2,1,0:T(8,128)(2,1)}, u32[]{:S(2)}) copy-start(bf16[1,256,1024]{2,1,0:T(8,128)(2,1)} %param.10) | copy-start | bytes 1572868
  25.5 28.4 %all-to-all-start = ((f32[32,40,128]{2,1,0:T(8,128)}), f32[32,40,128]{2,1,0:T(8,128)S(1)}, u32[]{:S(2)}, u32[]{:S(2)}) async-start(f32[32,40,128]{2,1,0:T(8,128)} %pad_maximum_fusion), calls=%async_computation | async-start | bytes 1310720 | tf_op jit(solution)/shard_map/all_to_all | solution.py:62
  55.4 27.7 %copy-start.10 = (bf16[32,8,8,128]{3,2,1,0:T(8,128)(2,1)S(1)}, bf16[32,8,8,128]{3,2,1,0:T(8,128)(2,1)}, u32[]{:S(2)}) copy-start(bf16[32,8,8,128]{3,2,1,0:T(8,128)(2,1)} %fusion.4) | copy-start | bytes 1572868
  55.7 27.4 %copy-start.6 = (f32[256,8,128]{0,2,1:T(8,128)S(1)}, f32[256,8,128]{0,2,1:T(8,128)}, u32[]{:S(2)}) copy-start(f32[256,8,128]{0,2,1:T(8,128)} %fusion.1) | copy-start | bytes 3145732
  57.3 27.0 %copy-start.11 = (f32[1024]{0:T(1024)S(1)}, f32[1024]{0:T(1024)}, u32[]{:S(2)}) copy-start(f32[1024]{0:T(1024)} %param.17) | copy-start | bytes 12292
  57.7 26.8 %copy-start.2 = (f32[8,512,256]{2,1,0:T(8,128)S(1)}, f32[8,512,256]{2,1,0:T(8,128)}, u32[]{:S(2)}) copy-start(f32[8,512,256]{2,1,0:T(8,128)} %copy-done.1) | copy-start | bytes 12582916
  57.7 26.8 %copy-start.5 = (bf16[512,1024]{1,0:T(8,128)(2,1)S(1)}, bf16[512,1024]{1,0:T(8,128)(2,1)}, u32[]{:S(2)}) copy-start(bf16[512,1024]{1,0:T(8,128)(2,1)} %param.19) | copy-start | bytes 3145732
  85.2 18.4 %copy-start.12 = (s32[1,2]{1,0:T(1,128)S(1)}, s32[1,2]{1,0:T(1,128)}, u32[]{:S(2)}) copy-start(s32[1,2]{1,0:T(1,128)} %param.12) | copy-start | bytes 28
  90.7 9.6 %collective-permute-start = (f32[2,512]{1,0:T(2,128)S(1)}, f32[2,512]{1,0:T(2,128)S(1)}, u32[]{:S(2)}, u32[]{:S(2)}) collective-permute-start(f32[2,512]{1,0:T(2,128)S(1)} %fusion.51), channel_id=1, source_target_pairs={{0,1},{1,0},{2,3},{3,2},{4,5},{5,4},{6,7},{7,6},{8,9},{9,8},{10,11... | collective-permute-start | bytes 12296 | tf_op jit(solution)/shard_map/ppermute | solution.py:17
  93.4 8.2 %collective-permute-start.1 = (f32[2,512]{1,0:T(2,128)S(1)}, f32[2,512]{1,0:T(2,128)S(1)}, u32[]{:S(2)}, u32[]{:S(2)}) collective-permute-start(f32[2,512]{1,0:T(2,128)S(1)} %fusion.51), channel_id=1, source_target_pairs={{0,2},{1,3},{2,0},{3,1},{4,6},{5,7},{6,4},{7,5},{8,10},{9,11},{10,... | collective-permute-start | bytes 12296 | tf_op jit(solution)/shard_map/ppermute | solution.py:17
  94.3 9.4 %collective-permute-start.2 = (f32[2,512]{1,0:T(2,128)S(1)}, f32[2,512]{1,0:T(2,128)S(1)}, u32[]{:S(2)}, u32[]{:S(2)}) collective-permute-start(f32[2,512]{1,0:T(2,128)S(1)} %fusion.51), channel_id=1, source_target_pairs={{0,3},{1,2},{2,1},{3,0},{4,7},{5,6},{6,5},{7,4},{8,11},{9,10},{10,... | collective-permute-start | bytes 12296 | tf_op jit(solution)/shard_map/ppermute | solution.py:17
  95.6 8.1 %collective-permute-start.3 = (f32[2,512]{1,0:T(2,128)S(1)}, f32[2,512]{1,0:T(2,128)S(1)}, u32[]{:S(2)}, u32[]{:S(2)}) collective-permute-start(f32[2,512]{1,0:T(2,128)S(1)} %fusion.51), channel_id=1, source_target_pairs={{0,4},{1,5},{2,6},{3,7},{4,0},{5,1},{6,2},{7,3},{8,12},{9,13},{10,... | collective-permute-start | bytes 12296 | tf_op jit(solution)/shard_map/ppermute | solution.py:17
  98.2 5.5 %collective-permute-start.4 = (f32[2,512]{1,0:T(2,128)S(1)}, f32[2,512]{1,0:T(2,128)S(1)}, u32[]{:S(2)}, u32[]{:S(2)}) collective-permute-start(f32[2,512]{1,0:T(2,128)S(1)} %fusion.51), channel_id=1, source_target_pairs={{0,5},{1,4},{2,7},{3,6},{4,1},{5,0},{6,3},{7,2},{8,13},{9,12},{10,... | collective-permute-start | bytes 12296 | tf_op jit(solution)/shard_map/ppermute | solution.py:17
  100.2 4.6 %collective-permute-start.5 = (f32[2,512]{1,0:T(2,128)S(1)}, f32[2,512]{1,0:T(2,128)S(1)}, u32[]{:S(2)}, u32[]{:S(2)}) collective-permute-start(f32[2,512]{1,0:T(2,128)S(1)} %fusion.51), channel_id=1, source_target_pairs={{0,6},{1,7},{2,4},{3,5},{4,2},{5,3},{6,0},{7,1},{8,14},{9,15},{10,... | collective-permute-start | bytes 12296 | tf_op jit(solution)/shard_map/ppermute | solution.py:17
  101.6 3.7 %collective-permute-start.6 = (f32[2,512]{1,0:T(2,128)S(1)}, f32[2,512]{1,0:T(2,128)S(1)}, u32[]{:S(2)}, u32[]{:S(2)}) collective-permute-start(f32[2,512]{1,0:T(2,128)S(1)} %fusion.51), channel_id=1, source_target_pairs={{0,7},{1,6},{2,5},{3,4},{4,3},{5,2},{6,1},{7,0},{8,15},{9,14},{10,... | collective-permute-start | bytes 12296 | tf_op jit(solution)/shard_map/ppermute | solution.py:17
  105.3 5.3 %collective-permute-start.7 = (f32[2,512]{1,0:T(2,128)S(1)}, f32[2,512]{1,0:T(2,128)S(1)}, u32[]{:S(2)}, u32[]{:S(2)}) collective-permute-start(f32[2,512]{1,0:T(2,128)S(1)} %add_add_fusion.1), channel_id=1, source_target_pairs={{0,8},{1,9},{2,10},{3,11},{4,12},{5,13},{6,14},{7,15},{8,0},{9,1},... | collective-permute-start | bytes 12296 | tf_op jit(solution)/shard_map/ppermute | solution.py:17
  106.6 4.0 %collective-permute-start.8 = (f32[2,512]{1,0:T(2,128)S(1)}, f32[2,512]{1,0:T(2,128)S(1)}, u32[]{:S(2)}, u32[]{:S(2)}) collective-permute-start(f32[2,512]{1,0:T(2,128)S(1)} %add_add_fusion.1), channel_id=1, source_target_pairs={{0,16},{1,17},{2,18},{3,19},{4,20},{5,21},{6,22},{7,23},{8,24},{9,... | collective-permute-start | bytes 12296 | tf_op jit(solution)/shard_map/ppermute | solution.py:17
  108.9 3.7 %collective-permute-start.9 = (f32[2,512]{1,0:T(2,128)S(1)}, f32[2,512]{1,0:T(2,128)S(1)}, u32[]{:S(2)}, u32[]{:S(2)}) collective-permute-start(f32[2,512]{1,0:T(2,128)S(1)} %add_add_fusion.1), channel_id=1, source_target_pairs={{0,24},{1,25},{2,26},{3,27},{4,28},{5,29},{6,30},{7,31},{8,16},{9,... | collective-permute-start | bytes 12296 | tf_op jit(solution)/shard_map/ppermute | solution.py:17
  114.4 7.8 %collective-permute-start.10 = (f32[]{:T(128)}, f32[]{:T(128)}, u32[]{:S(2)}, u32[]{:S(2)}) collective-permute-start(f32[]{:T(128)} %get-tuple-element.36), channel_id=1, source_target_pairs={{0,32},{32,0},{64,96},{96,64},{128,160},{160,128},{192,224},{224,1... | collective-permute-start | bytes 20 | tf_op jit(solution)/shard_map/ppermute | solution.py:17
  123.5 2.6 %collective-permute-start.11 = (f32[]{:T(128)}, f32[]{:T(128)}, u32[]{:S(2)}, u32[]{:S(2)}) collective-permute-start(f32[]{:T(128)} %add.147), channel_id=1, source_target_pairs={{0,64},{32,96},{64,0},{96,32},{128,192},{160,224},{192,128},{224,1... | collective-permute-start | bytes 20 | tf_op jit(solution)/shard_map/ppermute | solution.py:17
  126.8 4.1 %collective-permute-start.12 = (f32[]{:T(128)}, f32[]{:T(128)}, u32[]{:S(2)}, u32[]{:S(2)}) collective-permute-start(f32[]{:T(128)} %add.148), channel_id=1, source_target_pairs={{0,128},{32,160},{64,192},{96,224},{128,0},{160,32},{192,64},{224,... | collective-permute-start | bytes 20 | tf_op jit(solution)/shard_map/ppermute | solution.py:17

commit v13 on v12

--- a/solution.py
+++ b/solution.py
@@ -36,7 +36,8 @@
 
 
 def record_ids(length_row, positions):
-    starts = jnp.cumsum(length_row) - length_row
+    order = jnp.arange(length_row.shape[0])
+    starts = jnp.sum(jnp.where(order[None, :] < order[:, None], length_row[None, :], 0), axis=1)
     return jnp.sum((starts[:, None] <= positions[None, :]).astype(jnp.int32), axis=0) - 1
 
 
@@ -49,12 +50,11 @@
     per_owner = pair_count // count
     assert per_owner * count == pair_count and per_owner * fields < 8 * head_dim
     pad = 8 * head_dim - per_owner * fields - 1
-    owner_head = (jnp.arange(count) * rows) // head_dim
     slices = local_state.reshape(count, rows, head_dim)
     extra = jnp.concatenate(
         [
             stats.reshape(count, per_owner * fields),
-            carry[owner_head][:, None],
+            jnp.repeat(carry, count // head_count)[:, None],
             jnp.zeros((count, pad), jnp.float32),
         ],
         axis=1,
@@ -117,7 +117,8 @@
     q3 = queries.reshape(tok_rows, head_count, head_dim)
     k3 = key_rows.reshape(tok_rows, head_count, head_dim)
     v3 = value_rows.reshape(tok_rows, head_count, head_dim)
-    decay_cum = jnp.cumsum(log_decay[0], axis=1)
+    upper = (local_pos[:, None] <= local_pos[None, :]).astype(jnp.float32)
+    decay_cum = jnp.dot(log_decay[0], upper, precision=lax.Precision.HIGHEST)
     pair_mask = (local_pos[:, None] >= local_pos[None, :]) & (record[:, None] == record[None, :])
     linked = record == before_rec
     tail_rec = record == record[tok_rows - 1]

time: 134 us -> 132 us (0.985)
  other arithmetic: 17.2 us -> 14.5 us
    another operation x3 -> x0, other arithmetic: 2.26 us -> none
  transfers between devices with their start and end apart: 14 -> 14, of which waited for: 7 -> 7; matrix products, arithmetic and copies ran while one was open for 7% -> 8% of each run, Pallas kernels for 0% -> 0%
where the time goes in v13:
time: 132 us; the launch traced here: 130 us
  starting transfers between devices  41.6 us (32%)
  blocking collectives  25.2 us (19%)
  matrix products  16.1 us (12%)
  other arithmetic  14.5 us (11%)
  local copies, waits for them, and re-layouts  13.7 us (10%)
  waiting for transfers between devices  13.3 us (10%)
  between operations  5.74 us (4%)
    ppermute x13, starting transfers between devices, swapped(): return lax.ppermute(x, axis, [(i, i ^ bit) for i in range(count)])  29.4 us
    all_to_all x1, blocking collectives, exclusive_state_scan(): back = lax.all_to_all(sent_back, axis, 0, 0)  25.2 us
    all_to_all x1, starting transfers between devices, exclusive_state_scan(): got = lax.all_to_all(jnp.concatenate([slices, extra], axis=1), axis, 0, 0)  12.2 us
    all_to_all x1, waiting for transfers between devices, exclusive_state_scan(): got = lax.all_to_all(jnp.concatenate([slices, extra], axis=1), axis, 0, 0)  7.65 us
    unnamed x42, local copies, waits for them, and re-layouts  5.86 us
    ppermute x13, waiting for transfers between devices, swapped(): return lax.ppermute(x, axis, [(i, i ^ bit) for i in range(count)])  5.64 us
    dot_general x1, matrix products, local(): jnp.dot(features, w_query, preferred_element_type=jnp.float32)  3.28 us
    dot_general x1, matrix products, local(): jnp.einsum('hts,shd->thd', weights, v3, preferred_element_type=jnp.float32)  3.11 us
  transfers between devices with their start and end apart: 14, of which 7 were waited for; matrix products, arithmetic and copies ran while one was open for 8% of the time, Pallas kernels for 0%

profile of v13, /device:TPU:1, one launch (start us, length us, event | category | flops | bytes accessed | tf_op | source)
XLA Modules:
  0.0 130.1 jit_solution(11813530243065085152)
XLA Ops:
  0.7 0.9 fusion.60
  1.7 0.6 slice.72
  2.3 0.6 fusion.61
  3.5 0.8 fusion.41
  4.6 0.7 broadcast_compare_fusion.1
  6.1 1.8 %convolution_convert_fusion.1 = bf16[256,1024]{1,0:T(8,128)(2,1)S(1)} fusion(bf16[1024,1024]{1,0:T(8,128)(2,1)S(1)} %copy-done, bf16[1,256,1024]{2,1,0:T(8,128)(2,1)} %param.10), kind=kOutput, calls=%fused_computation.14 | convolution fusion | flops 537133056 | bytes 3145728 | tf_op jit(solution)/shard_map/dot_general | solution.py:116
  7.9 2.6 %convolution_convert_fusion.2 = bf16[256,1024]{1,0:T(8,128)(2,1)S(1)} fusion(bf16[1024,1024]{1,0:T(8,128)(2,1)} %param.15, bf16[1,256,1024]{2,1,0:T(8,128)(2,1)} %param.10), kind=kOutput, calls=%fused_computation.15 | convolution fusion | flops 537133056 | bytes 3145728 | tf_op jit(solution)/shard_map/dot_general | solution.py:115
  10.9 0.9 fusion.17
  12.3 0.7 convolution_multiply_fusion
  13.0 1.2 select_reduce_fusion.3
  14.2 1.5 %select_reduce_fusion.2 = f32[8,512,256]{2,1,0:T(8,128)S(1)} fusion(f32[8,2,512]{2,1,0:T(2,128)S(1)} %select_reduce_fusion.3, pred[2,256]{1,0:T(4,128)(4,1)S(1)} %iota_compare_fusion.8), kind=kLoop, calls=%fused_computation.2 | loop fusion | flops 3145728 | bytes 4227584 | tf_op jit(solution)/shard_map/reduce_sum | solution.py:155
  15.7 1.2 subtract_exponential_fusion
  17.0 1.9 %copy-done.1 = f32[8,512,256]{2,1,0:T(8,128)} copy-done((f32[8,512,256]{2,1,0:T(8,128)}, f32[8,512,256]{2,1,0:T(8,128)S(1)}, u32[]{:S(2)}) %copy-start.1) | copy-done | bytes 4194328
  18.9 1.2 select_reduce_fusion.1
  20.9 0.7 broadcast_select_fusion
  21.9 0.9 pad_maximum_fusion
  22.8 12.2 %all-to-all-start = ((f32[32,40,128]{2,1,0:T(8,128)}), f32[32,40,128]{2,1,0:T(8,128)S(1)}, u32[]{:S(2)}, u32[]{:S(2)}) async-start(f32[32,40,128]{2,1,0:T(8,128)} %pad_maximum_fusion), calls=%async_computation | async-start | bytes 1310720 | tf_op jit(solution)/shard_map/all_to_all | solution.py:62
  35.1 2.0 %copy.103 = bf16[256,1024]{0,1:T(8,128)(2,1)} copy(bf16[256,1024]{1,0:T(8,128)(2,1)} %copy-done.3) | data formatting | bytes 1048576 | tf_op jit(solution)/shard_map/reshape | solution.py:119
  37.2 3.3 %fusion.4 = bf16[32,8,8,128]{3,2,1,0:T(8,128)(2,1)} fusion(bf16[1024,1024]{1,0:T(8,128)(2,1)} %param.14, bf16[1,256,1024]{2,1,0:T(8,128)(2,1)} %param.10), kind=kOutput, calls=%fused_computation.16 | convolution fusion | flops 537133056 | bytes 3145728 | tf_op jit(solution)/shard_map/dot_general | solution.py:114
  40.5 3.1 %fusion.1 = f32[256,8,128]{0,2,1:T(8,128)} fusion(bf16[256,8,128]{0,2,1:T(8,128)(2,1)} %bitcast.171, f32[8,256]{1,0:T(8,128)S(1)} %bitcast.179, pred[256,256]{1,0:T(8,128)(4,1)S(1)} %fusion.40, bf16[32,8,8,128]{3,2,1,0:T(8,128)(2,1)} %fusion.4, bf16[256,1024]{1,0:T(8,128)(2,1)S(1)} %copy-done.5), kind=kOutput, calls=%fused_computation.9 | convolution fusion | flops 271581184 | bytes 2695168 | tf_op jit(solution)/shard_map/hts,shd->thd/dot_general | solution.py:145
  43.6 7.6 %all-to-all-done = f32[32,40,128]{2,1,0:T(8,128)S(1)} async-done(((f32[32,40,128]{2,1,0:T(8,128)}), f32[32,40,128]{2,1,0:T(8,128)S(1)}, u32[]{:S(2)}, u32[]{:S(2)}) %all-to-all-start) | async-done | bytes 655392 | tf_op jit(solution)/shard_map/all_to_all | solution.py:62
  53.1 0.6 select_reduce_fusion.4
  53.7 0.9 fusion.19
  55.0 25.2 %all_to_all.10 = f32[32,40,128]{2,1,0:T(8,128)S(1)} all-to-all(f32[32,40,128]{2,1,0:T(8,128)S(1)} %copy.91), channel_id=1, replica_groups=mesh['dp'=8,'ctx'=32] {'ctx'}, dimensions={0} | all-to-all | bytes 1310720 | tf_op jit(solution)/shard_map/all_to_all | solution.py:84
  80.4 1.0 fusion.66
  81.8 0.7 bitcast_multiply_fusion
  82.5 1.2 select_reduce_fusion
  84.4 1.1 fusion.65
  85.5 1.2 copy.104
  86.7 1.2 copy.105
  88.0 2.8 %collective-permute-start = (f32[2,512]{1,0:T(2,128)S(1)}, f32[2,512]{1,0:T(2,128)S(1)}, u32[]{:S(2)}, u32[]{:S(2)}) collective-permute-start(f32[2,512]{1,0:T(2,128)S(1)} %fusion.52), channel_id=1, source_target_pairs={{0,1},{1,0},{2,3},{3,2},{4,5},{5,4},{6,7},{7,6},{8,9},{9,8},{10,11... | collective-permute-start | bytes 12296 | tf_op jit(solution)/shard_map/ppermute | solution.py:17
  90.8 0.9 collective-permute-start.1
  91.6 1.3 collective-permute-start.2
  92.9 2.6 %collective-permute-start.3 = (f32[2,512]{1,0:T(2,128)S(1)}, f32[2,512]{1,0:T(2,128)S(1)}, u32[]{:S(2)}, u32[]{:S(2)}) collective-permute-start(f32[2,512]{1,0:T(2,128)S(1)} %fusion.52), channel_id=1, source_target_pairs={{0,4},{1,5},{2,6},{3,7},{4,0},{5,1},{6,2},{7,3},{8,12},{9,13},{10,... | collective-permute-start | bytes 12296 | tf_op jit(solution)/shard_map/ppermute | solution.py:17
  95.6 2.0 %collective-permute-start.4 = (f32[2,512]{1,0:T(2,128)S(1)}, f32[2,512]{1,0:T(2,128)S(1)}, u32[]{:S(2)}, u32[]{:S(2)}) collective-permute-start(f32[2,512]{1,0:T(2,128)S(1)} %fusion.52), channel_id=1, source_target_pairs={{0,5},{1,4},{2,7},{3,6},{4,1},{5,0},{6,3},{7,2},{8,13},{9,12},{10,... | collective-permute-start | bytes 12296 | tf_op jit(solution)/shard_map/ppermute | solution.py:17
  97.6 1.4 %collective-permute-start.5 = (f32[2,512]{1,0:T(2,128)S(1)}, f32[2,512]{1,0:T(2,128)S(1)}, u32[]{:S(2)}, u32[]{:S(2)}) collective-permute-start(f32[2,512]{1,0:T(2,128)S(1)} %fusion.52), channel_id=1, source_target_pairs={{0,6},{1,7},{2,4},{3,5},{4,2},{5,3},{6,0},{7,1},{8,14},{9,15},{10,... | collective-permute-start | bytes 12296 | tf_op jit(solution)/shard_map/ppermute | solution.py:17
  99.0 2.0 %collective-permute-start.6 = (f32[2,512]{1,0:T(2,128)S(1)}, f32[2,512]{1,0:T(2,128)S(1)}, u32[]{:S(2)}, u32[]{:S(2)}) collective-permute-start(f32[2,512]{1,0:T(2,128)S(1)} %fusion.52), channel_id=1, source_target_pairs={{0,7},{1,6},{2,5},{3,4},{4,3},{5,2},{6,1},{7,0},{8,15},{9,14},{10,... | collective-permute-start | bytes 12296 | tf_op jit(solution)/shard_map/ppermute | solution.py:17
  101.0 1.1 collective-permute-done.5
  102.6 1.3 %collective-permute-start.7 = (f32[2,512]{1,0:T(2,128)S(1)}, f32[2,512]{1,0:T(2,128)S(1)}, u32[]{:S(2)}, u32[]{:S(2)}) collective-permute-start(f32[2,512]{1,0:T(2,128)S(1)} %add_add_fusion.1), channel_id=1, source_target_pairs={{0,8},{1,9},{2,10},{3,11},{4,12},{5,13},{6,14},{7,15},{8,0},{9,1},... | collective-permute-start | bytes 12296 | tf_op jit(solution)/shard_map/ppermute | solution.py:17
  104.0 2.3 %collective-permute-start.8 = (f32[2,512]{1,0:T(2,128)S(1)}, f32[2,512]{1,0:T(2,128)S(1)}, u32[]{:S(2)}, u32[]{:S(2)}) collective-permute-start(f32[2,512]{1,0:T(2,128)S(1)} %add_add_fusion.1), channel_id=1, source_target_pairs={{0,16},{1,17},{2,18},{3,19},{4,20},{5,21},{6,22},{7,23},{8,24},{9,... | collective-permute-start | bytes 12296 | tf_op jit(solution)/shard_map/ppermute | solution.py:17
  107.0 1.0 copy.99
  108.0 2.0 %collective-permute-done.9 = f32[2,512]{1,0:T(2,128)S(1)} collective-permute-done((f32[2,512]{1,0:T(2,128)S(1)}, f32[2,512]{1,0:T(2,128)S(1)}, u32[]{:S(2)}, u32[]{:S(2)}) %collective-permute-start.9) | collective-permute-done | bytes 4128 | tf_op jit(solution)/shard_map/ppermute | solution.py:17
  109.9 0.7 fusion.58
  110.6 1.1 multiply_reduce_fusion.1
  111.8 6.8 %collective-permute-start.10 = (f32[]{:T(128)}, f32[]{:T(128)}, u32[]{:S(2)}, u32[]{:S(2)}) collective-permute-start(f32[]{:T(128)} %get-tuple-element.36), channel_id=1, source_target_pairs={{0,32},{32,0},{64,96},{96,64},{128,160},{160,128},{192,224},{224,1... | collective-permute-start | bytes 20 | tf_op jit(solution)/shard_map/ppermute | solution.py:17
  118.6 1.0 collective-permute-done.10
  120.9 2.0 %collective-permute-start.11 = (f32[]{:T(128)}, f32[]{:T(128)}, u32[]{:S(2)}, u32[]{:S(2)}) collective-permute-start(f32[]{:T(128)} %add.124), channel_id=1, source_target_pairs={{0,64},{32,96},{64,0},{96,32},{128,192},{160,224},{192,128},{224,1... | collective-permute-start | bytes 20 | tf_op jit(solution)/shard_map/ppermute | solution.py:17
  124.2 3.5 %collective-permute-start.12 = (f32[]{:T(128)}, f32[]{:T(128)}, u32[]{:S(2)}, u32[]{:S(2)}) collective-permute-start(f32[]{:T(128)} %add.125), channel_id=1, source_target_pairs={{0,128},{32,160},{64,192},{96,224},{128,0},{160,32},{192,64},{224,... | collective-permute-start | bytes 20 | tf_op jit(solution)/shard_map/ppermute | solution.py:17
  (97 shorter events, 8.7 us)
Async XLA Ops:
  0.6 5.4 %copy-start = (bf16[1024,1024]{1,0:T(8,128)(2,1)S(1)}, bf16[1024,1024]{1,0:T(8,128)(2,1)}, u32[]{:S(2)}) copy-start(bf16[1024,1024]{1,0:T(8,128)(2,1)} %param.16) | copy-start | bytes 6291460
  7.8 3.9 %copy-start.3 = (bf16[256,1024]{1,0:T(8,128)(2,1)}, bf16[256,1024]{1,0:T(8,128)(2,1)S(1)}, u32[]{:S(2)}) copy-start(bf16[256,1024]{1,0:T(8,128)(2,1)S(1)} %convolution_convert_fusion.1) | copy-start | bytes 1572868
  10.5 1.3 copy-start.4
  10.9 1.1 copy-start.9
  10.9 1.4 %copy-start.8 = (bf16[512,1024]{1,0:T(8,128)(2,1)S(1)}, bf16[512,1024]{1,0:T(8,128)(2,1)}, u32[]{:S(2)}) copy-start(bf16[512,1024]{1,0:T(8,128)(2,1)} %param.18) | copy-start | bytes 3145732
  16.9 1.9 %copy-start.1 = (f32[8,512,256]{2,1,0:T(8,128)}, f32[8,512,256]{2,1,0:T(8,128)S(1)}, u32[]{:S(2)}) copy-start(f32[8,512,256]{2,1,0:T(8,128)S(1)} %subtract_exponential_fusion) | copy-start | bytes 12582916
  18.9 1.2 copy-start.12
  20.9 19.6 %copy-start.5 = (bf16[256,1024]{1,0:T(8,128)(2,1)S(1)}, bf16[256,1024]{1,0:T(8,128)(2,1)}, u32[]{:S(2)}) copy-start(bf16[256,1024]{1,0:T(8,128)(2,1)} %copy-done.4) | copy-start | bytes 1572868
  22.8 28.4 %all-to-all-start = ((f32[32,40,128]{2,1,0:T(8,128)}), f32[32,40,128]{2,1,0:T(8,128)S(1)}, u32[]{:S(2)}, u32[]{:S(2)}) async-start(f32[32,40,128]{2,1,0:T(8,128)} %pad_maximum_fusion), calls=%async_computation | async-start | bytes 1310720 | tf_op jit(solution)/shard_map/all_to_all | solution.py:62
  52.7 27.6 %copy-start.10 = (bf16[32,8,8,128]{3,2,1,0:T(8,128)(2,1)S(1)}, bf16[32,8,8,128]{3,2,1,0:T(8,128)(2,1)}, u32[]{:S(2)}) copy-start(bf16[32,8,8,128]{3,2,1,0:T(8,128)(2,1)} %fusion.4) | copy-start | bytes 1572868
  53.0 27.3 %copy-start.7 = (f32[256,8,128]{0,2,1:T(8,128)S(1)}, f32[256,8,128]{0,2,1:T(8,128)}, u32[]{:S(2)}) copy-start(f32[256,8,128]{0,2,1:T(8,128)} %fusion.1) | copy-start | bytes 3145732
  54.6 26.9 %copy-start.11 = (f32[1024]{0:T(1024)S(1)}, f32[1024]{0:T(1024)}, u32[]{:S(2)}) copy-start(f32[1024]{0:T(1024)} %param.17) | copy-start | bytes 12292
  55.0 26.8 %copy-start.2 = (f32[8,512,256]{2,1,0:T(8,128)S(1)}, f32[8,512,256]{2,1,0:T(8,128)}, u32[]{:S(2)}) copy-start(f32[8,512,256]{2,1,0:T(8,128)} %copy-done.1) | copy-start | bytes 12582916
  55.0 26.8 %copy-start.6 = (bf16[512,1024]{1,0:T(8,128)(2,1)S(1)}, bf16[512,1024]{1,0:T(8,128)(2,1)}, u32[]{:S(2)}) copy-start(bf16[512,1024]{1,0:T(8,128)(2,1)} %param.19) | copy-start | bytes 3145732
  82.5 18.5 %copy-start.13 = (s32[1,2]{1,0:T(1,128)S(1)}, s32[1,2]{1,0:T(1,128)}, u32[]{:S(2)}) copy-start(s32[1,2]{1,0:T(1,128)} %param.12) | copy-start | bytes 28
  88.0 9.6 %collective-permute-start = (f32[2,512]{1,0:T(2,128)S(1)}, f32[2,512]{1,0:T(2,128)S(1)}, u32[]{:S(2)}, u32[]{:S(2)}) collective-permute-start(f32[2,512]{1,0:T(2,128)S(1)} %fusion.52), channel_id=1, source_target_pairs={{0,1},{1,0},{2,3},{3,2},{4,5},{5,4},{6,7},{7,6},{8,9},{9,8},{10,11... | collective-permute-start | bytes 12296 | tf_op jit(solution)/shard_map/ppermute | solution.py:17
  90.8 8.2 %collective-permute-start.1 = (f32[2,512]{1,0:T(2,128)S(1)}, f32[2,512]{1,0:T(2,128)S(1)}, u32[]{:S(2)}, u32[]{:S(2)}) collective-permute-start(f32[2,512]{1,0:T(2,128)S(1)} %fusion.52), channel_id=1, source_target_pairs={{0,2},{1,3},{2,0},{3,1},{4,6},{5,7},{6,4},{7,5},{8,10},{9,11},{10,... | collective-permute-start | bytes 12296 | tf_op jit(solution)/shard_map/ppermute | solution.py:17
  91.6 9.4 %collective-permute-start.2 = (f32[2,512]{1,0:T(2,128)S(1)}, f32[2,512]{1,0:T(2,128)S(1)}, u32[]{:S(2)}, u32[]{:S(2)}) collective-permute-start(f32[2,512]{1,0:T(2,128)S(1)} %fusion.52), channel_id=1, source_target_pairs={{0,3},{1,2},{2,1},{3,0},{4,7},{5,6},{6,5},{7,4},{8,11},{9,10},{10,... | collective-permute-start | bytes 12296 | tf_op jit(solution)/shard_map/ppermute | solution.py:17
  92.9 8.1 %collective-permute-start.3 = (f32[2,512]{1,0:T(2,128)S(1)}, f32[2,512]{1,0:T(2,128)S(1)}, u32[]{:S(2)}, u32[]{:S(2)}) collective-permute-start(f32[2,512]{1,0:T(2,128)S(1)} %fusion.52), channel_id=1, source_target_pairs={{0,4},{1,5},{2,6},{3,7},{4,0},{5,1},{6,2},{7,3},{8,12},{9,13},{10,... | collective-permute-start | bytes 12296 | tf_op jit(solution)/shard_map/ppermute | solution.py:17
  95.6 5.5 %collective-permute-start.4 = (f32[2,512]{1,0:T(2,128)S(1)}, f32[2,512]{1,0:T(2,128)S(1)}, u32[]{:S(2)}, u32[]{:S(2)}) collective-permute-start(f32[2,512]{1,0:T(2,128)S(1)} %fusion.52), channel_id=1, source_target_pairs={{0,5},{1,4},{2,7},{3,6},{4,1},{5,0},{6,3},{7,2},{8,13},{9,12},{10,... | collective-permute-start | bytes 12296 | tf_op jit(solution)/shard_map/ppermute | solution.py:17
  97.6 4.6 %collective-permute-start.5 = (f32[2,512]{1,0:T(2,128)S(1)}, f32[2,512]{1,0:T(2,128)S(1)}, u32[]{:S(2)}, u32[]{:S(2)}) collective-permute-start(f32[2,512]{1,0:T(2,128)S(1)} %fusion.52), channel_id=1, source_target_pairs={{0,6},{1,7},{2,4},{3,5},{4,2},{5,3},{6,0},{7,1},{8,14},{9,15},{10,... | collective-permute-start | bytes 12296 | tf_op jit(solution)/shard_map/ppermute | solution.py:17
  99.0 3.7 %collective-permute-start.6 = (f32[2,512]{1,0:T(2,128)S(1)}, f32[2,512]{1,0:T(2,128)S(1)}, u32[]{:S(2)}, u32[]{:S(2)}) collective-permute-start(f32[2,512]{1,0:T(2,128)S(1)} %fusion.52), channel_id=1, source_target_pairs={{0,7},{1,6},{2,5},{3,4},{4,3},{5,2},{6,1},{7,0},{8,15},{9,14},{10,... | collective-permute-start | bytes 12296 | tf_op jit(solution)/shard_map/ppermute | solution.py:17
  102.6 5.3 %collective-permute-start.7 = (f32[2,512]{1,0:T(2,128)S(1)}, f32[2,512]{1,0:T(2,128)S(1)}, u32[]{:S(2)}, u32[]{:S(2)}) collective-permute-start(f32[2,512]{1,0:T(2,128)S(1)} %add_add_fusion.1), channel_id=1, source_target_pairs={{0,8},{1,9},{2,10},{3,11},{4,12},{5,13},{6,14},{7,15},{8,0},{9,1},... | collective-permute-start | bytes 12296 | tf_op jit(solution)/shard_map/ppermute | solution.py:17
  104.0 4.0 %collective-permute-start.8 = (f32[2,512]{1,0:T(2,128)S(1)}, f32[2,512]{1,0:T(2,128)S(1)}, u32[]{:S(2)}, u32[]{:S(2)}) collective-permute-start(f32[2,512]{1,0:T(2,128)S(1)} %add_add_fusion.1), channel_id=1, source_target_pairs={{0,16},{1,17},{2,18},{3,19},{4,20},{5,21},{6,22},{7,23},{8,24},{9,... | collective-permute-start | bytes 12296 | tf_op jit(solution)/shard_map/ppermute | solution.py:17
  106.3 3.7 %collective-permute-start.9 = (f32[2,512]{1,0:T(2,128)S(1)}, f32[2,512]{1,0:T(2,128)S(1)}, u32[]{:S(2)}, u32[]{:S(2)}) collective-permute-start(f32[2,512]{1,0:T(2,128)S(1)} %add_add_fusion.1), channel_id=1, source_target_pairs={{0,24},{1,25},{2,26},{3,27},{4,28},{5,29},{6,30},{7,31},{8,16},{9,... | collective-permute-start | bytes 12296 | tf_op jit(solution)/shard_map/ppermute | solution.py:17
  111.8 7.8 %collective-permute-start.10 = (f32[]{:T(128)}, f32[]{:T(128)}, u32[]{:S(2)}, u32[]{:S(2)}) collective-permute-start(f32[]{:T(128)} %get-tuple-element.36), channel_id=1, source_target_pairs={{0,32},{32,0},{64,96},{96,64},{128,160},{160,128},{192,224},{224,1... | collective-permute-start | bytes 20 | tf_op jit(solution)/shard_map/ppermute | solution.py:17
  120.9 2.6 %collective-permute-start.11 = (f32[]{:T(128)}, f32[]{:T(128)}, u32[]{:S(2)}, u32[]{:S(2)}) collective-permute-start(f32[]{:T(128)} %add.124), channel_id=1, source_target_pairs={{0,64},{32,96},{64,0},{96,32},{128,192},{160,224},{192,128},{224,1... | collective-permute-start | bytes 20 | tf_op jit(solution)/shard_map/ppermute | solution.py:17
  124.2 4.1 %collective-permute-start.12 = (f32[]{:T(128)}, f32[]{:T(128)}, u32[]{:S(2)}, u32[]{:S(2)}) collective-permute-start(f32[]{:T(128)} %add.125), channel_id=1, source_target_pairs={{0,128},{32,160},{64,192},{96,224},{128,0},{160,32},{192,64},{224,... | collective-permute-start | bytes 20 | tf_op jit(solution)/shard_map/ppermute | solution.py:17

commit v14 on v13

--- a/solution.py
+++ b/solution.py
@@ -191,8 +191,12 @@
 
     y3 = out_rows.reshape(tok_rows, head_count, head_dim)
     label_value = jnp.einsum("lhd,thd->hlt", lw3, y3, preferred_element_type=jnp.float32)
+    late_tok = maxima[:, record_count - 1, :, None]
+    for r in range(record_count - 2, -1, -1):
+        late_tok = jnp.where(record[None, None, :] == r, maxima[:, r, :, None], late_tok)
+    late_weight = jnp.exp(pscore - late_tok)
     weighted = jnp.sum(
-        jnp.where(member[None, :, None, :], (pool_weight * label_value)[:, None], 0.0), axis=3
+        jnp.where(member[None, :, None, :], (late_weight * label_value)[:, None], 0.0), axis=3
     )
     part = jnp.sum(weighted * rescale, axis=0)
     count = lax.axis_size("ctx")

time: 132 us -> 132 us (level)
  blocking collectives: 25.2 us -> 0 us
  waiting for transfers between devices: 13.3 us -> 30.1 us
  starting transfers between devices: 41.6 us -> 49.9 us
  matrix products: 16.1 us -> 18 us
    all_to_all x1 -> x0, blocking collectives: 25.2 us -> none  [exclusive_state_scan(): back = lax.all_to_all(sent_back, axis, 0, 0)]
    all_to_all x0 -> x1, waiting for transfers between devices: none -> 16.8 us  [exclusive_state_scan(): back = lax.all_to_all(sent_back, axis, 0, 0)]
    all_to_all x0 -> x1, starting transfers between devices: none -> 8.39 us  [exclusive_state_scan(): back = lax.all_to_all(sent_back, axis, 0, 0)]
    unnamed x42 -> x41, local copies, waits for them, and re-layouts: 5.86 us -> 3.95 us
    dot_general x1, matrix products: 1.01 us -> 2.37 us  [local(): jnp.einsum('thd,hde->the', q_decayed, incoming, precision=lax.Precision.H...]
  transfers between devices with their start and end apart: 14 -> 15, of which waited for: 7 -> 8; matrix products, arithmetic and copies ran while one was open for 8% -> 8% of each run, Pallas kernels for 0% -> 0%
where the time goes in v14:
time: 132 us; the launch traced here: 131 us
  starting transfers between devices  49.9 us (38%)
  waiting for transfers between devices  30.1 us (23%)
  matrix products  18 us (14%)
  other arithmetic  14.5 us (11%)
  local copies, waits for them, and re-layouts  12.6 us (10%)
  between operations  5.74 us (4%)
    ppermute x13, starting transfers between devices, swapped(): return lax.ppermute(x, axis, [(i, i ^ bit) for i in range(count)])  29.3 us
    all_to_all x1, waiting for transfers between devices, exclusive_state_scan(): back = lax.all_to_all(sent_back, axis, 0, 0)  16.8 us
    all_to_all x1, starting transfers between devices, exclusive_state_scan(): got = lax.all_to_all(jnp.concatenate([slices, extra], axis=1), axis, 0, 0)  12.2 us
    all_to_all x1, starting transfers between devices, exclusive_state_scan(): back = lax.all_to_all(sent_back, axis, 0, 0)  8.39 us
    all_to_all x1, waiting for transfers between devices, exclusive_state_scan(): got = lax.all_to_all(jnp.concatenate([slices, extra], axis=1), axis, 0, 0)  7.65 us
    ppermute x13, waiting for transfers between devices, swapped(): return lax.ppermute(x, axis, [(i, i ^ bit) for i in range(count)])  5.64 us
    unnamed x41, local copies, waits for them, and re-layouts  3.95 us
    dot_general x1, matrix products, local(): jnp.dot(features, w_query, preferred_element_type=jnp.float32)  3.28 us
  transfers between devices with their start and end apart: 15, of which 8 were waited for; matrix products, arithmetic and copies ran while one was open for 8% of the time, Pallas kernels for 0%

profile of v14, /device:TPU:1, one launch (start us, length us, event | category | flops | bytes accessed | tf_op | source)
XLA Modules:
  0.0 130.8 jit_solution(5911923246584858517)
XLA Ops:
  0.7 0.9 fusion.60
  2.3 0.6 fusion.61
  3.5 0.8 fusion.41
  4.6 0.7 broadcast_compare_fusion
  6.1 1.8 %convolution_convert_fusion.1 = bf16[256,1024]{1,0:T(8,128)(2,1)S(1)} fusion(bf16[1024,1024]{1,0:T(8,128)(2,1)S(1)} %copy-done, bf16[1,256,1024]{2,1,0:T(8,128)(2,1)} %param.10), kind=kOutput, calls=%fused_computation.14 | convolution fusion | flops 537133056 | bytes 3145728 | tf_op jit(solution)/shard_map/dot_general | solution.py:116
  7.9 2.6 %convolution_convert_fusion.2 = bf16[256,1024]{1,0:T(8,128)(2,1)S(1)} fusion(bf16[1024,1024]{1,0:T(8,128)(2,1)} %param.15, bf16[1,256,1024]{2,1,0:T(8,128)(2,1)} %param.10), kind=kOutput, calls=%fused_computation.15 | convolution fusion | flops 537133056 | bytes 3145728 | tf_op jit(solution)/shard_map/dot_general | solution.py:115
  10.9 0.9 fusion.17
  12.3 0.7 convolution_multiply_fusion
  13.0 1.2 select_reduce_fusion.3
  14.2 1.5 %select_reduce_fusion.2 = f32[8,512,256]{2,1,0:T(8,128)S(1)} fusion(f32[8,2,512]{2,1,0:T(2,128)S(1)} %select_reduce_fusion.3, pred[2,256]{1,0:T(4,128)(4,1)S(1)} %iota_compare_fusion.8), kind=kLoop, calls=%fused_computation.2 | loop fusion | flops 3145728 | bytes 4227584 | tf_op jit(solution)/shard_map/reduce_sum | solution.py:155
  15.7 1.2 subtract_exponential_fusion
  17.0 1.2 select_reduce_fusion.1
  19.0 0.7 broadcast_select_fusion
  20.0 0.9 pad_maximum_fusion
  20.9 12.2 %all-to-all-start = ((f32[32,40,128]{2,1,0:T(8,128)}), f32[32,40,128]{2,1,0:T(8,128)S(1)}, u32[]{:S(2)}, u32[]{:S(2)}) async-start(f32[32,40,128]{2,1,0:T(8,128)} %pad_maximum_fusion), calls=%async_computation | async-start | bytes 1310720 | tf_op jit(solution)/shard_map/all_to_all | solution.py:62
  33.2 2.0 %copy.109 = bf16[256,1024]{0,1:T(8,128)(2,1)} copy(bf16[256,1024]{1,0:T(8,128)(2,1)} %copy-done.3) | data formatting | bytes 1048576 | tf_op jit(solution)/shard_map/reshape | solution.py:119
  35.3 3.3 %fusion.4 = bf16[32,8,8,128]{3,2,1,0:T(8,128)(2,1)} fusion(bf16[1024,1024]{1,0:T(8,128)(2,1)} %param.14, bf16[1,256,1024]{2,1,0:T(8,128)(2,1)} %param.10), kind=kOutput, calls=%fused_computation.16 | convolution fusion | flops 537133056 | bytes 3145728 | tf_op jit(solution)/shard_map/dot_general | solution.py:114
  38.6 3.1 %fusion.1 = f32[256,8,128]{0,2,1:T(8,128)} fusion(bf16[256,8,128]{0,2,1:T(8,128)(2,1)} %bitcast.175, f32[8,256]{1,0:T(8,128)S(1)} %bitcast.183, pred[256,256]{1,0:T(8,128)(4,1)S(1)} %fusion.40, bf16[32,8,8,128]{3,2,1,0:T(8,128)(2,1)} %fusion.4, bf16[256,1024]{1,0:T(8,128)(2,1)S(1)} %copy-done.5), kind=kOutput, calls=%fused_computation.9 | convolution fusion | flops 271581184 | bytes 2695168 | tf_op jit(solution)/shard_map/hts,shd->thd/dot_general | solution.py:145
  41.7 7.7 %all-to-all-done = f32[32,40,128]{2,1,0:T(8,128)S(1)} async-done(((f32[32,40,128]{2,1,0:T(8,128)}), f32[32,40,128]{2,1,0:T(8,128)S(1)}, u32[]{:S(2)}, u32[]{:S(2)}) %all-to-all-start) | async-done | bytes 655392 | tf_op jit(solution)/shard_map/all_to_all | solution.py:62
  51.1 0.6 select_reduce_fusion.4
  51.8 0.9 fusion.19
  52.7 1.2 copy.97
  54.0 8.4 %all-to-all-start.1 = ((f32[32,40,128]{2,1,0:T(8,128)}), f32[32,40,128]{2,1,0:T(8,128)S(1)}, u32[]{:S(2)}, u32[]{:S(2)}) async-start(f32[32,40,128]{2,1,0:T(8,128)} %copy.97), calls=%async_computation.1 | async-start | bytes 1310720 | tf_op jit(solution)/shard_map/all_to_all | solution.py:84
  62.4 16.8 %all-to-all-done.1 = f32[32,40,128]{2,1,0:T(8,128)S(1)} async-done(((f32[32,40,128]{2,1,0:T(8,128)}), f32[32,40,128]{2,1,0:T(8,128)S(1)}, u32[]{:S(2)}, u32[]{:S(2)}) %all-to-all-start.1) | async-done | bytes 655392 | tf_op jit(solution)/shard_map/all_to_all | solution.py:84
  79.3 2.4 %fusion.67 = (f32[256,8]{0,1:T(8,128)S(1)}, f32[256,8,128]{0,2,1:T(8,128)S(1)}) fusion(f32[256,8,128]{0,2,1:T(8,128)} %fusion.1, f32[8,128,128]{2,1,0:T(8,128)S(1)} %bitcast.169, f32[256,8]{0,1:T(8,128)S(1)} %get-tuple-element.34, bf16[32,8,8,128]{3,2,1,0:T(8,128)(2,1)S(1)} %copy-done.9), kind=kOutput, calls=%fused_computation.131 | convolution fusion | flops 202635264 | bytes 3162112 | tf_op jit(solution)/shard_map/thd,hde->the/dot_general | solution.py:181
  82.0 1.2 bitcast_multiply_fusion
  83.3 1.2 select_reduce_fusion
  85.1 1.1 fusion.65
  86.2 1.2 copy.112
  87.5 1.2 copy.113
  88.7 2.8 %collective-permute-start = (f32[2,512]{1,0:T(2,128)S(1)}, f32[2,512]{1,0:T(2,128)S(1)}, u32[]{:S(2)}, u32[]{:S(2)}) collective-permute-start(f32[2,512]{1,0:T(2,128)S(1)} %fusion.52), channel_id=1, source_target_pairs={{0,1},{1,0},{2,3},{3,2},{4,5},{5,4},{6,7},{7,6},{8,9},{9,8},{10,11... | collective-permute-start | bytes 12296 | tf_op jit(solution)/shard_map/ppermute | solution.py:17
  91.5 0.9 collective-permute-start.1
  92.4 1.3 collective-permute-start.2
  93.7 2.6 %collective-permute-start.3 = (f32[2,512]{1,0:T(2,128)S(1)}, f32[2,512]{1,0:T(2,128)S(1)}, u32[]{:S(2)}, u32[]{:S(2)}) collective-permute-start(f32[2,512]{1,0:T(2,128)S(1)} %fusion.52), channel_id=1, source_target_pairs={{0,4},{1,5},{2,6},{3,7},{4,0},{5,1},{6,2},{7,3},{8,12},{9,13},{10,... | collective-permute-start | bytes 12296 | tf_op jit(solution)/shard_map/ppermute | solution.py:17
  96.3 2.0 %collective-permute-start.4 = (f32[2,512]{1,0:T(2,128)S(1)}, f32[2,512]{1,0:T(2,128)S(1)}, u32[]{:S(2)}, u32[]{:S(2)}) collective-permute-start(f32[2,512]{1,0:T(2,128)S(1)} %fusion.52), channel_id=1, source_target_pairs={{0,5},{1,4},{2,7},{3,6},{4,1},{5,0},{6,3},{7,2},{8,13},{9,12},{10,... | collective-permute-start | bytes 12296 | tf_op jit(solution)/shard_map/ppermute | solution.py:17
  98.3 1.3 %collective-permute-start.5 = (f32[2,512]{1,0:T(2,128)S(1)}, f32[2,512]{1,0:T(2,128)S(1)}, u32[]{:S(2)}, u32[]{:S(2)}) collective-permute-start(f32[2,512]{1,0:T(2,128)S(1)} %fusion.52), channel_id=1, source_target_pairs={{0,6},{1,7},{2,4},{3,5},{4,2},{5,3},{6,0},{7,1},{8,14},{9,15},{10,... | collective-permute-start | bytes 12296 | tf_op jit(solution)/shard_map/ppermute | solution.py:17
  99.7 2.0 %collective-permute-start.6 = (f32[2,512]{1,0:T(2,128)S(1)}, f32[2,512]{1,0:T(2,128)S(1)}, u32[]{:S(2)}, u32[]{:S(2)}) collective-permute-start(f32[2,512]{1,0:T(2,128)S(1)} %fusion.52), channel_id=1, source_target_pairs={{0,7},{1,6},{2,5},{3,4},{4,3},{5,2},{6,1},{7,0},{8,15},{9,14},{10,... | collective-permute-start | bytes 12296 | tf_op jit(solution)/shard_map/ppermute | solution.py:17
  101.8 1.1 collective-permute-done.5
  103.4 1.3 %collective-permute-start.7 = (f32[2,512]{1,0:T(2,128)S(1)}, f32[2,512]{1,0:T(2,128)S(1)}, u32[]{:S(2)}, u32[]{:S(2)}) collective-permute-start(f32[2,512]{1,0:T(2,128)S(1)} %add_add_fusion.1), channel_id=1, source_target_pairs={{0,8},{1,9},{2,10},{3,11},{4,12},{5,13},{6,14},{7,15},{8,0},{9,1},... | collective-permute-start | bytes 12296 | tf_op jit(solution)/shard_map/ppermute | solution.py:17
  104.7 2.3 %collective-permute-start.8 = (f32[2,512]{1,0:T(2,128)S(1)}, f32[2,512]{1,0:T(2,128)S(1)}, u32[]{:S(2)}, u32[]{:S(2)}) collective-permute-start(f32[2,512]{1,0:T(2,128)S(1)} %add_add_fusion.1), channel_id=1, source_target_pairs={{0,16},{1,17},{2,18},{3,19},{4,20},{5,21},{6,22},{7,23},{8,24},{9,... | collective-permute-start | bytes 12296 | tf_op jit(solution)/shard_map/ppermute | solution.py:17
  107.7 1.0 copy.105
  108.7 2.0 %collective-permute-done.9 = f32[2,512]{1,0:T(2,128)S(1)} collective-permute-done((f32[2,512]{1,0:T(2,128)S(1)}, f32[2,512]{1,0:T(2,128)S(1)}, u32[]{:S(2)}, u32[]{:S(2)}) %collective-permute-start.9) | collective-permute-done | bytes 4128 | tf_op jit(solution)/shard_map/ppermute | solution.py:17
  110.7 0.7 fusion.58
  111.4 1.1 multiply_reduce_fusion.1
  112.5 6.8 %collective-permute-start.10 = (f32[]{:T(128)}, f32[]{:T(128)}, u32[]{:S(2)}, u32[]{:S(2)}) collective-permute-start(f32[]{:T(128)} %get-tuple-element.39), channel_id=1, source_target_pairs={{0,32},{32,0},{64,96},{96,64},{128,160},{160,128},{192,224},{224,1... | collective-permute-start | bytes 20 | tf_op jit(solution)/shard_map/ppermute | solution.py:17
  119.3 1.0 collective-permute-done.10
  121.6 2.0 %collective-permute-start.11 = (f32[]{:T(128)}, f32[]{:T(128)}, u32[]{:S(2)}, u32[]{:S(2)}) collective-permute-start(f32[]{:T(128)} %add.128), channel_id=1, source_target_pairs={{0,64},{32,96},{64,0},{96,32},{128,192},{160,224},{192,128},{224,1... | collective-permute-start | bytes 20 | tf_op jit(solution)/shard_map/ppermute | solution.py:17
  124.9 3.6 %collective-permute-start.12 = (f32[]{:T(128)}, f32[]{:T(128)}, u32[]{:S(2)}, u32[]{:S(2)}) collective-permute-start(f32[]{:T(128)} %add.129), channel_id=1, source_target_pairs={{0,128},{32,160},{64,192},{96,224},{128,0},{160,32},{192,64},{224,... | collective-permute-start | bytes 20 | tf_op jit(solution)/shard_map/ppermute | solution.py:17
  (98 shorter events, 8.8 us)
Async XLA Ops:
  0.6 5.4 %copy-start = (bf16[1024,1024]{1,0:T(8,128)(2,1)S(1)}, bf16[1024,1024]{1,0:T(8,128)(2,1)}, u32[]{:S(2)}) copy-start(bf16[1024,1024]{1,0:T(8,128)(2,1)} %param.16) | copy-start | bytes 6291460
  7.8 3.9 %copy-start.3 = (bf16[256,1024]{1,0:T(8,128)(2,1)}, bf16[256,1024]{1,0:T(8,128)(2,1)S(1)}, u32[]{:S(2)}) copy-start(bf16[256,1024]{1,0:T(8,128)(2,1)S(1)} %convolution_convert_fusion.1) | copy-start | bytes 1572868
  10.5 1.3 copy-start.4
  10.9 1.1 copy-start.8
  10.9 1.4 %copy-start.7 = (bf16[512,1024]{1,0:T(8,128)(2,1)S(1)}, bf16[512,1024]{1,0:T(8,128)(2,1)}, u32[]{:S(2)}) copy-start(bf16[512,1024]{1,0:T(8,128)(2,1)} %param.18) | copy-start | bytes 3145732
  13.0 2.8 %copy-start.1 = (f32[8,512,256]{2,1,0:T(8,128)}, f32[8,512,256]{2,1,0:T(8,128)S(1)}, u32[]{:S(2)}) copy-start(f32[8,512,256]{2,1,0:T(8,128)S(1)} %convolution_multiply_fusion) | copy-start | bytes 12582916
  17.0 1.2 copy-start.11
  19.0 19.6 %copy-start.5 = (bf16[256,1024]{1,0:T(8,128)(2,1)S(1)}, bf16[256,1024]{1,0:T(8,128)(2,1)}, u32[]{:S(2)}) copy-start(bf16[256,1024]{1,0:T(8,128)(2,1)} %copy-done.4) | copy-start | bytes 1572868
  20.9 28.4 %all-to-all-start = ((f32[32,40,128]{2,1,0:T(8,128)}), f32[32,40,128]{2,1,0:T(8,128)S(1)}, u32[]{:S(2)}, u32[]{:S(2)}) async-start(f32[32,40,128]{2,1,0:T(8,128)} %pad_maximum_fusion), calls=%async_computation | async-start | bytes 1310720 | tf_op jit(solution)/shard_map/all_to_all | solution.py:62
  52.6 26.6 %copy-start.9 = (bf16[32,8,8,128]{3,2,1,0:T(8,128)(2,1)S(1)}, bf16[32,8,8,128]{3,2,1,0:T(8,128)(2,1)}, u32[]{:S(2)}) copy-start(bf16[32,8,8,128]{3,2,1,0:T(8,128)(2,1)} %fusion.4) | copy-start | bytes 1572868
  52.7 29.1 %copy-start.10 = (f32[1024]{0:T(1024)S(1)}, f32[1024]{0:T(1024)}, u32[]{:S(2)}) copy-start(f32[1024]{0:T(1024)} %param.17) | copy-start | bytes 12292
  54.0 25.2 %all-to-all-start.1 = ((f32[32,40,128]{2,1,0:T(8,128)}), f32[32,40,128]{2,1,0:T(8,128)S(1)}, u32[]{:S(2)}, u32[]{:S(2)}) async-start(f32[32,40,128]{2,1,0:T(8,128)} %copy.97), calls=%async_computation.1 | async-start | bytes 1310720 | tf_op jit(solution)/shard_map/all_to_all | solution.py:84
  79.2 2.8 %copy-start.2 = (f32[8,512,256]{2,1,0:T(8,128)S(1)}, f32[8,512,256]{2,1,0:T(8,128)}, u32[]{:S(2)}) copy-start(f32[8,512,256]{2,1,0:T(8,128)} %copy-done.1) | copy-start | bytes 12582916
  79.2 2.8 %copy-start.6 = (bf16[512,1024]{1,0:T(8,128)(2,1)S(1)}, bf16[512,1024]{1,0:T(8,128)(2,1)}, u32[]{:S(2)}) copy-start(bf16[512,1024]{1,0:T(8,128)(2,1)} %param.19) | copy-start | bytes 3145732
  83.3 18.5 %copy-start.12 = (s32[1,2]{1,0:T(1,128)S(1)}, s32[1,2]{1,0:T(1,128)}, u32[]{:S(2)}) copy-start(s32[1,2]{1,0:T(1,128)} %param.12) | copy-start | bytes 28
  88.7 9.6 %collective-permute-start = (f32[2,512]{1,0:T(2,128)S(1)}, f32[2,512]{1,0:T(2,128)S(1)}, u32[]{:S(2)}, u32[]{:S(2)}) collective-permute-start(f32[2,512]{1,0:T(2,128)S(1)} %fusion.52), channel_id=1, source_target_pairs={{0,1},{1,0},{2,3},{3,2},{4,5},{5,4},{6,7},{7,6},{8,9},{9,8},{10,11... | collective-permute-start | bytes 12296 | tf_op jit(solution)/shard_map/ppermute | solution.py:17
  91.5 8.2 %collective-permute-start.1 = (f32[2,512]{1,0:T(2,128)S(1)}, f32[2,512]{1,0:T(2,128)S(1)}, u32[]{:S(2)}, u32[]{:S(2)}) collective-permute-start(f32[2,512]{1,0:T(2,128)S(1)} %fusion.52), channel_id=1, source_target_pairs={{0,2},{1,3},{2,0},{3,1},{4,6},{5,7},{6,4},{7,5},{8,10},{9,11},{10,... | collective-permute-start | bytes 12296 | tf_op jit(solution)/shard_map/ppermute | solution.py:17
  92.4 9.4 %collective-permute-start.2 = (f32[2,512]{1,0:T(2,128)S(1)}, f32[2,512]{1,0:T(2,128)S(1)}, u32[]{:S(2)}, u32[]{:S(2)}) collective-permute-start(f32[2,512]{1,0:T(2,128)S(1)} %fusion.52), channel_id=1, source_target_pairs={{0,3},{1,2},{2,1},{3,0},{4,7},{5,6},{6,5},{7,4},{8,11},{9,10},{10,... | collective-permute-start | bytes 12296 | tf_op jit(solution)/shard_map/ppermute | solution.py:17
  93.7 8.1 %collective-permute-start.3 = (f32[2,512]{1,0:T(2,128)S(1)}, f32[2,512]{1,0:T(2,128)S(1)}, u32[]{:S(2)}, u32[]{:S(2)}) collective-permute-start(f32[2,512]{1,0:T(2,128)S(1)} %fusion.52), channel_id=1, source_target_pairs={{0,4},{1,5},{2,6},{3,7},{4,0},{5,1},{6,2},{7,3},{8,12},{9,13},{10,... | collective-permute-start | bytes 12296 | tf_op jit(solution)/shard_map/ppermute | solution.py:17
  96.3 5.5 %collective-permute-start.4 = (f32[2,512]{1,0:T(2,128)S(1)}, f32[2,512]{1,0:T(2,128)S(1)}, u32[]{:S(2)}, u32[]{:S(2)}) collective-permute-start(f32[2,512]{1,0:T(2,128)S(1)} %fusion.52), channel_id=1, source_target_pairs={{0,5},{1,4},{2,7},{3,6},{4,1},{5,0},{6,3},{7,2},{8,13},{9,12},{10,... | collective-permute-start | bytes 12296 | tf_op jit(solution)/shard_map/ppermute | solution.py:17
  98.3 4.6 %collective-permute-start.5 = (f32[2,512]{1,0:T(2,128)S(1)}, f32[2,512]{1,0:T(2,128)S(1)}, u32[]{:S(2)}, u32[]{:S(2)}) collective-permute-start(f32[2,512]{1,0:T(2,128)S(1)} %fusion.52), channel_id=1, source_target_pairs={{0,6},{1,7},{2,4},{3,5},{4,2},{5,3},{6,0},{7,1},{8,14},{9,15},{10,... | collective-permute-start | bytes 12296 | tf_op jit(solution)/shard_map/ppermute | solution.py:17
  99.7 3.7 %collective-permute-start.6 = (f32[2,512]{1,0:T(2,128)S(1)}, f32[2,512]{1,0:T(2,128)S(1)}, u32[]{:S(2)}, u32[]{:S(2)}) collective-permute-start(f32[2,512]{1,0:T(2,128)S(1)} %fusion.52), channel_id=1, source_target_pairs={{0,7},{1,6},{2,5},{3,4},{4,3},{5,2},{6,1},{7,0},{8,15},{9,14},{10,... | collective-permute-start | bytes 12296 | tf_op jit(solution)/shard_map/ppermute | solution.py:17
  103.4 5.3 %collective-permute-start.7 = (f32[2,512]{1,0:T(2,128)S(1)}, f32[2,512]{1,0:T(2,128)S(1)}, u32[]{:S(2)}, u32[]{:S(2)}) collective-permute-start(f32[2,512]{1,0:T(2,128)S(1)} %add_add_fusion.1), channel_id=1, source_target_pairs={{0,8},{1,9},{2,10},{3,11},{4,12},{5,13},{6,14},{7,15},{8,0},{9,1},... | collective-permute-start | bytes 12296 | tf_op jit(solution)/shard_map/ppermute | solution.py:17
  104.7 4.0 %collective-permute-start.8 = (f32[2,512]{1,0:T(2,128)S(1)}, f32[2,512]{1,0:T(2,128)S(1)}, u32[]{:S(2)}, u32[]{:S(2)}) collective-permute-start(f32[2,512]{1,0:T(2,128)S(1)} %add_add_fusion.1), channel_id=1, source_target_pairs={{0,16},{1,17},{2,18},{3,19},{4,20},{5,21},{6,22},{7,23},{8,24},{9,... | collective-permute-start | bytes 12296 | tf_op jit(solution)/shard_map/ppermute | solution.py:17
  107.0 3.7 %collective-permute-start.9 = (f32[2,512]{1,0:T(2,128)S(1)}, f32[2,512]{1,0:T(2,128)S(1)}, u32[]{:S(2)}, u32[]{:S(2)}) collective-permute-start(f32[2,512]{1,0:T(2,128)S(1)} %add_add_fusion.1), channel_id=1, source_target_pairs={{0,24},{1,25},{2,26},{3,27},{4,28},{5,29},{6,30},{7,31},{8,16},{9,... | collective-permute-start | bytes 12296 | tf_op jit(solution)/shard_map/ppermute | solution.py:17
  112.5 7.8 %collective-permute-start.10 = (f32[]{:T(128)}, f32[]{:T(128)}, u32[]{:S(2)}, u32[]{:S(2)}) collective-permute-start(f32[]{:T(128)} %get-tuple-element.39), channel_id=1, source_target_pairs={{0,32},{32,0},{64,96},{96,64},{128,160},{160,128},{192,224},{224,1... | collective-permute-start | bytes 20 | tf_op jit(solution)/shard_map/ppermute | solution.py:17
  121.6 2.6 %collective-permute-start.11 = (f32[]{:T(128)}, f32[]{:T(128)}, u32[]{:S(2)}, u32[]{:S(2)}) collective-permute-start(f32[]{:T(128)} %add.128), channel_id=1, source_target_pairs={{0,64},{32,96},{64,0},{96,32},{128,192},{160,224},{192,128},{224,1... | collective-permute-start | bytes 20 | tf_op jit(solution)/shard_map/ppermute | solution.py:17
  124.9 4.1 %collective-permute-start.12 = (f32[]{:T(128)}, f32[]{:T(128)}, u32[]{:S(2)}, u32[]{:S(2)}) collective-permute-start(f32[]{:T(128)} %add.129), channel_id=1, source_target_pairs={{0,128},{32,160},{64,192},{96,224},{128,0},{160,32},{192,64},{224,... | collective-permute-start | bytes 20 | tf_op jit(solution)/shard_map/ppermute | solution.py:17

commit v15 on v13

--- a/solution.py
+++ b/solution.py
@@ -196,11 +196,14 @@
     )
     part = jnp.sum(weighted * rescale, axis=0)
     count = lax.axis_size("ctx")
-    inner = min(count, 8)
-    assert count % inner == 0 and inner & (inner - 1) == 0
-    part = group_sum(part, "ctx", 1, inner)
-    if count > inner:
-        part = group_sum(part, "ctx", inner, count // inner)
+    assert count & (count - 1) == 0
+    stride = 1
+    for size in (4, 2, 4):
+        size = min(size, count // stride)
+        if size > 1:
+            part = group_sum(part, "ctx", stride, size)
+            stride *= size
+    assert stride == count
     logits = part
     target = (total_counts + 0.5) / (lengths[0].astype(jnp.float32)[:, None] + 1.0)
     rec_loss = jnp.mean(jax.nn.softplus(logits) - target * logits, axis=1)

time: 132 us -> 131 us (level)
  starting transfers between devices: 41.6 us -> 35.7 us
  waiting for transfers between devices: 13.3 us -> 18.4 us
    ppermute x13 -> x10, starting transfers between devices: 29.4 us -> 23.4 us  [swapped(): return lax.ppermute(x, axis, [(i, i ^ bit) for i in range(count)])]
    ppermute x13 -> x10, waiting for transfers between devices: 5.64 us -> 10.8 us  [swapped(): return lax.ppermute(x, axis, [(i, i ^ bit) for i in range(count)])]
  transfers between devices with their start and end apart: 14 -> 11, of which waited for: 7 -> 8; matrix products, arithmetic and copies ran while one was open for 8% -> 8% of each run, Pallas kernels for 0% -> 0%
where the time goes in v15:
time: 131 us; the launch traced here: 129 us
  starting transfers between devices  35.7 us (27%)
  blocking collectives  25.2 us (19%)
  waiting for transfers between devices  18.4 us (14%)
  matrix products  16.1 us (12%)
  other arithmetic  14.5 us (11%)
  local copies, waits for them, and re-layouts  13.7 us (10%)
  between operations  5.72 us (4%)
    all_to_all x1, blocking collectives, exclusive_state_scan(): back = lax.all_to_all(sent_back, axis, 0, 0)  25.2 us
    ppermute x10, starting transfers between devices, swapped(): return lax.ppermute(x, axis, [(i, i ^ bit) for i in range(count)])  23.4 us
    all_to_all x1, starting transfers between devices, exclusive_state_scan(): got = lax.all_to_all(jnp.concatenate([slices, extra], axis=1), axis, 0, 0)  12.2 us
    ppermute x10, waiting for transfers between devices, swapped(): return lax.ppermute(x, axis, [(i, i ^ bit) for i in range(count)])  10.8 us
    all_to_all x1, waiting for transfers between devices, exclusive_state_scan(): got = lax.all_to_all(jnp.concatenate([slices, extra], axis=1), axis, 0, 0)  7.65 us
    unnamed x42, local copies, waits for them, and re-layouts  5.86 us
    dot_general x1, matrix products, local(): jnp.dot(features, w_query, preferred_element_type=jnp.float32)  3.28 us
    dot_general x1, matrix products, local(): jnp.einsum('hts,shd->thd', weights, v3, preferred_element_type=jnp.float32)  3.11 us
  transfers between devices with their start and end apart: 11, of which 8 were waited for; matrix products, arithmetic and copies ran while one was open for 8% of the time, Pallas kernels for 0%

profile of v15, /device:TPU:1, one launch (start us, length us, event | category | flops | bytes accessed | tf_op | source)
XLA Modules:
  0.0 129.3 jit_solution(5719757350508093065)
XLA Ops:
  0.7 0.9 fusion.60
  1.7 0.6 slice.72
  2.3 0.6 fusion.61
  3.5 0.8 fusion.41
  4.6 0.7 broadcast_compare_fusion.1
  6.1 1.8 %convolution_convert_fusion.1 = bf16[256,1024]{1,0:T(8,128)(2,1)S(1)} fusion(bf16[1024,1024]{1,0:T(8,128)(2,1)S(1)} %copy-done, bf16[1,256,1024]{2,1,0:T(8,128)(2,1)} %param.10), kind=kOutput, calls=%fused_computation.14 | convolution fusion | flops 537133056 | bytes 3145728 | tf_op jit(solution)/shard_map/dot_general | solution.py:116
  7.9 2.6 %convolution_convert_fusion.2 = bf16[256,1024]{1,0:T(8,128)(2,1)S(1)} fusion(bf16[1024,1024]{1,0:T(8,128)(2,1)} %param.15, bf16[1,256,1024]{2,1,0:T(8,128)(2,1)} %param.10), kind=kOutput, calls=%fused_computation.15 | convolution fusion | flops 537133056 | bytes 3145728 | tf_op jit(solution)/shard_map/dot_general | solution.py:115
  10.9 0.9 fusion.17
  12.3 0.7 convolution_multiply_fusion
  13.0 1.2 select_reduce_fusion.3
  14.2 1.5 %select_reduce_fusion.2 = f32[8,512,256]{2,1,0:T(8,128)S(1)} fusion(f32[8,2,512]{2,1,0:T(2,128)S(1)} %select_reduce_fusion.3, pred[2,256]{1,0:T(4,128)(4,1)S(1)} %iota_compare_fusion.8), kind=kLoop, calls=%fused_computation.2 | loop fusion | flops 3145728 | bytes 4227584 | tf_op jit(solution)/shard_map/reduce_sum | solution.py:155
  15.7 1.2 subtract_exponential_fusion
  17.0 1.9 %copy-done.1 = f32[8,512,256]{2,1,0:T(8,128)} copy-done((f32[8,512,256]{2,1,0:T(8,128)}, f32[8,512,256]{2,1,0:T(8,128)S(1)}, u32[]{:S(2)}) %copy-start.1) | copy-done | bytes 4194328
  18.9 1.2 select_reduce_fusion.1
  20.9 0.7 broadcast_select_fusion
  21.9 0.9 pad_maximum_fusion
  22.8 12.2 %all-to-all-start = ((f32[32,40,128]{2,1,0:T(8,128)}), f32[32,40,128]{2,1,0:T(8,128)S(1)}, u32[]{:S(2)}, u32[]{:S(2)}) async-start(f32[32,40,128]{2,1,0:T(8,128)} %pad_maximum_fusion), calls=%async_computation | async-start | bytes 1310720 | tf_op jit(solution)/shard_map/all_to_all | solution.py:62
  35.1 2.0 %copy.103 = bf16[256,1024]{0,1:T(8,128)(2,1)} copy(bf16[256,1024]{1,0:T(8,128)(2,1)} %copy-done.3) | data formatting | bytes 1048576 | tf_op jit(solution)/shard_map/reshape | solution.py:119
  37.2 3.3 %fusion.4 = bf16[32,8,8,128]{3,2,1,0:T(8,128)(2,1)} fusion(bf16[1024,1024]{1,0:T(8,128)(2,1)} %param.14, bf16[1,256,1024]{2,1,0:T(8,128)(2,1)} %param.10), kind=kOutput, calls=%fused_computation.16 | convolution fusion | flops 537133056 | bytes 3145728 | tf_op jit(solution)/shard_map/dot_general | solution.py:114
  40.5 3.1 %fusion.1 = f32[256,8,128]{0,2,1:T(8,128)} fusion(bf16[256,8,128]{0,2,1:T(8,128)(2,1)} %bitcast.171, f32[8,256]{1,0:T(8,128)S(1)} %bitcast.179, pred[256,256]{1,0:T(8,128)(4,1)S(1)} %fusion.40, bf16[32,8,8,128]{3,2,1,0:T(8,128)(2,1)} %fusion.4, bf16[256,1024]{1,0:T(8,128)(2,1)S(1)} %copy-done.5), kind=kOutput, calls=%fused_computation.9 | convolution fusion | flops 271581184 | bytes 2695168 | tf_op jit(solution)/shard_map/hts,shd->thd/dot_general | solution.py:145
  43.6 7.6 %all-to-all-done = f32[32,40,128]{2,1,0:T(8,128)S(1)} async-done(((f32[32,40,128]{2,1,0:T(8,128)}), f32[32,40,128]{2,1,0:T(8,128)S(1)}, u32[]{:S(2)}, u32[]{:S(2)}) %all-to-all-start) | async-done | bytes 655392 | tf_op jit(solution)/shard_map/all_to_all | solution.py:62
  53.1 0.6 select_reduce_fusion.4
  53.7 0.9 fusion.19
  55.0 25.2 %all_to_all.10 = f32[32,40,128]{2,1,0:T(8,128)S(1)} all-to-all(f32[32,40,128]{2,1,0:T(8,128)S(1)} %copy.91), channel_id=1, replica_groups=mesh['dp'=8,'ctx'=32] {'ctx'}, dimensions={0} | all-to-all | bytes 1310720 | tf_op jit(solution)/shard_map/all_to_all | solution.py:84
  80.4 1.0 fusion.66
  81.8 0.7 bitcast_multiply_fusion
  82.5 1.2 select_reduce_fusion
  84.4 1.1 fusion.65
  85.5 1.2 copy.104
  86.7 1.2 copy.105
  88.0 2.8 %collective-permute-start = (f32[2,512]{1,0:T(2,128)S(1)}, f32[2,512]{1,0:T(2,128)S(1)}, u32[]{:S(2)}, u32[]{:S(2)}) collective-permute-start(f32[2,512]{1,0:T(2,128)S(1)} %fusion.52), channel_id=1, source_target_pairs={{0,1},{1,0},{2,3},{3,2},{4,5},{5,4},{6,7},{7,6},{8,9},{9,8},{10,11... | collective-permute-start | bytes 12296 | tf_op jit(solution)/shard_map/ppermute | solution.py:17
  90.8 0.9 collective-permute-start.1
  91.6 1.3 %collective-permute-start.2 = (f32[2,512]{1,0:T(2,128)S(1)}, f32[2,512]{1,0:T(2,128)S(1)}, u32[]{:S(2)}, u32[]{:S(2)}) collective-permute-start(f32[2,512]{1,0:T(2,128)S(1)} %fusion.52), channel_id=1, source_target_pairs={{0,3},{1,2},{2,1},{3,0},{4,7},{5,6},{6,5},{7,4},{8,11},{9,10},{10,... | collective-permute-start | bytes 12296 | tf_op jit(solution)/shard_map/ppermute | solution.py:17
  92.9 1.2 collective-permute-done.1
  94.1 1.8 %collective-permute-done.2 = f32[2,512]{1,0:T(2,128)S(1)} collective-permute-done((f32[2,512]{1,0:T(2,128)S(1)}, f32[2,512]{1,0:T(2,128)S(1)}, u32[]{:S(2)}, u32[]{:S(2)}) %collective-permute-start.2) | collective-permute-done | bytes 4128 | tf_op jit(solution)/shard_map/ppermute | solution.py:17
  95.9 1.7 %collective-permute-start.3 = (f32[2,512]{1,0:T(2,128)S(1)}, f32[2,512]{1,0:T(2,128)S(1)}, u32[]{:S(2)}, u32[]{:S(2)}) collective-permute-start(f32[2,512]{1,0:T(2,128)S(1)} %add_add_fusion.1), channel_id=1, source_target_pairs={{0,4},{1,5},{2,6},{3,7},{4,0},{5,1},{6,2},{7,3},{8,12},{9,13},{10,... | collective-permute-start | bytes 12296 | tf_op jit(solution)/shard_map/ppermute | solution.py:17
  97.6 4.7 %collective-permute-done.3 = f32[2,512]{1,0:T(2,128)S(1)} collective-permute-done((f32[2,512]{1,0:T(2,128)S(1)}, f32[2,512]{1,0:T(2,128)S(1)}, u32[]{:S(2)}, u32[]{:S(2)}) %collective-permute-start.3) | collective-permute-done | bytes 4128 | tf_op jit(solution)/shard_map/ppermute | solution.py:17
  102.4 0.9 collective-permute-start.4
  103.3 1.7 %collective-permute-start.5 = (f32[2,512]{1,0:T(2,128)S(1)}, f32[2,512]{1,0:T(2,128)S(1)}, u32[]{:S(2)}, u32[]{:S(2)}) collective-permute-start(f32[2,512]{1,0:T(2,128)S(1)} %add.103), channel_id=1, source_target_pairs={{0,16},{1,17},{2,18},{3,19},{4,20},{5,21},{6,22},{7,23},{8,24},{9,... | collective-permute-start | bytes 12296 | tf_op jit(solution)/shard_map/ppermute | solution.py:17
  105.0 1.2 collective-permute-start.6
  106.6 1.0 copy.99
  107.6 1.0 collective-permute-done.6
  108.7 0.7 fusion.58
  109.4 1.1 multiply_reduce_fusion.1
  110.5 7.3 %collective-permute-start.7 = (f32[]{:T(128)}, f32[]{:T(128)}, u32[]{:S(2)}, u32[]{:S(2)}) collective-permute-start(f32[]{:T(128)} %get-tuple-element.36), channel_id=1, source_target_pairs={{0,32},{32,0},{64,96},{96,64},{128,160},{160,128},{192,224},{224,1... | collective-permute-start | bytes 20 | tf_op jit(solution)/shard_map/ppermute | solution.py:17
  117.8 1.0 collective-permute-done.7
  120.1 2.0 %collective-permute-start.8 = (f32[]{:T(128)}, f32[]{:T(128)}, u32[]{:S(2)}, u32[]{:S(2)}) collective-permute-start(f32[]{:T(128)} %add.112), channel_id=1, source_target_pairs={{0,64},{32,96},{64,0},{96,32},{128,192},{160,224},{192,128},{224,1... | collective-permute-start | bytes 20 | tf_op jit(solution)/shard_map/ppermute | solution.py:17
  123.4 3.5 %collective-permute-start.9 = (f32[]{:T(128)}, f32[]{:T(128)}, u32[]{:S(2)}, u32[]{:S(2)}) collective-permute-start(f32[]{:T(128)} %add.113), channel_id=1, source_target_pairs={{0,128},{32,160},{64,192},{96,224},{128,0},{160,32},{192,64},{224,... | collective-permute-start | bytes 20 | tf_op jit(solution)/shard_map/ppermute | solution.py:17
  (92 shorter events, 7.9 us)
Async XLA Ops:
  0.6 5.4 %copy-start = (bf16[1024,1024]{1,0:T(8,128)(2,1)S(1)}, bf16[1024,1024]{1,0:T(8,128)(2,1)}, u32[]{:S(2)}) copy-start(bf16[1024,1024]{1,0:T(8,128)(2,1)} %param.16) | copy-start | bytes 6291460
  7.8 3.9 %copy-start.3 = (bf16[256,1024]{1,0:T(8,128)(2,1)}, bf16[256,1024]{1,0:T(8,128)(2,1)S(1)}, u32[]{:S(2)}) copy-start(bf16[256,1024]{1,0:T(8,128)(2,1)S(1)} %convolution_convert_fusion.1) | copy-start | bytes 1572868
  10.5 1.3 copy-start.4
  10.9 1.1 copy-start.9
  10.9 1.4 %copy-start.8 = (bf16[512,1024]{1,0:T(8,128)(2,1)S(1)}, bf16[512,1024]{1,0:T(8,128)(2,1)}, u32[]{:S(2)}) copy-start(bf16[512,1024]{1,0:T(8,128)(2,1)} %param.18) | copy-start | bytes 3145732
  16.9 1.9 %copy-start.1 = (f32[8,512,256]{2,1,0:T(8,128)}, f32[8,512,256]{2,1,0:T(8,128)S(1)}, u32[]{:S(2)}) copy-start(f32[8,512,256]{2,1,0:T(8,128)S(1)} %subtract_exponential_fusion) | copy-start | bytes 12582916
  18.9 1.2 copy-start.12
  20.9 19.6 %copy-start.5 = (bf16[256,1024]{1,0:T(8,128)(2,1)S(1)}, bf16[256,1024]{1,0:T(8,128)(2,1)}, u32[]{:S(2)}) copy-start(bf16[256,1024]{1,0:T(8,128)(2,1)} %copy-done.4) | copy-start | bytes 1572868
  22.8 28.4 %all-to-all-start = ((f32[32,40,128]{2,1,0:T(8,128)}), f32[32,40,128]{2,1,0:T(8,128)S(1)}, u32[]{:S(2)}, u32[]{:S(2)}) async-start(f32[32,40,128]{2,1,0:T(8,128)} %pad_maximum_fusion), calls=%async_computation | async-start | bytes 1310720 | tf_op jit(solution)/shard_map/all_to_all | solution.py:62
  52.7 27.6 %copy-start.10 = (bf16[32,8,8,128]{3,2,1,0:T(8,128)(2,1)S(1)}, bf16[32,8,8,128]{3,2,1,0:T(8,128)(2,1)}, u32[]{:S(2)}) copy-start(bf16[32,8,8,128]{3,2,1,0:T(8,128)(2,1)} %fusion.4) | copy-start | bytes 1572868
  53.0 27.3 %copy-start.7 = (f32[256,8,128]{0,2,1:T(8,128)S(1)}, f32[256,8,128]{0,2,1:T(8,128)}, u32[]{:S(2)}) copy-start(f32[256,8,128]{0,2,1:T(8,128)} %fusion.1) | copy-start | bytes 3145732
  54.6 26.9 %copy-start.11 = (f32[1024]{0:T(1024)S(1)}, f32[1024]{0:T(1024)}, u32[]{:S(2)}) copy-start(f32[1024]{0:T(1024)} %param.17) | copy-start | bytes 12292
  55.0 26.8 %copy-start.2 = (f32[8,512,256]{2,1,0:T(8,128)S(1)}, f32[8,512,256]{2,1,0:T(8,128)}, u32[]{:S(2)}) copy-start(f32[8,512,256]{2,1,0:T(8,128)} %copy-done.1) | copy-start | bytes 12582916
  55.0 26.8 %copy-start.6 = (bf16[512,1024]{1,0:T(8,128)(2,1)S(1)}, bf16[512,1024]{1,0:T(8,128)(2,1)}, u32[]{:S(2)}) copy-start(bf16[512,1024]{1,0:T(8,128)(2,1)} %param.19) | copy-start | bytes 3145732
  82.5 15.1 %copy-start.13 = (s32[1,2]{1,0:T(1,128)S(1)}, s32[1,2]{1,0:T(1,128)}, u32[]{:S(2)}) copy-start(s32[1,2]{1,0:T(1,128)} %param.12) | copy-start | bytes 28
  88.0 5.0 %collective-permute-start = (f32[2,512]{1,0:T(2,128)S(1)}, f32[2,512]{1,0:T(2,128)S(1)}, u32[]{:S(2)}, u32[]{:S(2)}) collective-permute-start(f32[2,512]{1,0:T(2,128)S(1)} %fusion.52), channel_id=1, source_target_pairs={{0,1},{1,0},{2,3},{3,2},{4,5},{5,4},{6,7},{7,6},{8,9},{9,8},{10,11... | collective-permute-start | bytes 12296 | tf_op jit(solution)/shard_map/ppermute | solution.py:17
  90.8 3.4 %collective-permute-start.1 = (f32[2,512]{1,0:T(2,128)S(1)}, f32[2,512]{1,0:T(2,128)S(1)}, u32[]{:S(2)}, u32[]{:S(2)}) collective-permute-start(f32[2,512]{1,0:T(2,128)S(1)} %fusion.52), channel_id=1, source_target_pairs={{0,2},{1,3},{2,0},{3,1},{4,6},{5,7},{6,4},{7,5},{8,10},{9,11},{10,... | collective-permute-start | bytes 12296 | tf_op jit(solution)/shard_map/ppermute | solution.py:17
  91.6 4.3 %collective-permute-start.2 = (f32[2,512]{1,0:T(2,128)S(1)}, f32[2,512]{1,0:T(2,128)S(1)}, u32[]{:S(2)}, u32[]{:S(2)}) collective-permute-start(f32[2,512]{1,0:T(2,128)S(1)} %fusion.52), channel_id=1, source_target_pairs={{0,3},{1,2},{2,1},{3,0},{4,7},{5,6},{6,5},{7,4},{8,11},{9,10},{10,... | collective-permute-start | bytes 12296 | tf_op jit(solution)/shard_map/ppermute | solution.py:17
  95.9 6.4 %collective-permute-start.3 = (f32[2,512]{1,0:T(2,128)S(1)}, f32[2,512]{1,0:T(2,128)S(1)}, u32[]{:S(2)}, u32[]{:S(2)}) collective-permute-start(f32[2,512]{1,0:T(2,128)S(1)} %add_add_fusion.1), channel_id=1, source_target_pairs={{0,4},{1,5},{2,6},{3,7},{4,0},{5,1},{6,2},{7,3},{8,12},{9,13},{10,... | collective-permute-start | bytes 12296 | tf_op jit(solution)/shard_map/ppermute | solution.py:17
  102.4 5.2 %collective-permute-start.4 = (f32[2,512]{1,0:T(2,128)S(1)}, f32[2,512]{1,0:T(2,128)S(1)}, u32[]{:S(2)}, u32[]{:S(2)}) collective-permute-start(f32[2,512]{1,0:T(2,128)S(1)} %add.103), channel_id=1, source_target_pairs={{0,8},{1,9},{2,10},{3,11},{4,12},{5,13},{6,14},{7,15},{8,0},{9,1},... | collective-permute-start | bytes 12296 | tf_op jit(solution)/shard_map/ppermute | solution.py:17
  103.3 4.3 %collective-permute-start.5 = (f32[2,512]{1,0:T(2,128)S(1)}, f32[2,512]{1,0:T(2,128)S(1)}, u32[]{:S(2)}, u32[]{:S(2)}) collective-permute-start(f32[2,512]{1,0:T(2,128)S(1)} %add.103), channel_id=1, source_target_pairs={{0,16},{1,17},{2,18},{3,19},{4,20},{5,21},{6,22},{7,23},{8,24},{9,... | collective-permute-start | bytes 12296 | tf_op jit(solution)/shard_map/ppermute | solution.py:17
  105.0 3.7 %collective-permute-start.6 = (f32[2,512]{1,0:T(2,128)S(1)}, f32[2,512]{1,0:T(2,128)S(1)}, u32[]{:S(2)}, u32[]{:S(2)}) collective-permute-start(f32[2,512]{1,0:T(2,128)S(1)} %add.103), channel_id=1, source_target_pairs={{0,24},{1,25},{2,26},{3,27},{4,28},{5,29},{6,30},{7,31},{8,16},{9,... | collective-permute-start | bytes 12296 | tf_op jit(solution)/shard_map/ppermute | solution.py:17
  110.5 8.3 %collective-permute-start.7 = (f32[]{:T(128)}, f32[]{:T(128)}, u32[]{:S(2)}, u32[]{:S(2)}) collective-permute-start(f32[]{:T(128)} %get-tuple-element.36), channel_id=1, source_target_pairs={{0,32},{32,0},{64,96},{96,64},{128,160},{160,128},{192,224},{224,1... | collective-permute-start | bytes 20 | tf_op jit(solution)/shard_map/ppermute | solution.py:17
  120.1 2.6 %collective-permute-start.8 = (f32[]{:T(128)}, f32[]{:T(128)}, u32[]{:S(2)}, u32[]{:S(2)}) collective-permute-start(f32[]{:T(128)} %add.112), channel_id=1, source_target_pairs={{0,64},{32,96},{64,0},{96,32},{128,192},{160,224},{192,128},{224,1... | collective-permute-start | bytes 20 | tf_op jit(solution)/shard_map/ppermute | solution.py:17
  123.4 4.1 %collective-permute-start.9 = (f32[]{:T(128)}, f32[]{:T(128)}, u32[]{:S(2)}, u32[]{:S(2)}) collective-permute-start(f32[]{:T(128)} %add.113), channel_id=1, source_target_pairs={{0,128},{32,160},{64,192},{96,224},{128,0},{160,32},{192,64},{224,... | collective-permute-start | bytes 20 | tf_op jit(solution)/shard_map/ppermute | solution.py:17

commit v16 on v15

--- a/solution.py
+++ b/solution.py
@@ -198,7 +198,7 @@
     count = lax.axis_size("ctx")
     assert count & (count - 1) == 0
     stride = 1
-    for size in (4, 2, 4):
+    for size in (4, 2, 2, 2):
         size = min(size, count // stride)
         if size > 1:
             part = group_sum(part, "ctx", stride, size)

time: 131 us -> 132 us (level)
    ppermute x10 -> x9, starting transfers between devices: 23.4 us -> 24.3 us  [swapped(): return lax.ppermute(x, axis, [(i, i ^ bit) for i in range(count)])]
    ppermute x10 -> x9, waiting for transfers between devices: 10.8 us -> 11.3 us  [swapped(): return lax.ppermute(x, axis, [(i, i ^ bit) for i in range(count)])]
  transfers between devices with their start and end apart: 11 -> 10, of which waited for: 8 -> 8; matrix products, arithmetic and copies ran while one was open for 8% -> 8% of each run, Pallas kernels for 0% -> 0%
where the time goes in v16:
time: 132 us; the launch traced here: 131 us
  starting transfers between devices  36.5 us (28%)
  blocking collectives  25.2 us (19%)
  waiting for transfers between devices  18.9 us (14%)
  matrix products  16.1 us (12%)
  other arithmetic  14.5 us (11%)
  local copies, waits for them, and re-layouts  13.7 us (10%)
  between operations  5.72 us (4%)
    all_to_all x1, blocking collectives, exclusive_state_scan(): back = lax.all_to_all(sent_back, axis, 0, 0)  25.2 us
    ppermute x9, starting transfers between devices, swapped(): return lax.ppermute(x, axis, [(i, i ^ bit) for i in range(count)])  24.3 us
    all_to_all x1, starting transfers between devices, exclusive_state_scan(): got = lax.all_to_all(jnp.concatenate([slices, extra], axis=1), axis, 0, 0)  12.2 us
    ppermute x9, waiting for transfers between devices, swapped(): return lax.ppermute(x, axis, [(i, i ^ bit) for i in range(count)])  11.3 us
    all_to_all x1, waiting for transfers between devices, exclusive_state_scan(): got = lax.all_to_all(jnp.concatenate([slices, extra], axis=1), axis, 0, 0)  7.65 us
    unnamed x42, local copies, waits for them, and re-layouts  5.86 us
    dot_general x1, matrix products, local(): jnp.dot(features, w_query, preferred_element_type=jnp.float32)  3.28 us
    dot_general x1, matrix products, local(): jnp.einsum('hts,shd->thd', weights, v3, preferred_element_type=jnp.float32)  3.11 us
  transfers between devices with their start and end apart: 10, of which 8 were waited for; matrix products, arithmetic and copies ran while one was open for 8% of the time, Pallas kernels for 0%

profile of v16, /device:TPU:1, one launch (start us, length us, event | category | flops | bytes accessed | tf_op | source)
XLA Modules:
  0.0 130.6 jit_solution(12654965880819245208)
XLA Ops:
  0.7 0.9 fusion.60
  1.7 0.6 slice.72
  2.3 0.6 fusion.61
  3.5 0.8 fusion.41
  4.6 0.7 broadcast_compare_fusion.1
  5.3 0.6 slice.82
  6.1 1.8 %convolution_convert_fusion.1 = bf16[256,1024]{1,0:T(8,128)(2,1)S(1)} fusion(bf16[1024,1024]{1,0:T(8,128)(2,1)S(1)} %copy-done, bf16[1,256,1024]{2,1,0:T(8,128)(2,1)} %param.10), kind=kOutput, calls=%fused_computation.14 | convolution fusion | flops 537133056 | bytes 3145728 | tf_op jit(solution)/shard_map/dot_general | solution.py:116
  7.9 2.6 %convolution_convert_fusion.2 = bf16[256,1024]{1,0:T(8,128)(2,1)S(1)} fusion(bf16[1024,1024]{1,0:T(8,128)(2,1)} %param.15, bf16[1,256,1024]{2,1,0:T(8,128)(2,1)} %param.10), kind=kOutput, calls=%fused_computation.15 | convolution fusion | flops 537133056 | bytes 3145728 | tf_op jit(solution)/shard_map/dot_general | solution.py:115
  10.9 0.9 fusion.17
  12.3 0.7 convolution_multiply_fusion
  13.0 1.2 select_reduce_fusion.3
  14.2 1.5 %select_reduce_fusion.2 = f32[8,512,256]{2,1,0:T(8,128)S(1)} fusion(f32[8,2,512]{2,1,0:T(2,128)S(1)} %select_reduce_fusion.3, pred[2,256]{1,0:T(4,128)(4,1)S(1)} %iota_compare_fusion.8), kind=kLoop, calls=%fused_computation.2 | loop fusion | flops 3145728 | bytes 4227584 | tf_op jit(solution)/shard_map/reduce_sum | solution.py:155
  15.7 1.2 subtract_exponential_fusion
  17.0 1.9 %copy-done.1 = f32[8,512,256]{2,1,0:T(8,128)} copy-done((f32[8,512,256]{2,1,0:T(8,128)}, f32[8,512,256]{2,1,0:T(8,128)S(1)}, u32[]{:S(2)}) %copy-start.1) | copy-done | bytes 4194328
  18.9 1.2 select_reduce_fusion.1
  20.9 0.7 broadcast_select_fusion
  21.9 0.9 pad_maximum_fusion
  22.8 12.2 %all-to-all-start = ((f32[32,40,128]{2,1,0:T(8,128)}), f32[32,40,128]{2,1,0:T(8,128)S(1)}, u32[]{:S(2)}, u32[]{:S(2)}) async-start(f32[32,40,128]{2,1,0:T(8,128)} %pad_maximum_fusion), calls=%async_computation | async-start | bytes 1310720 | tf_op jit(solution)/shard_map/all_to_all | solution.py:62
  35.1 2.0 %copy.103 = bf16[256,1024]{0,1:T(8,128)(2,1)} copy(bf16[256,1024]{1,0:T(8,128)(2,1)} %copy-done.3) | data formatting | bytes 1048576 | tf_op jit(solution)/shard_map/reshape | solution.py:119
  37.2 3.3 %fusion.4 = bf16[32,8,8,128]{3,2,1,0:T(8,128)(2,1)} fusion(bf16[1024,1024]{1,0:T(8,128)(2,1)} %param.14, bf16[1,256,1024]{2,1,0:T(8,128)(2,1)} %param.10), kind=kOutput, calls=%fused_computation.16 | convolution fusion | flops 537133056 | bytes 3145728 | tf_op jit(solution)/shard_map/dot_general | solution.py:114
  40.5 3.1 %fusion.1 = f32[256,8,128]{0,2,1:T(8,128)} fusion(bf16[256,8,128]{0,2,1:T(8,128)(2,1)} %bitcast.172, f32[8,256]{1,0:T(8,128)S(1)} %bitcast.180, pred[256,256]{1,0:T(8,128)(4,1)S(1)} %fusion.40, bf16[32,8,8,128]{3,2,1,0:T(8,128)(2,1)} %fusion.4, bf16[256,1024]{1,0:T(8,128)(2,1)S(1)} %copy-done.5), kind=kOutput, calls=%fused_computation.9 | convolution fusion | flops 271581184 | bytes 2695168 | tf_op jit(solution)/shard_map/hts,shd->thd/dot_general | solution.py:145
  43.6 7.6 %all-to-all-done = f32[32,40,128]{2,1,0:T(8,128)S(1)} async-done(((f32[32,40,128]{2,1,0:T(8,128)}), f32[32,40,128]{2,1,0:T(8,128)S(1)}, u32[]{:S(2)}, u32[]{:S(2)}) %all-to-all-start) | async-done | bytes 655392 | tf_op jit(solution)/shard_map/all_to_all | solution.py:62
  53.1 0.6 select_reduce_fusion.4
  53.7 0.9 fusion.19
  55.0 25.2 %all_to_all.10 = f32[32,40,128]{2,1,0:T(8,128)S(1)} all-to-all(f32[32,40,128]{2,1,0:T(8,128)S(1)} %copy.91), channel_id=1, replica_groups=mesh['dp'=8,'ctx'=32] {'ctx'}, dimensions={0} | all-to-all | bytes 1310720 | tf_op jit(solution)/shard_map/all_to_all | solution.py:84
  80.4 1.0 fusion.66
  81.8 0.7 bitcast_multiply_fusion
  82.5 1.2 select_reduce_fusion
  84.4 1.1 fusion.65
  85.5 1.2 copy.104
  86.7 1.2 copy.105
  88.0 2.8 %collective-permute-start = (f32[2,512]{1,0:T(2,128)S(1)}, f32[2,512]{1,0:T(2,128)S(1)}, u32[]{:S(2)}, u32[]{:S(2)}) collective-permute-start(f32[2,512]{1,0:T(2,128)S(1)} %fusion.52), channel_id=1, source_target_pairs={{0,1},{1,0},{2,3},{3,2},{4,5},{5,4},{6,7},{7,6},{8,9},{9,8},{10,11... | collective-permute-start | bytes 12296 | tf_op jit(solution)/shard_map/ppermute | solution.py:17
  90.8 0.9 collective-permute-start.1
  91.6 1.3 collective-permute-start.2
  92.9 1.2 collective-permute-done.1
  94.1 1.8 %collective-permute-done.2 = f32[2,512]{1,0:T(2,128)S(1)} collective-permute-done((f32[2,512]{1,0:T(2,128)S(1)}, f32[2,512]{1,0:T(2,128)S(1)}, u32[]{:S(2)}, u32[]{:S(2)}) %collective-permute-start.2) | collective-permute-done | bytes 4128 | tf_op jit(solution)/shard_map/ppermute | solution.py:17
  95.9 1.7 %collective-permute-start.3 = (f32[2,512]{1,0:T(2,128)S(1)}, f32[2,512]{1,0:T(2,128)S(1)}, u32[]{:S(2)}, u32[]{:S(2)}) collective-permute-start(f32[2,512]{1,0:T(2,128)S(1)} %add_add_fusion), channel_id=1, source_target_pairs={{0,4},{1,5},{2,6},{3,7},{4,0},{5,1},{6,2},{7,3},{8,12},{9,13},{10,... | collective-permute-start | bytes 12296 | tf_op jit(solution)/shard_map/ppermute | solution.py:17
  97.6 4.7 %collective-permute-done.3 = f32[2,512]{1,0:T(2,128)S(1)} collective-permute-done((f32[2,512]{1,0:T(2,128)S(1)}, f32[2,512]{1,0:T(2,128)S(1)}, u32[]{:S(2)}, u32[]{:S(2)}) %collective-permute-start.3) | collective-permute-done | bytes 4128 | tf_op jit(solution)/shard_map/ppermute | solution.py:17
  102.4 0.9 collective-permute-start.4
  103.3 1.5 %collective-permute-done.4 = f32[2,512]{1,0:T(2,128)S(1)} collective-permute-done((f32[2,512]{1,0:T(2,128)S(1)}, f32[2,512]{1,0:T(2,128)S(1)}, u32[]{:S(2)}, u32[]{:S(2)}) %collective-permute-start.4) | collective-permute-done | bytes 4128 | tf_op jit(solution)/shard_map/ppermute | solution.py:17
  104.8 2.6 %collective-permute-start.5 = (f32[2,512]{1,0:T(2,128)S(1)}, f32[2,512]{1,0:T(2,128)S(1)}, u32[]{:S(2)}, u32[]{:S(2)}) collective-permute-start(f32[2,512]{1,0:T(2,128)S(1)} %add.101), channel_id=1, source_target_pairs={{0,16},{1,17},{2,18},{3,19},{4,20},{5,21},{6,22},{7,23},{8,24},{9,... | collective-permute-start | bytes 12296 | tf_op jit(solution)/shard_map/ppermute | solution.py:17
  107.8 1.0 copy.99
  108.8 0.7 fusion.58
  109.5 1.1 multiply_reduce_fusion.1
  110.6 8.5 %collective-permute-start.6 = (f32[]{:T(128)}, f32[]{:T(128)}, u32[]{:S(2)}, u32[]{:S(2)}) collective-permute-start(f32[]{:T(128)} %get-tuple-element.36), channel_id=1, source_target_pairs={{0,32},{32,0},{64,96},{96,64},{128,160},{160,128},{192,224},{224,1... | collective-permute-start | bytes 20 | tf_op jit(solution)/shard_map/ppermute | solution.py:17
  119.1 1.0 collective-permute-done.6
  121.4 2.0 %collective-permute-start.7 = (f32[]{:T(128)}, f32[]{:T(128)}, u32[]{:S(2)}, u32[]{:S(2)}) collective-permute-start(f32[]{:T(128)} %add.108), channel_id=1, source_target_pairs={{0,64},{32,96},{64,0},{96,32},{128,192},{160,224},{192,128},{224,1... | collective-permute-start | bytes 20 | tf_op jit(solution)/shard_map/ppermute | solution.py:17
  124.7 3.5 %collective-permute-start.8 = (f32[]{:T(128)}, f32[]{:T(128)}, u32[]{:S(2)}, u32[]{:S(2)}) collective-permute-start(f32[]{:T(128)} %add.109), channel_id=1, source_target_pairs={{0,128},{32,160},{64,192},{96,224},{128,0},{160,32},{192,64},{224,... | collective-permute-start | bytes 20 | tf_op jit(solution)/shard_map/ppermute | solution.py:17
  (91 shorter events, 7.3 us)
Async XLA Ops:
  0.6 5.4 %copy-start = (bf16[1024,1024]{1,0:T(8,128)(2,1)S(1)}, bf16[1024,1024]{1,0:T(8,128)(2,1)}, u32[]{:S(2)}) copy-start(bf16[1024,1024]{1,0:T(8,128)(2,1)} %param.16) | copy-start | bytes 6291460
  7.8 3.9 %copy-start.3 = (bf16[256,1024]{1,0:T(8,128)(2,1)}, bf16[256,1024]{1,0:T(8,128)(2,1)S(1)}, u32[]{:S(2)}) copy-start(bf16[256,1024]{1,0:T(8,128)(2,1)S(1)} %convolution_convert_fusion.1) | copy-start | bytes 1572868
  10.5 1.3 copy-start.4
  10.9 1.1 copy-start.9
  10.9 1.4 %copy-start.8 = (bf16[512,1024]{1,0:T(8,128)(2,1)S(1)}, bf16[512,1024]{1,0:T(8,128)(2,1)}, u32[]{:S(2)}) copy-start(bf16[512,1024]{1,0:T(8,128)(2,1)} %param.18) | copy-start | bytes 3145732
  16.9 1.9 %copy-start.1 = (f32[8,512,256]{2,1,0:T(8,128)}, f32[8,512,256]{2,1,0:T(8,128)S(1)}, u32[]{:S(2)}) copy-start(f32[8,512,256]{2,1,0:T(8,128)S(1)} %subtract_exponential_fusion) | copy-start | bytes 12582916
  18.9 1.2 copy-start.12
  20.9 19.6 %copy-start.5 = (bf16[256,1024]{1,0:T(8,128)(2,1)S(1)}, bf16[256,1024]{1,0:T(8,128)(2,1)}, u32[]{:S(2)}) copy-start(bf16[256,1024]{1,0:T(8,128)(2,1)} %copy-done.4) | copy-start | bytes 1572868
  22.8 28.4 %all-to-all-start = ((f32[32,40,128]{2,1,0:T(8,128)}), f32[32,40,128]{2,1,0:T(8,128)S(1)}, u32[]{:S(2)}, u32[]{:S(2)}) async-start(f32[32,40,128]{2,1,0:T(8,128)} %pad_maximum_fusion), calls=%async_computation | async-start | bytes 1310720 | tf_op jit(solution)/shard_map/all_to_all | solution.py:62
  52.7 27.6 %copy-start.10 = (bf16[32,8,8,128]{3,2,1,0:T(8,128)(2,1)S(1)}, bf16[32,8,8,128]{3,2,1,0:T(8,128)(2,1)}, u32[]{:S(2)}) copy-start(bf16[32,8,8,128]{3,2,1,0:T(8,128)(2,1)} %fusion.4) | copy-start | bytes 1572868
  53.0 27.3 %copy-start.7 = (f32[256,8,128]{0,2,1:T(8,128)S(1)}, f32[256,8,128]{0,2,1:T(8,128)}, u32[]{:S(2)}) copy-start(f32[256,8,128]{0,2,1:T(8,128)} %fusion.1) | copy-start | bytes 3145732
  54.6 26.9 %copy-start.11 = (f32[1024]{0:T(1024)S(1)}, f32[1024]{0:T(1024)}, u32[]{:S(2)}) copy-start(f32[1024]{0:T(1024)} %param.17) | copy-start | bytes 12292
  55.0 26.8 %copy-start.2 = (f32[8,512,256]{2,1,0:T(8,128)S(1)}, f32[8,512,256]{2,1,0:T(8,128)}, u32[]{:S(2)}) copy-start(f32[8,512,256]{2,1,0:T(8,128)} %copy-done.1) | copy-start | bytes 12582916
  55.0 26.8 %copy-start.6 = (bf16[512,1024]{1,0:T(8,128)(2,1)S(1)}, bf16[512,1024]{1,0:T(8,128)(2,1)}, u32[]{:S(2)}) copy-start(bf16[512,1024]{1,0:T(8,128)(2,1)} %param.19) | copy-start | bytes 3145732
  82.5 20.8 %copy-start.13 = (s32[1,2]{1,0:T(1,128)S(1)}, s32[1,2]{1,0:T(1,128)}, u32[]{:S(2)}) copy-start(s32[1,2]{1,0:T(1,128)} %param.12) | copy-start | bytes 28
  88.0 5.0 %collective-permute-start = (f32[2,512]{1,0:T(2,128)S(1)}, f32[2,512]{1,0:T(2,128)S(1)}, u32[]{:S(2)}, u32[]{:S(2)}) collective-permute-start(f32[2,512]{1,0:T(2,128)S(1)} %fusion.52), channel_id=1, source_target_pairs={{0,1},{1,0},{2,3},{3,2},{4,5},{5,4},{6,7},{7,6},{8,9},{9,8},{10,11... | collective-permute-start | bytes 12296 | tf_op jit(solution)/shard_map/ppermute | solution.py:17
  90.8 3.4 %collective-permute-start.1 = (f32[2,512]{1,0:T(2,128)S(1)}, f32[2,512]{1,0:T(2,128)S(1)}, u32[]{:S(2)}, u32[]{:S(2)}) collective-permute-start(f32[2,512]{1,0:T(2,128)S(1)} %fusion.52), channel_id=1, source_target_pairs={{0,2},{1,3},{2,0},{3,1},{4,6},{5,7},{6,4},{7,5},{8,10},{9,11},{10,... | collective-permute-start | bytes 12296 | tf_op jit(solution)/shard_map/ppermute | solution.py:17
  91.6 4.3 %collective-permute-start.2 = (f32[2,512]{1,0:T(2,128)S(1)}, f32[2,512]{1,0:T(2,128)S(1)}, u32[]{:S(2)}, u32[]{:S(2)}) collective-permute-start(f32[2,512]{1,0:T(2,128)S(1)} %fusion.52), channel_id=1, source_target_pairs={{0,3},{1,2},{2,1},{3,0},{4,7},{5,6},{6,5},{7,4},{8,11},{9,10},{10,... | collective-permute-start | bytes 12296 | tf_op jit(solution)/shard_map/ppermute | solution.py:17
  95.9 6.4 %collective-permute-start.3 = (f32[2,512]{1,0:T(2,128)S(1)}, f32[2,512]{1,0:T(2,128)S(1)}, u32[]{:S(2)}, u32[]{:S(2)}) collective-permute-start(f32[2,512]{1,0:T(2,128)S(1)} %add_add_fusion), channel_id=1, source_target_pairs={{0,4},{1,5},{2,6},{3,7},{4,0},{5,1},{6,2},{7,3},{8,12},{9,13},{10,... | collective-permute-start | bytes 12296 | tf_op jit(solution)/shard_map/ppermute | solution.py:17
  102.4 2.5 %collective-permute-start.4 = (f32[2,512]{1,0:T(2,128)S(1)}, f32[2,512]{1,0:T(2,128)S(1)}, u32[]{:S(2)}, u32[]{:S(2)}) collective-permute-start(f32[2,512]{1,0:T(2,128)S(1)} %add.100), channel_id=1, source_target_pairs={{0,8},{1,9},{2,10},{3,11},{4,12},{5,13},{6,14},{7,15},{8,0},{9,1},... | collective-permute-start | bytes 12296 | tf_op jit(solution)/shard_map/ppermute | solution.py:17
  104.8 4.0 %collective-permute-start.5 = (f32[2,512]{1,0:T(2,128)S(1)}, f32[2,512]{1,0:T(2,128)S(1)}, u32[]{:S(2)}, u32[]{:S(2)}) collective-permute-start(f32[2,512]{1,0:T(2,128)S(1)} %add.101), channel_id=1, source_target_pairs={{0,16},{1,17},{2,18},{3,19},{4,20},{5,21},{6,22},{7,23},{8,24},{9,... | collective-permute-start | bytes 12296 | tf_op jit(solution)/shard_map/ppermute | solution.py:17
  110.6 9.4 %collective-permute-start.6 = (f32[]{:T(128)}, f32[]{:T(128)}, u32[]{:S(2)}, u32[]{:S(2)}) collective-permute-start(f32[]{:T(128)} %get-tuple-element.36), channel_id=1, source_target_pairs={{0,32},{32,0},{64,96},{96,64},{128,160},{160,128},{192,224},{224,1... | collective-permute-start | bytes 20 | tf_op jit(solution)/shard_map/ppermute | solution.py:17
  121.4 2.6 %collective-permute-start.7 = (f32[]{:T(128)}, f32[]{:T(128)}, u32[]{:S(2)}, u32[]{:S(2)}) collective-permute-start(f32[]{:T(128)} %add.108), channel_id=1, source_target_pairs={{0,64},{32,96},{64,0},{96,32},{128,192},{160,224},{192,128},{224,1... | collective-permute-start | bytes 20 | tf_op jit(solution)/shard_map/ppermute | solution.py:17
  124.7 4.1 %collective-permute-start.8 = (f32[]{:T(128)}, f32[]{:T(128)}, u32[]{:S(2)}, u32[]{:S(2)}) collective-permute-start(f32[]{:T(128)} %add.109), channel_id=1, source_target_pairs={{0,128},{32,160},{64,192},{96,224},{128,0},{160,32},{192,64},{224,... | collective-permute-start | bytes 20 | tf_op jit(solution)/shard_map/ppermute | solution.py:17

commit v17 on v15

--- a/solution.py
+++ b/solution.py
@@ -166,15 +166,13 @@
         [
             jnp.transpose(maxima, (1, 2, 0)),
             jnp.transpose(mass, (1, 2, 0)),
-            counts[:, :, None],
         ],
         axis=2,
-    ).reshape(record_count * label_count, 2 * head_count + 1)
+    ).reshape(record_count * label_count, 2 * head_count)
     incoming, totals, intra = exclusive_state_scan(local_state, carry, stats, intra, "ctx")
-    totals = totals.reshape(record_count, label_count, 2 * head_count + 1)
+    totals = totals.reshape(record_count, label_count, 2 * head_count)
     top = jnp.transpose(totals[:, :, :head_count], (2, 0, 1))
     total_mass = jnp.transpose(totals[:, :, head_count:2 * head_count], (2, 0, 1))
-    total_counts = totals[:, :, 2 * head_count]
     rescale = jnp.exp(maxima - top) / total_mass
 
     q_decayed = q3.astype(jnp.float32) * jnp.where(linked[None, :], jnp.exp(decay_cum), 0.0).T[:, :, None]
@@ -194,7 +192,7 @@
     weighted = jnp.sum(
         jnp.where(member[None, :, None, :], (pool_weight * label_value)[:, None], 0.0), axis=3
     )
-    part = jnp.sum(weighted * rescale, axis=0)
+    part = jnp.stack([jnp.sum(weighted * rescale, axis=0), counts])
     count = lax.axis_size("ctx")
     assert count & (count - 1) == 0
     stride = 1
@@ -204,7 +202,8 @@
             part = group_sum(part, "ctx", stride, size)
             stride *= size
     assert stride == count
-    logits = part
+    logits = part[0]
+    total_counts = part[1]
     target = (total_counts + 0.5) / (lengths[0].astype(jnp.float32)[:, None] + 1.0)
     rec_loss = jnp.mean(jax.nn.softplus(logits) - target * logits, axis=1)
     loss_sum = jnp.sum(rec_loss)

time: 131 us -> 131 us (level)
  blocking collectives: 25.2 us -> 0 us
  waiting for transfers between devices: 18.4 us -> 35.3 us
  starting transfers between devices: 35.7 us -> 44.2 us
    all_to_all x1 -> x0, blocking collectives: 25.2 us -> none  [exclusive_state_scan(): back = lax.all_to_all(sent_back, axis, 0, 0)]
    all_to_all x0 -> x1, waiting for transfers between devices: none -> 16.6 us  [exclusive_state_scan(): back = lax.all_to_all(sent_back, axis, 0, 0)]
    all_to_all x0 -> x1, starting transfers between devices: none -> 8.39 us  [exclusive_state_scan(): back = lax.all_to_all(sent_back, axis, 0, 0)]
    dot_general x1, matrix products: 1.01 us -> 2.37 us  [local(): jnp.einsum('thd,hde->the', q_decayed, incoming, precision=lax.Precision.H...]
    unnamed x42 -> x39, local copies, waits for them, and re-layouts: 5.86 us -> 5.83 us
  transfers between devices with their start and end apart: 11 -> 12, of which waited for: 8 -> 10; matrix products, arithmetic and copies ran while one was open for 8% -> 8% of each run, Pallas kernels for 0% -> 0%
where the time goes in v17:
time: 131 us; the launch traced here: 130 us
  starting transfers between devices  44.2 us (34%)
  waiting for transfers between devices  35.3 us (27%)
  matrix products  17.4 us (13%)
  other arithmetic  13.8 us (11%)
  local copies, waits for them, and re-layouts  13.4 us (10%)
  between operations  5.71 us (4%)
    ppermute x10, starting transfers between devices, swapped(): return lax.ppermute(x, axis, [(i, i ^ bit) for i in range(count)])  23.6 us
    all_to_all x1, waiting for transfers between devices, exclusive_state_scan(): back = lax.all_to_all(sent_back, axis, 0, 0)  16.6 us
    all_to_all x1, starting transfers between devices, exclusive_state_scan(): got = lax.all_to_all(jnp.concatenate([slices, extra], axis=1), axis, 0, 0)  12.2 us
    ppermute x10, waiting for transfers between devices, swapped(): return lax.ppermute(x, axis, [(i, i ^ bit) for i in range(count)])  11.1 us
    all_to_all x1, starting transfers between devices, exclusive_state_scan(): back = lax.all_to_all(sent_back, axis, 0, 0)  8.39 us
    all_to_all x1, waiting for transfers between devices, exclusive_state_scan(): got = lax.all_to_all(jnp.concatenate([slices, extra], axis=1), axis, 0, 0)  7.65 us
    unnamed x39, local copies, waits for them, and re-layouts  5.83 us
    dot_general x1, matrix products, local(): jnp.dot(features, w_query, preferred_element_type=jnp.float32)  3.28 us
  transfers between devices with their start and end apart: 12, of which 10 were waited for; matrix products, arithmetic and copies ran while one was open for 8% of the time, Pallas kernels for 0%

profile of v17, /device:TPU:1, one launch (start us, length us, event | category | flops | bytes accessed | tf_op | source)
XLA Modules:
  0.0 129.9 jit_solution(17067242989884117467)
XLA Ops:
  0.7 0.9 fusion.64
  2.3 0.6 fusion.65
  3.5 0.8 fusion.39
  4.6 0.7 broadcast_compare_fusion.1
  6.1 1.8 %convolution_convert_fusion.1 = bf16[256,1024]{1,0:T(8,128)(2,1)S(1)} fusion(bf16[1024,1024]{1,0:T(8,128)(2,1)S(1)} %copy-done, bf16[1,256,1024]{2,1,0:T(8,128)(2,1)} %param.10), kind=kOutput, calls=%fused_computation.14 | convolution fusion | flops 537133056 | bytes 3145728 | tf_op jit(solution)/shard_map/dot_general | solution.py:116
  7.9 2.6 %convolution_convert_fusion.2 = bf16[256,1024]{1,0:T(8,128)(2,1)S(1)} fusion(bf16[1024,1024]{1,0:T(8,128)(2,1)} %param.15, bf16[1,256,1024]{2,1,0:T(8,128)(2,1)} %param.10), kind=kOutput, calls=%fused_computation.15 | convolution fusion | flops 537133056 | bytes 3145728 | tf_op jit(solution)/shard_map/dot_general | solution.py:115
  10.9 0.9 fusion.17
  12.3 0.7 convolution_multiply_fusion
  13.0 1.2 select_reduce_fusion.3
  14.2 1.5 %select_reduce_fusion.2 = f32[8,512,256]{2,1,0:T(8,128)S(1)} fusion(f32[8,2,512]{2,1,0:T(2,128)S(1)} %select_reduce_fusion.3, pred[2,256]{1,0:T(4,128)(4,1)S(1)} %iota_compare_fusion.8), kind=kLoop, calls=%fused_computation.2 | loop fusion | flops 3145728 | bytes 4227584 | tf_op jit(solution)/shard_map/reduce_sum | solution.py:155
  15.7 1.2 subtract_exponential_fusion
  17.0 1.9 %copy-done.1 = f32[8,512,256]{2,1,0:T(8,128)} copy-done((f32[8,512,256]{2,1,0:T(8,128)}, f32[8,512,256]{2,1,0:T(8,128)S(1)}, u32[]{:S(2)}) %copy-start.1) | copy-done | bytes 4194328
  18.9 1.2 select_reduce_fusion.1
  20.6 0.7 broadcast_select_fusion
  21.6 0.9 pad_maximum_fusion
  22.5 12.2 %all-to-all-start = ((f32[32,40,128]{2,1,0:T(8,128)}), f32[32,40,128]{2,1,0:T(8,128)S(1)}, u32[]{:S(2)}, u32[]{:S(2)}) async-start(f32[32,40,128]{2,1,0:T(8,128)} %pad_maximum_fusion), calls=%async_computation | async-start | bytes 1310720 | tf_op jit(solution)/shard_map/all_to_all | solution.py:62
  34.7 2.0 %copy.83 = bf16[256,1024]{0,1:T(8,128)(2,1)} copy(bf16[256,1024]{1,0:T(8,128)(2,1)} %copy-done.3) | data formatting | bytes 1048576 | tf_op jit(solution)/shard_map/reshape | solution.py:119
  36.9 3.3 %fusion.4 = bf16[32,8,8,128]{3,2,1,0:T(8,128)(2,1)} fusion(bf16[1024,1024]{1,0:T(8,128)(2,1)} %param.14, bf16[1,256,1024]{2,1,0:T(8,128)(2,1)} %param.10), kind=kOutput, calls=%fused_computation.16 | convolution fusion | flops 537133056 | bytes 3145728 | tf_op jit(solution)/shard_map/dot_general | solution.py:114
  40.1 3.1 %fusion.1 = f32[256,8,128]{0,2,1:T(8,128)} fusion(bf16[256,8,128]{0,2,1:T(8,128)(2,1)} %bitcast.198, f32[8,256]{1,0:T(8,128)S(1)} %bitcast.205, pred[256,256]{1,0:T(8,128)(4,1)S(1)} %fusion.38, bf16[32,8,8,128]{3,2,1,0:T(8,128)(2,1)} %fusion.4, bf16[256,1024]{1,0:T(8,128)(2,1)S(1)} %copy-done.5), kind=kOutput, calls=%fused_computation.9 | convolution fusion | flops 271581184 | bytes 2695168 | tf_op jit(solution)/shard_map/hts,shd->thd/dot_general | solution.py:145
  43.3 7.6 %all-to-all-done = f32[32,40,128]{2,1,0:T(8,128)S(1)} async-done(((f32[32,40,128]{2,1,0:T(8,128)}), f32[32,40,128]{2,1,0:T(8,128)S(1)}, u32[]{:S(2)}, u32[]{:S(2)}) %all-to-all-start) | async-done | bytes 655392 | tf_op jit(solution)/shard_map/all_to_all | solution.py:62
  52.3 0.9 fusion.19
  53.3 1.2 copy.71
  54.5 8.4 %all-to-all-start.1 = ((f32[32,40,128]{2,1,0:T(8,128)}), f32[32,40,128]{2,1,0:T(8,128)S(1)}, u32[]{:S(2)}, u32[]{:S(2)}) async-start(f32[32,40,128]{2,1,0:T(8,128)} %copy.71), calls=%async_computation.1 | async-start | bytes 1310720 | tf_op jit(solution)/shard_map/all_to_all | solution.py:84
  63.2 16.6 %all-to-all-done.1 = f32[32,40,128]{2,1,0:T(8,128)S(1)} async-done(((f32[32,40,128]{2,1,0:T(8,128)}), f32[32,40,128]{2,1,0:T(8,128)S(1)}, u32[]{:S(2)}, u32[]{:S(2)}) %all-to-all-start.1) | async-done | bytes 655392 | tf_op jit(solution)/shard_map/all_to_all | solution.py:84
  79.8 2.4 %fusion.70 = (f32[256,8]{0,1:T(8,128)S(1)}, f32[256,8,128]{0,2,1:T(8,128)S(1)}) fusion(f32[256,8,128]{0,2,1:T(8,128)} %fusion.1, f32[8,128,128]{2,1,0:T(8,128)S(1)} %bitcast.188, f32[256,8]{0,1:T(8,128)S(1)} %get-tuple-element.28, bf16[32,8,8,128]{3,2,1,0:T(8,128)(2,1)S(1)} %copy-done.9), kind=kOutput, calls=%fused_computation.132 | convolution fusion | flops 202635264 | bytes 3162112 | tf_op jit(solution)/shard_map/thd,hde->the/dot_general | solution.py:179
  82.6 0.7 bitcast_multiply_fusion
  83.3 1.2 select_reduce_fusion
  84.8 1.1 fusion.69
  85.9 1.2 copy.84
  87.1 1.2 copy.85
  88.4 2.8 %collective-permute-start = (f32[2,2,512]{2,1,0:T(2,128)S(1)}, f32[2,2,512]{2,1,0:T(2,128)S(1)}, u32[]{:S(2)}, u32[]{:S(2)}) collective-permute-start(f32[2,2,512]{2,1,0:T(2,128)S(1)} %pad_maximum_fusion.4), channel_id=1, source_target_pairs={{0,1},{1,0},{2,3},{3,2},{4,5},{5,4},{6,7},{7,6},{8,9},{9,8},{10,11... | collective-permute-start | bytes 24584 | tf_op jit(solution)/shard_map/ppermute | solution.py:17
  91.2 0.9 collective-permute-start.1
  92.1 1.3 collective-permute-start.2
  93.4 1.2 collective-permute-done.1
  94.6 1.8 %collective-permute-done.2 = f32[2,2,512]{2,1,0:T(2,128)S(1)} collective-permute-done((f32[2,2,512]{2,1,0:T(2,128)S(1)}, f32[2,2,512]{2,1,0:T(2,128)S(1)}, u32[]{:S(2)}, u32[]{:S(2)}) %collective-permute-start.2) | collective-permute-done | bytes 8224 | tf_op jit(solution)/shard_map/ppermute | solution.py:17
  96.4 1.7 %collective-permute-start.3 = (f32[2,2,512]{2,1,0:T(2,128)S(1)}, f32[2,2,512]{2,1,0:T(2,128)S(1)}, u32[]{:S(2)}, u32[]{:S(2)}) collective-permute-start(f32[2,2,512]{2,1,0:T(2,128)S(1)} %add_add_fusion.1), channel_id=1, source_target_pairs={{0,4},{1,5},{2,6},{3,7},{4,0},{5,1},{6,2},{7,3},{8,12},{9,13},{10,... | collective-permute-start | bytes 24584 | tf_op jit(solution)/shard_map/ppermute | solution.py:17
  98.1 4.8 %collective-permute-done.3 = f32[2,2,512]{2,1,0:T(2,128)S(1)} collective-permute-done((f32[2,2,512]{2,1,0:T(2,128)S(1)}, f32[2,2,512]{2,1,0:T(2,128)S(1)}, u32[]{:S(2)}, u32[]{:S(2)}) %collective-permute-start.3) | collective-permute-done | bytes 8224 | tf_op jit(solution)/shard_map/ppermute | solution.py:17
  102.9 0.9 collective-permute-start.4
  103.8 1.5 %collective-permute-start.5 = (f32[2,2,512]{2,1,0:T(2,128)S(1)}, f32[2,2,512]{2,1,0:T(2,128)S(1)}, u32[]{:S(2)}, u32[]{:S(2)}) collective-permute-start(f32[2,2,512]{2,1,0:T(2,128)S(1)} %add.103), channel_id=1, source_target_pairs={{0,16},{1,17},{2,18},{3,19},{4,20},{5,21},{6,22},{7,23},{8,24},{9,... | collective-permute-start | bytes 24584 | tf_op jit(solution)/shard_map/ppermute | solution.py:17
  105.3 1.4 %collective-permute-start.6 = (f32[2,2,512]{2,1,0:T(2,128)S(1)}, f32[2,2,512]{2,1,0:T(2,128)S(1)}, u32[]{:S(2)}, u32[]{:S(2)}) collective-permute-start(f32[2,2,512]{2,1,0:T(2,128)S(1)} %add.103), channel_id=1, source_target_pairs={{0,24},{1,25},{2,26},{3,27},{4,28},{5,29},{6,30},{7,31},{8,16},{9,... | collective-permute-start | bytes 24584 | tf_op jit(solution)/shard_map/ppermute | solution.py:17
  106.8 1.0 copy.79
  108.1 0.9 collective-permute-done.6
  109.0 0.7 fusion.62
  109.7 1.1 multiply_reduce_fusion.1
  110.9 7.5 %collective-permute-start.7 = (f32[]{:T(128)}, f32[]{:T(128)}, u32[]{:S(2)}, u32[]{:S(2)}) collective-permute-start(f32[]{:T(128)} %get-tuple-element.32), channel_id=1, source_target_pairs={{0,32},{32,0},{64,96},{96,64},{128,160},{160,128},{192,224},{224,1... | collective-permute-start | bytes 20 | tf_op jit(solution)/shard_map/ppermute | solution.py:17
  118.4 1.0 collective-permute-done.7
  120.7 2.0 %collective-permute-start.8 = (f32[]{:T(128)}, f32[]{:T(128)}, u32[]{:S(2)}, u32[]{:S(2)}) collective-permute-start(f32[]{:T(128)} %add.112), channel_id=1, source_target_pairs={{0,64},{32,96},{64,0},{96,32},{128,192},{160,224},{192,128},{224,1... | collective-permute-start | bytes 20 | tf_op jit(solution)/shard_map/ppermute | solution.py:17
  123.9 3.6 %collective-permute-start.9 = (f32[]{:T(128)}, f32[]{:T(128)}, u32[]{:S(2)}, u32[]{:S(2)}) collective-permute-start(f32[]{:T(128)} %add.113), channel_id=1, source_target_pairs={{0,128},{32,160},{64,192},{96,224},{128,0},{160,32},{192,64},{224,... | collective-permute-start | bytes 20 | tf_op jit(solution)/shard_map/ppermute | solution.py:17
  (89 shorter events, 7.2 us)
Async XLA Ops:
  0.6 5.4 %copy-start = (bf16[1024,1024]{1,0:T(8,128)(2,1)S(1)}, bf16[1024,1024]{1,0:T(8,128)(2,1)}, u32[]{:S(2)}) copy-start(bf16[1024,1024]{1,0:T(8,128)(2,1)} %param.16) | copy-start | bytes 6291460
  7.8 3.9 %copy-start.3 = (bf16[256,1024]{1,0:T(8,128)(2,1)}, bf16[256,1024]{1,0:T(8,128)(2,1)S(1)}, u32[]{:S(2)}) copy-start(bf16[256,1024]{1,0:T(8,128)(2,1)S(1)} %convolution_convert_fusion.1) | copy-start | bytes 1572868
  10.5 1.3 copy-start.4
  10.9 1.1 copy-start.8
  10.9 1.4 %copy-start.7 = (bf16[512,1024]{1,0:T(8,128)(2,1)S(1)}, bf16[512,1024]{1,0:T(8,128)(2,1)}, u32[]{:S(2)}) copy-start(bf16[512,1024]{1,0:T(8,128)(2,1)} %param.18) | copy-start | bytes 3145732
  16.9 1.9 %copy-start.1 = (f32[8,512,256]{2,1,0:T(8,128)}, f32[8,512,256]{2,1,0:T(8,128)S(1)}, u32[]{:S(2)}) copy-start(f32[8,512,256]{2,1,0:T(8,128)S(1)} %subtract_exponential_fusion) | copy-start | bytes 12582916
  20.6 19.6 %copy-start.5 = (bf16[256,1024]{1,0:T(8,128)(2,1)S(1)}, bf16[256,1024]{1,0:T(8,128)(2,1)}, u32[]{:S(2)}) copy-start(bf16[256,1024]{1,0:T(8,128)(2,1)} %copy-done.4) | copy-start | bytes 1572868
  22.5 28.4 %all-to-all-start = ((f32[32,40,128]{2,1,0:T(8,128)}), f32[32,40,128]{2,1,0:T(8,128)S(1)}, u32[]{:S(2)}, u32[]{:S(2)}) async-start(f32[32,40,128]{2,1,0:T(8,128)} %pad_maximum_fusion), calls=%async_computation | async-start | bytes 1310720 | tf_op jit(solution)/shard_map/all_to_all | solution.py:62
  43.3 19.7 %copy-start.11 = (s32[1,256]{1,0:T(1,128)S(1)}, s32[1,256]{1,0:T(1,128)}, u32[]{:S(2)}) copy-start(s32[1,256]{1,0:T(1,128)} %param.13) | copy-start | bytes 3076
  53.2 26.6 %copy-start.9 = (bf16[32,8,8,128]{3,2,1,0:T(8,128)(2,1)S(1)}, bf16[32,8,8,128]{3,2,1,0:T(8,128)(2,1)}, u32[]{:S(2)}) copy-start(bf16[32,8,8,128]{3,2,1,0:T(8,128)(2,1)} %fusion.4) | copy-start | bytes 1572868
  53.3 29.1 %copy-start.10 = (f32[1024]{0:T(1024)S(1)}, f32[1024]{0:T(1024)}, u32[]{:S(2)}) copy-start(f32[1024]{0:T(1024)} %param.17) | copy-start | bytes 12292
  54.5 25.2 %all-to-all-start.1 = ((f32[32,40,128]{2,1,0:T(8,128)}), f32[32,40,128]{2,1,0:T(8,128)S(1)}, u32[]{:S(2)}, u32[]{:S(2)}) async-start(f32[32,40,128]{2,1,0:T(8,128)} %copy.71), calls=%async_computation.1 | async-start | bytes 1310720 | tf_op jit(solution)/shard_map/all_to_all | solution.py:84
  79.8 2.8 %copy-start.2 = (f32[8,512,256]{2,1,0:T(8,128)S(1)}, f32[8,512,256]{2,1,0:T(8,128)}, u32[]{:S(2)}) copy-start(f32[8,512,256]{2,1,0:T(8,128)} %copy-done.1) | copy-start | bytes 12582916
  79.8 2.8 %copy-start.6 = (bf16[512,1024]{1,0:T(8,128)(2,1)S(1)}, bf16[512,1024]{1,0:T(8,128)(2,1)}, u32[]{:S(2)}) copy-start(bf16[512,1024]{1,0:T(8,128)(2,1)} %param.19) | copy-start | bytes 3145732
  83.3 23.4 %copy-start.12 = (s32[1,2]{1,0:T(1,128)S(1)}, s32[1,2]{1,0:T(1,128)}, u32[]{:S(2)}) copy-start(s32[1,2]{1,0:T(1,128)} %param.12) | copy-start | bytes 28
  88.4 4.9 %collective-permute-start = (f32[2,2,512]{2,1,0:T(2,128)S(1)}, f32[2,2,512]{2,1,0:T(2,128)S(1)}, u32[]{:S(2)}, u32[]{:S(2)}) collective-permute-start(f32[2,2,512]{2,1,0:T(2,128)S(1)} %pad_maximum_fusion.4), channel_id=1, source_target_pairs={{0,1},{1,0},{2,3},{3,2},{4,5},{5,4},{6,7},{7,6},{8,9},{9,8},{10,11... | collective-permute-start | bytes 24584 | tf_op jit(solution)/shard_map/ppermute | solution.py:17
  91.2 3.4 %collective-permute-start.1 = (f32[2,2,512]{2,1,0:T(2,128)S(1)}, f32[2,2,512]{2,1,0:T(2,128)S(1)}, u32[]{:S(2)}, u32[]{:S(2)}) collective-permute-start(f32[2,2,512]{2,1,0:T(2,128)S(1)} %pad_maximum_fusion.4), channel_id=1, source_target_pairs={{0,2},{1,3},{2,0},{3,1},{4,6},{5,7},{6,4},{7,5},{8,10},{9,11},{10,... | collective-permute-start | bytes 24584 | tf_op jit(solution)/shard_map/ppermute | solution.py:17
  92.1 4.3 %collective-permute-start.2 = (f32[2,2,512]{2,1,0:T(2,128)S(1)}, f32[2,2,512]{2,1,0:T(2,128)S(1)}, u32[]{:S(2)}, u32[]{:S(2)}) collective-permute-start(f32[2,2,512]{2,1,0:T(2,128)S(1)} %pad_maximum_fusion.4), channel_id=1, source_target_pairs={{0,3},{1,2},{2,1},{3,0},{4,7},{5,6},{6,5},{7,4},{8,11},{9,10},{10,... | collective-permute-start | bytes 24584 | tf_op jit(solution)/shard_map/ppermute | solution.py:17
  96.4 6.5 %collective-permute-start.3 = (f32[2,2,512]{2,1,0:T(2,128)S(1)}, f32[2,2,512]{2,1,0:T(2,128)S(1)}, u32[]{:S(2)}, u32[]{:S(2)}) collective-permute-start(f32[2,2,512]{2,1,0:T(2,128)S(1)} %add_add_fusion.1), channel_id=1, source_target_pairs={{0,4},{1,5},{2,6},{3,7},{4,0},{5,1},{6,2},{7,3},{8,12},{9,13},{10,... | collective-permute-start | bytes 24584 | tf_op jit(solution)/shard_map/ppermute | solution.py:17
  102.9 4.9 %collective-permute-start.4 = (f32[2,2,512]{2,1,0:T(2,128)S(1)}, f32[2,2,512]{2,1,0:T(2,128)S(1)}, u32[]{:S(2)}, u32[]{:S(2)}) collective-permute-start(f32[2,2,512]{2,1,0:T(2,128)S(1)} %add.103), channel_id=1, source_target_pairs={{0,8},{1,9},{2,10},{3,11},{4,12},{5,13},{6,14},{7,15},{8,0},{9,1},... | collective-permute-start | bytes 24584 | tf_op jit(solution)/shard_map/ppermute | solution.py:17
  103.8 4.3 %collective-permute-start.5 = (f32[2,2,512]{2,1,0:T(2,128)S(1)}, f32[2,2,512]{2,1,0:T(2,128)S(1)}, u32[]{:S(2)}, u32[]{:S(2)}) collective-permute-start(f32[2,2,512]{2,1,0:T(2,128)S(1)} %add.103), channel_id=1, source_target_pairs={{0,16},{1,17},{2,18},{3,19},{4,20},{5,21},{6,22},{7,23},{8,24},{9,... | collective-permute-start | bytes 24584 | tf_op jit(solution)/shard_map/ppermute | solution.py:17
  105.3 3.7 %collective-permute-start.6 = (f32[2,2,512]{2,1,0:T(2,128)S(1)}, f32[2,2,512]{2,1,0:T(2,128)S(1)}, u32[]{:S(2)}, u32[]{:S(2)}) collective-permute-start(f32[2,2,512]{2,1,0:T(2,128)S(1)} %add.103), channel_id=1, source_target_pairs={{0,24},{1,25},{2,26},{3,27},{4,28},{5,29},{6,30},{7,31},{8,16},{9,... | collective-permute-start | bytes 24584 | tf_op jit(solution)/shard_map/ppermute | solution.py:17
  110.9 8.5 %collective-permute-start.7 = (f32[]{:T(128)}, f32[]{:T(128)}, u32[]{:S(2)}, u32[]{:S(2)}) collective-permute-start(f32[]{:T(128)} %get-tuple-element.32), channel_id=1, source_target_pairs={{0,32},{32,0},{64,96},{96,64},{128,160},{160,128},{192,224},{224,1... | collective-permute-start | bytes 20 | tf_op jit(solution)/shard_map/ppermute | solution.py:17
  120.7 2.6 %collective-permute-start.8 = (f32[]{:T(128)}, f32[]{:T(128)}, u32[]{:S(2)}, u32[]{:S(2)}) collective-permute-start(f32[]{:T(128)} %add.112), channel_id=1, source_target_pairs={{0,64},{32,96},{64,0},{96,32},{128,192},{160,224},{192,128},{224,1... | collective-permute-start | bytes 20 | tf_op jit(solution)/shard_map/ppermute | solution.py:17
  123.9 4.1 %collective-permute-start.9 = (f32[]{:T(128)}, f32[]{:T(128)}, u32[]{:S(2)}, u32[]{:S(2)}) collective-permute-start(f32[]{:T(128)} %add.113), channel_id=1, source_target_pairs={{0,128},{32,160},{64,192},{96,224},{128,0},{160,32},{192,64},{224,... | collective-permute-start | bytes 20 | tf_op jit(solution)/shard_map/ppermute | solution.py:17

commit v18 on v15

--- a/solution.py
+++ b/solution.py
@@ -74,7 +74,7 @@
     spans = jnp.prod(jnp.where(inside, factors[None, None, :], 1.0), axis=2)
     mix = jnp.where(block[None, :] < block[:, None], spans, 0.0)
     scanned = jnp.dot(
-        mix, got[:, :rows, :].reshape(count, rows * head_dim), precision=lax.Precision.HIGHEST
+        mix, got[:, :rows, :].reshape(count, rows * head_dim), precision=lax.Precision.HIGH
     )
     back_extra = jnp.broadcast_to(
         jnp.concatenate([combined, jnp.zeros((1, pad + 1), jnp.float32)], axis=1),

time: 131 us -> 130 us (level)
  no operation moved by 1% of the time
where the time goes in v18:
time: 130 us; the launch traced here: 129 us
  starting transfers between devices  35.8 us (28%)
  blocking collectives  25.3 us (19%)
  waiting for transfers between devices  18.2 us (14%)
  matrix products  15.9 us (12%)
  other arithmetic  14.5 us (11%)
  local copies, waits for them, and re-layouts  13.7 us (11%)
  between operations  5.72 us (4%)
    all_to_all x1, blocking collectives, exclusive_state_scan(): back = lax.all_to_all(sent_back, axis, 0, 0)  25.3 us
    ppermute x10, starting transfers between devices, swapped(): return lax.ppermute(x, axis, [(i, i ^ bit) for i in range(count)])  23.6 us
    all_to_all x1, starting transfers between devices, exclusive_state_scan(): got = lax.all_to_all(jnp.concatenate([slices, extra], axis=1), axis, 0, 0)  12.2 us
    ppermute x10, waiting for transfers between devices, swapped(): return lax.ppermute(x, axis, [(i, i ^ bit) for i in range(count)])  10.6 us
    all_to_all x1, waiting for transfers between devices, exclusive_state_scan(): got = lax.all_to_all(jnp.concatenate([slices, extra], axis=1), axis, 0, 0)  7.65 us
    unnamed x42, local copies, waits for them, and re-layouts  5.86 us
    dot_general x1, matrix products, local(): jnp.dot(features, w_query, preferred_element_type=jnp.float32)  3.28 us
    dot_general x1, matrix products, local(): jnp.einsum('hts,shd->thd', weights, v3, preferred_element_type=jnp.float32)  3.11 us
  transfers between devices with their start and end apart: 11, of which 8 were waited for; matrix products, arithmetic and copies ran while one was open for 8% of the time, Pallas kernels for 0%

profile of v18, /device:TPU:1, one launch (start us, length us, event | category | flops | bytes accessed | tf_op | source)
XLA Modules:
  0.0 129.1 jit_solution(16209032243721876525)
XLA Ops:
  0.7 0.9 fusion.60
  1.7 0.6 slice.72
  2.3 0.6 fusion.61
  3.5 0.8 fusion.41
  4.6 0.7 broadcast_compare_fusion.1
  6.1 1.8 %convolution_convert_fusion.1 = bf16[256,1024]{1,0:T(8,128)(2,1)S(1)} fusion(bf16[1024,1024]{1,0:T(8,128)(2,1)S(1)} %copy-done, bf16[1,256,1024]{2,1,0:T(8,128)(2,1)} %param.10), kind=kOutput, calls=%fused_computation.14 | convolution fusion | flops 537133056 | bytes 3145728 | tf_op jit(solution)/shard_map/dot_general | solution.py:116
  7.9 2.6 %convolution_convert_fusion.2 = bf16[256,1024]{1,0:T(8,128)(2,1)S(1)} fusion(bf16[1024,1024]{1,0:T(8,128)(2,1)} %param.15, bf16[1,256,1024]{2,1,0:T(8,128)(2,1)} %param.10), kind=kOutput, calls=%fused_computation.15 | convolution fusion | flops 537133056 | bytes 3145728 | tf_op jit(solution)/shard_map/dot_general | solution.py:115
  10.9 0.9 fusion.17
  12.3 0.7 convolution_multiply_fusion
  13.0 1.2 select_reduce_fusion.3
  14.2 1.5 %select_reduce_fusion.2 = f32[8,512,256]{2,1,0:T(8,128)S(1)} fusion(f32[8,2,512]{2,1,0:T(2,128)S(1)} %select_reduce_fusion.3, pred[2,256]{1,0:T(4,128)(4,1)S(1)} %iota_compare_fusion.8), kind=kLoop, calls=%fused_computation.2 | loop fusion | flops 3145728 | bytes 4227584 | tf_op jit(solution)/shard_map/reduce_sum | solution.py:155
  15.7 1.2 subtract_exponential_fusion
  17.0 1.9 %copy-done.1 = f32[8,512,256]{2,1,0:T(8,128)} copy-done((f32[8,512,256]{2,1,0:T(8,128)}, f32[8,512,256]{2,1,0:T(8,128)S(1)}, u32[]{:S(2)}) %copy-start.1) | copy-done | bytes 4194328
  18.9 1.2 select_reduce_fusion.1
  20.9 0.7 broadcast_select_fusion
  21.9 0.9 pad_maximum_fusion
  22.8 12.2 %all-to-all-start = ((f32[32,40,128]{2,1,0:T(8,128)}), f32[32,40,128]{2,1,0:T(8,128)S(1)}, u32[]{:S(2)}, u32[]{:S(2)}) async-start(f32[32,40,128]{2,1,0:T(8,128)} %pad_maximum_fusion), calls=%async_computation | async-start | bytes 1310720 | tf_op jit(solution)/shard_map/all_to_all | solution.py:62
  35.1 2.0 %copy.103 = bf16[256,1024]{0,1:T(8,128)(2,1)} copy(bf16[256,1024]{1,0:T(8,128)(2,1)} %copy-done.3) | data formatting | bytes 1048576 | tf_op jit(solution)/shard_map/reshape | solution.py:119
  37.2 3.3 %fusion.4 = bf16[32,8,8,128]{3,2,1,0:T(8,128)(2,1)} fusion(bf16[1024,1024]{1,0:T(8,128)(2,1)} %param.14, bf16[1,256,1024]{2,1,0:T(8,128)(2,1)} %param.10), kind=kOutput, calls=%fused_computation.16 | convolution fusion | flops 537133056 | bytes 3145728 | tf_op jit(solution)/shard_map/dot_general | solution.py:114
  40.5 3.1 %fusion.1 = f32[256,8,128]{0,2,1:T(8,128)} fusion(bf16[256,8,128]{0,2,1:T(8,128)(2,1)} %bitcast.171, f32[8,256]{1,0:T(8,128)S(1)} %bitcast.179, pred[256,256]{1,0:T(8,128)(4,1)S(1)} %fusion.40, bf16[32,8,8,128]{3,2,1,0:T(8,128)(2,1)} %fusion.4, bf16[256,1024]{1,0:T(8,128)(2,1)S(1)} %copy-done.5), kind=kOutput, calls=%fused_computation.9 | convolution fusion | flops 271581184 | bytes 2695168 | tf_op jit(solution)/shard_map/hts,shd->thd/dot_general | solution.py:145
  43.6 7.6 %all-to-all-done = f32[32,40,128]{2,1,0:T(8,128)S(1)} async-done(((f32[32,40,128]{2,1,0:T(8,128)}), f32[32,40,128]{2,1,0:T(8,128)S(1)}, u32[]{:S(2)}, u32[]{:S(2)}) %all-to-all-start) | async-done | bytes 655392 | tf_op jit(solution)/shard_map/all_to_all | solution.py:62
  53.1 0.6 select_reduce_fusion.4
  53.7 0.6 fusion.19
  54.8 25.3 %all_to_all.10 = f32[32,40,128]{2,1,0:T(8,128)S(1)} all-to-all(f32[32,40,128]{2,1,0:T(8,128)S(1)} %copy.91), channel_id=1, replica_groups=mesh['dp'=8,'ctx'=32] {'ctx'}, dimensions={0} | all-to-all | bytes 1310720 | tf_op jit(solution)/shard_map/all_to_all | solution.py:84
  80.2 1.0 fusion.66
  81.6 0.7 bitcast_multiply_fusion
  82.3 1.2 select_reduce_fusion
  84.2 1.1 fusion.65
  85.3 1.2 copy.104
  86.5 1.2 copy.105
  87.8 2.7 %collective-permute-start = (f32[2,512]{1,0:T(2,128)S(1)}, f32[2,512]{1,0:T(2,128)S(1)}, u32[]{:S(2)}, u32[]{:S(2)}) collective-permute-start(f32[2,512]{1,0:T(2,128)S(1)} %fusion.52), channel_id=1, source_target_pairs={{0,1},{1,0},{2,3},{3,2},{4,5},{5,4},{6,7},{7,6},{8,9},{9,8},{10,11... | collective-permute-start | bytes 12296 | tf_op jit(solution)/shard_map/ppermute | solution.py:17
  90.5 0.9 collective-permute-start.1
  91.4 1.3 %collective-permute-start.2 = (f32[2,512]{1,0:T(2,128)S(1)}, f32[2,512]{1,0:T(2,128)S(1)}, u32[]{:S(2)}, u32[]{:S(2)}) collective-permute-start(f32[2,512]{1,0:T(2,128)S(1)} %fusion.52), channel_id=1, source_target_pairs={{0,3},{1,2},{2,1},{3,0},{4,7},{5,6},{6,5},{7,4},{8,11},{9,10},{10,... | collective-permute-start | bytes 12296 | tf_op jit(solution)/shard_map/ppermute | solution.py:17
  92.7 1.2 collective-permute-done.1
  93.9 1.8 %collective-permute-done.2 = f32[2,512]{1,0:T(2,128)S(1)} collective-permute-done((f32[2,512]{1,0:T(2,128)S(1)}, f32[2,512]{1,0:T(2,128)S(1)}, u32[]{:S(2)}, u32[]{:S(2)}) %collective-permute-start.2) | collective-permute-done | bytes 4128 | tf_op jit(solution)/shard_map/ppermute | solution.py:17
  95.7 1.7 %collective-permute-start.3 = (f32[2,512]{1,0:T(2,128)S(1)}, f32[2,512]{1,0:T(2,128)S(1)}, u32[]{:S(2)}, u32[]{:S(2)}) collective-permute-start(f32[2,512]{1,0:T(2,128)S(1)} %add_add_fusion.1), channel_id=1, source_target_pairs={{0,4},{1,5},{2,6},{3,7},{4,0},{5,1},{6,2},{7,3},{8,12},{9,13},{10,... | collective-permute-start | bytes 12296 | tf_op jit(solution)/shard_map/ppermute | solution.py:17
  97.4 4.7 %collective-permute-done.3 = f32[2,512]{1,0:T(2,128)S(1)} collective-permute-done((f32[2,512]{1,0:T(2,128)S(1)}, f32[2,512]{1,0:T(2,128)S(1)}, u32[]{:S(2)}, u32[]{:S(2)}) %collective-permute-start.3) | collective-permute-done | bytes 4128 | tf_op jit(solution)/shard_map/ppermute | solution.py:17
  102.1 0.9 collective-permute-start.4
  103.1 1.5 %collective-permute-start.5 = (f32[2,512]{1,0:T(2,128)S(1)}, f32[2,512]{1,0:T(2,128)S(1)}, u32[]{:S(2)}, u32[]{:S(2)}) collective-permute-start(f32[2,512]{1,0:T(2,128)S(1)} %add.103), channel_id=1, source_target_pairs={{0,16},{1,17},{2,18},{3,19},{4,20},{5,21},{6,22},{7,23},{8,24},{9,... | collective-permute-start | bytes 12296 | tf_op jit(solution)/shard_map/ppermute | solution.py:17
  104.5 1.5 %collective-permute-start.6 = (f32[2,512]{1,0:T(2,128)S(1)}, f32[2,512]{1,0:T(2,128)S(1)}, u32[]{:S(2)}, u32[]{:S(2)}) collective-permute-start(f32[2,512]{1,0:T(2,128)S(1)} %add.103), channel_id=1, source_target_pairs={{0,24},{1,25},{2,26},{3,27},{4,28},{5,29},{6,30},{7,31},{8,16},{9,... | collective-permute-start | bytes 12296 | tf_op jit(solution)/shard_map/ppermute | solution.py:17
  106.4 1.0 copy.99
  107.4 0.8 collective-permute-done.6
  108.2 0.7 fusion.58
  108.9 1.1 multiply_reduce_fusion.1
  110.0 7.5 %collective-permute-start.7 = (f32[]{:T(128)}, f32[]{:T(128)}, u32[]{:S(2)}, u32[]{:S(2)}) collective-permute-start(f32[]{:T(128)} %get-tuple-element.36), channel_id=1, source_target_pairs={{0,32},{32,0},{64,96},{96,64},{128,160},{160,128},{192,224},{224,1... | collective-permute-start | bytes 20 | tf_op jit(solution)/shard_map/ppermute | solution.py:17
  117.6 1.0 collective-permute-done.7
  119.9 2.0 %collective-permute-start.8 = (f32[]{:T(128)}, f32[]{:T(128)}, u32[]{:S(2)}, u32[]{:S(2)}) collective-permute-start(f32[]{:T(128)} %add.112), channel_id=1, source_target_pairs={{0,64},{32,96},{64,0},{96,32},{128,192},{160,224},{192,128},{224,1... | collective-permute-start | bytes 20 | tf_op jit(solution)/shard_map/ppermute | solution.py:17
  123.2 3.5 %collective-permute-start.9 = (f32[]{:T(128)}, f32[]{:T(128)}, u32[]{:S(2)}, u32[]{:S(2)}) collective-permute-start(f32[]{:T(128)} %add.113), channel_id=1, source_target_pairs={{0,128},{32,160},{64,192},{96,224},{128,0},{160,32},{192,64},{224,... | collective-permute-start | bytes 20 | tf_op jit(solution)/shard_map/ppermute | solution.py:17
  (92 shorter events, 7.9 us)
Async XLA Ops:
  0.6 5.4 %copy-start = (bf16[1024,1024]{1,0:T(8,128)(2,1)S(1)}, bf16[1024,1024]{1,0:T(8,128)(2,1)}, u32[]{:S(2)}) copy-start(bf16[1024,1024]{1,0:T(8,128)(2,1)} %param.16) | copy-start | bytes 6291460
  7.8 3.9 %copy-start.3 = (bf16[256,1024]{1,0:T(8,128)(2,1)}, bf16[256,1024]{1,0:T(8,128)(2,1)S(1)}, u32[]{:S(2)}) copy-start(bf16[256,1024]{1,0:T(8,128)(2,1)S(1)} %convolution_convert_fusion.1) | copy-start | bytes 1572868
  10.5 1.3 copy-start.4
  10.9 1.1 copy-start.9
  10.9 1.4 %copy-start.8 = (bf16[512,1024]{1,0:T(8,128)(2,1)S(1)}, bf16[512,1024]{1,0:T(8,128)(2,1)}, u32[]{:S(2)}) copy-start(bf16[512,1024]{1,0:T(8,128)(2,1)} %param.18) | copy-start | bytes 3145732
  16.9 1.9 %copy-start.1 = (f32[8,512,256]{2,1,0:T(8,128)}, f32[8,512,256]{2,1,0:T(8,128)S(1)}, u32[]{:S(2)}) copy-start(f32[8,512,256]{2,1,0:T(8,128)S(1)} %subtract_exponential_fusion) | copy-start | bytes 12582916
  18.9 1.2 copy-start.12
  20.9 19.6 %copy-start.5 = (bf16[256,1024]{1,0:T(8,128)(2,1)S(1)}, bf16[256,1024]{1,0:T(8,128)(2,1)}, u32[]{:S(2)}) copy-start(bf16[256,1024]{1,0:T(8,128)(2,1)} %copy-done.4) | copy-start | bytes 1572868
  22.8 28.4 %all-to-all-start = ((f32[32,40,128]{2,1,0:T(8,128)}), f32[32,40,128]{2,1,0:T(8,128)S(1)}, u32[]{:S(2)}, u32[]{:S(2)}) async-start(f32[32,40,128]{2,1,0:T(8,128)} %pad_maximum_fusion), calls=%async_computation | async-start | bytes 1310720 | tf_op jit(solution)/shard_map/all_to_all | solution.py:62
  52.7 27.4 %copy-start.10 = (bf16[32,8,8,128]{3,2,1,0:T(8,128)(2,1)S(1)}, bf16[32,8,8,128]{3,2,1,0:T(8,128)(2,1)}, u32[]{:S(2)}) copy-start(bf16[32,8,8,128]{3,2,1,0:T(8,128)(2,1)} %fusion.4) | copy-start | bytes 1572868
  53.0 27.2 %copy-start.7 = (f32[256,8,128]{0,2,1:T(8,128)S(1)}, f32[256,8,128]{0,2,1:T(8,128)}, u32[]{:S(2)}) copy-start(f32[256,8,128]{0,2,1:T(8,128)} %fusion.1) | copy-start | bytes 3145732
  54.4 27.0 %copy-start.11 = (f32[1024]{0:T(1024)S(1)}, f32[1024]{0:T(1024)}, u32[]{:S(2)}) copy-start(f32[1024]{0:T(1024)} %param.17) | copy-start | bytes 12292
  54.8 26.8 %copy-start.2 = (f32[8,512,256]{2,1,0:T(8,128)S(1)}, f32[8,512,256]{2,1,0:T(8,128)}, u32[]{:S(2)}) copy-start(f32[8,512,256]{2,1,0:T(8,128)} %copy-done.1) | copy-start | bytes 12582916
  54.8 26.8 %copy-start.6 = (bf16[512,1024]{1,0:T(8,128)(2,1)S(1)}, bf16[512,1024]{1,0:T(8,128)(2,1)}, u32[]{:S(2)}) copy-start(bf16[512,1024]{1,0:T(8,128)(2,1)} %param.19) | copy-start | bytes 3145732
  82.3 15.1 %copy-start.13 = (s32[1,2]{1,0:T(1,128)S(1)}, s32[1,2]{1,0:T(1,128)}, u32[]{:S(2)}) copy-start(s32[1,2]{1,0:T(1,128)} %param.12) | copy-start | bytes 28
  87.8 4.9 %collective-permute-start = (f32[2,512]{1,0:T(2,128)S(1)}, f32[2,512]{1,0:T(2,128)S(1)}, u32[]{:S(2)}, u32[]{:S(2)}) collective-permute-start(f32[2,512]{1,0:T(2,128)S(1)} %fusion.52), channel_id=1, source_target_pairs={{0,1},{1,0},{2,3},{3,2},{4,5},{5,4},{6,7},{7,6},{8,9},{9,8},{10,11... | collective-permute-start | bytes 12296 | tf_op jit(solution)/shard_map/ppermute | solution.py:17
  90.5 3.4 %collective-permute-start.1 = (f32[2,512]{1,0:T(2,128)S(1)}, f32[2,512]{1,0:T(2,128)S(1)}, u32[]{:S(2)}, u32[]{:S(2)}) collective-permute-start(f32[2,512]{1,0:T(2,128)S(1)} %fusion.52), channel_id=1, source_target_pairs={{0,2},{1,3},{2,0},{3,1},{4,6},{5,7},{6,4},{7,5},{8,10},{9,11},{10,... | collective-permute-start | bytes 12296 | tf_op jit(solution)/shard_map/ppermute | solution.py:17
  91.4 4.3 %collective-permute-start.2 = (f32[2,512]{1,0:T(2,128)S(1)}, f32[2,512]{1,0:T(2,128)S(1)}, u32[]{:S(2)}, u32[]{:S(2)}) collective-permute-start(f32[2,512]{1,0:T(2,128)S(1)} %fusion.52), channel_id=1, source_target_pairs={{0,3},{1,2},{2,1},{3,0},{4,7},{5,6},{6,5},{7,4},{8,11},{9,10},{10,... | collective-permute-start | bytes 12296 | tf_op jit(solution)/shard_map/ppermute | solution.py:17
  95.7 6.4 %collective-permute-start.3 = (f32[2,512]{1,0:T(2,128)S(1)}, f32[2,512]{1,0:T(2,128)S(1)}, u32[]{:S(2)}, u32[]{:S(2)}) collective-permute-start(f32[2,512]{1,0:T(2,128)S(1)} %add_add_fusion.1), channel_id=1, source_target_pairs={{0,4},{1,5},{2,6},{3,7},{4,0},{5,1},{6,2},{7,3},{8,12},{9,13},{10,... | collective-permute-start | bytes 12296 | tf_op jit(solution)/shard_map/ppermute | solution.py:17
  102.1 5.2 %collective-permute-start.4 = (f32[2,512]{1,0:T(2,128)S(1)}, f32[2,512]{1,0:T(2,128)S(1)}, u32[]{:S(2)}, u32[]{:S(2)}) collective-permute-start(f32[2,512]{1,0:T(2,128)S(1)} %add.103), channel_id=1, source_target_pairs={{0,8},{1,9},{2,10},{3,11},{4,12},{5,13},{6,14},{7,15},{8,0},{9,1},... | collective-permute-start | bytes 12296 | tf_op jit(solution)/shard_map/ppermute | solution.py:17
  103.1 4.3 %collective-permute-start.5 = (f32[2,512]{1,0:T(2,128)S(1)}, f32[2,512]{1,0:T(2,128)S(1)}, u32[]{:S(2)}, u32[]{:S(2)}) collective-permute-start(f32[2,512]{1,0:T(2,128)S(1)} %add.103), channel_id=1, source_target_pairs={{0,16},{1,17},{2,18},{3,19},{4,20},{5,21},{6,22},{7,23},{8,24},{9,... | collective-permute-start | bytes 12296 | tf_op jit(solution)/shard_map/ppermute | solution.py:17
  104.5 3.7 %collective-permute-start.6 = (f32[2,512]{1,0:T(2,128)S(1)}, f32[2,512]{1,0:T(2,128)S(1)}, u32[]{:S(2)}, u32[]{:S(2)}) collective-permute-start(f32[2,512]{1,0:T(2,128)S(1)} %add.103), channel_id=1, source_target_pairs={{0,24},{1,25},{2,26},{3,27},{4,28},{5,29},{6,30},{7,31},{8,16},{9,... | collective-permute-start | bytes 12296 | tf_op jit(solution)/shard_map/ppermute | solution.py:17
  110.0 8.5 %collective-permute-start.7 = (f32[]{:T(128)}, f32[]{:T(128)}, u32[]{:S(2)}, u32[]{:S(2)}) collective-permute-start(f32[]{:T(128)} %get-tuple-element.36), channel_id=1, source_target_pairs={{0,32},{32,0},{64,96},{96,64},{128,160},{160,128},{192,224},{224,1... | collective-permute-start | bytes 20 | tf_op jit(solution)/shard_map/ppermute | solution.py:17
  119.9 2.6 %collective-permute-start.8 = (f32[]{:T(128)}, f32[]{:T(128)}, u32[]{:S(2)}, u32[]{:S(2)}) collective-permute-start(f32[]{:T(128)} %add.112), channel_id=1, source_target_pairs={{0,64},{32,96},{64,0},{96,32},{128,192},{160,224},{192,128},{224,1... | collective-permute-start | bytes 20 | tf_op jit(solution)/shard_map/ppermute | solution.py:17
  123.2 4.1 %collective-permute-start.9 = (f32[]{:T(128)}, f32[]{:T(128)}, u32[]{:S(2)}, u32[]{:S(2)}) collective-permute-start(f32[]{:T(128)} %add.113), channel_id=1, source_target_pairs={{0,128},{32,160},{64,192},{96,224},{128,0},{160,32},{192,64},{224,... | collective-permute-start | bytes 20 | tf_op jit(solution)/shard_map/ppermute | solution.py:17

commit v19 on v18

--- a/solution.py
+++ b/solution.py
@@ -152,9 +152,9 @@
     maxima = jnp.max(
         jnp.where(member[None, :, None, :], pscore[:, None, :, :], NEG_FILL), axis=3
     )
-    maxima_tok = jnp.sum(
-        jnp.where(member[None, :, None, :], maxima[:, :, :, None], 0.0), axis=1
-    )
+    maxima_tok = maxima[:, record_count - 1, :, None]
+    for r in range(record_count - 2, -1, -1):
+        maxima_tok = jnp.where(record[None, None, :] == r, maxima[:, r, :, None], maxima_tok)
     pool_weight = jnp.exp(pscore - maxima_tok)
     mass = jnp.sum(jnp.where(member[None, :, None, :], pool_weight[:, None], 0.0), axis=3)
     label_hot = (label_ids[0][:, None] == jnp.arange(label_count, dtype=jnp.int32)[None, :]).astype(

time: 130 us -> 129 us (level)
  other arithmetic: 14.5 us -> 13.2 us
    reduce_sum x1 -> x0, other arithmetic: 1.55 us -> none  [local(): jnp.sum(jnp.where(member[None, :, None, :], maxima[:, :, :, None], 0.0),...]
    unnamed x42 -> x43, local copies, waits for them, and re-layouts: 5.86 us -> 5.87 us
where the time goes in v19:
time: 129 us; the launch traced here: 128 us
  starting transfers between devices  35.7 us (28%)
  blocking collectives  25.3 us (20%)
  waiting for transfers between devices  18.4 us (14%)
  matrix products  15.9 us (12%)
  local copies, waits for them, and re-layouts  13.7 us (11%)
  other arithmetic  13.2 us (10%)
  between operations  5.73 us (4%)
    all_to_all x1, blocking collectives, exclusive_state_scan(): back = lax.all_to_all(sent_back, axis, 0, 0)  25.3 us
    ppermute x10, starting transfers between devices, swapped(): return lax.ppermute(x, axis, [(i, i ^ bit) for i in range(count)])  23.6 us
    all_to_all x1, starting transfers between devices, exclusive_state_scan(): got = lax.all_to_all(jnp.concatenate([slices, extra], axis=1), axis, 0, 0)  12 us
    ppermute x10, waiting for transfers between devices, swapped(): return lax.ppermute(x, axis, [(i, i ^ bit) for i in range(count)])  10.6 us
    all_to_all x1, waiting for transfers between devices, exclusive_state_scan(): got = lax.all_to_all(jnp.concatenate([slices, extra], axis=1), axis, 0, 0)  7.83 us
    unnamed x43, local copies, waits for them, and re-layouts  5.87 us
    dot_general x1, matrix products, local(): jnp.dot(features, w_query, preferred_element_type=jnp.float32)  3.28 us
    dot_general x1, matrix products, local(): jnp.einsum('hts,shd->thd', weights, v3, preferred_element_type=jnp.float32)  3.11 us
  transfers between devices with their start and end apart: 11, of which 8 were waited for; matrix products, arithmetic and copies ran while one was open for 8% of the time, Pallas kernels for 0%

profile of v19, /device:TPU:1, one launch (start us, length us, event | category | flops | bytes accessed | tf_op | source)
XLA Modules:
  0.0 127.8 jit_solution(12914549226569800214)
XLA Ops:
  0.7 0.9 fusion.60
  1.7 0.6 slice.78
  2.3 0.6 fusion.61
  3.5 0.8 fusion.41
  4.6 0.7 broadcast_compare_fusion.2
  5.3 0.6 slice.90
  6.1 1.8 %convolution_convert_fusion.1 = bf16[256,1024]{1,0:T(8,128)(2,1)S(1)} fusion(bf16[1024,1024]{1,0:T(8,128)(2,1)S(1)} %copy-done, bf16[1,256,1024]{2,1,0:T(8,128)(2,1)} %param.10), kind=kOutput, calls=%fused_computation.13 | convolution fusion | flops 537133056 | bytes 3145728 | tf_op jit(solution)/shard_map/dot_general | solution.py:116
  7.9 2.6 %convolution_convert_fusion.2 = bf16[256,1024]{1,0:T(8,128)(2,1)S(1)} fusion(bf16[1024,1024]{1,0:T(8,128)(2,1)} %param.15, bf16[1,256,1024]{2,1,0:T(8,128)(2,1)} %param.10), kind=kOutput, calls=%fused_computation.14 | convolution fusion | flops 537133056 | bytes 3145728 | tf_op jit(solution)/shard_map/dot_general | solution.py:115
  10.9 0.9 fusion.17
  12.3 0.7 convolution_multiply_fusion
  13.0 1.2 select_reduce_fusion.2
  14.2 1.4 %subtract_exponential_fusion = f32[8,512,256]{2,1,0:T(8,128)S(1)} fusion(f32[8,512,256]{2,1,0:T(8,128)S(1)} %convolution_multiply_fusion, f32[8,512]{1,0:T(8,128)S(1)} %get-tuple-element.43, f32[8,512]{1,0:T(8,128)S(1)} %get-tuple-element.44, pred[256]{0:T(512)(128)(4,1)S(1)} %get-tuple-element.37), kind=kLoop, calls=%fused_computation.4 | loop fusion | flops 2097152 | bytes 8421632 | tf_op jit(solution)/shard_map/exp | solution.py:158
  15.7 1.9 %copy-done.1 = f32[8,512,256]{2,1,0:T(8,128)} copy-done((f32[8,512,256]{2,1,0:T(8,128)}, f32[8,512,256]{2,1,0:T(8,128)S(1)}, u32[]{:S(2)}) %copy-start.1) | copy-done | bytes 4194328
  17.6 1.2 select_reduce_fusion.1
  19.6 0.7 broadcast_select_fusion
  20.7 0.9 pad_maximum_fusion
  21.6 12.0 %all-to-all-start = ((f32[32,40,128]{2,1,0:T(8,128)}), f32[32,40,128]{2,1,0:T(8,128)S(1)}, u32[]{:S(2)}, u32[]{:S(2)}) async-start(f32[32,40,128]{2,1,0:T(8,128)} %pad_maximum_fusion), calls=%async_computation | async-start | bytes 1310720 | tf_op jit(solution)/shard_map/all_to_all | solution.py:62
  33.6 2.0 %copy.106 = bf16[256,1024]{0,1:T(8,128)(2,1)} copy(bf16[256,1024]{1,0:T(8,128)(2,1)} %copy-done.3) | data formatting | bytes 1048576 | tf_op jit(solution)/shard_map/reshape | solution.py:119
  35.8 3.3 %fusion.4 = bf16[32,8,8,128]{3,2,1,0:T(8,128)(2,1)} fusion(bf16[1024,1024]{1,0:T(8,128)(2,1)} %param.14, bf16[1,256,1024]{2,1,0:T(8,128)(2,1)} %param.10), kind=kOutput, calls=%fused_computation.15 | convolution fusion | flops 537133056 | bytes 3145728 | tf_op jit(solution)/shard_map/dot_general | solution.py:114
  39.0 3.1 %fusion.1 = f32[256,8,128]{0,2,1:T(8,128)} fusion(bf16[256,8,128]{0,2,1:T(8,128)(2,1)} %bitcast.175, f32[8,256]{1,0:T(8,128)S(1)} %bitcast.183, pred[256,256]{1,0:T(8,128)(4,1)S(1)} %fusion.40, bf16[32,8,8,128]{3,2,1,0:T(8,128)(2,1)} %fusion.4, bf16[256,1024]{1,0:T(8,128)(2,1)S(1)} %copy-done.5), kind=kOutput, calls=%fused_computation.8 | convolution fusion | flops 271581184 | bytes 2695168 | tf_op jit(solution)/shard_map/hts,shd->thd/dot_general | solution.py:145
  42.1 7.8 %all-to-all-done = f32[32,40,128]{2,1,0:T(8,128)S(1)} async-done(((f32[32,40,128]{2,1,0:T(8,128)}), f32[32,40,128]{2,1,0:T(8,128)S(1)}, u32[]{:S(2)}, u32[]{:S(2)}) %all-to-all-start) | async-done | bytes 655392 | tf_op jit(solution)/shard_map/all_to_all | solution.py:62
  51.8 0.6 select_reduce_fusion.3
  52.4 0.6 fusion.19
  53.5 25.3 %all_to_all.10 = f32[32,40,128]{2,1,0:T(8,128)S(1)} all-to-all(f32[32,40,128]{2,1,0:T(8,128)S(1)} %copy.94), channel_id=1, replica_groups=mesh['dp'=8,'ctx'=32] {'ctx'}, dimensions={0} | all-to-all | bytes 1310720 | tf_op jit(solution)/shard_map/all_to_all | solution.py:84
  78.9 1.0 fusion.67
  80.3 0.7 bitcast_multiply_fusion
  81.1 1.2 select_reduce_fusion
  82.9 1.1 fusion.65
  84.0 1.2 copy.109
  85.2 1.2 copy.110
  86.5 2.8 %collective-permute-start = (f32[2,512]{1,0:T(2,128)S(1)}, f32[2,512]{1,0:T(2,128)S(1)}, u32[]{:S(2)}, u32[]{:S(2)}) collective-permute-start(f32[2,512]{1,0:T(2,128)S(1)} %fusion.52), channel_id=1, source_target_pairs={{0,1},{1,0},{2,3},{3,2},{4,5},{5,4},{6,7},{7,6},{8,9},{9,8},{10,11... | collective-permute-start | bytes 12296 | tf_op jit(solution)/shard_map/ppermute | solution.py:17
  89.3 0.9 collective-permute-start.1
  90.2 1.3 %collective-permute-start.2 = (f32[2,512]{1,0:T(2,128)S(1)}, f32[2,512]{1,0:T(2,128)S(1)}, u32[]{:S(2)}, u32[]{:S(2)}) collective-permute-start(f32[2,512]{1,0:T(2,128)S(1)} %fusion.52), channel_id=1, source_target_pairs={{0,3},{1,2},{2,1},{3,0},{4,7},{5,6},{6,5},{7,4},{8,11},{9,10},{10,... | collective-permute-start | bytes 12296 | tf_op jit(solution)/shard_map/ppermute | solution.py:17
  91.4 1.2 collective-permute-done.1
  92.6 1.8 %collective-permute-done.2 = f32[2,512]{1,0:T(2,128)S(1)} collective-permute-done((f32[2,512]{1,0:T(2,128)S(1)}, f32[2,512]{1,0:T(2,128)S(1)}, u32[]{:S(2)}, u32[]{:S(2)}) %collective-permute-start.2) | collective-permute-done | bytes 4128 | tf_op jit(solution)/shard_map/ppermute | solution.py:17
  94.4 1.7 %collective-permute-start.3 = (f32[2,512]{1,0:T(2,128)S(1)}, f32[2,512]{1,0:T(2,128)S(1)}, u32[]{:S(2)}, u32[]{:S(2)}) collective-permute-start(f32[2,512]{1,0:T(2,128)S(1)} %add_add_fusion.1), channel_id=1, source_target_pairs={{0,4},{1,5},{2,6},{3,7},{4,0},{5,1},{6,2},{7,3},{8,12},{9,13},{10,... | collective-permute-start | bytes 12296 | tf_op jit(solution)/shard_map/ppermute | solution.py:17
  96.1 4.7 %collective-permute-done.3 = f32[2,512]{1,0:T(2,128)S(1)} collective-permute-done((f32[2,512]{1,0:T(2,128)S(1)}, f32[2,512]{1,0:T(2,128)S(1)}, u32[]{:S(2)}, u32[]{:S(2)}) %collective-permute-start.3) | collective-permute-done | bytes 4128 | tf_op jit(solution)/shard_map/ppermute | solution.py:17
  100.9 0.8 collective-permute-start.4
  101.7 1.6 %collective-permute-start.5 = (f32[2,512]{1,0:T(2,128)S(1)}, f32[2,512]{1,0:T(2,128)S(1)}, u32[]{:S(2)}, u32[]{:S(2)}) collective-permute-start(f32[2,512]{1,0:T(2,128)S(1)} %add.107), channel_id=1, source_target_pairs={{0,16},{1,17},{2,18},{3,19},{4,20},{5,21},{6,22},{7,23},{8,24},{9,... | collective-permute-start | bytes 12296 | tf_op jit(solution)/shard_map/ppermute | solution.py:17
  103.3 1.5 %collective-permute-start.6 = (f32[2,512]{1,0:T(2,128)S(1)}, f32[2,512]{1,0:T(2,128)S(1)}, u32[]{:S(2)}, u32[]{:S(2)}) collective-permute-start(f32[2,512]{1,0:T(2,128)S(1)} %add.107), channel_id=1, source_target_pairs={{0,24},{1,25},{2,26},{3,27},{4,28},{5,29},{6,30},{7,31},{8,16},{9,... | collective-permute-start | bytes 12296 | tf_op jit(solution)/shard_map/ppermute | solution.py:17
  105.1 1.0 copy.102
  106.1 0.8 collective-permute-done.6
  106.9 0.7 fusion.58
  107.6 1.1 multiply_reduce_fusion.1
  108.8 7.5 %collective-permute-start.7 = (f32[]{:T(128)}, f32[]{:T(128)}, u32[]{:S(2)}, u32[]{:S(2)}) collective-permute-start(f32[]{:T(128)} %get-tuple-element.39), channel_id=1, source_target_pairs={{0,32},{32,0},{64,96},{96,64},{128,160},{160,128},{192,224},{224,1... | collective-permute-start | bytes 20 | tf_op jit(solution)/shard_map/ppermute | solution.py:17
  116.3 1.0 collective-permute-done.7
  118.6 2.0 %collective-permute-start.8 = (f32[]{:T(128)}, f32[]{:T(128)}, u32[]{:S(2)}, u32[]{:S(2)}) collective-permute-start(f32[]{:T(128)} %add.116), channel_id=1, source_target_pairs={{0,64},{32,96},{64,0},{96,32},{128,192},{160,224},{192,128},{224,1... | collective-permute-start | bytes 20 | tf_op jit(solution)/shard_map/ppermute | solution.py:17
  121.9 3.6 %collective-permute-start.9 = (f32[]{:T(128)}, f32[]{:T(128)}, u32[]{:S(2)}, u32[]{:S(2)}) collective-permute-start(f32[]{:T(128)} %add.117), channel_id=1, source_target_pairs={{0,128},{32,160},{64,192},{96,224},{128,0},{160,32},{192,64},{224,... | collective-permute-start | bytes 20 | tf_op jit(solution)/shard_map/ppermute | solution.py:17
  (93 shorter events, 7.3 us)
Async XLA Ops:
  0.6 5.4 %copy-start = (bf16[1024,1024]{1,0:T(8,128)(2,1)S(1)}, bf16[1024,1024]{1,0:T(8,128)(2,1)}, u32[]{:S(2)}) copy-start(bf16[1024,1024]{1,0:T(8,128)(2,1)} %param.16) | copy-start | bytes 6291460
  7.8 3.9 %copy-start.3 = (bf16[256,1024]{1,0:T(8,128)(2,1)}, bf16[256,1024]{1,0:T(8,128)(2,1)S(1)}, u32[]{:S(2)}) copy-start(bf16[256,1024]{1,0:T(8,128)(2,1)S(1)} %convolution_convert_fusion.1) | copy-start | bytes 1572868
  10.5 1.3 copy-start.4
  10.9 1.1 copy-start.9
  10.9 1.4 %copy-start.8 = (bf16[512,1024]{1,0:T(8,128)(2,1)S(1)}, bf16[512,1024]{1,0:T(8,128)(2,1)}, u32[]{:S(2)}) copy-start(bf16[512,1024]{1,0:T(8,128)(2,1)} %param.18) | copy-start | bytes 3145732
  15.7 1.9 %copy-start.1 = (f32[8,512,256]{2,1,0:T(8,128)}, f32[8,512,256]{2,1,0:T(8,128)S(1)}, u32[]{:S(2)}) copy-start(f32[8,512,256]{2,1,0:T(8,128)S(1)} %subtract_exponential_fusion) | copy-start | bytes 12582916
  17.6 1.2 copy-start.12
  19.6 19.4 %copy-start.5 = (bf16[256,1024]{1,0:T(8,128)(2,1)S(1)}, bf16[256,1024]{1,0:T(8,128)(2,1)}, u32[]{:S(2)}) copy-start(bf16[256,1024]{1,0:T(8,128)(2,1)} %copy-done.4) | copy-start | bytes 1572868
  21.6 28.4 %all-to-all-start = ((f32[32,40,128]{2,1,0:T(8,128)}), f32[32,40,128]{2,1,0:T(8,128)S(1)}, u32[]{:S(2)}, u32[]{:S(2)}) async-start(f32[32,40,128]{2,1,0:T(8,128)} %pad_maximum_fusion), calls=%async_computation | async-start | bytes 1310720 | tf_op jit(solution)/shard_map/all_to_all | solution.py:62
  51.5 27.4 %copy-start.10 = (bf16[32,8,8,128]{3,2,1,0:T(8,128)(2,1)S(1)}, bf16[32,8,8,128]{3,2,1,0:T(8,128)(2,1)}, u32[]{:S(2)}) copy-start(bf16[32,8,8,128]{3,2,1,0:T(8,128)(2,1)} %fusion.4) | copy-start | bytes 1572868
  51.7 27.2 %copy-start.7 = (f32[256,8,128]{0,2,1:T(8,128)S(1)}, f32[256,8,128]{0,2,1:T(8,128)}, u32[]{:S(2)}) copy-start(f32[256,8,128]{0,2,1:T(8,128)} %fusion.1) | copy-start | bytes 3145732
  53.1 27.0 %copy-start.11 = (f32[1024]{0:T(1024)S(1)}, f32[1024]{0:T(1024)}, u32[]{:S(2)}) copy-start(f32[1024]{0:T(1024)} %param.17) | copy-start | bytes 12292
  53.5 26.8 %copy-start.2 = (f32[8,512,256]{2,1,0:T(8,128)S(1)}, f32[8,512,256]{2,1,0:T(8,128)}, u32[]{:S(2)}) copy-start(f32[8,512,256]{2,1,0:T(8,128)} %copy-done.1) | copy-start | bytes 12582916
  53.5 26.8 %copy-start.6 = (bf16[512,1024]{1,0:T(8,128)(2,1)S(1)}, bf16[512,1024]{1,0:T(8,128)(2,1)}, u32[]{:S(2)}) copy-start(bf16[512,1024]{1,0:T(8,128)(2,1)} %param.19) | copy-start | bytes 3145732
  81.0 15.1 %copy-start.13 = (s32[1,2]{1,0:T(1,128)S(1)}, s32[1,2]{1,0:T(1,128)}, u32[]{:S(2)}) copy-start(s32[1,2]{1,0:T(1,128)} %param.12) | copy-start | bytes 28
  86.5 4.9 %collective-permute-start = (f32[2,512]{1,0:T(2,128)S(1)}, f32[2,512]{1,0:T(2,128)S(1)}, u32[]{:S(2)}, u32[]{:S(2)}) collective-permute-start(f32[2,512]{1,0:T(2,128)S(1)} %fusion.52), channel_id=1, source_target_pairs={{0,1},{1,0},{2,3},{3,2},{4,5},{5,4},{6,7},{7,6},{8,9},{9,8},{10,11... | collective-permute-start | bytes 12296 | tf_op jit(solution)/shard_map/ppermute | solution.py:17
  89.3 3.4 %collective-permute-start.1 = (f32[2,512]{1,0:T(2,128)S(1)}, f32[2,512]{1,0:T(2,128)S(1)}, u32[]{:S(2)}, u32[]{:S(2)}) collective-permute-start(f32[2,512]{1,0:T(2,128)S(1)} %fusion.52), channel_id=1, source_target_pairs={{0,2},{1,3},{2,0},{3,1},{4,6},{5,7},{6,4},{7,5},{8,10},{9,11},{10,... | collective-permute-start | bytes 12296 | tf_op jit(solution)/shard_map/ppermute | solution.py:17
  90.2 4.3 %collective-permute-start.2 = (f32[2,512]{1,0:T(2,128)S(1)}, f32[2,512]{1,0:T(2,128)S(1)}, u32[]{:S(2)}, u32[]{:S(2)}) collective-permute-start(f32[2,512]{1,0:T(2,128)S(1)} %fusion.52), channel_id=1, source_target_pairs={{0,3},{1,2},{2,1},{3,0},{4,7},{5,6},{6,5},{7,4},{8,11},{9,10},{10,... | collective-permute-start | bytes 12296 | tf_op jit(solution)/shard_map/ppermute | solution.py:17
  94.4 6.4 %collective-permute-start.3 = (f32[2,512]{1,0:T(2,128)S(1)}, f32[2,512]{1,0:T(2,128)S(1)}, u32[]{:S(2)}, u32[]{:S(2)}) collective-permute-start(f32[2,512]{1,0:T(2,128)S(1)} %add_add_fusion.1), channel_id=1, source_target_pairs={{0,4},{1,5},{2,6},{3,7},{4,0},{5,1},{6,2},{7,3},{8,12},{9,13},{10,... | collective-permute-start | bytes 12296 | tf_op jit(solution)/shard_map/ppermute | solution.py:17
  100.9 5.2 %collective-permute-start.4 = (f32[2,512]{1,0:T(2,128)S(1)}, f32[2,512]{1,0:T(2,128)S(1)}, u32[]{:S(2)}, u32[]{:S(2)}) collective-permute-start(f32[2,512]{1,0:T(2,128)S(1)} %add.107), channel_id=1, source_target_pairs={{0,8},{1,9},{2,10},{3,11},{4,12},{5,13},{6,14},{7,15},{8,0},{9,1},... | collective-permute-start | bytes 12296 | tf_op jit(solution)/shard_map/ppermute | solution.py:17
  101.7 4.4 %collective-permute-start.5 = (f32[2,512]{1,0:T(2,128)S(1)}, f32[2,512]{1,0:T(2,128)S(1)}, u32[]{:S(2)}, u32[]{:S(2)}) collective-permute-start(f32[2,512]{1,0:T(2,128)S(1)} %add.107), channel_id=1, source_target_pairs={{0,16},{1,17},{2,18},{3,19},{4,20},{5,21},{6,22},{7,23},{8,24},{9,... | collective-permute-start | bytes 12296 | tf_op jit(solution)/shard_map/ppermute | solution.py:17
  103.3 3.7 %collective-permute-start.6 = (f32[2,512]{1,0:T(2,128)S(1)}, f32[2,512]{1,0:T(2,128)S(1)}, u32[]{:S(2)}, u32[]{:S(2)}) collective-permute-start(f32[2,512]{1,0:T(2,128)S(1)} %add.107), channel_id=1, source_target_pairs={{0,24},{1,25},{2,26},{3,27},{4,28},{5,29},{6,30},{7,31},{8,16},{9,... | collective-permute-start | bytes 12296 | tf_op jit(solution)/shard_map/ppermute | solution.py:17
  108.8 8.5 %collective-permute-start.7 = (f32[]{:T(128)}, f32[]{:T(128)}, u32[]{:S(2)}, u32[]{:S(2)}) collective-permute-start(f32[]{:T(128)} %get-tuple-element.39), channel_id=1, source_target_pairs={{0,32},{32,0},{64,96},{96,64},{128,160},{160,128},{192,224},{224,1... | collective-permute-start | bytes 20 | tf_op jit(solution)/shard_map/ppermute | solution.py:17
  118.6 2.6 %collective-permute-start.8 = (f32[]{:T(128)}, f32[]{:T(128)}, u32[]{:S(2)}, u32[]{:S(2)}) collective-permute-start(f32[]{:T(128)} %add.116), channel_id=1, source_target_pairs={{0,64},{32,96},{64,0},{96,32},{128,192},{160,224},{192,128},{224,1... | collective-permute-start | bytes 20 | tf_op jit(solution)/shard_map/ppermute | solution.py:17
  121.9 4.1 %collective-permute-start.9 = (f32[]{:T(128)}, f32[]{:T(128)}, u32[]{:S(2)}, u32[]{:S(2)}) collective-permute-start(f32[]{:T(128)} %add.117), channel_id=1, source_target_pairs={{0,128},{32,160},{64,192},{96,224},{128,0},{160,32},{192,64},{224,... | collective-permute-start | bytes 20 | tf_op jit(solution)/shard_map/ppermute | solution.py:17
